TPU v7x, 512 devices: a whole 4x8x8 slice. The times are simulated.
512 devices in a mesh: tm: 16 (over y_lo, x), space: 32 (over z, y_hi, core).
Axes of the slice: x: 4, y: 8 (y_hi: 2, y_lo: 4; y = y_hi * 4 + y_lo), z: 8, core: 2. Of those that a mesh axis runs over, the one named last changes fastest.
Arguments:
- frames: bfloat16 [16, 64, 96, 384], P('tm', 'space'), may hold values from -8 to 8
- cache_in: bfloat16 [2, 64, 96, 384], P(None, 'space'), may hold values from -6 to 6
- norm_gain: bfloat16 [384], replicated, may hold values from 0.5 to 1.5
- w_qkv: bfloat16 [384, 1152], replicated, may hold values from -0.5 to 0.5
- b_qkv: bfloat16 [1152], replicated, may hold values from -3 to 3
- w_proj: bfloat16 [384, 384], replicated, may hold values from -1.25 to 1.25
- b_proj: bfloat16 [384], replicated, may hold values from -2 to 2
- w_time: bfloat16 [3, 384, 768], replicated, may hold values from -0.1875 to 0.1875
- b_time: bfloat16 [768], replicated, may hold values from -3 to 3
- w_space: bfloat16 [3, 3, 384, 192], replicated, may hold values from -0.109375 to 0.109375
- b_space: bfloat16 [192], replicated, may hold values from -3 to 3
Outputs:
- decoded: bfloat16 [32, 128, 192, 192], P('tm', 'space')
All inputs are finite; a program needn't handle non-finite values.
Results may differ from a plain program's by a relative error of at most 0.01.
Values may be sent and summed in bfloat16 or wider, within the bound.
No kernel may reach another device: no remote copies, remote signals or barrier semaphores. Data moves between devices by JAX's collectives and lax.ppermute only.
A program may use at most 64 MiB of HBM per device.

v0:
```python
import jax
import jax.numpy as jnp
from jax import lax
from jax.sharding import PartitionSpec as P

EPSILON = 1e-06


def shifted(value, axis, steps):
    count = lax.axis_size(axis)
    leading, last = (max(0, -steps), min(count, count - steps))
    return lax.ppermute(value, axis, [(source, source + steps) for source in range(leading, last)])


def with_halo(block, sides, width):
    for axis, dim in sides:
        count = lax.axis_size(axis)
        forward = [(i, i + 1) for i in range(count - 1)]
        backward = [(target, source) for source, target in forward]
        low = lax.ppermute(
            lax.slice_in_dim(block, block.shape[dim] - width, None, axis=dim), axis, forward
        )
        high = lax.ppermute(lax.slice_in_dim(block, 0, width, axis=dim), axis, backward)
        block = jnp.concatenate([low, block, high], axis=dim)
    return block


def normalize(frames, norm_gain):
    widened = frames.astype(jnp.float32)
    inverse = lax.rsqrt(jnp.mean(widened * widened, axis=-1, keepdims=True) + EPSILON)
    return (widened * inverse * norm_gain.astype(jnp.float32)).astype(jnp.bfloat16)


def project(rows, weight, bias):
    return (
        jnp.dot(rows, weight, preferred_element_type=jnp.float32) + bias.astype(jnp.float32)
    ).astype(jnp.bfloat16)


def attend(running, queries, key_rows, value_rows):
    best, mass, total_sum = running
    scores = lax.dot_general(
        queries, key_rows, (((1,), (1,)), ((), ())), preferred_element_type=jnp.float32
    ) * queries.shape[1] ** (-0.5)
    new_best = jnp.maximum(best, jnp.max(scores, axis=1, keepdims=True))
    weights = jnp.exp(scores - new_best)
    mass = jnp.sum(weights, axis=1, keepdims=True)
    total_sum = jnp.dot(
        weights.astype(jnp.bfloat16), value_rows, preferred_element_type=jnp.float32
    )
    return (new_best, mass, total_sum)


def body(
    frames, cache_in, norm_gain, w_qkv, b_qkv, w_proj, b_proj, w_time, b_time, w_space, b_space
):
    channels = frames.shape[-1]
    rows = frames.shape[1]
    width = frames.shape[2]
    normed = normalize(frames, norm_gain).reshape(-1, channels)
    queries = project(normed, w_qkv[:, :channels], b_qkv[:channels])
    count = queries.shape[0]
    start_state = (
        jnp.full((count, 1), -1e30, jnp.float32),
        jnp.zeros((count, 1), jnp.float32),
        jnp.zeros((count, channels), jnp.float32),
    )
    key_rows = project(normed, w_qkv[:, channels : 2 * channels], b_qkv[channels : 2 * channels])
    value_rows = project(normed, w_qkv[:, 2 * channels :], b_qkv[2 * channels :])
    final = attend(
        start_state,
        queries,
        lax.all_gather(key_rows, "space", axis=0, tiled=True),
        lax.all_gather(value_rows, "space", axis=0, tiled=True),
    )
    mixed = (final[2] / final[1]).astype(jnp.bfloat16)
    hidden = (
        frames.reshape(-1, channels).astype(jnp.float32)
        + jnp.dot(mixed, w_proj, preferred_element_type=jnp.float32)
        + b_proj.astype(jnp.float32)
    ).astype(jnp.bfloat16)
    position = lax.axis_index("tm")
    carried = cache_in.reshape(2, -1, channels)
    near_frame = shifted(hidden, "tm", 1)
    near_frame = jnp.where(position == 0, carried[1], near_frame)
    far_frame = shifted(near_frame, "tm", 1)
    far_frame = jnp.where(position == 0, carried[0], far_frame)
    timed = b_time.astype(jnp.float32) + jnp.dot(
        far_frame, w_time[0], preferred_element_type=jnp.float32
    )
    timed = timed + jnp.dot(near_frame, w_time[1], preferred_element_type=jnp.float32)
    timed = (timed + jnp.dot(hidden, w_time[2], preferred_element_type=jnp.float32)).astype(
        jnp.bfloat16
    )
    paired = jnp.stack([timed[:, :channels], timed[:, channels:]]).reshape(2, rows, width, channels)
    padded = with_halo(paired, (("space", 1),), 1)
    upsampled = jnp.repeat(jnp.repeat(padded, 2, axis=1)[:, 1 : 2 * rows + 3], 2, axis=2)
    upsampled = jnp.pad(upsampled, ((0, 0), (0, 0), (1, 1), (0, 0)))
    out_channels = w_space.shape[-1]
    result = jnp.zeros((8 * rows * width, out_channels), jnp.float32) + b_space.astype(jnp.float32)
    for row_tap in range(3):
        for col_tap in range(3):
            window = upsampled[
                :, row_tap : row_tap + 2 * rows, col_tap : col_tap + 2 * width
            ].reshape(-1, channels)
            result = result + jnp.dot(
                window, w_space[row_tap, col_tap], preferred_element_type=jnp.float32
            )
    return result.astype(jnp.bfloat16).reshape(2, 2 * rows, 2 * width, out_channels)


def solution(mesh):
    return jax.shard_map(
        body,
        mesh=mesh,
        in_specs=(
            P("tm", "space", None, None),
            P(None, "space", None, None),
            P(),
            P(),
            P(),
            P(),
            P(),
            P(),
            P(),
            P(),
            P(),
        ),
        out_specs=P("tm", "space", None, None),
        check_vma=False,
    )
```

profile of v0, /device:TPU:41, one launch (start us, length us, event | category | flops | bytes accessed | tf_op | source)
XLA Modules:
  0.0 299.0 jit_solution(5765174925009961391)
XLA Ops:
  6.5 0.0 copy-start
  6.5 0.0 all-gather.3.cloned.1.call-start
  6.6 1.1 multiply_reduce_fusion
  7.7 0.7 convert_element_type.64
  8.4 0.8 slice_convert_fusion.2
  9.2 1.0 multiply_convert_fusion
  10.2 1.9 fusion.11
  12.1 0.0 all-gather.3.cloned.1.call-update
  12.1 0.0 all-gather.5.cloned.1.call-start
  12.2 0.0 copy-done.5
  12.2 0.9 fusion.12
  13.1 0.0 all-gather.5.cloned.1.call-update
  13.1 0.0 copy-done.7
  13.1 0.0 copy-done.6
  13.2 109.9 %all-gather.3.cloned.1.call-done = bf16[6144,384]{1,0:T(8,128)(2,1)} async-done(((bf16[192,384]{1,0:T(8,128)(2,1)}), bf16[6144,384]{1,0:T(8,128)(2,1)}) %all-gather.3.cloned.1.call-update) | async-done | bytes 4718608 | tf_op jit(solution)/shard_map/all_gather | solution.py:73
  123.1 6.6 %fusion.57 = (f32[192]{0:T(256)S(1)}, f32[192,6144]{1,0:T(8,128)}) fusion(bf16[6144,384]{1,0:T(8,128)(2,1)} %all-gather.3.cloned.1.call-done, bf16[192,384]{1,0:T(8,128)(2,1)S(1)} %bitcast.91, bf16[384,1152]{1,0:T(8,128)(2,1)S(1)} %copy-done.5, f32[384]{0:T(512)S(1)} %get-tuple-element.20), kind=kOutput, calls=%fused_computation.84 | convolution fusion | flops 965099328 | bytes 9882368 | tf_op jit(solution)/shard_map/dot_general | solution.py:42
  129.7 3.2 %fusion = f32[192]{0:T(256)S(1)} fusion(f32[192,6144]{1,0:T(8,128)} %get-tuple-element.24, f32[192]{0:T(256)S(1)} %broadcast_maximum_fusion), kind=kLoop, calls=%fused_computation.2 | loop fusion | flops 2359104 | bytes 4720128 | tf_op jit(solution)/shard_map/reduce_sum | solution.py:47
  132.9 97.4 %all-gather.5.cloned.1.call-done = bf16[6144,384]{1,0:T(8,128)(2,1)} async-done(((bf16[192,384]{1,0:T(8,128)(2,1)}), bf16[6144,384]{1,0:T(8,128)(2,1)}) %all-gather.5.cloned.1.call-update) | async-done | bytes 4718608 | tf_op jit(solution)/shard_map/all_gather | solution.py:74
  230.3 5.5 %fusion.13 = bf16[192,384]{1,0:T(8,128)(2,1)S(1)} fusion(bf16[384,384]{1,0:T(8,128)(2,1)S(1)} %copy-done, bf16[6144,384]{1,0:T(8,128)(2,1)} %all-gather.5.cloned.1.call-done, f32[192,6144]{1,0:T(8,128)} %get-tuple-element.24, f32[192]{0:T(256)S(1)} %broadcast_maximum_fusion, f32[384]{0:T(512)S(1)} %convert_element_type.74, f32[192]{0:T(256)S(1)} %fusion, ...), kind=kOutput, calls=%fused_computation.28 | convolution fusion | flops 965394432 | bytes 10030080 | tf_op jit(solution)/shard_map/dot_general | solution.py:79
  235.8 3.1 %collective-permute-start = (bf16[192,384]{1,0:T(8,128)(2,1)S(1)}, bf16[192,384]{1,0:T(8,128)(2,1)S(1)}, u32[]{:S(2)}, u32[]{:S(2)}) collective-permute-start(bf16[192,384]{1,0:T(8,128)(2,1)S(1)} %fusion.13), channel_id=1, source_target_pairs={{0,32},{32,64},{64,96},{96,128},{128,160},{160,192},{192,224},{224... | collective-permute-start | bytes 442376 | tf_op jit(solution)/shard_map/ppermute | solution.py:12
  238.9 0.3 fusion.22
  239.2 5.7 %collective-permute-done = bf16[192,384]{1,0:T(8,128)(2,1)S(1)} collective-permute-done((bf16[192,384]{1,0:T(8,128)(2,1)S(1)}, bf16[192,384]{1,0:T(8,128)(2,1)S(1)}, u32[]{:S(2)}, u32[]{:S(2)}) %collective-permute-start) | collective-permute-done | bytes 147488 | tf_op jit(solution)/shard_map/ppermute | solution.py:12
  245.0 1.9 collective-permute-start.1
  246.9 0.3 fusion.24
  247.2 5.8 %collective-permute-done.1 = bf16[192,384]{1,0:T(8,128)(2,1)S(1)} collective-permute-done((bf16[192,384]{1,0:T(8,128)(2,1)S(1)}, bf16[192,384]{1,0:T(8,128)(2,1)S(1)}, u32[]{:S(2)}, u32[]{:S(2)}) %collective-permute-start.1) | collective-permute-done | bytes 147488 | tf_op jit(solution)/shard_map/ppermute | solution.py:12
  253.0 0.0 copy-start.8
  253.0 0.3 fusion.8
  253.5 8.8 %collective-permute-start.2 = (bf16[2,1,96,384]{3,2,1,0:T(8,128)(2,1)S(1)}, bf16[2,1,96,384]{3,2,1,0:T(8,128)(2,1)S(1)}, u32[]{:S(2)}, u32[]{:S(2)}) collective-permute-start(bf16[2,1,96,384]{3,2,1,0:T(8,128)(2,1)S(1)} %get-tuple-element.14), channel_id=1, source_target_pairs={{0,1},{1,2},{2,3},{3,4},{4,5},{5,6},{6,7},{7,8},{8,9},{9,10},{10,1... | collective-permute-start | bytes 442376 | tf_op jit(solution)/shard_map/ppermute | solution.py:20
  262.2 2.1 collective-permute-start.3
  264.4 1.3 collective-permute-done.2
  265.7 9.4 %collective-permute-done.3 = bf16[2,1,96,384]{3,2,1,0:T(8,128)(2,1)S(1)} collective-permute-done((bf16[2,1,96,384]{3,2,1,0:T(8,128)(2,1)S(1)}, bf16[2,1,96,384]{3,2,1,0:T(8,128)(2,1)S(1)}, u32[]{:S(2)}, u32[]{:S(2)}) %collective-permute-start.3) | collective-permute-done | bytes 147488 | tf_op jit(solution)/shard_map/ppermute | solution.py:23
  275.1 0.1 pad_maximum_fusion
  275.2 0.1 broadcast_in_dim.7
  275.3 0.1 slice.145
  275.4 2.3 broadcast_in_dim.8
  277.7 4.0 %reshape.81 = bf16[2,6,192,384]{3,2,1,0:T(8,128)(2,1)S(1)} reshape(bf16[2,6,96,2,384]{4,3,2,1,0:T(2,128)(2,1)} %broadcast_in_dim.8) | data formatting | bytes 3538944 | tf_op jit(solution)/shard_map/reshape | solution.py:97
  281.7 0.0 copy-start.2
  281.7 4.0 %pad_slice_fusion = (bf16[2,4,192,384]{3,2,1,0:T(8,128)(2,1)S(1)}, bf16[2,4,192,384]{3,2,1,0:T(8,128)(2,1)S(1)}, bf16[2,4,192,384]{3,2,1,0:T(8,128)(2,1)S(1)}, b...) fusion(bf16[2,6,192,384]{3,2,1,0:T(8,128)(2,1)S(1)} %reshape.81), kind=kLoop, calls=%fused_computation.31 | loop fusion | bytes 15925248 | tf_op jit(solution)/shard_map/slice | solution.py:103
  285.7 0.6 convolution_add_fusion.8
  286.3 0.6 convolution_add_fusion.7
  286.9 0.6 convolution_add_fusion.6
  287.5 0.6 convolution_add_fusion.5
  288.0 0.6 convolution_add_fusion.4
  288.6 0.6 convolution_add_fusion.3
  289.2 0.6 convolution_add_fusion.2
  289.8 0.6 convolution_add_fusion.1
  290.4 0.6 fusion.2
  291.0 1.2 copy.13
  (22 shorter events, 0.2 us)
Async XLA Ops:
  6.5 223.7 %copy-start = (bf16[384,384]{1,0:T(8,128)(2,1)S(1)}, bf16[384,384]{1,0:T(8,128)(2,1)}, u32[]{:S(2)}) copy-start(bf16[384,384]{1,0:T(8,128)(2,1)} %param.16) | copy-start | bytes 884740
  6.5 5.6 %copy-start.5 = (bf16[384,1152]{1,0:T(8,128)(2,1)S(1)}, bf16[384,1152]{1,0:T(8,128)(2,1)}, u32[]{:S(2)}) copy-start(bf16[384,1152]{1,0:T(8,128)(2,1)} %param.14) | copy-start | bytes 2654212
  6.5 6.6 %copy-start.7 = (bf16[384]{0:T(512)(128)(2,1)S(1)}, bf16[384]{0:T(512)(128)(2,1)}, u32[]{:S(2)}) copy-start(bf16[384]{0:T(512)(128)(2,1)} %param.17) | copy-start | bytes 2308
  6.5 6.6 %copy-start.6 = (bf16[768]{0:T(1024)(128)(2,1)S(1)}, bf16[768]{0:T(1024)(128)(2,1)}, u32[]{:S(2)}) copy-start(bf16[768]{0:T(1024)(128)(2,1)} %param.19) | copy-start | bytes 4612
  6.5 6.6 %copy-start.4 = (bf16[2,2,96,384]{3,2,1,0:T(8,128)(2,1)S(1)}, bf16[2,2,96,384]{3,2,1,0:T(8,128)(2,1)}, u32[]{:S(2)}) copy-start(bf16[2,2,96,384]{3,2,1,0:T(8,128)(2,1)} %param.12) | copy-start | bytes 884740
  6.5 116.6 %all-gather.3.cloned.1.call-start = ((), (), s32[]{:S(2)}) async-start(), calls=%async_computation | async-start | bytes 4866048 | tf_op jit(solution)/shard_map/all_gather | solution.py:73
  12.1 218.1 %all-gather.5.cloned.1.call-start = ((), (), s32[]{:S(2)}) async-start(), calls=%async_computation.1 | async-start | bytes 4866048 | tf_op jit(solution)/shard_map/all_gather | solution.py:74
  129.7 100.6 %copy-start.3 = (bf16[1,2,96,384]{3,2,1,0:T(8,128)(2,1)S(1)}, bf16[1,2,96,384]{3,2,1,0:T(8,128)(2,1)}, u32[]{:S(2)}) copy-start(bf16[1,2,96,384]{3,2,1,0:T(8,128)(2,1)} %param.11) | copy-start | bytes 442372
  230.3 8.6 %copy-start.1 = (bf16[3,384,768]{2,1,0:T(8,128)(2,1)S(1)}, bf16[3,384,768]{2,1,0:T(8,128)(2,1)}, u32[]{:S(2)}) copy-start(bf16[3,384,768]{2,1,0:T(8,128)(2,1)} %param.18) | copy-start | bytes 5308420
  235.8 9.1 %collective-permute-start = (bf16[192,384]{1,0:T(8,128)(2,1)S(1)}, bf16[192,384]{1,0:T(8,128)(2,1)S(1)}, u32[]{:S(2)}, u32[]{:S(2)}) collective-permute-start(bf16[192,384]{1,0:T(8,128)(2,1)S(1)} %fusion.13), channel_id=1, source_target_pairs={{0,32},{32,64},{64,96},{96,128},{128,160},{160,192},{192,224},{224... | collective-permute-start | bytes 442376 | tf_op jit(solution)/shard_map/ppermute | solution.py:12
  245.0 8.0 %collective-permute-start.1 = (bf16[192,384]{1,0:T(8,128)(2,1)S(1)}, bf16[192,384]{1,0:T(8,128)(2,1)S(1)}, u32[]{:S(2)}, u32[]{:S(2)}) collective-permute-start(bf16[192,384]{1,0:T(8,128)(2,1)S(1)} %bitcast_select_fusion), channel_id=1, source_target_pairs={{0,32},{32,64},{64,96},{96,128},{128,160},{160,192},{192,224},{224... | collective-permute-start | bytes 442376 | tf_op jit(solution)/shard_map/ppermute | solution.py:12
  253.0 11.3 %copy-start.8 = (bf16[192]{0:T(256)(128)(2,1)S(1)}, bf16[192]{0:T(256)(128)(2,1)}, u32[]{:S(2)}) copy-start(bf16[192]{0:T(256)(128)(2,1)} %param.21) | copy-start | bytes 1156
  253.5 12.2 %collective-permute-start.2 = (bf16[2,1,96,384]{3,2,1,0:T(8,128)(2,1)S(1)}, bf16[2,1,96,384]{3,2,1,0:T(8,128)(2,1)S(1)}, u32[]{:S(2)}, u32[]{:S(2)}) collective-permute-start(bf16[2,1,96,384]{3,2,1,0:T(8,128)(2,1)S(1)} %get-tuple-element.14), channel_id=1, source_target_pairs={{0,1},{1,2},{2,3},{3,4},{4,5},{5,6},{6,7},{7,8},{8,9},{9,10},{10,1... | collective-permute-start | bytes 442376 | tf_op jit(solution)/shard_map/ppermute | solution.py:20
  262.2 12.8 %collective-permute-start.3 = (bf16[2,1,96,384]{3,2,1,0:T(8,128)(2,1)S(1)}, bf16[2,1,96,384]{3,2,1,0:T(8,128)(2,1)S(1)}, u32[]{:S(2)}, u32[]{:S(2)}) collective-permute-start(bf16[2,1,96,384]{3,2,1,0:T(8,128)(2,1)S(1)} %get-tuple-element.15), channel_id=1, source_target_pairs={{1,0},{2,1},{3,2},{4,3},{5,4},{6,5},{7,6},{8,7},{9,8},{10,9},{11,1... | collective-permute-start | bytes 442376 | tf_op jit(solution)/shard_map/ppermute | solution.py:23
  281.7 4.0 %copy-start.2 = (bf16[3,3,384,192]{2,3,1,0:T(8,128)(2,1)S(1)}, bf16[3,3,384,192]{2,3,1,0:T(8,128)(2,1)}, u32[]{:S(2)}) copy-start(bf16[3,3,384,192]{2,3,1,0:T(8,128)(2,1)} %param.20) | copy-start | bytes 3981316
Sparse Core Ops, SparseCore 0:
  12.2 110.8 all-gather.2
  126.5 103.7 all-gather.4
where the time goes:
time: 299 us
  waiting for transfers between devices  230 us (77%)
  matrix products  21 us (7%)
  starting transfers between devices  16 us (5%)
  between operations  13.7 us (5%)
  local copies, waits for them, and re-layouts  11.8 us (4%)
  other arithmetic  7.01 us (2%)
    all_gather x1, waiting for transfers between devices, body(): lax.all_gather(key_rows, 'space', axis=0, tiled=True)  110 us
    all_gather x1, waiting for transfers between devices, body(): lax.all_gather(value_rows, 'space', axis=0, tiled=True)  97.4 us
    ppermute x2, waiting for transfers between devices, shifted(): lax.ppermute(value, axis, [(source, source + steps) for source in range(l...  11.5 us
    ppermute x1, waiting for transfers between devices, with_halo(): lax.ppermute(lax.slice_in_dim(block, 0, width, axis=dim), axis, backward)  9.36 us
    ppermute x1, starting transfers between devices, with_halo(): lax.ppermute(lax.slice_in_dim(block, block.shape[dim] - width, None, axis...  8.77 us
    dot_general x1, matrix products, attend(): lax.dot_general(queries, key_rows, (((1,), (1,)), ((), ())), preferred_el...  6.56 us
  transfers between devices with their start and end apart: 6, of which 6 were waited for; matrix products, arithmetic and copies ran while one was open for 4% of the time, Pallas kernels for 0%

commit v1 on v0

--- a/solution.py
+++ b/solution.py
@@ -57,6 +57,7 @@
     channels = frames.shape[-1]
     rows = frames.shape[1]
     width = frames.shape[2]
+    whole = lax.all_gather(frames.reshape(-1, channels), "space", axis=0, tiled=True)
     normed = normalize(frames, norm_gain).reshape(-1, channels)
     queries = project(normed, w_qkv[:, :channels], b_qkv[:channels])
     count = queries.shape[0]
@@ -65,14 +66,10 @@
         jnp.zeros((count, 1), jnp.float32),
         jnp.zeros((count, channels), jnp.float32),
     )
-    key_rows = project(normed, w_qkv[:, channels : 2 * channels], b_qkv[channels : 2 * channels])
-    value_rows = project(normed, w_qkv[:, 2 * channels :], b_qkv[2 * channels :])
-    final = attend(
-        start_state,
-        queries,
-        lax.all_gather(key_rows, "space", axis=0, tiled=True),
-        lax.all_gather(value_rows, "space", axis=0, tiled=True),
-    )
+    normed_all = normalize(whole, norm_gain)
+    key_rows = project(normed_all, w_qkv[:, channels : 2 * channels], b_qkv[channels : 2 * channels])
+    value_rows = project(normed_all, w_qkv[:, 2 * channels :], b_qkv[2 * channels :])
+    final = attend(start_state, queries, key_rows, value_rows)
     mixed = (final[2] / final[1]).astype(jnp.bfloat16)
     hidden = (
         frames.reshape(-1, channels).astype(jnp.float32)
@@ -83,7 +80,8 @@
     carried = cache_in.reshape(2, -1, channels)
     near_frame = shifted(hidden, "tm", 1)
     near_frame = jnp.where(position == 0, carried[1], near_frame)
-    far_frame = shifted(near_frame, "tm", 1)
+    far_frame = shifted(hidden, "tm", 2)
+    far_frame = jnp.where(position == 1, carried[1], far_frame)
     far_frame = jnp.where(position == 0, carried[0], far_frame)
     timed = b_time.astype(jnp.float32) + jnp.dot(
         far_frame, w_time[0], preferred_element_type=jnp.float32

time: 299 us -> 204 us (0.68)
  the two profiles are of different devices: /device:TPU:41 before, /device:TPU:49 now
where the time goes in v1:
time: 204 us; the launch traced here: 203 us
  waiting for transfers between devices  125 us (61%)
  matrix products  24.1 us (12%)
  starting transfers between devices  15.7 us (8%)
  between operations  13.7 us (7%)
  local copies, waits for them, and re-layouts  12.8 us (6%)
  other arithmetic  11.6 us (6%)
    all_gather x1, waiting for transfers between devices, body(): lax.all_gather(frames.reshape(-1, channels), 'space', axis=0, tiled=True)  108 us
    ppermute x1, waiting for transfers between devices, with_halo(): lax.ppermute(lax.slice_in_dim(block, 0, width, axis=dim), axis, backward)  8.74 us
    dot_general x1, matrix products, attend(): jnp.dot(weights.astype(jnp.bfloat16), value_rows, preferred_element_type=...  8.41 us
    dot_general x1, matrix products, attend(): lax.dot_general(queries, key_rows, (((1,), (1,)), ((), ())), preferred_el...  8.06 us
    ppermute x2, starting transfers between devices, shifted(): lax.ppermute(value, axis, [(source, source + steps) for source in range(l...  6.8 us
    ppermute x1, starting transfers between devices, with_halo(): lax.ppermute(lax.slice_in_dim(block, block.shape[dim] - width, None, axis...  6.78 us
    ppermute x2, waiting for transfers between devices, shifted(): lax.ppermute(value, axis, [(source, source + steps) for source in range(l...  6.31 us
    dot_general x9, matrix products, body(): jnp.dot(window, w_space[row_tap, col_tap], preferred_element_type=jnp.flo...  5.18 us
  transfers between devices with their start and end apart: 5, of which 5 were waited for; matrix products, arithmetic and copies ran while one was open for 4% of the time, Pallas kernels for 0%

profile of v1, /device:TPU:49, one launch (start us, length us, event | category | flops | bytes accessed | tf_op | source)
XLA Modules:
  0.0 203.1 jit_solution(68712272117767527)
XLA Ops:
  6.5 0.0 copy-start
  6.5 0.7 all-gather.2.cloned.1.call-update
  7.3 0.7 convert_element_type.67
  7.9 0.7 convert_element_type.79
  8.6 0.7 convert_element_type.64
  9.3 1.0 fusion.38
  10.3 0.8 slice_convert_fusion.1
  11.2 1.0 fusion.40
  12.2 1.0 fusion.67
  13.2 1.2 fusion.18
  14.4 108.0 %all-gather.2.cloned.1.call-done = bf16[6144,384]{1,0:T(8,128)(2,1)} async-done(((bf16[192,384]{1,0:T(8,128)(2,1)}), bf16[6144,384]{1,0:T(8,128)(2,1)}) %all-gather.2.cloned.1.call-update) | async-done | bytes 4718608 | tf_op jit(solution)/shard_map/all_gather | solution.py:60
  122.4 3.3 %fusion = f32[6144]{0:T(1024)S(1)} fusion(bf16[6144,384]{1,0:T(8,128)(2,1)} %all-gather.2.cloned.1.call-done), kind=kLoop, calls=%fused_computation.2 | loop fusion | flops 7071744 | bytes 4743168 | tf_op jit(solution)/shard_map/reduce_sum | solution.py:30
  125.8 8.1 %fusion.68 = (f32[192]{0:T(256)S(1)}, f32[192,6144]{1,0:T(8,128)}) fusion(bf16[192,384]{1,0:T(8,128)(2,1)S(1)} %fusion.18, f32[384]{0:T(512)S(1)} %get-tuple-element.22, bf16[6144,384]{1,0:T(8,128)(2,1)} %all-gather.2.cloned.1.call-done, f32[384]{0:T(512)S(1)} %convert_element_type.67, f32[6144]{0:T(1024)S(1)} %add_rsqrt_fusion, bf16[384,1152]{1,0:T(8,128)(2,1)} %param.14), kind=kOutput, calls=%fused_computation.90 | convolution fusion | flops 2734423808 | bytes 9907968 | tf_op jit(solution)/shard_map/dot_general | solution.py:42
  133.8 3.1 %fusion.3 = f32[192]{0:T(256)S(1)} fusion(f32[192,6144]{1,0:T(8,128)} %get-tuple-element.26, f32[192]{0:T(256)S(1)} %broadcast_maximum_fusion), kind=kLoop, calls=%fused_computation.9 | loop fusion | flops 2359104 | bytes 4720128 | tf_op jit(solution)/shard_map/reduce_sum | solution.py:47
  137.0 0.0 copy-start.2
  137.0 8.4 %fusion.25 = bf16[192,384]{1,0:T(8,128)(2,1)S(1)} fusion(f32[384]{0:T(512)S(1)} %get-tuple-element.24, bf16[6144,384]{1,0:T(8,128)(2,1)} %all-gather.2.cloned.1.call-done, f32[384]{0:T(512)S(1)} %convert_element_type.67, f32[6144]{0:T(1024)S(1)} %add_rsqrt_fusion, f32[192,6144]{1,0:T(8,128)} %get-tuple-element.26, f32[192]{0:T(256)S(1)} %broadcast_maximum_fusion, ...), kind=kOutput, calls=%fused_computation.33 | convolution fusion | flops 2734571520 | bytes 9908736 | tf_op jit(solution)/shard_map/dot_general | solution.py:48
  145.4 0.2 fusion.19
  145.7 4.6 %collective-permute-start = (bf16[192,384]{1,0:T(8,128)(2,1)S(1)}, bf16[192,384]{1,0:T(8,128)(2,1)S(1)}, u32[]{:S(2)}, u32[]{:S(2)}) collective-permute-start(bf16[192,384]{1,0:T(8,128)(2,1)S(1)} %fusion.19), channel_id=1, source_target_pairs={{0,64},{32,96},{64,128},{96,160},{128,192},{160,224},{192,256},{22... | collective-permute-start | bytes 442376 | tf_op jit(solution)/shard_map/ppermute | solution.py:12
  150.3 2.2 %collective-permute-start.1 = (bf16[192,384]{1,0:T(8,128)(2,1)S(1)}, bf16[192,384]{1,0:T(8,128)(2,1)S(1)}, u32[]{:S(2)}, u32[]{:S(2)}) collective-permute-start(bf16[192,384]{1,0:T(8,128)(2,1)S(1)} %fusion.19), channel_id=1, source_target_pairs={{0,32},{32,64},{64,96},{96,128},{128,160},{160,192},{192,224},{224... | collective-permute-start | bytes 442376 | tf_op jit(solution)/shard_map/ppermute | solution.py:12
  152.5 0.3 fusion.30
  152.8 2.3 %collective-permute-done = bf16[192,384]{1,0:T(8,128)(2,1)S(1)} collective-permute-done((bf16[192,384]{1,0:T(8,128)(2,1)S(1)}, bf16[192,384]{1,0:T(8,128)(2,1)S(1)}, u32[]{:S(2)}, u32[]{:S(2)}) %collective-permute-start) | collective-permute-done | bytes 147488 | tf_op jit(solution)/shard_map/ppermute | solution.py:12
  155.1 4.0 %collective-permute-done.1 = bf16[192,384]{1,0:T(8,128)(2,1)S(1)} collective-permute-done((bf16[192,384]{1,0:T(8,128)(2,1)S(1)}, bf16[192,384]{1,0:T(8,128)(2,1)S(1)}, u32[]{:S(2)}, u32[]{:S(2)}) %collective-permute-start.1) | collective-permute-done | bytes 147488 | tf_op jit(solution)/shard_map/ppermute | solution.py:12
  159.1 0.1 fusion.56
  159.2 0.3 fusion.32
  159.5 0.0 copy-start.4
  159.5 0.3 fusion.16
  159.9 6.8 %collective-permute-start.2 = (bf16[2,1,96,384]{3,2,1,0:T(8,128)(2,1)S(1)}, bf16[2,1,96,384]{3,2,1,0:T(8,128)(2,1)S(1)}, u32[]{:S(2)}, u32[]{:S(2)}) collective-permute-start(bf16[2,1,96,384]{3,2,1,0:T(8,128)(2,1)S(1)} %get-tuple-element.14), channel_id=1, source_target_pairs={{0,1},{1,2},{2,3},{3,4},{4,5},{5,6},{6,7},{7,8},{8,9},{9,10},{10,1... | collective-permute-start | bytes 442376 | tf_op jit(solution)/shard_map/ppermute | solution.py:20
  166.7 2.1 %collective-permute-start.3 = (bf16[2,1,96,384]{3,2,1,0:T(8,128)(2,1)S(1)}, bf16[2,1,96,384]{3,2,1,0:T(8,128)(2,1)S(1)}, u32[]{:S(2)}, u32[]{:S(2)}) collective-permute-start(bf16[2,1,96,384]{3,2,1,0:T(8,128)(2,1)S(1)} %get-tuple-element.15), channel_id=1, source_target_pairs={{1,0},{2,1},{3,2},{4,3},{5,4},{6,5},{7,6},{8,7},{9,8},{10,9},{11,1... | collective-permute-start | bytes 442376 | tf_op jit(solution)/shard_map/ppermute | solution.py:23
  168.8 0.0 copy-done.4
  168.9 1.6 collective-permute-done.2
  170.4 8.7 %collective-permute-done.3 = bf16[2,1,96,384]{3,2,1,0:T(8,128)(2,1)S(1)} collective-permute-done((bf16[2,1,96,384]{3,2,1,0:T(8,128)(2,1)S(1)}, bf16[2,1,96,384]{3,2,1,0:T(8,128)(2,1)S(1)}, u32[]{:S(2)}, u32[]{:S(2)}) %collective-permute-start.3) | collective-permute-done | bytes 147488 | tf_op jit(solution)/shard_map/ppermute | solution.py:23
  179.2 0.1 pad_maximum_fusion
  179.3 0.1 broadcast_in_dim.7
  179.4 0.1 slice.146
  179.5 2.3 %broadcast_in_dim.8 = bf16[2,6,96,2,384]{4,3,2,1,0:T(2,128)(2,1)} broadcast(bf16[2,6,96,384]{3,2,1,0:T(8,128)(2,1)S(1)} %slice.146), dimensions={0,1,2,4} | broadcast | bytes 2654208 | tf_op jit(solution)/shard_map/broadcast_in_dim | solution.py:95
  181.8 4.0 %reshape.92 = bf16[2,6,192,384]{3,2,1,0:T(8,128)(2,1)S(1)} reshape(bf16[2,6,96,2,384]{4,3,2,1,0:T(2,128)(2,1)} %broadcast_in_dim.8) | data formatting | bytes 3538944 | tf_op jit(solution)/shard_map/reshape | solution.py:95
  185.8 0.0 copy-start.3
  185.8 4.0 %pad_slice_fusion = (bf16[2,4,192,384]{3,2,1,0:T(8,128)(2,1)S(1)}, bf16[2,4,192,384]{3,2,1,0:T(8,128)(2,1)S(1)}, bf16[2,4,192,384]{3,2,1,0:T(8,128)(2,1)S(1)}, b...) fusion(bf16[2,6,192,384]{3,2,1,0:T(8,128)(2,1)S(1)} %reshape.92), kind=kLoop, calls=%fused_computation.34 | loop fusion | bytes 15925248 | tf_op jit(solution)/shard_map/slice | solution.py:101
  189.9 0.6 convolution_add_fusion.8
  190.4 0.6 convolution_add_fusion.7
  191.0 0.6 convolution_add_fusion.6
  191.6 0.6 convolution_add_fusion.5
  192.2 0.6 convolution_add_fusion.4
  192.8 0.6 convolution_add_fusion.3
  193.4 0.6 convolution_add_fusion.2
  193.9 0.6 convolution_add_fusion.1
  194.5 0.6 fusion.5
  195.1 1.2 copy.13
  (12 shorter events, 0.1 us)
Async XLA Ops:
  6.5 138.9 %copy-start = (bf16[384,384]{1,0:T(8,128)(2,1)S(1)}, bf16[384,384]{1,0:T(8,128)(2,1)}, u32[]{:S(2)}) copy-start(bf16[384,384]{1,0:T(8,128)(2,1)} %param.16) | copy-start | bytes 884740
  6.5 115.9 %all-gather.2.cloned.1.call-start = ((), (), s32[]{:S(2)}) async-start(), calls=%async_computation | async-start | bytes 4866048 | tf_op jit(solution)/shard_map/all_gather | solution.py:60
  137.0 8.4 %copy-start.1 = (bf16[1,2,96,384]{3,2,1,0:T(8,128)(2,1)S(1)}, bf16[1,2,96,384]{3,2,1,0:T(8,128)(2,1)}, u32[]{:S(2)}) copy-start(bf16[1,2,96,384]{3,2,1,0:T(8,128)(2,1)} %param.11) | copy-start | bytes 442372
  137.0 15.5 %copy-start.2 = (bf16[3,384,768]{2,1,0:T(8,128)(2,1)S(1)}, bf16[3,384,768]{2,1,0:T(8,128)(2,1)}, u32[]{:S(2)}) copy-start(bf16[3,384,768]{2,1,0:T(8,128)(2,1)} %param.18) | copy-start | bytes 5308420
  145.7 9.4 %collective-permute-start = (bf16[192,384]{1,0:T(8,128)(2,1)S(1)}, bf16[192,384]{1,0:T(8,128)(2,1)S(1)}, u32[]{:S(2)}, u32[]{:S(2)}) collective-permute-start(bf16[192,384]{1,0:T(8,128)(2,1)S(1)} %fusion.19), channel_id=1, source_target_pairs={{0,64},{32,96},{64,128},{96,160},{128,192},{160,224},{192,256},{22... | collective-permute-start | bytes 442376 | tf_op jit(solution)/shard_map/ppermute | solution.py:12
  150.3 8.9 %collective-permute-start.1 = (bf16[192,384]{1,0:T(8,128)(2,1)S(1)}, bf16[192,384]{1,0:T(8,128)(2,1)S(1)}, u32[]{:S(2)}, u32[]{:S(2)}) collective-permute-start(bf16[192,384]{1,0:T(8,128)(2,1)S(1)} %fusion.19), channel_id=1, source_target_pairs={{0,32},{32,64},{64,96},{96,128},{128,160},{160,192},{192,224},{224... | collective-permute-start | bytes 442376 | tf_op jit(solution)/shard_map/ppermute | solution.py:12
  159.5 9.3 %copy-start.4 = (bf16[192]{0:T(256)(128)(2,1)S(1)}, bf16[192]{0:T(256)(128)(2,1)}, u32[]{:S(2)}) copy-start(bf16[192]{0:T(256)(128)(2,1)} %param.21) | copy-start | bytes 1156
  159.9 10.5 %collective-permute-start.2 = (bf16[2,1,96,384]{3,2,1,0:T(8,128)(2,1)S(1)}, bf16[2,1,96,384]{3,2,1,0:T(8,128)(2,1)S(1)}, u32[]{:S(2)}, u32[]{:S(2)}) collective-permute-start(bf16[2,1,96,384]{3,2,1,0:T(8,128)(2,1)S(1)} %get-tuple-element.14), channel_id=1, source_target_pairs={{0,1},{1,2},{2,3},{3,4},{4,5},{5,6},{6,7},{7,8},{8,9},{9,10},{10,1... | collective-permute-start | bytes 442376 | tf_op jit(solution)/shard_map/ppermute | solution.py:20
  166.7 12.4 %collective-permute-start.3 = (bf16[2,1,96,384]{3,2,1,0:T(8,128)(2,1)S(1)}, bf16[2,1,96,384]{3,2,1,0:T(8,128)(2,1)S(1)}, u32[]{:S(2)}, u32[]{:S(2)}) collective-permute-start(bf16[2,1,96,384]{3,2,1,0:T(8,128)(2,1)S(1)} %get-tuple-element.15), channel_id=1, source_target_pairs={{1,0},{2,1},{3,2},{4,3},{5,4},{6,5},{7,6},{8,7},{9,8},{10,9},{11,1... | collective-permute-start | bytes 442376 | tf_op jit(solution)/shard_map/ppermute | solution.py:23
  185.8 4.1 %copy-start.3 = (bf16[3,3,384,192]{2,3,1,0:T(8,128)(2,1)S(1)}, bf16[3,3,384,192]{2,3,1,0:T(8,128)(2,1)}, u32[]{:S(2)}) copy-start(bf16[3,3,384,192]{2,3,1,0:T(8,128)(2,1)} %param.20) | copy-start | bytes 3981316
Sparse Core Ops, SparseCore 0:
  10.7 111.6 all-gather.1

commit v2 on v1

--- a/solution.py
+++ b/solution.py
@@ -23,6 +23,31 @@
         high = lax.ppermute(lax.slice_in_dim(block, 0, width, axis=dim), axis, backward)
         block = jnp.concatenate([low, block, high], axis=dim)
     return block
+
+
+def gather_space(block):
+    count = lax.axis_size("space")
+    rings = count // 4
+
+    def moved(value, target):
+        return lax.ppermute(value, "space", [(s, target(s)) for s in range(count)])
+
+    partner = moved(block, lambda s: s ^ 2)
+    own = jnp.concatenate([block, partner], axis=0)
+    forward = lambda s: ((s // 4 + 1) % rings) * 4 + s % 4
+    backward = lambda s: ((s // 4 - 1) % rings) * 4 + s % 4
+    pieces = [own]
+    ahead, behind = own, own
+    for _ in range(rings // 2 - 1):
+        ahead = moved(ahead, forward)
+        behind = moved(behind, backward)
+        pieces += [ahead, behind]
+    half = own.shape[0] // 2
+    pieces.append(moved(ahead[:half], forward))
+    pieces.append(moved(behind[half:], backward))
+    mine = jnp.concatenate(pieces, axis=0)
+    other = [moved(piece, lambda s: s ^ 1) for piece in pieces]
+    return jnp.concatenate([mine] + other, axis=0)
 
 
 def normalize(frames, norm_gain):
@@ -57,7 +82,7 @@
     channels = frames.shape[-1]
     rows = frames.shape[1]
     width = frames.shape[2]
-    whole = lax.all_gather(frames.reshape(-1, channels), "space", axis=0, tiled=True)
+    whole = gather_space(frames.reshape(-1, channels))
     normed = normalize(frames, norm_gain).reshape(-1, channels)
     queries = project(normed, w_qkv[:, :channels], b_qkv[:channels])
     count = queries.shape[0]

time: 204 us -> 155 us (0.76)
  the two profiles are of different devices: /device:TPU:49 before, /device:TPU:9 now
where the time goes in v2:
time: 155 us; the launch traced here: 154 us
  starting transfers between devices  81.4 us (53%)
  matrix products  24.1 us (16%)
  waiting for transfers between devices  23.4 us (15%)
  local copies, waits for them, and re-layouts  14.7 us (9%)
  other arithmetic  10.2 us (7%)
    ppermute x18, starting transfers between devices, moved(): return lax.ppermute(value, 'space', [(s, target(s)) for s in range(count)])  64.4 us
    ppermute x1, waiting for transfers between devices, with_halo(): lax.ppermute(lax.slice_in_dim(block, 0, width, axis=dim), axis, backward)  9.77 us
    dot_general x1, matrix products, attend(): jnp.dot(weights.astype(jnp.bfloat16), value_rows, preferred_element_type=...  8.4 us
    dot_general x1, matrix products, attend(): lax.dot_general(queries, key_rows, (((1,), (1,)), ((), ())), preferred_el...  8.07 us
    ppermute x1, starting transfers between devices, with_halo(): lax.ppermute(lax.slice_in_dim(block, block.shape[dim] - width, None, axis...  7.9 us
    ppermute x18, waiting for transfers between devices, moved(): return lax.ppermute(value, 'space', [(s, target(s)) for s in range(count)])  7.26 us
    ppermute x2, starting transfers between devices, shifted(): lax.ppermute(value, axis, [(source, source + steps) for source in range(l...  6.88 us
    ppermute x2, waiting for transfers between devices, shifted(): lax.ppermute(value, axis, [(source, source + steps) for source in range(l...  6.41 us
  transfers between devices with their start and end apart: 22, of which 7 were waited for; matrix products, arithmetic and copies ran while one was open for 5% of the time, Pallas kernels for 0%

profile of v2, /device:TPU:9, one launch (start us, length us, event | category | flops | bytes accessed | tf_op | source)
XLA Modules:
  0.0 154.5 jit_solution(36099821784858372)
XLA Ops:
  0.0 6.7 %collective-permute-start = (bf16[192,384]{1,0:T(8,128)(2,1)}, bf16[192,384]{1,0:T(8,128)(2,1)S(1)}, u32[]{:S(2)}, u32[]{:S(2)}) collective-permute-start(bf16[192,384]{1,0:T(8,128)(2,1)} %bitcast.83), channel_id=1, source_target_pairs={{0,2},{1,3},{2,0},{3,1},{4,6},{5,7},{6,4},{7,5},{8,10},{9,11},{10,... | collective-permute-start | bytes 442376 | tf_op jit(solution)/shard_map/ppermute | solution.py:33
  6.7 1.0 fusion.38
  7.7 0.7 convert_element_type.67
  8.4 1.0 fusion.67
  9.4 1.0 fusion.40
  10.9 0.9 pad_maximum_fusion.1
  11.8 4.0 %collective-permute-start.1 = (bf16[384,384]{1,0:T(8,128)(2,1)S(1)}, bf16[384,384]{1,0:T(8,128)(2,1)S(1)}, u32[]{:S(2)}, u32[]{:S(2)}) collective-permute-start(bf16[384,384]{1,0:T(8,128)(2,1)S(1)} %pad_maximum_fusion.1), channel_id=1, source_target_pairs={{0,4},{1,5},{2,6},{3,7},{4,8},{5,9},{6,10},{7,11},{8,12},{9,13},{1... | collective-permute-start | bytes 884744 | tf_op jit(solution)/shard_map/ppermute | solution.py:33
  15.8 8.6 %collective-permute-start.2 = (bf16[384,384]{1,0:T(8,128)(2,1)S(1)}, bf16[384,384]{1,0:T(8,128)(2,1)S(1)}, u32[]{:S(2)}, u32[]{:S(2)}) collective-permute-start(bf16[384,384]{1,0:T(8,128)(2,1)S(1)} %pad_maximum_fusion.1), channel_id=1, source_target_pairs={{0,28},{1,29},{2,30},{3,31},{4,0},{5,1},{6,2},{7,3},{8,4},{9,5},{1... | collective-permute-start | bytes 884744 | tf_op jit(solution)/shard_map/ppermute | solution.py:33
  24.4 0.8 slice_convert_fusion.1
  25.2 0.7 convert_element_type.79
  25.9 0.7 convert_element_type.64
  26.6 1.2 fusion.18
  27.8 1.9 %collective-permute-start.3 = (bf16[384,384]{1,0:T(8,128)(2,1)S(1)}, bf16[384,384]{1,0:T(8,128)(2,1)S(1)}, u32[]{:S(2)}, u32[]{:S(2)}) collective-permute-start(bf16[384,384]{1,0:T(8,128)(2,1)S(1)} %collective-permute-done.1), channel_id=1, source_target_pairs={{0,4},{1,5},{2,6},{3,7},{4,8},{5,9},{6,10},{7,11},{8,12},{9,13},{1... | collective-permute-start | bytes 884744 | tf_op jit(solution)/shard_map/ppermute | solution.py:33
  29.7 4.6 %collective-permute-start.4 = (bf16[384,384]{1,0:T(8,128)(2,1)S(1)}, bf16[384,384]{1,0:T(8,128)(2,1)S(1)}, u32[]{:S(2)}, u32[]{:S(2)}) collective-permute-start(bf16[384,384]{1,0:T(8,128)(2,1)S(1)} %collective-permute-done.2), channel_id=1, source_target_pairs={{0,28},{1,29},{2,30},{3,31},{4,0},{5,1},{6,2},{7,3},{8,4},{9,5},{1... | collective-permute-start | bytes 884744 | tf_op jit(solution)/shard_map/ppermute | solution.py:33
  34.4 7.0 %collective-permute-start.9 = (bf16[384,384]{1,0:T(8,128)(2,1)S(1)}, bf16[384,384]{1,0:T(8,128)(2,1)S(1)}, u32[]{:S(2)}, u32[]{:S(2)}) collective-permute-start(bf16[384,384]{1,0:T(8,128)(2,1)S(1)} %pad_maximum_fusion.1), channel_id=1, source_target_pairs={{0,1},{1,0},{2,3},{3,2},{4,5},{5,4},{6,7},{7,6},{8,9},{9,8},{10,11... | collective-permute-start | bytes 884744 | tf_op jit(solution)/shard_map/ppermute | solution.py:33
  41.4 1.9 %collective-permute-start.10 = (bf16[384,384]{1,0:T(8,128)(2,1)S(1)}, bf16[384,384]{1,0:T(8,128)(2,1)S(1)}, u32[]{:S(2)}, u32[]{:S(2)}) collective-permute-start(bf16[384,384]{1,0:T(8,128)(2,1)S(1)} %collective-permute-done.1), channel_id=1, source_target_pairs={{0,1},{1,0},{2,3},{3,2},{4,5},{5,4},{6,7},{7,6},{8,9},{9,8},{10,11... | collective-permute-start | bytes 884744 | tf_op jit(solution)/shard_map/ppermute | solution.py:33
  43.3 2.4 %collective-permute-start.11 = (bf16[384,384]{1,0:T(8,128)(2,1)S(1)}, bf16[384,384]{1,0:T(8,128)(2,1)S(1)}, u32[]{:S(2)}, u32[]{:S(2)}) collective-permute-start(bf16[384,384]{1,0:T(8,128)(2,1)S(1)} %collective-permute-done.2), channel_id=1, source_target_pairs={{0,1},{1,0},{2,3},{3,2},{4,5},{5,4},{6,7},{7,6},{8,9},{9,8},{10,11... | collective-permute-start | bytes 884744 | tf_op jit(solution)/shard_map/ppermute | solution.py:33
  45.8 1.9 %collective-permute-start.5 = (bf16[384,384]{1,0:T(8,128)(2,1)S(1)}, bf16[384,384]{1,0:T(8,128)(2,1)S(1)}, u32[]{:S(2)}, u32[]{:S(2)}) collective-permute-start(bf16[384,384]{1,0:T(8,128)(2,1)S(1)} %collective-permute-done.3), channel_id=1, source_target_pairs={{0,4},{1,5},{2,6},{3,7},{4,8},{5,9},{6,10},{7,11},{8,12},{9,13},{1... | collective-permute-start | bytes 884744 | tf_op jit(solution)/shard_map/ppermute | solution.py:33
  47.7 4.6 %collective-permute-start.6 = (bf16[384,384]{1,0:T(8,128)(2,1)S(1)}, bf16[384,384]{1,0:T(8,128)(2,1)S(1)}, u32[]{:S(2)}, u32[]{:S(2)}) collective-permute-start(bf16[384,384]{1,0:T(8,128)(2,1)S(1)} %collective-permute-done.4), channel_id=1, source_target_pairs={{0,28},{1,29},{2,30},{3,31},{4,0},{5,1},{6,2},{7,3},{8,4},{9,5},{1... | collective-permute-start | bytes 884744 | tf_op jit(solution)/shard_map/ppermute | solution.py:33
  52.5 5.0 %collective-permute-done.5 = bf16[384,384]{1,0:T(8,128)(2,1)S(1)} collective-permute-done((bf16[384,384]{1,0:T(8,128)(2,1)S(1)}, bf16[384,384]{1,0:T(8,128)(2,1)S(1)}, u32[]{:S(2)}, u32[]{:S(2)}) %collective-permute-start.5) | collective-permute-done | bytes 294944 | tf_op jit(solution)/shard_map/ppermute | solution.py:33
  57.5 1.9 %collective-permute-start.7 = (bf16[192,384]{1,0:T(8,128)(2,1)S(1)}, bf16[192,384]{1,0:T(8,128)(2,1)S(1)}, u32[]{:S(2)}, u32[]{:S(2)}) collective-permute-start(bf16[192,384]{1,0:T(8,128)(2,1)S(1)} %slice.150), channel_id=1, source_target_pairs={{0,4},{1,5},{2,6},{3,7},{4,8},{5,9},{6,10},{7,11},{8,12},{9,13},{1... | collective-permute-start | bytes 442376 | tf_op jit(solution)/shard_map/ppermute | solution.py:33
  59.4 4.6 %collective-permute-start.8 = (bf16[192,384]{1,0:T(8,128)(2,1)S(1)}, bf16[192,384]{1,0:T(8,128)(2,1)S(1)}, u32[]{:S(2)}, u32[]{:S(2)}) collective-permute-start(bf16[192,384]{1,0:T(8,128)(2,1)S(1)} %slice.151), channel_id=1, source_target_pairs={{0,28},{1,29},{2,30},{3,31},{4,0},{5,1},{6,2},{7,3},{8,4},{9,5},{1... | collective-permute-start | bytes 442376 | tf_op jit(solution)/shard_map/ppermute | solution.py:33
  64.1 1.0 collective-permute-done.7
  65.1 3.6 %collective-permute-start.12 = (bf16[384,384]{1,0:T(8,128)(2,1)S(1)}, bf16[384,384]{1,0:T(8,128)(2,1)S(1)}, u32[]{:S(2)}, u32[]{:S(2)}) collective-permute-start(bf16[384,384]{1,0:T(8,128)(2,1)S(1)} %collective-permute-done.3), channel_id=1, source_target_pairs={{0,1},{1,0},{2,3},{3,2},{4,5},{5,4},{6,7},{7,6},{8,9},{9,8},{10,11... | collective-permute-start | bytes 884744 | tf_op jit(solution)/shard_map/ppermute | solution.py:33
  68.8 1.9 %collective-permute-start.13 = (bf16[384,384]{1,0:T(8,128)(2,1)S(1)}, bf16[384,384]{1,0:T(8,128)(2,1)S(1)}, u32[]{:S(2)}, u32[]{:S(2)}) collective-permute-start(bf16[384,384]{1,0:T(8,128)(2,1)S(1)} %collective-permute-done.4), channel_id=1, source_target_pairs={{0,1},{1,0},{2,3},{3,2},{4,5},{5,4},{6,7},{7,6},{8,9},{9,8},{10,11... | collective-permute-start | bytes 884744 | tf_op jit(solution)/shard_map/ppermute | solution.py:33
  70.8 2.4 %collective-permute-start.14 = (bf16[384,384]{1,0:T(8,128)(2,1)S(1)}, bf16[384,384]{1,0:T(8,128)(2,1)S(1)}, u32[]{:S(2)}, u32[]{:S(2)}) collective-permute-start(bf16[384,384]{1,0:T(8,128)(2,1)S(1)} %collective-permute-done.5), channel_id=1, source_target_pairs={{0,1},{1,0},{2,3},{3,2},{4,5},{5,4},{6,7},{7,6},{8,9},{9,8},{10,11... | collective-permute-start | bytes 884744 | tf_op jit(solution)/shard_map/ppermute | solution.py:33
  73.2 1.9 %collective-permute-start.15 = (bf16[384,384]{1,0:T(8,128)(2,1)S(1)}, bf16[384,384]{1,0:T(8,128)(2,1)S(1)}, u32[]{:S(2)}, u32[]{:S(2)}) collective-permute-start(bf16[384,384]{1,0:T(8,128)(2,1)S(1)} %collective-permute-done.6), channel_id=1, source_target_pairs={{0,1},{1,0},{2,3},{3,2},{4,5},{5,4},{6,7},{7,6},{8,9},{9,8},{10,11... | collective-permute-start | bytes 884744 | tf_op jit(solution)/shard_map/ppermute | solution.py:33
  75.2 2.4 %collective-permute-start.16 = (bf16[192,384]{1,0:T(8,128)(2,1)S(1)}, bf16[192,384]{1,0:T(8,128)(2,1)S(1)}, u32[]{:S(2)}, u32[]{:S(2)}) collective-permute-start(bf16[192,384]{1,0:T(8,128)(2,1)S(1)} %collective-permute-done.7), channel_id=1, source_target_pairs={{0,1},{1,0},{2,3},{3,2},{4,5},{5,4},{6,7},{7,6},{8,9},{9,8},{10,11... | collective-permute-start | bytes 442376 | tf_op jit(solution)/shard_map/ppermute | solution.py:33
  77.7 2.1 %collective-permute-start.17 = (bf16[192,384]{1,0:T(8,128)(2,1)S(1)}, bf16[192,384]{1,0:T(8,128)(2,1)S(1)}, u32[]{:S(2)}, u32[]{:S(2)}) collective-permute-start(bf16[192,384]{1,0:T(8,128)(2,1)S(1)} %collective-permute-done.8), channel_id=1, source_target_pairs={{0,1},{1,0},{2,3},{3,2},{4,5},{5,4},{6,7},{7,6},{8,9},{9,8},{10,11... | collective-permute-start | bytes 442376 | tf_op jit(solution)/shard_map/ppermute | solution.py:33
  80.1 0.9 collective-permute-done.17
  81.0 1.0 fusion
  82.0 1.1 copy-done.1
  83.2 8.1 %fusion.68 = (f32[192]{0:T(256)S(1)}, f32[192,6144]{1,0:T(8,128)}) fusion(bf16[192,384]{1,0:T(8,128)(2,1)S(1)} %fusion.18, f32[384]{0:T(512)S(1)} %get-tuple-element.22, bf16[6144,384]{1,0:T(8,128)(2,1)} %copy-done.1, f32[384]{0:T(512)S(1)} %convert_element_type.67, f32[6144]{0:T(1024)S(1)} %add_rsqrt_fusion, bf16[384,1152]{1,0:T(8,128)(2,1)} %param.14), kind=kOutput, calls=%fused_computation.110 | convolution fusion | flops 2734423808 | bytes 9907968 | tf_op jit(solution)/shard_map/dot_general | solution.py:67
  91.2 3.1 %fusion.3 = f32[192]{0:T(256)S(1)} fusion(f32[192,6144]{1,0:T(8,128)} %get-tuple-element.26, f32[192]{0:T(256)S(1)} %broadcast_maximum_fusion), kind=kLoop, calls=%fused_computation.9 | loop fusion | flops 2359104 | bytes 4720128 | tf_op jit(solution)/shard_map/reduce_sum | solution.py:72
  94.4 8.4 %fusion.25 = bf16[192,384]{1,0:T(8,128)(2,1)S(1)} fusion(f32[384]{0:T(512)S(1)} %get-tuple-element.24, bf16[6144,384]{1,0:T(8,128)(2,1)} %copy-done.1, f32[384]{0:T(512)S(1)} %convert_element_type.67, f32[6144]{0:T(1024)S(1)} %add_rsqrt_fusion, f32[192,6144]{1,0:T(8,128)} %get-tuple-element.26, f32[192]{0:T(256)S(1)} %broadcast_maximum_fusion, ...), kind=kOutput, calls=%fused_computation.33 | convolution fusion | flops 2734571520 | bytes 9908736 | tf_op jit(solution)/shard_map/dot_general | solution.py:73
  103.0 4.7 %collective-permute-start.18 = (bf16[192,384]{1,0:T(8,128)(2,1)S(1)}, bf16[192,384]{1,0:T(8,128)(2,1)S(1)}, u32[]{:S(2)}, u32[]{:S(2)}) collective-permute-start(bf16[192,384]{1,0:T(8,128)(2,1)S(1)} %fusion.19), channel_id=1, source_target_pairs={{0,64},{32,96},{64,128},{96,160},{128,192},{160,224},{192,256},{22... | collective-permute-start | bytes 442376 | tf_op jit(solution)/shard_map/ppermute | solution.py:12
  107.7 2.2 %collective-permute-start.19 = (bf16[192,384]{1,0:T(8,128)(2,1)S(1)}, bf16[192,384]{1,0:T(8,128)(2,1)S(1)}, u32[]{:S(2)}, u32[]{:S(2)}) collective-permute-start(bf16[192,384]{1,0:T(8,128)(2,1)S(1)} %fusion.19), channel_id=1, source_target_pairs={{0,32},{32,64},{64,96},{96,128},{128,160},{160,192},{192,224},{224... | collective-permute-start | bytes 442376 | tf_op jit(solution)/shard_map/ppermute | solution.py:12
  110.3 2.3 %collective-permute-done.18 = bf16[192,384]{1,0:T(8,128)(2,1)S(1)} collective-permute-done((bf16[192,384]{1,0:T(8,128)(2,1)S(1)}, bf16[192,384]{1,0:T(8,128)(2,1)S(1)}, u32[]{:S(2)}, u32[]{:S(2)}) %collective-permute-start.18) | collective-permute-done | bytes 147488 | tf_op jit(solution)/shard_map/ppermute | solution.py:12
  112.6 4.1 %collective-permute-done.19 = bf16[192,384]{1,0:T(8,128)(2,1)S(1)} collective-permute-done((bf16[192,384]{1,0:T(8,128)(2,1)S(1)}, bf16[192,384]{1,0:T(8,128)(2,1)S(1)}, u32[]{:S(2)}, u32[]{:S(2)}) %collective-permute-start.19) | collective-permute-done | bytes 147488 | tf_op jit(solution)/shard_map/ppermute | solution.py:12
  117.5 7.9 %collective-permute-start.20 = (bf16[2,1,96,384]{3,2,1,0:T(8,128)(2,1)S(1)}, bf16[2,1,96,384]{3,2,1,0:T(8,128)(2,1)S(1)}, u32[]{:S(2)}, u32[]{:S(2)}) collective-permute-start(bf16[2,1,96,384]{3,2,1,0:T(8,128)(2,1)S(1)} %get-tuple-element.14), channel_id=1, source_target_pairs={{0,1},{1,2},{2,3},{3,4},{4,5},{5,6},{6,7},{7,8},{8,9},{9,10},{10,1... | collective-permute-start | bytes 442376 | tf_op jit(solution)/shard_map/ppermute | solution.py:20
  125.4 2.1 %collective-permute-start.21 = (bf16[2,1,96,384]{3,2,1,0:T(8,128)(2,1)S(1)}, bf16[2,1,96,384]{3,2,1,0:T(8,128)(2,1)S(1)}, u32[]{:S(2)}, u32[]{:S(2)}) collective-permute-start(bf16[2,1,96,384]{3,2,1,0:T(8,128)(2,1)S(1)} %get-tuple-element.15), channel_id=1, source_target_pairs={{1,0},{2,1},{3,2},{4,3},{5,4},{6,5},{7,6},{8,7},{9,8},{10,9},{11,1... | collective-permute-start | bytes 442376 | tf_op jit(solution)/shard_map/ppermute | solution.py:23
  127.6 9.8 %collective-permute-done.21 = bf16[2,1,96,384]{3,2,1,0:T(8,128)(2,1)S(1)} collective-permute-done((bf16[2,1,96,384]{3,2,1,0:T(8,128)(2,1)S(1)}, bf16[2,1,96,384]{3,2,1,0:T(8,128)(2,1)S(1)}, u32[]{:S(2)}, u32[]{:S(2)}) %collective-permute-start.21) | collective-permute-done | bytes 147488 | tf_op jit(solution)/shard_map/ppermute | solution.py:23
  137.7 2.3 %broadcast_in_dim.8 = bf16[2,6,96,2,384]{4,3,2,1,0:T(2,128)(2,1)} broadcast(bf16[2,6,96,384]{3,2,1,0:T(8,128)(2,1)S(1)} %slice.156), dimensions={0,1,2,4} | broadcast | bytes 2654208 | tf_op jit(solution)/shard_map/broadcast_in_dim | solution.py:120
  140.0 4.0 %reshape.92 = bf16[2,6,192,384]{3,2,1,0:T(8,128)(2,1)S(1)} reshape(bf16[2,6,96,2,384]{4,3,2,1,0:T(2,128)(2,1)} %broadcast_in_dim.8) | data formatting | bytes 3538944 | tf_op jit(solution)/shard_map/reshape | solution.py:120
  144.0 4.0 %pad_slice_fusion = (bf16[2,4,192,384]{3,2,1,0:T(8,128)(2,1)S(1)}, bf16[2,4,192,384]{3,2,1,0:T(8,128)(2,1)S(1)}, bf16[2,4,192,384]{3,2,1,0:T(8,128)(2,1)S(1)}, b...) fusion(bf16[2,6,192,384]{3,2,1,0:T(8,128)(2,1)S(1)} %reshape.92), kind=kLoop, calls=%fused_computation.34 | loop fusion | bytes 15925248 | tf_op jit(solution)/shard_map/slice | solution.py:126
  148.6 0.6 convolution_add_fusion.7
  149.2 0.6 convolution_add_fusion.6
  153.3 1.2 copy.13
  (69 shorter events, 7.0 us)
Async XLA Ops:
  0.0 102.8 %copy-start = (bf16[384,384]{1,0:T(8,128)(2,1)S(1)}, bf16[384,384]{1,0:T(8,128)(2,1)}, u32[]{:S(2)}) copy-start(bf16[384,384]{1,0:T(8,128)(2,1)} %param.16) | copy-start | bytes 884740
  0.0 34.3 %copy-start.2 = (bf16[1,2,96,384]{3,2,1,0:T(8,128)(2,1)S(1)}, bf16[1,2,96,384]{3,2,1,0:T(8,128)(2,1)}, u32[]{:S(2)}) copy-start(bf16[1,2,96,384]{3,2,1,0:T(8,128)(2,1)} %param.11) | copy-start | bytes 442372
  0.0 10.9 %collective-permute-start = (bf16[192,384]{1,0:T(8,128)(2,1)}, bf16[192,384]{1,0:T(8,128)(2,1)S(1)}, u32[]{:S(2)}, u32[]{:S(2)}) collective-permute-start(bf16[192,384]{1,0:T(8,128)(2,1)} %bitcast.83), channel_id=1, source_target_pairs={{0,2},{1,3},{2,0},{3,1},{4,6},{5,7},{6,4},{7,5},{8,10},{9,11},{10,... | collective-permute-start | bytes 442376 | tf_op jit(solution)/shard_map/ppermute | solution.py:33
  11.8 16.0 %collective-permute-start.1 = (bf16[384,384]{1,0:T(8,128)(2,1)S(1)}, bf16[384,384]{1,0:T(8,128)(2,1)S(1)}, u32[]{:S(2)}, u32[]{:S(2)}) collective-permute-start(bf16[384,384]{1,0:T(8,128)(2,1)S(1)} %pad_maximum_fusion.1), channel_id=1, source_target_pairs={{0,4},{1,5},{2,6},{3,7},{4,8},{5,9},{6,10},{7,11},{8,12},{9,13},{1... | collective-permute-start | bytes 884744 | tf_op jit(solution)/shard_map/ppermute | solution.py:33
  15.8 13.9 %collective-permute-start.2 = (bf16[384,384]{1,0:T(8,128)(2,1)S(1)}, bf16[384,384]{1,0:T(8,128)(2,1)S(1)}, u32[]{:S(2)}, u32[]{:S(2)}) collective-permute-start(bf16[384,384]{1,0:T(8,128)(2,1)S(1)} %pad_maximum_fusion.1), channel_id=1, source_target_pairs={{0,28},{1,29},{2,30},{3,31},{4,0},{5,1},{6,2},{7,3},{8,4},{9,5},{1... | collective-permute-start | bytes 884744 | tf_op jit(solution)/shard_map/ppermute | solution.py:33
  27.8 18.0 %collective-permute-start.3 = (bf16[384,384]{1,0:T(8,128)(2,1)S(1)}, bf16[384,384]{1,0:T(8,128)(2,1)S(1)}, u32[]{:S(2)}, u32[]{:S(2)}) collective-permute-start(bf16[384,384]{1,0:T(8,128)(2,1)S(1)} %collective-permute-done.1), channel_id=1, source_target_pairs={{0,4},{1,5},{2,6},{3,7},{4,8},{5,9},{6,10},{7,11},{8,12},{9,13},{1... | collective-permute-start | bytes 884744 | tf_op jit(solution)/shard_map/ppermute | solution.py:33
  29.7 18.0 %collective-permute-start.4 = (bf16[384,384]{1,0:T(8,128)(2,1)S(1)}, bf16[384,384]{1,0:T(8,128)(2,1)S(1)}, u32[]{:S(2)}, u32[]{:S(2)}) collective-permute-start(bf16[384,384]{1,0:T(8,128)(2,1)S(1)} %collective-permute-done.2), channel_id=1, source_target_pairs={{0,28},{1,29},{2,30},{3,31},{4,0},{5,1},{6,2},{7,3},{8,4},{9,5},{1... | collective-permute-start | bytes 884744 | tf_op jit(solution)/shard_map/ppermute | solution.py:33
  34.4 36.4 %collective-permute-start.9 = (bf16[384,384]{1,0:T(8,128)(2,1)S(1)}, bf16[384,384]{1,0:T(8,128)(2,1)S(1)}, u32[]{:S(2)}, u32[]{:S(2)}) collective-permute-start(bf16[384,384]{1,0:T(8,128)(2,1)S(1)} %pad_maximum_fusion.1), channel_id=1, source_target_pairs={{0,1},{1,0},{2,3},{3,2},{4,5},{5,4},{6,7},{7,6},{8,9},{9,8},{10,11... | collective-permute-start | bytes 884744 | tf_op jit(solution)/shard_map/ppermute | solution.py:33
  41.4 31.8 %collective-permute-start.10 = (bf16[384,384]{1,0:T(8,128)(2,1)S(1)}, bf16[384,384]{1,0:T(8,128)(2,1)S(1)}, u32[]{:S(2)}, u32[]{:S(2)}) collective-permute-start(bf16[384,384]{1,0:T(8,128)(2,1)S(1)} %collective-permute-done.1), channel_id=1, source_target_pairs={{0,1},{1,0},{2,3},{3,2},{4,5},{5,4},{6,7},{7,6},{8,9},{9,8},{10,11... | collective-permute-start | bytes 884744 | tf_op jit(solution)/shard_map/ppermute | solution.py:33
  43.3 31.9 %collective-permute-start.11 = (bf16[384,384]{1,0:T(8,128)(2,1)S(1)}, bf16[384,384]{1,0:T(8,128)(2,1)S(1)}, u32[]{:S(2)}, u32[]{:S(2)}) collective-permute-start(bf16[384,384]{1,0:T(8,128)(2,1)S(1)} %collective-permute-done.2), channel_id=1, source_target_pairs={{0,1},{1,0},{2,3},{3,2},{4,5},{5,4},{6,7},{7,6},{8,9},{9,8},{10,11... | collective-permute-start | bytes 884744 | tf_op jit(solution)/shard_map/ppermute | solution.py:33
  45.8 11.7 %collective-permute-start.5 = (bf16[384,384]{1,0:T(8,128)(2,1)S(1)}, bf16[384,384]{1,0:T(8,128)(2,1)S(1)}, u32[]{:S(2)}, u32[]{:S(2)}) collective-permute-start(bf16[384,384]{1,0:T(8,128)(2,1)S(1)} %collective-permute-done.3), channel_id=1, source_target_pairs={{0,4},{1,5},{2,6},{3,7},{4,8},{5,9},{6,10},{7,11},{8,12},{9,13},{1... | collective-permute-start | bytes 884744 | tf_op jit(solution)/shard_map/ppermute | solution.py:33
  47.7 11.7 %collective-permute-start.6 = (bf16[384,384]{1,0:T(8,128)(2,1)S(1)}, bf16[384,384]{1,0:T(8,128)(2,1)S(1)}, u32[]{:S(2)}, u32[]{:S(2)}) collective-permute-start(bf16[384,384]{1,0:T(8,128)(2,1)S(1)} %collective-permute-done.4), channel_id=1, source_target_pairs={{0,28},{1,29},{2,30},{3,31},{4,0},{5,1},{6,2},{7,3},{8,4},{9,5},{1... | collective-permute-start | bytes 884744 | tf_op jit(solution)/shard_map/ppermute | solution.py:33
  57.5 7.6 %collective-permute-start.7 = (bf16[192,384]{1,0:T(8,128)(2,1)S(1)}, bf16[192,384]{1,0:T(8,128)(2,1)S(1)}, u32[]{:S(2)}, u32[]{:S(2)}) collective-permute-start(bf16[192,384]{1,0:T(8,128)(2,1)S(1)} %slice.150), channel_id=1, source_target_pairs={{0,4},{1,5},{2,6},{3,7},{4,8},{5,9},{6,10},{7,11},{8,12},{9,13},{1... | collective-permute-start | bytes 442376 | tf_op jit(solution)/shard_map/ppermute | solution.py:33
  59.4 9.3 %collective-permute-start.8 = (bf16[192,384]{1,0:T(8,128)(2,1)S(1)}, bf16[192,384]{1,0:T(8,128)(2,1)S(1)}, u32[]{:S(2)}, u32[]{:S(2)}) collective-permute-start(bf16[192,384]{1,0:T(8,128)(2,1)S(1)} %slice.151), channel_id=1, source_target_pairs={{0,28},{1,29},{2,30},{3,31},{4,0},{5,1},{6,2},{7,3},{8,4},{9,5},{1... | collective-permute-start | bytes 442376 | tf_op jit(solution)/shard_map/ppermute | solution.py:33
  65.1 12.6 %collective-permute-start.12 = (bf16[384,384]{1,0:T(8,128)(2,1)S(1)}, bf16[384,384]{1,0:T(8,128)(2,1)S(1)}, u32[]{:S(2)}, u32[]{:S(2)}) collective-permute-start(bf16[384,384]{1,0:T(8,128)(2,1)S(1)} %collective-permute-done.3), channel_id=1, source_target_pairs={{0,1},{1,0},{2,3},{3,2},{4,5},{5,4},{6,7},{7,6},{8,9},{9,8},{10,11... | collective-permute-start | bytes 884744 | tf_op jit(solution)/shard_map/ppermute | solution.py:33
  68.8 11.1 %collective-permute-start.13 = (bf16[384,384]{1,0:T(8,128)(2,1)S(1)}, bf16[384,384]{1,0:T(8,128)(2,1)S(1)}, u32[]{:S(2)}, u32[]{:S(2)}) collective-permute-start(bf16[384,384]{1,0:T(8,128)(2,1)S(1)} %collective-permute-done.4), channel_id=1, source_target_pairs={{0,1},{1,0},{2,3},{3,2},{4,5},{5,4},{6,7},{7,6},{8,9},{9,8},{10,11... | collective-permute-start | bytes 884744 | tf_op jit(solution)/shard_map/ppermute | solution.py:33
  70.8 9.2 %collective-permute-start.14 = (bf16[384,384]{1,0:T(8,128)(2,1)S(1)}, bf16[384,384]{1,0:T(8,128)(2,1)S(1)}, u32[]{:S(2)}, u32[]{:S(2)}) collective-permute-start(bf16[384,384]{1,0:T(8,128)(2,1)S(1)} %collective-permute-done.5), channel_id=1, source_target_pairs={{0,1},{1,0},{2,3},{3,2},{4,5},{5,4},{6,7},{7,6},{8,9},{9,8},{10,11... | collective-permute-start | bytes 884744 | tf_op jit(solution)/shard_map/ppermute | solution.py:33
  73.2 6.8 %collective-permute-start.15 = (bf16[384,384]{1,0:T(8,128)(2,1)S(1)}, bf16[384,384]{1,0:T(8,128)(2,1)S(1)}, u32[]{:S(2)}, u32[]{:S(2)}) collective-permute-start(bf16[384,384]{1,0:T(8,128)(2,1)S(1)} %collective-permute-done.6), channel_id=1, source_target_pairs={{0,1},{1,0},{2,3},{3,2},{4,5},{5,4},{6,7},{7,6},{8,9},{9,8},{10,11... | collective-permute-start | bytes 884744 | tf_op jit(solution)/shard_map/ppermute | solution.py:33
  75.2 4.9 %collective-permute-start.16 = (bf16[192,384]{1,0:T(8,128)(2,1)S(1)}, bf16[192,384]{1,0:T(8,128)(2,1)S(1)}, u32[]{:S(2)}, u32[]{:S(2)}) collective-permute-start(bf16[192,384]{1,0:T(8,128)(2,1)S(1)} %collective-permute-done.7), channel_id=1, source_target_pairs={{0,1},{1,0},{2,3},{3,2},{4,5},{5,4},{6,7},{7,6},{8,9},{9,8},{10,11... | collective-permute-start | bytes 442376 | tf_op jit(solution)/shard_map/ppermute | solution.py:33
  77.7 3.3 %collective-permute-start.17 = (bf16[192,384]{1,0:T(8,128)(2,1)S(1)}, bf16[192,384]{1,0:T(8,128)(2,1)S(1)}, u32[]{:S(2)}, u32[]{:S(2)}) collective-permute-start(bf16[192,384]{1,0:T(8,128)(2,1)S(1)} %collective-permute-done.8), channel_id=1, source_target_pairs={{0,1},{1,0},{2,3},{3,2},{4,5},{5,4},{6,7},{7,6},{8,9},{9,8},{10,11... | collective-permute-start | bytes 442376 | tf_op jit(solution)/shard_map/ppermute | solution.py:33
  81.0 2.1 %copy-start.1 = (bf16[6144,384]{1,0:T(8,128)(2,1)}, bf16[6144,384]{1,0:T(8,128)(2,1)S(1)}, u32[]{:S(2)}) copy-start(bf16[6144,384]{1,0:T(8,128)(2,1)S(1)} %constant_dynamic-update-slice_fusion) | copy-start | bytes 14155780
  94.4 15.6 %copy-start.3 = (bf16[3,384,768]{2,1,0:T(8,128)(2,1)S(1)}, bf16[3,384,768]{2,1,0:T(8,128)(2,1)}, u32[]{:S(2)}) copy-start(bf16[3,384,768]{2,1,0:T(8,128)(2,1)} %param.18) | copy-start | bytes 5308420
  103.0 9.6 %collective-permute-start.18 = (bf16[192,384]{1,0:T(8,128)(2,1)S(1)}, bf16[192,384]{1,0:T(8,128)(2,1)S(1)}, u32[]{:S(2)}, u32[]{:S(2)}) collective-permute-start(bf16[192,384]{1,0:T(8,128)(2,1)S(1)} %fusion.19), channel_id=1, source_target_pairs={{0,64},{32,96},{64,128},{96,160},{128,192},{160,224},{192,256},{22... | collective-permute-start | bytes 442376 | tf_op jit(solution)/shard_map/ppermute | solution.py:12
  107.7 9.0 %collective-permute-start.19 = (bf16[192,384]{1,0:T(8,128)(2,1)S(1)}, bf16[192,384]{1,0:T(8,128)(2,1)S(1)}, u32[]{:S(2)}, u32[]{:S(2)}) collective-permute-start(bf16[192,384]{1,0:T(8,128)(2,1)S(1)} %fusion.19), channel_id=1, source_target_pairs={{0,32},{32,64},{64,96},{96,128},{128,160},{160,192},{192,224},{224... | collective-permute-start | bytes 442376 | tf_op jit(solution)/shard_map/ppermute | solution.py:12
  117.1 10.5 %copy-start.5 = (bf16[192]{0:T(256)(128)(2,1)S(1)}, bf16[192]{0:T(256)(128)(2,1)}, u32[]{:S(2)}) copy-start(bf16[192]{0:T(256)(128)(2,1)} %param.21) | copy-start | bytes 1156
  117.5 10.1 %collective-permute-start.20 = (bf16[2,1,96,384]{3,2,1,0:T(8,128)(2,1)S(1)}, bf16[2,1,96,384]{3,2,1,0:T(8,128)(2,1)S(1)}, u32[]{:S(2)}, u32[]{:S(2)}) collective-permute-start(bf16[2,1,96,384]{3,2,1,0:T(8,128)(2,1)S(1)} %get-tuple-element.14), channel_id=1, source_target_pairs={{0,1},{1,2},{2,3},{3,4},{4,5},{5,6},{6,7},{7,8},{8,9},{9,10},{10,1... | collective-permute-start | bytes 442376 | tf_op jit(solution)/shard_map/ppermute | solution.py:20
  125.4 11.9 %collective-permute-start.21 = (bf16[2,1,96,384]{3,2,1,0:T(8,128)(2,1)S(1)}, bf16[2,1,96,384]{3,2,1,0:T(8,128)(2,1)S(1)}, u32[]{:S(2)}, u32[]{:S(2)}) collective-permute-start(bf16[2,1,96,384]{3,2,1,0:T(8,128)(2,1)S(1)} %get-tuple-element.15), channel_id=1, source_target_pairs={{1,0},{2,1},{3,2},{4,3},{5,4},{6,5},{7,6},{8,7},{9,8},{10,9},{11,1... | collective-permute-start | bytes 442376 | tf_op jit(solution)/shard_map/ppermute | solution.py:23
  144.0 4.1 %copy-start.4 = (bf16[3,3,384,192]{2,3,1,0:T(8,128)(2,1)S(1)}, bf16[3,3,384,192]{2,3,1,0:T(8,128)(2,1)}, u32[]{:S(2)}) copy-start(bf16[3,3,384,192]{2,3,1,0:T(8,128)(2,1)} %param.20) | copy-start | bytes 3981316

commit v3 on v2

--- a/solution.py
+++ b/solution.py
@@ -36,18 +36,20 @@
     own = jnp.concatenate([block, partner], axis=0)
     forward = lambda s: ((s // 4 + 1) % rings) * 4 + s % 4
     backward = lambda s: ((s // 4 - 1) % rings) * 4 + s % 4
-    pieces = [own]
+    batches = [[own]]
     ahead, behind = own, own
-    for _ in range(rings // 2 - 1):
+    for step in range(rings // 2 - 1):
         ahead = moved(ahead, forward)
         behind = moved(behind, backward)
-        pieces += [ahead, behind]
+        batches[-1] += [ahead, behind]
+        if step == 0:
+            batches.append([])
     half = own.shape[0] // 2
-    pieces.append(moved(ahead[:half], forward))
-    pieces.append(moved(behind[half:], backward))
-    mine = jnp.concatenate(pieces, axis=0)
-    other = [moved(piece, lambda s: s ^ 1) for piece in pieces]
-    return jnp.concatenate([mine] + other, axis=0)
+    batches[-1].append(moved(ahead[:half], forward))
+    batches[-1].append(moved(behind[half:], backward))
+    mine = [jnp.concatenate(batch, axis=0) for batch in batches]
+    other = [moved(chunk, lambda s: s ^ 1) for chunk in mine]
+    return mine + other
 
 
 def normalize(frames, norm_gain):
@@ -68,9 +70,10 @@
         queries, key_rows, (((1,), (1,)), ((), ())), preferred_element_type=jnp.float32
     ) * queries.shape[1] ** (-0.5)
     new_best = jnp.maximum(best, jnp.max(scores, axis=1, keepdims=True))
+    correction = jnp.exp(best - new_best)
     weights = jnp.exp(scores - new_best)
-    mass = jnp.sum(weights, axis=1, keepdims=True)
-    total_sum = jnp.dot(
+    mass = mass * correction + jnp.sum(weights, axis=1, keepdims=True)
+    total_sum = total_sum * correction + jnp.dot(
         weights.astype(jnp.bfloat16), value_rows, preferred_element_type=jnp.float32
     )
     return (new_best, mass, total_sum)
@@ -82,19 +85,20 @@
     channels = frames.shape[-1]
     rows = frames.shape[1]
     width = frames.shape[2]
-    whole = gather_space(frames.reshape(-1, channels))
+    chunks = gather_space(frames.reshape(-1, channels))
     normed = normalize(frames, norm_gain).reshape(-1, channels)
     queries = project(normed, w_qkv[:, :channels], b_qkv[:channels])
     count = queries.shape[0]
-    start_state = (
-        jnp.full((count, 1), -1e30, jnp.float32),
+    final = (
+        jnp.full((count, 1), -jnp.inf, jnp.float32),
         jnp.zeros((count, 1), jnp.float32),
         jnp.zeros((count, channels), jnp.float32),
     )
-    normed_all = normalize(whole, norm_gain)
-    key_rows = project(normed_all, w_qkv[:, channels : 2 * channels], b_qkv[channels : 2 * channels])
-    value_rows = project(normed_all, w_qkv[:, 2 * channels :], b_qkv[2 * channels :])
-    final = attend(start_state, queries, key_rows, value_rows)
+    for chunk in chunks:
+        normed_chunk = normalize(chunk, norm_gain)
+        key_rows = project(normed_chunk, w_qkv[:, channels : 2 * channels], b_qkv[channels : 2 * channels])
+        value_rows = project(normed_chunk, w_qkv[:, 2 * channels :], b_qkv[2 * channels :])
+        final = attend(final, queries, key_rows, value_rows)
     mixed = (final[2] / final[1]).astype(jnp.bfloat16)
     hidden = (
         frames.reshape(-1, channels).astype(jnp.float32)

time: 155 us -> 160 us (1.032)
  starting transfers between devices: 81.4 us -> 66.2 us
  matrix products: 24.1 us -> 37.6 us
  other arithmetic: 10.2 us -> 17.6 us
  local copies, waits for them, and re-layouts: 14.7 us -> 12.9 us
    ppermute x18 -> x11, starting transfers between devices: 64.4 us -> 49.6 us  [moved(): return lax.ppermute(value, 'space', [(s, target(s)) for s in range(count)])]
    dot_general x1 -> x4, matrix products: 8.07 us -> 15.7 us  [attend(): lax.dot_general(queries, key_rows, (((1,), (1,)), ((), ())), preferred_el...]
    dot_general x1 -> x4, matrix products: 8.4 us -> 13.6 us  [attend(): jnp.dot(weights.astype(jnp.bfloat16), value_rows, preferred_element_type=...]
    rsqrt x2 -> x5, other arithmetic: 0.01 us -> 2.43 us  [normalize(): lax.rsqrt(jnp.mean(widened * widened, axis=-1, keepdims=True) + EPSILON)]
    reduce_sum x2 -> x5, other arithmetic: 2.04 us -> 4.31 us  [normalize(): jnp.mean(widened * widened, axis=-1, keepdims=True) + EPSILON]
    ppermute x1, waiting for transfers between devices: 0.01 us -> 1.7 us  [with_halo(): lax.ppermute(lax.slice_in_dim(block, block.shape[dim] - width, None, axis...]
    ppermute x18 -> x11, waiting for transfers between devices: 7.26 us -> 7.84 us  [moved(): return lax.ppermute(value, 'space', [(s, target(s)) for s in range(count)])]
  transfers between devices with their start and end apart: 22 -> 15, of which waited for: 7 -> 8; matrix products, arithmetic and copies ran while one was open for 5% -> 16% of each run, Pallas kernels for 0% -> 0%
where the time goes in v3:
time: 160 us; the launch traced here: 159 us
  starting transfers between devices  66.2 us (41%)
  matrix products  37.6 us (24%)
  waiting for transfers between devices  24.4 us (15%)
  other arithmetic  17.6 us (11%)
  local copies, waits for them, and re-layouts  12.9 us (8%)
    ppermute x11, starting transfers between devices, moved(): return lax.ppermute(value, 'space', [(s, target(s)) for s in range(count)])  49.6 us
    dot_general x4, matrix products, attend(): lax.dot_general(queries, key_rows, (((1,), (1,)), ((), ())), preferred_el...  15.7 us
    dot_general x4, matrix products, attend(): jnp.dot(weights.astype(jnp.bfloat16), value_rows, preferred_element_type=...  13.6 us
    ppermute x1, waiting for transfers between devices, with_halo(): lax.ppermute(lax.slice_in_dim(block, 0, width, axis=dim), axis, backward)  8.3 us
    ppermute x11, waiting for transfers between devices, moved(): return lax.ppermute(value, 'space', [(s, target(s)) for s in range(count)])  7.84 us
    ppermute x1, starting transfers between devices, with_halo(): lax.ppermute(lax.slice_in_dim(block, block.shape[dim] - width, None, axis...  7.77 us
    ppermute x2, starting transfers between devices, shifted(): lax.ppermute(value, axis, [(source, source + steps) for source in range(l...  6.87 us
    ppermute x2, waiting for transfers between devices, shifted(): lax.ppermute(value, axis, [(source, source + steps) for source in range(l...  6.55 us
  transfers between devices with their start and end apart: 15, of which 8 were waited for; matrix products, arithmetic and copies ran while one was open for 16% of the time, Pallas kernels for 0%

profile of v3, /device:TPU:9, one launch (start us, length us, event | category | flops | bytes accessed | tf_op | source)
XLA Modules:
  0.0 159.2 jit_solution(2590005454546933517)
XLA Ops:
  0.0 6.7 %collective-permute-start = (bf16[192,384]{1,0:T(8,128)(2,1)}, bf16[192,384]{1,0:T(8,128)(2,1)S(1)}, u32[]{:S(2)}, u32[]{:S(2)}) collective-permute-start(bf16[192,384]{1,0:T(8,128)(2,1)} %bitcast.86), channel_id=1, source_target_pairs={{0,2},{1,3},{2,0},{3,1},{4,6},{5,7},{6,4},{7,5},{8,10},{9,11},{10,... | collective-permute-start | bytes 442376 | tf_op jit(solution)/shard_map/ppermute | solution.py:33
  6.7 1.0 fusion.76
  7.7 0.7 convert_element_type.121
  8.4 1.0 fusion.78
  9.5 1.4 collective-permute-done
  10.9 0.9 pad_maximum_fusion.2
  11.8 4.0 %collective-permute-start.1 = (bf16[384,384]{1,0:T(8,128)(2,1)S(1)}, bf16[384,384]{1,0:T(8,128)(2,1)S(1)}, u32[]{:S(2)}, u32[]{:S(2)}) collective-permute-start(bf16[384,384]{1,0:T(8,128)(2,1)S(1)} %pad_maximum_fusion.2), channel_id=1, source_target_pairs={{0,4},{1,5},{2,6},{3,7},{4,8},{5,9},{6,10},{7,11},{8,12},{9,13},{1... | collective-permute-start | bytes 884744 | tf_op jit(solution)/shard_map/ppermute | solution.py:33
  15.8 8.6 %collective-permute-start.2 = (bf16[384,384]{1,0:T(8,128)(2,1)S(1)}, bf16[384,384]{1,0:T(8,128)(2,1)S(1)}, u32[]{:S(2)}, u32[]{:S(2)}) collective-permute-start(bf16[384,384]{1,0:T(8,128)(2,1)S(1)} %pad_maximum_fusion.2), channel_id=1, source_target_pairs={{0,28},{1,29},{2,30},{3,31},{4,0},{5,1},{6,2},{7,3},{8,4},{9,5},{1... | collective-permute-start | bytes 884744 | tf_op jit(solution)/shard_map/ppermute | solution.py:33
  24.4 1.4 slice_convert_fusion.1
  25.8 1.3 convert_element_type.148
  27.1 0.7 convert_element_type.118
  27.8 1.9 %fusion.42 = bf16[192,384]{1,0:T(8,128)(2,1)} fusion(bf16[192,384]{1,0:T(8,128)(2,1)S(1)} %bitcast.95, bf16[384,1152]{1,0:T(8,128)(2,1)} %param.14, f32[384]{0:T(512)S(1)} %get-tuple-element.32), kind=kOutput, calls=%fused_computation.76 | convolution fusion | flops 56770560 | bytes 591360 | tf_op jit(solution)/shard_map/dot_general | solution.py:63
  29.6 1.9 %collective-permute-start.3 = (bf16[384,384]{1,0:T(8,128)(2,1)S(1)}, bf16[384,384]{1,0:T(8,128)(2,1)S(1)}, u32[]{:S(2)}, u32[]{:S(2)}) collective-permute-start(bf16[384,384]{1,0:T(8,128)(2,1)S(1)} %collective-permute-done.1), channel_id=1, source_target_pairs={{0,4},{1,5},{2,6},{3,7},{4,8},{5,9},{6,10},{7,11},{8,12},{9,13},{1... | collective-permute-start | bytes 884744 | tf_op jit(solution)/shard_map/ppermute | solution.py:33
  31.6 4.6 %collective-permute-start.4 = (bf16[384,384]{1,0:T(8,128)(2,1)S(1)}, bf16[384,384]{1,0:T(8,128)(2,1)S(1)}, u32[]{:S(2)}, u32[]{:S(2)}) collective-permute-start(bf16[384,384]{1,0:T(8,128)(2,1)S(1)} %collective-permute-done.2), channel_id=1, source_target_pairs={{0,28},{1,29},{2,30},{3,31},{4,0},{5,1},{6,2},{7,3},{8,4},{9,5},{1... | collective-permute-start | bytes 884744 | tf_op jit(solution)/shard_map/ppermute | solution.py:33
  36.2 0.7 fusion.126
  36.8 1.1 fusion.15
  38.0 7.0 %collective-permute-start.9 = (bf16[1152,384]{1,0:T(8,128)(2,1)}, bf16[1152,384]{1,0:T(8,128)(2,1)}, u32[]{:S(2)}, u32[]{:S(2)}) collective-permute-start(bf16[1152,384]{1,0:T(8,128)(2,1)} %get-tuple-element.13), channel_id=1, source_target_pairs={{0,1},{1,0},{2,3},{3,2},{4,5},{5,4},{6,7},{7,6},{8,9},{9,8},{10,11... | collective-permute-start | bytes 2654216 | tf_op jit(solution)/shard_map/ppermute | solution.py:33
  45.0 1.9 %collective-permute-start.5 = (bf16[384,384]{1,0:T(8,128)(2,1)S(1)}, bf16[384,384]{1,0:T(8,128)(2,1)S(1)}, u32[]{:S(2)}, u32[]{:S(2)}) collective-permute-start(bf16[384,384]{1,0:T(8,128)(2,1)S(1)} %collective-permute-done.3), channel_id=1, source_target_pairs={{0,4},{1,5},{2,6},{3,7},{4,8},{5,9},{6,10},{7,11},{8,12},{9,13},{1... | collective-permute-start | bytes 884744 | tf_op jit(solution)/shard_map/ppermute | solution.py:33
  46.9 4.6 %collective-permute-start.6 = (bf16[384,384]{1,0:T(8,128)(2,1)S(1)}, bf16[384,384]{1,0:T(8,128)(2,1)S(1)}, u32[]{:S(2)}, u32[]{:S(2)}) collective-permute-start(bf16[384,384]{1,0:T(8,128)(2,1)S(1)} %collective-permute-done.4), channel_id=1, source_target_pairs={{0,28},{1,29},{2,30},{3,31},{4,0},{5,1},{6,2},{7,3},{8,4},{9,5},{1... | collective-permute-start | bytes 884744 | tf_op jit(solution)/shard_map/ppermute | solution.py:33
  52.2 4.4 %collective-permute-done.5 = bf16[384,384]{1,0:T(8,128)(2,1)S(1)} collective-permute-done((bf16[384,384]{1,0:T(8,128)(2,1)S(1)}, bf16[384,384]{1,0:T(8,128)(2,1)S(1)}, u32[]{:S(2)}, u32[]{:S(2)}) %collective-permute-start.5) | collective-permute-done | bytes 294944 | tf_op jit(solution)/shard_map/ppermute | solution.py:33
  56.6 1.9 %collective-permute-start.7 = (bf16[192,384]{1,0:T(8,128)(2,1)S(1)}, bf16[192,384]{1,0:T(8,128)(2,1)S(1)}, u32[]{:S(2)}, u32[]{:S(2)}) collective-permute-start(bf16[192,384]{1,0:T(8,128)(2,1)S(1)} %slice.162), channel_id=1, source_target_pairs={{0,4},{1,5},{2,6},{3,7},{4,8},{5,9},{6,10},{7,11},{8,12},{9,13},{1... | collective-permute-start | bytes 442376 | tf_op jit(solution)/shard_map/ppermute | solution.py:33
  58.6 4.6 %collective-permute-start.8 = (bf16[192,384]{1,0:T(8,128)(2,1)S(1)}, bf16[192,384]{1,0:T(8,128)(2,1)S(1)}, u32[]{:S(2)}, u32[]{:S(2)}) collective-permute-start(bf16[192,384]{1,0:T(8,128)(2,1)S(1)} %slice.163), channel_id=1, source_target_pairs={{0,28},{1,29},{2,30},{3,31},{4,0},{5,1},{6,2},{7,3},{8,4},{9,5},{1... | collective-permute-start | bytes 442376 | tf_op jit(solution)/shard_map/ppermute | solution.py:33
  63.3 1.0 collective-permute-done.7
  64.3 1.0 collective-permute-done.8
  65.3 3.9 %collective-permute-start.10 = (bf16[1920,384]{1,0:T(8,128)(2,1)S(1)}, bf16[1920,384]{1,0:T(8,128)(2,1)S(1)}, u32[]{:S(2)}, u32[]{:S(2)}) collective-permute-start(bf16[1920,384]{1,0:T(8,128)(2,1)S(1)} %constant_dynamic-update-slice_fusion), channel_id=1, source_target_pairs={{0,1},{1,0},{2,3},{3,2},{4,5},{5,4},{6,7},{7,6},{8,9},{9,8},{10,11... | collective-permute-start | bytes 4423688 | tf_op jit(solution)/shard_map/ppermute | solution.py:33
  69.2 3.3 %fusion.137 = (f32[192]{0:T(256)S(1)}, f32[192,1152]{1,0:T(8,128)}) fusion(bf16[192,384]{1,0:T(8,128)(2,1)} %fusion.42, f32[384]{0:T(512)S(1)} %get-tuple-element.31, bf16[1152,384]{1,0:T(8,128)(2,1)} %get-tuple-element.13, f32[384]{0:T(512)S(1)} %convert_element_type.121, f32[1152]{0:T(1024)} %add_rsqrt_fusion.3, bf16[384,1152]{1,0:T(8,128)(2,1)} %param.14), kind=kOutput, calls=%fused_computation.172 | convolution fusion | flops 512704320 | bytes 2223872 | tf_op jit(solution)/shard_map/dot_general | solution.py:69
  73.5 4.3 %fusion.142 = (f32[192]{0:T(256)}, f32[192,1920]{1,0:T(8,128)}) fusion(bf16[192,384]{1,0:T(8,128)(2,1)} %fusion.42, f32[384]{0:T(512)S(1)} %get-tuple-element.31, bf16[1920,384]{1,0:T(8,128)(2,1)S(1)} %constant_dynamic-update-slice_fusion, f32[384]{0:T(512)S(1)} %convert_element_type.121, f32[1920]{0:T(1024)} %add_rsqrt_fusion.2, bf16[384,1152]{1,0:T(8,128)(2,1)} %param.14), kind=kOutput, calls=%fused_computation.173 | convolution fusion | flops 854507328 | bytes 3403520 | tf_op jit(solution)/shard_map/dot_general | solution.py:69
  77.8 1.4 fusion.18
  79.8 3.8 %fusion.132 = (f32[192]{0:T(256)}, f32[192,1152]{1,0:T(8,128)}) fusion(bf16[192,384]{1,0:T(8,128)(2,1)} %fusion.42, f32[384]{0:T(512)S(1)} %get-tuple-element.31, bf16[1152,384]{1,0:T(8,128)(2,1)} %collective-permute-done.9, f32[1152]{0:T(1024)} %add_rsqrt_fusion.1, f32[384]{0:T(512)S(1)} %convert_element_type.121, bf16[384,1152]{1,0:T(8,128)(2,1)} %param.14), kind=kOutput, calls=%fused_computation.171 | convolution fusion | flops 512704320 | bytes 2223872 | tf_op jit(solution)/shard_map/dot_general | solution.py:69
  84.6 4.3 %fusion.127 = (f32[192]{0:T(256)}, f32[192,1920]{1,0:T(8,128)}) fusion(bf16[192,384]{1,0:T(8,128)(2,1)} %fusion.42, f32[384]{0:T(512)S(1)} %get-tuple-element.31, bf16[1920,384]{1,0:T(8,128)(2,1)S(1)} %collective-permute-done.10, f32[1920]{0:T(1024)} %add_rsqrt_fusion, f32[384]{0:T(512)S(1)} %convert_element_type.121, bf16[384,1152]{1,0:T(8,128)(2,1)} %param.14), kind=kOutput, calls=%fused_computation.170 | convolution fusion | flops 854507328 | bytes 3403520 | tf_op jit(solution)/shard_map/dot_general | solution.py:69
  88.9 1.2 fusion.124
  90.1 3.7 %fusion.28 = f32[192,384]{1,0:T(8,128)} fusion(f32[384]{0:T(512)} %get-tuple-element.33, f32[192,1920]{1,0:T(8,128)} %get-tuple-element.42, f32[192]{0:T(256)} %get-tuple-element.11, bf16[1920,384]{1,0:T(8,128)(2,1)S(1)} %constant_dynamic-update-slice_fusion, f32[384]{0:T(512)} %copy-done.10, f32[1920]{0:T(1024)} %add_rsqrt_fusion.2, ...), kind=kOutput, calls=%fused_computation.59 | convolution fusion | flops 854507520 | bytes 3552256 | tf_op jit(solution)/shard_map/dot_general | solution.py:76
  93.8 2.5 %fusion.23 = (f32[192]{0:T(256)S(1)}, f32[192]{0:T(256)S(1)}) fusion(f32[192,1920]{1,0:T(8,128)} %get-tuple-element.42, f32[192]{0:T(256)} %get-tuple-element.11, f32[192,1920]{1,0:T(8,128)} %get-tuple-element.36, f32[192]{0:T(256)S(1)} %get-tuple-element.9), kind=kLoop, calls=%fused_computation.54 | loop fusion | flops 1474176 | bytes 2952192 | tf_op jit(solution)/shard_map/reduce_sum | solution.py:75
  97.6 3.5 %fusion.40 = f32[192,384]{1,0:T(8,128)} fusion(f32[192,384]{1,0:T(8,128)} %fusion.28, f32[384]{0:T(512)} %get-tuple-element.33, f32[192,1152]{1,0:T(8,128)} %get-tuple-element.40, f32[192]{0:T(256)S(1)} %get-tuple-element.39, bf16[1152,384]{1,0:T(8,128)(2,1)} %get-tuple-element.13, f32[384]{0:T(512)} %copy-done.10, f32[1152]{0:T(1024)} %add_rsqrt_fusion.3, ...), kind=kOutput, calls=%fused_computation.74 | convolution fusion | flops 512999424 | bytes 2670336 | tf_op jit(solution)/shard_map/dot_general | solution.py:76
  101.1 3.2 %fusion.27 = f32[192,384]{1,0:T(8,128)} fusion(f32[384]{0:T(512)} %get-tuple-element.33, f32[192,1920]{1,0:T(8,128)S(1)} %copy-done.3, f32[192]{0:T(256)S(1)} %get-tuple-element.9, bf16[1920,384]{1,0:T(8,128)(2,1)S(1)} %collective-permute-done.10, f32[1920]{0:T(1024)} %add_rsqrt_fusion, f32[384]{0:T(512)} %copy-done.10, bf16[384,1152]{1,0:T(8,128)(2,1)} %param.14), kind=kOutput, calls=%fused_computation.58 | convolution fusion | flops 854507520 | bytes 3552000 | tf_op jit(solution)/shard_map/dot_general | solution.py:76
  104.4 3.1 %fusion.41 = bf16[192,384]{1,0:T(8,128)(2,1)S(1)} fusion(f32[192,384]{1,0:T(8,128)} %fusion.27, f32[192,384]{1,0:T(8,128)} %fusion.40, f32[384]{0:T(512)} %get-tuple-element.33, f32[192,1152]{1,0:T(8,128)} %get-tuple-element.38, f32[192]{0:T(256)S(1)} %get-tuple-element.10, bf16[1152,384]{1,0:T(8,128)(2,1)} %collective-permute-done.9, ...), kind=kOutput, calls=%fused_computation.75 | convolution fusion | flops 513073152 | bytes 2816256 | tf_op jit(solution)/shard_map/dot_general | solution.py:76
  107.8 4.6 %collective-permute-start.11 = (bf16[192,384]{1,0:T(8,128)(2,1)S(1)}, bf16[192,384]{1,0:T(8,128)(2,1)S(1)}, u32[]{:S(2)}, u32[]{:S(2)}) collective-permute-start(bf16[192,384]{1,0:T(8,128)(2,1)S(1)} %fusion.43), channel_id=1, source_target_pairs={{0,64},{32,96},{64,128},{96,160},{128,192},{160,224},{192,256},{22... | collective-permute-start | bytes 442376 | tf_op jit(solution)/shard_map/ppermute | solution.py:12
  112.5 2.2 %collective-permute-start.12 = (bf16[192,384]{1,0:T(8,128)(2,1)S(1)}, bf16[192,384]{1,0:T(8,128)(2,1)S(1)}, u32[]{:S(2)}, u32[]{:S(2)}) collective-permute-start(bf16[192,384]{1,0:T(8,128)(2,1)S(1)} %fusion.43), channel_id=1, source_target_pairs={{0,32},{32,64},{64,96},{96,128},{128,160},{160,192},{192,224},{224... | collective-permute-start | bytes 442376 | tf_op jit(solution)/shard_map/ppermute | solution.py:12
  115.0 2.5 %collective-permute-done.11 = bf16[192,384]{1,0:T(8,128)(2,1)S(1)} collective-permute-done((bf16[192,384]{1,0:T(8,128)(2,1)S(1)}, bf16[192,384]{1,0:T(8,128)(2,1)S(1)}, u32[]{:S(2)}, u32[]{:S(2)}) %collective-permute-start.11) | collective-permute-done | bytes 147488 | tf_op jit(solution)/shard_map/ppermute | solution.py:12
  117.5 4.1 %collective-permute-done.12 = bf16[192,384]{1,0:T(8,128)(2,1)S(1)} collective-permute-done((bf16[192,384]{1,0:T(8,128)(2,1)S(1)}, bf16[192,384]{1,0:T(8,128)(2,1)S(1)}, u32[]{:S(2)}, u32[]{:S(2)}) %collective-permute-start.12) | collective-permute-done | bytes 147488 | tf_op jit(solution)/shard_map/ppermute | solution.py:12
  122.4 7.8 %collective-permute-start.13 = (bf16[2,1,96,384]{3,2,1,0:T(8,128)(2,1)S(1)}, bf16[2,1,96,384]{3,2,1,0:T(8,128)(2,1)S(1)}, u32[]{:S(2)}, u32[]{:S(2)}) collective-permute-start(bf16[2,1,96,384]{3,2,1,0:T(8,128)(2,1)S(1)} %get-tuple-element.23), channel_id=1, source_target_pairs={{0,1},{1,2},{2,3},{3,4},{4,5},{5,6},{6,7},{7,8},{8,9},{9,10},{10,1... | collective-permute-start | bytes 442376 | tf_op jit(solution)/shard_map/ppermute | solution.py:20
  130.2 1.9 %collective-permute-start.14 = (bf16[2,1,96,384]{3,2,1,0:T(8,128)(2,1)S(1)}, bf16[2,1,96,384]{3,2,1,0:T(8,128)(2,1)S(1)}, u32[]{:S(2)}, u32[]{:S(2)}) collective-permute-start(bf16[2,1,96,384]{3,2,1,0:T(8,128)(2,1)S(1)} %get-tuple-element.24), channel_id=1, source_target_pairs={{1,0},{2,1},{3,2},{4,3},{5,4},{6,5},{7,6},{8,7},{9,8},{10,9},{11,1... | collective-permute-start | bytes 442376 | tf_op jit(solution)/shard_map/ppermute | solution.py:23
  132.1 1.7 %collective-permute-done.13 = bf16[2,1,96,384]{3,2,1,0:T(8,128)(2,1)S(1)} collective-permute-done((bf16[2,1,96,384]{3,2,1,0:T(8,128)(2,1)S(1)}, bf16[2,1,96,384]{3,2,1,0:T(8,128)(2,1)S(1)}, u32[]{:S(2)}, u32[]{:S(2)}) %collective-permute-start.13) | collective-permute-done | bytes 147488 | tf_op jit(solution)/shard_map/ppermute | solution.py:20
  133.8 8.3 %collective-permute-done.14 = bf16[2,1,96,384]{3,2,1,0:T(8,128)(2,1)S(1)} collective-permute-done((bf16[2,1,96,384]{3,2,1,0:T(8,128)(2,1)S(1)}, bf16[2,1,96,384]{3,2,1,0:T(8,128)(2,1)S(1)}, u32[]{:S(2)}, u32[]{:S(2)}) %collective-permute-start.14) | collective-permute-done | bytes 147488 | tf_op jit(solution)/shard_map/ppermute | solution.py:23
  142.4 2.3 %broadcast_in_dim.11 = bf16[2,6,96,2,384]{4,3,2,1,0:T(2,128)(2,1)} broadcast(bf16[2,6,96,384]{3,2,1,0:T(8,128)(2,1)S(1)} %slice.168), dimensions={0,1,2,4} | broadcast | bytes 2654208 | tf_op jit(solution)/shard_map/broadcast_in_dim | solution.py:124
  144.7 4.0 %reshape.204 = bf16[2,6,192,384]{3,2,1,0:T(8,128)(2,1)S(1)} reshape(bf16[2,6,96,2,384]{4,3,2,1,0:T(2,128)(2,1)} %broadcast_in_dim.11) | data formatting | bytes 3538944 | tf_op jit(solution)/shard_map/reshape | solution.py:124
  148.7 4.0 %pad_slice_fusion = (bf16[2,4,192,384]{3,2,1,0:T(8,128)(2,1)S(1)}, bf16[2,4,192,384]{3,2,1,0:T(8,128)(2,1)S(1)}, bf16[2,4,192,384]{3,2,1,0:T(8,128)(2,1)S(1)}, b...) fusion(bf16[2,6,192,384]{3,2,1,0:T(8,128)(2,1)S(1)} %reshape.204), kind=kLoop, calls=%fused_computation.78 | loop fusion | bytes 15925248 | tf_op jit(solution)/shard_map/slice | solution.py:130
  158.0 1.2 copy.13
  (72 shorter events, 11.5 us)
Async XLA Ops:
  0.0 107.5 %copy-start = (bf16[384,384]{1,0:T(8,128)(2,1)S(1)}, bf16[384,384]{1,0:T(8,128)(2,1)}, u32[]{:S(2)}) copy-start(bf16[384,384]{1,0:T(8,128)(2,1)} %param.16) | copy-start | bytes 884740
  0.0 36.8 %copy-start.1 = (bf16[1,2,96,384]{3,2,1,0:T(8,128)(2,1)S(1)}, bf16[1,2,96,384]{3,2,1,0:T(8,128)(2,1)}, u32[]{:S(2)}) copy-start(bf16[1,2,96,384]{3,2,1,0:T(8,128)(2,1)} %param.11) | copy-start | bytes 442372
  0.0 36.1 %copy-start.8 = (bf16[2,2,96,384]{3,2,1,0:T(8,128)(2,1)S(1)}, bf16[2,2,96,384]{3,2,1,0:T(8,128)(2,1)}, u32[]{:S(2)}) copy-start(bf16[2,2,96,384]{3,2,1,0:T(8,128)(2,1)} %param.12) | copy-start | bytes 884740
  0.0 10.9 %collective-permute-start = (bf16[192,384]{1,0:T(8,128)(2,1)}, bf16[192,384]{1,0:T(8,128)(2,1)S(1)}, u32[]{:S(2)}, u32[]{:S(2)}) collective-permute-start(bf16[192,384]{1,0:T(8,128)(2,1)} %bitcast.86), channel_id=1, source_target_pairs={{0,2},{1,3},{2,0},{3,1},{4,6},{5,7},{6,4},{7,5},{8,10},{9,11},{10,... | collective-permute-start | bytes 442376 | tf_op jit(solution)/shard_map/ppermute | solution.py:33
  8.4 76.2 %copy-start.10 = (f32[384]{0:T(512)}, f32[384]{0:T(512)S(1)}, u32[]{:S(2)}) copy-start(f32[384]{0:T(512)S(1)} %convert_element_type.121) | copy-start | bytes 4612
  11.8 17.8 %collective-permute-start.1 = (bf16[384,384]{1,0:T(8,128)(2,1)S(1)}, bf16[384,384]{1,0:T(8,128)(2,1)S(1)}, u32[]{:S(2)}, u32[]{:S(2)}) collective-permute-start(bf16[384,384]{1,0:T(8,128)(2,1)S(1)} %pad_maximum_fusion.2), channel_id=1, source_target_pairs={{0,4},{1,5},{2,6},{3,7},{4,8},{5,9},{6,10},{7,11},{8,12},{9,13},{1... | collective-permute-start | bytes 884744 | tf_op jit(solution)/shard_map/ppermute | solution.py:33
  15.8 15.7 %collective-permute-start.2 = (bf16[384,384]{1,0:T(8,128)(2,1)S(1)}, bf16[384,384]{1,0:T(8,128)(2,1)S(1)}, u32[]{:S(2)}, u32[]{:S(2)}) collective-permute-start(bf16[384,384]{1,0:T(8,128)(2,1)S(1)} %pad_maximum_fusion.2), channel_id=1, source_target_pairs={{0,28},{1,29},{2,30},{3,31},{4,0},{5,1},{6,2},{7,3},{8,4},{9,5},{1... | collective-permute-start | bytes 884744 | tf_op jit(solution)/shard_map/ppermute | solution.py:33
  29.6 15.3 %collective-permute-start.3 = (bf16[384,384]{1,0:T(8,128)(2,1)S(1)}, bf16[384,384]{1,0:T(8,128)(2,1)S(1)}, u32[]{:S(2)}, u32[]{:S(2)}) collective-permute-start(bf16[384,384]{1,0:T(8,128)(2,1)S(1)} %collective-permute-done.1), channel_id=1, source_target_pairs={{0,4},{1,5},{2,6},{3,7},{4,8},{5,9},{6,10},{7,11},{8,12},{9,13},{1... | collective-permute-start | bytes 884744 | tf_op jit(solution)/shard_map/ppermute | solution.py:33
  31.6 15.3 %collective-permute-start.4 = (bf16[384,384]{1,0:T(8,128)(2,1)S(1)}, bf16[384,384]{1,0:T(8,128)(2,1)S(1)}, u32[]{:S(2)}, u32[]{:S(2)}) collective-permute-start(bf16[384,384]{1,0:T(8,128)(2,1)S(1)} %collective-permute-done.2), channel_id=1, source_target_pairs={{0,28},{1,29},{2,30},{3,31},{4,0},{5,1},{6,2},{7,3},{8,4},{9,5},{1... | collective-permute-start | bytes 884744 | tf_op jit(solution)/shard_map/ppermute | solution.py:33
  38.0 39.8 %collective-permute-start.9 = (bf16[1152,384]{1,0:T(8,128)(2,1)}, bf16[1152,384]{1,0:T(8,128)(2,1)}, u32[]{:S(2)}, u32[]{:S(2)}) collective-permute-start(bf16[1152,384]{1,0:T(8,128)(2,1)} %get-tuple-element.13), channel_id=1, source_target_pairs={{0,1},{1,0},{2,3},{3,2},{4,5},{5,4},{6,7},{7,6},{8,9},{9,8},{10,11... | collective-permute-start | bytes 2654216 | tf_op jit(solution)/shard_map/ppermute | solution.py:33
  45.0 11.7 %collective-permute-start.5 = (bf16[384,384]{1,0:T(8,128)(2,1)S(1)}, bf16[384,384]{1,0:T(8,128)(2,1)S(1)}, u32[]{:S(2)}, u32[]{:S(2)}) collective-permute-start(bf16[384,384]{1,0:T(8,128)(2,1)S(1)} %collective-permute-done.3), channel_id=1, source_target_pairs={{0,4},{1,5},{2,6},{3,7},{4,8},{5,9},{6,10},{7,11},{8,12},{9,13},{1... | collective-permute-start | bytes 884744 | tf_op jit(solution)/shard_map/ppermute | solution.py:33
  46.9 11.7 %collective-permute-start.6 = (bf16[384,384]{1,0:T(8,128)(2,1)S(1)}, bf16[384,384]{1,0:T(8,128)(2,1)S(1)}, u32[]{:S(2)}, u32[]{:S(2)}) collective-permute-start(bf16[384,384]{1,0:T(8,128)(2,1)S(1)} %collective-permute-done.4), channel_id=1, source_target_pairs={{0,28},{1,29},{2,30},{3,31},{4,0},{5,1},{6,2},{7,3},{8,4},{9,5},{1... | collective-permute-start | bytes 884744 | tf_op jit(solution)/shard_map/ppermute | solution.py:33
  56.6 7.6 %collective-permute-start.7 = (bf16[192,384]{1,0:T(8,128)(2,1)S(1)}, bf16[192,384]{1,0:T(8,128)(2,1)S(1)}, u32[]{:S(2)}, u32[]{:S(2)}) collective-permute-start(bf16[192,384]{1,0:T(8,128)(2,1)S(1)} %slice.162), channel_id=1, source_target_pairs={{0,4},{1,5},{2,6},{3,7},{4,8},{5,9},{6,10},{7,11},{8,12},{9,13},{1... | collective-permute-start | bytes 442376 | tf_op jit(solution)/shard_map/ppermute | solution.py:33
  58.6 6.7 %collective-permute-start.8 = (bf16[192,384]{1,0:T(8,128)(2,1)S(1)}, bf16[192,384]{1,0:T(8,128)(2,1)S(1)}, u32[]{:S(2)}, u32[]{:S(2)}) collective-permute-start(bf16[192,384]{1,0:T(8,128)(2,1)S(1)} %slice.163), channel_id=1, source_target_pairs={{0,28},{1,29},{2,30},{3,31},{4,0},{5,1},{6,2},{7,3},{8,4},{9,5},{1... | collective-permute-start | bytes 442376 | tf_op jit(solution)/shard_map/ppermute | solution.py:33
  65.3 18.4 %collective-permute-start.10 = (bf16[1920,384]{1,0:T(8,128)(2,1)S(1)}, bf16[1920,384]{1,0:T(8,128)(2,1)S(1)}, u32[]{:S(2)}, u32[]{:S(2)}) collective-permute-start(bf16[1920,384]{1,0:T(8,128)(2,1)S(1)} %constant_dynamic-update-slice_fusion), channel_id=1, source_target_pairs={{0,1},{1,0},{2,3},{3,2},{4,5},{5,4},{6,7},{7,6},{8,9},{9,8},{10,11... | collective-permute-start | bytes 4423688 | tf_op jit(solution)/shard_map/ppermute | solution.py:33
  93.8 2.5 %copy-start.5 = (f32[192,1152]{1,0:T(8,128)S(1)}, f32[192,1152]{1,0:T(8,128)}, u32[]{:S(2)}) copy-start(f32[192,1152]{1,0:T(8,128)} %get-tuple-element.38) | copy-start | bytes 2654212
  93.8 2.5 %copy-start.6 = (f32[192,1152]{1,0:T(8,128)S(1)}, f32[192,1152]{1,0:T(8,128)}, u32[]{:S(2)}) copy-start(f32[192,1152]{1,0:T(8,128)} %get-tuple-element.40) | copy-start | bytes 2654212
  96.3 0.6 copy-start.9
  97.6 3.6 %copy-start.3 = (f32[192,1920]{1,0:T(8,128)S(1)}, f32[192,1920]{1,0:T(8,128)}, u32[]{:S(2)}) copy-start(f32[192,1920]{1,0:T(8,128)} %get-tuple-element.36) | copy-start | bytes 4423684
  101.1 3.3 %copy-start.11 = (f32[384]{0:T(512)S(1)}, f32[384]{0:T(512)}, u32[]{:S(2)}) copy-start(f32[384]{0:T(512)} %copy-done.10) | copy-start | bytes 4612
  104.4 3.2 %copy-start.12 = (f32[384]{0:T(512)S(1)}, f32[384]{0:T(512)}, u32[]{:S(2)}) copy-start(f32[384]{0:T(512)} %convert_element_type.148) | copy-start | bytes 4612
  104.4 10.3 %copy-start.2 = (bf16[3,384,768]{2,1,0:T(8,128)(2,1)S(1)}, bf16[3,384,768]{2,1,0:T(8,128)(2,1)}, u32[]{:S(2)}) copy-start(bf16[3,384,768]{2,1,0:T(8,128)(2,1)} %param.18) | copy-start | bytes 5308420
  107.5 14.0 %copy-start.7 = (bf16[1,2,96,384]{3,2,1,0:T(8,128)(2,1)S(1)}, bf16[1,2,96,384]{3,2,1,0:T(8,128)(2,1)}, u32[]{:S(2)}) copy-start(bf16[1,2,96,384]{3,2,1,0:T(8,128)(2,1)} %get-tuple-element.28) | copy-start | bytes 442372
  107.8 9.7 %collective-permute-start.11 = (bf16[192,384]{1,0:T(8,128)(2,1)S(1)}, bf16[192,384]{1,0:T(8,128)(2,1)S(1)}, u32[]{:S(2)}, u32[]{:S(2)}) collective-permute-start(bf16[192,384]{1,0:T(8,128)(2,1)S(1)} %fusion.43), channel_id=1, source_target_pairs={{0,64},{32,96},{64,128},{96,160},{128,192},{160,224},{192,256},{22... | collective-permute-start | bytes 442376 | tf_op jit(solution)/shard_map/ppermute | solution.py:12
  112.5 9.1 %collective-permute-start.12 = (bf16[192,384]{1,0:T(8,128)(2,1)S(1)}, bf16[192,384]{1,0:T(8,128)(2,1)S(1)}, u32[]{:S(2)}, u32[]{:S(2)}) collective-permute-start(bf16[192,384]{1,0:T(8,128)(2,1)S(1)} %fusion.43), channel_id=1, source_target_pairs={{0,32},{32,64},{64,96},{96,128},{128,160},{160,192},{192,224},{224... | collective-permute-start | bytes 442376 | tf_op jit(solution)/shard_map/ppermute | solution.py:12
  122.0 10.1 %copy-start.13 = (bf16[192]{0:T(256)(128)(2,1)S(1)}, bf16[192]{0:T(256)(128)(2,1)}, u32[]{:S(2)}) copy-start(bf16[192]{0:T(256)(128)(2,1)} %param.21) | copy-start | bytes 1156
  122.4 11.4 %collective-permute-start.13 = (bf16[2,1,96,384]{3,2,1,0:T(8,128)(2,1)S(1)}, bf16[2,1,96,384]{3,2,1,0:T(8,128)(2,1)S(1)}, u32[]{:S(2)}, u32[]{:S(2)}) collective-permute-start(bf16[2,1,96,384]{3,2,1,0:T(8,128)(2,1)S(1)} %get-tuple-element.23), channel_id=1, source_target_pairs={{0,1},{1,2},{2,3},{3,4},{4,5},{5,6},{6,7},{7,8},{8,9},{9,10},{10,1... | collective-permute-start | bytes 442376 | tf_op jit(solution)/shard_map/ppermute | solution.py:20
  130.2 11.9 %collective-permute-start.14 = (bf16[2,1,96,384]{3,2,1,0:T(8,128)(2,1)S(1)}, bf16[2,1,96,384]{3,2,1,0:T(8,128)(2,1)S(1)}, u32[]{:S(2)}, u32[]{:S(2)}) collective-permute-start(bf16[2,1,96,384]{3,2,1,0:T(8,128)(2,1)S(1)} %get-tuple-element.24), channel_id=1, source_target_pairs={{1,0},{2,1},{3,2},{4,3},{5,4},{6,5},{7,6},{8,7},{9,8},{10,9},{11,1... | collective-permute-start | bytes 442376 | tf_op jit(solution)/shard_map/ppermute | solution.py:23
  148.7 4.0 %copy-start.4 = (bf16[3,3,384,192]{2,3,1,0:T(8,128)(2,1)S(1)}, bf16[3,3,384,192]{2,3,1,0:T(8,128)(2,1)}, u32[]{:S(2)}) copy-start(bf16[3,3,384,192]{2,3,1,0:T(8,128)(2,1)} %param.20) | copy-start | bytes 3981316

commit v4 on v3

--- a/solution.py
+++ b/solution.py
@@ -1,6 +1,10 @@
+import functools
+
 import jax
 import jax.numpy as jnp
 from jax import lax
+from jax.experimental import pallas as pl
+from jax.experimental.pallas import tpu as pltpu
 from jax.sharding import PartitionSpec as P
 
 EPSILON = 1e-06
@@ -78,6 +82,69 @@
     )
     return (new_best, mass, total_sum)
 
+BLOCK = 384
+
+
+def attention_kernel(*refs, sizes, channels):
+    q_ref, gain_ref, wk_ref, bk_ref, wv_ref, bv_ref = refs[:6]
+    chunk_refs = refs[6:6 + len(sizes)]
+    out_ref = refs[6 + len(sizes)]
+    queries = q_ref[...]
+    gain = gain_ref[...]
+    wk = wk_ref[...]
+    wv = wv_ref[...]
+    bk = bk_ref[...]
+    bv = bv_ref[...]
+    count = queries.shape[0]
+    best = jnp.full((count, 1), -jnp.inf, jnp.float32)
+    mass = jnp.zeros((count, 1), jnp.float32)
+    total = jnp.zeros((count, channels), jnp.float32)
+    for chunk_ref, size in zip(chunk_refs, sizes):
+        for start in range(0, size, BLOCK):
+            rows = chunk_ref[start:start + BLOCK, :].astype(jnp.float32)
+            inverse = lax.rsqrt(jnp.mean(rows * rows, axis=-1, keepdims=True) + EPSILON)
+            normed = (rows * inverse * gain).astype(jnp.bfloat16)
+            keys = (jnp.dot(normed, wk, preferred_element_type=jnp.float32) + bk).astype(jnp.bfloat16)
+            values = (jnp.dot(normed, wv, preferred_element_type=jnp.float32) + bv).astype(jnp.bfloat16)
+            scores = lax.dot_general(
+                queries, keys, (((1,), (1,)), ((), ())), preferred_element_type=jnp.float32
+            ) * channels ** (-0.5)
+            new_best = jnp.maximum(best, jnp.max(scores, axis=1, keepdims=True))
+            correction = jnp.exp(best - new_best)
+            weights = jnp.exp(scores - new_best)
+            mass = mass * correction + jnp.sum(weights, axis=1, keepdims=True)
+            total = total * correction + jnp.dot(
+                weights.astype(jnp.bfloat16), values, preferred_element_type=jnp.float32
+            )
+            best = new_best
+    out_ref[...] = (total / mass).astype(out_ref.dtype)
+
+
+def fused_attention(queries, chunks, norm_gain, w_qkv, b_qkv):
+    channels = queries.shape[1]
+    sizes = tuple(c.shape[0] for c in chunks)
+    gain = norm_gain.astype(jnp.float32).reshape(1, channels)
+    wk = w_qkv[:, channels:2 * channels]
+    wv = w_qkv[:, 2 * channels:]
+    bk = b_qkv[channels:2 * channels].astype(jnp.float32).reshape(1, channels)
+    bv = b_qkv[2 * channels:].astype(jnp.float32).reshape(1, channels)
+    vmem = pltpu.MemorySpace.VMEM
+    spec = pl.BlockSpec(memory_space=vmem)
+    total_rows = sum(sizes)
+    flops = 2 * total_rows * channels * (2 * channels + 2 * queries.shape[0])
+    return pl.pallas_call(
+        functools.partial(attention_kernel, sizes=sizes, channels=channels),
+        out_shape=jax.ShapeDtypeStruct(queries.shape, jnp.bfloat16),
+        in_specs=[spec] * (6 + len(chunks)),
+        out_specs=spec,
+        compiler_params=pltpu.CompilerParams(vmem_limit_bytes=48 * 1024 * 1024),
+        cost_estimate=pl.CostEstimate(
+            flops=flops,
+            transcendentals=total_rows * queries.shape[0],
+            bytes_accessed=2 * total_rows * channels + 4 * channels * channels + 4 * queries.size,
+        ),
+    )(queries, gain, wk, bk, wv, bv, *chunks)
+
 
 def body(
     frames, cache_in, norm_gain, w_qkv, b_qkv, w_proj, b_proj, w_time, b_time, w_space, b_space
@@ -88,18 +155,7 @@
     chunks = gather_space(frames.reshape(-1, channels))
     normed = normalize(frames, norm_gain).reshape(-1, channels)
     queries = project(normed, w_qkv[:, :channels], b_qkv[:channels])
-    count = queries.shape[0]
-    final = (
-        jnp.full((count, 1), -jnp.inf, jnp.float32),
-        jnp.zeros((count, 1), jnp.float32),
-        jnp.zeros((count, channels), jnp.float32),
-    )
-    for chunk in chunks:
-        normed_chunk = normalize(chunk, norm_gain)
-        key_rows = project(normed_chunk, w_qkv[:, channels : 2 * channels], b_qkv[channels : 2 * channels])
-        value_rows = project(normed_chunk, w_qkv[:, 2 * channels :], b_qkv[2 * channels :])
-        final = attend(final, queries, key_rows, value_rows)
-    mixed = (final[2] / final[1]).astype(jnp.bfloat16)
+    mixed = fused_attention(queries, chunks, norm_gain, w_qkv, b_qkv)
     hidden = (
         frames.reshape(-1, channels).astype(jnp.float32)
         + jnp.dot(mixed, w_proj, preferred_element_type=jnp.float32)

time: 160 us -> 137 us (0.86)
  the two profiles are of different devices: /device:TPU:9 before, /device:TPU:17 now
where the time goes in v4:
time: 137 us; the launch traced here: 136 us
  starting transfers between devices  60.1 us (44%)
  waiting for transfers between devices  37.5 us (27%)
  Pallas kernels  12.8 us (9%)
  local copies, waits for them, and re-layouts  12.1 us (9%)
  matrix products  6.79 us (5%)
  other arithmetic  6.51 us (5%)
    ppermute x11, starting transfers between devices, moved(): return lax.ppermute(value, 'space', [(s, target(s)) for s in range(count)])  47.2 us
    ppermute x11, waiting for transfers between devices, moved(): return lax.ppermute(value, 'space', [(s, target(s)) for s in range(count)])  21.9 us
    pallas_call x1, Pallas kernels, fused_attention(): pl.pallas_call(functools.partial(attention_kernel, sizes=sizes, channels=...  12.8 us
    ppermute x1, waiting for transfers between devices, with_halo(): lax.ppermute(lax.slice_in_dim(block, 0, width, axis=dim), axis, backward)  8.69 us
    ppermute x2, starting transfers between devices, shifted(): lax.ppermute(value, axis, [(source, source + steps) for source in range(l...  6.87 us
    ppermute x2, waiting for transfers between devices, shifted(): lax.ppermute(value, axis, [(source, source + steps) for source in range(l...  6.46 us
    dot_general x9, matrix products, body(): jnp.dot(window, w_space[row_tap, col_tap], preferred_element_type=jnp.flo...  5.18 us
    ppermute x1, starting transfers between devices, with_halo(): lax.ppermute(lax.slice_in_dim(block, block.shape[dim] - width, None, axis...  4.06 us
  transfers between devices with their start and end apart: 15, of which 11 were waited for; matrix products, arithmetic and copies ran while one was open for 5% of the time, Pallas kernels for 0%

profile of v4, /device:TPU:17, one launch (start us, length us, event | category | flops | bytes accessed | tf_op | source)
XLA Modules:
  0.0 136.4 jit_solution(11037499815275076828)
XLA Ops:
  0.0 5.8 %collective-permute-start = (bf16[192,384]{1,0:T(8,128)(2,1)}, bf16[192,384]{1,0:T(8,128)(2,1)S(1)}, u32[]{:S(2)}, u32[]{:S(2)}) collective-permute-start(bf16[192,384]{1,0:T(8,128)(2,1)} %bitcast.82), channel_id=1, source_target_pairs={{0,2},{1,3},{2,0},{3,1},{4,6},{5,7},{6,4},{7,5},{8,10},{9,11},{10,... | collective-permute-start | bytes 442376 | tf_op jit(solution)/shard_map/ppermute | solution.py:37
  5.8 7.7 %collective-permute-done = bf16[192,384]{1,0:T(8,128)(2,1)S(1)} collective-permute-done((bf16[192,384]{1,0:T(8,128)(2,1)}, bf16[192,384]{1,0:T(8,128)(2,1)S(1)}, u32[]{:S(2)}, u32[]{:S(2)}) %collective-permute-start) | collective-permute-done | bytes 147488 | tf_op jit(solution)/shard_map/ppermute | solution.py:37
  13.4 0.9 pad_maximum_fusion.2
  14.4 5.6 %collective-permute-start.1 = (bf16[384,384]{1,0:T(8,128)(2,1)S(1)}, bf16[384,384]{1,0:T(8,128)(2,1)S(1)}, u32[]{:S(2)}, u32[]{:S(2)}) collective-permute-start(bf16[384,384]{1,0:T(8,128)(2,1)S(1)} %pad_maximum_fusion.2), channel_id=1, source_target_pairs={{0,4},{1,5},{2,6},{3,7},{4,8},{5,9},{6,10},{7,11},{8,12},{9,13},{1... | collective-permute-start | bytes 884744 | tf_op jit(solution)/shard_map/ppermute | solution.py:37
  20.0 8.6 %collective-permute-start.2 = (bf16[384,384]{1,0:T(8,128)(2,1)S(1)}, bf16[384,384]{1,0:T(8,128)(2,1)S(1)}, u32[]{:S(2)}, u32[]{:S(2)}) collective-permute-start(bf16[384,384]{1,0:T(8,128)(2,1)S(1)} %pad_maximum_fusion.2), channel_id=1, source_target_pairs={{0,28},{1,29},{2,30},{3,31},{4,0},{5,1},{6,2},{7,3},{8,4},{9,5},{1... | collective-permute-start | bytes 884744 | tf_op jit(solution)/shard_map/ppermute | solution.py:37
  28.6 4.8 %collective-permute-done.1 = bf16[384,384]{1,0:T(8,128)(2,1)S(1)} collective-permute-done((bf16[384,384]{1,0:T(8,128)(2,1)S(1)}, bf16[384,384]{1,0:T(8,128)(2,1)S(1)}, u32[]{:S(2)}, u32[]{:S(2)}) %collective-permute-start.1) | collective-permute-done | bytes 294944 | tf_op jit(solution)/shard_map/ppermute | solution.py:37
  33.4 1.9 %collective-permute-start.3 = (bf16[384,384]{1,0:T(8,128)(2,1)S(1)}, bf16[384,384]{1,0:T(8,128)(2,1)S(1)}, u32[]{:S(2)}, u32[]{:S(2)}) collective-permute-start(bf16[384,384]{1,0:T(8,128)(2,1)S(1)} %collective-permute-done.1), channel_id=1, source_target_pairs={{0,4},{1,5},{2,6},{3,7},{4,8},{5,9},{6,10},{7,11},{8,12},{9,13},{1... | collective-permute-start | bytes 884744 | tf_op jit(solution)/shard_map/ppermute | solution.py:37
  35.4 4.6 %collective-permute-start.4 = (bf16[384,384]{1,0:T(8,128)(2,1)S(1)}, bf16[384,384]{1,0:T(8,128)(2,1)S(1)}, u32[]{:S(2)}, u32[]{:S(2)}) collective-permute-start(bf16[384,384]{1,0:T(8,128)(2,1)S(1)} %collective-permute-done.2), channel_id=1, source_target_pairs={{0,28},{1,29},{2,30},{3,31},{4,0},{5,1},{6,2},{7,3},{8,4},{9,5},{1... | collective-permute-start | bytes 884744 | tf_op jit(solution)/shard_map/ppermute | solution.py:37
  39.9 4.0 %collective-permute-done.3 = bf16[384,384]{1,0:T(8,128)(2,1)S(1)} collective-permute-done((bf16[384,384]{1,0:T(8,128)(2,1)S(1)}, bf16[384,384]{1,0:T(8,128)(2,1)S(1)}, u32[]{:S(2)}, u32[]{:S(2)}) %collective-permute-start.3) | collective-permute-done | bytes 294944 | tf_op jit(solution)/shard_map/ppermute | solution.py:37
  43.9 1.9 %collective-permute-start.5 = (bf16[384,384]{1,0:T(8,128)(2,1)S(1)}, bf16[384,384]{1,0:T(8,128)(2,1)S(1)}, u32[]{:S(2)}, u32[]{:S(2)}) collective-permute-start(bf16[384,384]{1,0:T(8,128)(2,1)S(1)} %collective-permute-done.3), channel_id=1, source_target_pairs={{0,4},{1,5},{2,6},{3,7},{4,8},{5,9},{6,10},{7,11},{8,12},{9,13},{1... | collective-permute-start | bytes 884744 | tf_op jit(solution)/shard_map/ppermute | solution.py:37
  45.9 4.6 %collective-permute-start.6 = (bf16[384,384]{1,0:T(8,128)(2,1)S(1)}, bf16[384,384]{1,0:T(8,128)(2,1)S(1)}, u32[]{:S(2)}, u32[]{:S(2)}) collective-permute-start(bf16[384,384]{1,0:T(8,128)(2,1)S(1)} %collective-permute-done.4), channel_id=1, source_target_pairs={{0,28},{1,29},{2,30},{3,31},{4,0},{5,1},{6,2},{7,3},{8,4},{9,5},{1... | collective-permute-start | bytes 884744 | tf_op jit(solution)/shard_map/ppermute | solution.py:37
  50.4 1.4 %slice_convert_fusion = (f32[384]{0:T(512)S(1)}, f32[384]{0:T(512)}, f32[384]{0:T(512)S(1)}) fusion(bf16[1152]{0:T(1024)(128)(2,1)} %param.15), kind=kLoop, calls=%fused_computation.73 | loop fusion | flops 1152 | bytes 6912 | tf_op jit(solution)/shard_map/reshape | solution.py:130
  51.9 1.6 %collective-permute-done.5 = bf16[384,384]{1,0:T(8,128)(2,1)S(1)} collective-permute-done((bf16[384,384]{1,0:T(8,128)(2,1)S(1)}, bf16[384,384]{1,0:T(8,128)(2,1)S(1)}, u32[]{:S(2)}, u32[]{:S(2)}) %collective-permute-start.5) | collective-permute-done | bytes 294944 | tf_op jit(solution)/shard_map/ppermute | solution.py:37
  53.6 1.9 %collective-permute-start.7 = (bf16[192,384]{1,0:T(8,128)(2,1)S(1)}, bf16[192,384]{1,0:T(8,128)(2,1)S(1)}, u32[]{:S(2)}, u32[]{:S(2)}) collective-permute-start(bf16[192,384]{1,0:T(8,128)(2,1)S(1)} %slice.150), channel_id=1, source_target_pairs={{0,4},{1,5},{2,6},{3,7},{4,8},{5,9},{6,10},{7,11},{8,12},{9,13},{1... | collective-permute-start | bytes 442376 | tf_op jit(solution)/shard_map/ppermute | solution.py:37
  55.5 4.6 %collective-permute-start.8 = (bf16[192,384]{1,0:T(8,128)(2,1)S(1)}, bf16[192,384]{1,0:T(8,128)(2,1)S(1)}, u32[]{:S(2)}, u32[]{:S(2)}) collective-permute-start(bf16[192,384]{1,0:T(8,128)(2,1)S(1)} %slice.151), channel_id=1, source_target_pairs={{0,28},{1,29},{2,30},{3,31},{4,0},{5,1},{6,2},{7,3},{8,4},{9,5},{1... | collective-permute-start | bytes 442376 | tf_op jit(solution)/shard_map/ppermute | solution.py:37
  60.2 0.4 collective-permute-done.7
  60.7 1.5 %collective-permute-done.8 = bf16[192,384]{1,0:T(8,128)(2,1)S(1)} collective-permute-done((bf16[192,384]{1,0:T(8,128)(2,1)S(1)}, bf16[192,384]{1,0:T(8,128)(2,1)S(1)}, u32[]{:S(2)}, u32[]{:S(2)}) %collective-permute-start.8) | collective-permute-done | bytes 147488 | tf_op jit(solution)/shard_map/ppermute | solution.py:37
  62.2 5.9 %collective-permute-start.10 = (bf16[1920,384]{1,0:T(8,128)(2,1)S(1)}, bf16[1920,384]{1,0:T(8,128)(2,1)S(1)}, u32[]{:S(2)}, u32[]{:S(2)}) collective-permute-start(bf16[1920,384]{1,0:T(8,128)(2,1)S(1)} %constant_dynamic-update-slice_fusion.refs_7_), channel_id=1, source_target_pairs={{0,1},{1,0},{2,3},{3,2},{4,5},{5,4},{6,7},{7,6},{8,9},{9,8},{10,11... | collective-permute-start | bytes 4423688 | tf_op jit(solution)/shard_map/ppermute | solution.py:37
  68.2 0.7 fusion.15
  68.9 0.6 convert_element_type.45
  69.5 0.7 convert_element_type.42
  70.2 0.7 add_rsqrt_fusion
  70.9 1.2 pad_maximum_fusion.refs_6_
  72.1 1.9 %collective-permute-start.9 = (bf16[1152,384]{1,0:T(8,128)(2,1)S(1)}, bf16[1152,384]{1,0:T(8,128)(2,1)S(1)}, u32[]{:S(2)}, u32[]{:S(2)}) collective-permute-start(bf16[1152,384]{1,0:T(8,128)(2,1)S(1)} %pad_maximum_fusion.refs_6_), channel_id=1, source_target_pairs={{0,1},{1,0},{2,3},{3,2},{4,5},{5,4},{6,7},{7,6},{8,9},{9,8},{10,11... | collective-permute-start | bytes 2654216 | tf_op jit(solution)/shard_map/ppermute | solution.py:37
  74.6 1.9 %collective-permute-done.9.refs_8_ = bf16[1152,384]{1,0:T(8,128)(2,1)S(1)} collective-permute-done((bf16[1152,384]{1,0:T(8,128)(2,1)S(1)}, bf16[1152,384]{1,0:T(8,128)(2,1)S(1)}, u32[]{:S(2)}, u32[]{:S(2)}) %collective-permute-start.9) | collective-permute-done | bytes 884768 | tf_op jit(solution)/shard_map/ppermute | solution.py:37
  76.5 12.8 %shard_map.109 = bf16[192,384]{1,0:T(8,128)(2,1)S(1)} custom-call(bf16[192,384]{1,0:T(8,128)(2,1)S(1)} %fusion.5.refs_0_, f32[1,384]{1,0:T(1,128)S(1)} %reshape.88.refs_1_, bf16[384,384]{1,0:T(8,128)(2,1)S(1)} %get-tuple-element.15.refs_2_, f32[1,384]{1,0:T(1,128)S(1)} %reshape.106.refs_3_, bf16[384,384]{1,0:T(8,128)(2,1)S(1)} %get-tuple-element.14.refs_4_, ...), custom_call_target="tpu_custom_call" | custom-call | flops 5435817984 | bytes 5603328 | tf_op jit(solution)/shard_map/pallas_call | solution.py:135
  89.2 0.4 fusion.6
  89.7 4.7 %collective-permute-start.11 = (bf16[192,384]{1,0:T(8,128)(2,1)S(1)}, bf16[192,384]{1,0:T(8,128)(2,1)S(1)}, u32[]{:S(2)}, u32[]{:S(2)}) collective-permute-start(bf16[192,384]{1,0:T(8,128)(2,1)S(1)} %fusion.6), channel_id=1, source_target_pairs={{0,64},{32,96},{64,128},{96,160},{128,192},{160,224},{192,256},{22... | collective-permute-start | bytes 442376 | tf_op jit(solution)/shard_map/ppermute | solution.py:16
  94.3 2.2 %collective-permute-start.12 = (bf16[192,384]{1,0:T(8,128)(2,1)S(1)}, bf16[192,384]{1,0:T(8,128)(2,1)S(1)}, u32[]{:S(2)}, u32[]{:S(2)}) collective-permute-start(bf16[192,384]{1,0:T(8,128)(2,1)S(1)} %fusion.6), channel_id=1, source_target_pairs={{0,32},{32,64},{64,96},{96,128},{128,160},{160,192},{192,224},{224... | collective-permute-start | bytes 442376 | tf_op jit(solution)/shard_map/ppermute | solution.py:16
  96.9 2.4 %collective-permute-done.11 = bf16[192,384]{1,0:T(8,128)(2,1)S(1)} collective-permute-done((bf16[192,384]{1,0:T(8,128)(2,1)S(1)}, bf16[192,384]{1,0:T(8,128)(2,1)S(1)}, u32[]{:S(2)}, u32[]{:S(2)}) %collective-permute-start.11) | collective-permute-done | bytes 147488 | tf_op jit(solution)/shard_map/ppermute | solution.py:16
  99.2 4.1 %collective-permute-done.12 = bf16[192,384]{1,0:T(8,128)(2,1)S(1)} collective-permute-done((bf16[192,384]{1,0:T(8,128)(2,1)S(1)}, bf16[192,384]{1,0:T(8,128)(2,1)S(1)}, u32[]{:S(2)}, u32[]{:S(2)}) %collective-permute-start.12) | collective-permute-done | bytes 147488 | tf_op jit(solution)/shard_map/ppermute | solution.py:16
  104.2 4.1 %collective-permute-start.13 = (bf16[2,1,96,384]{3,2,1,0:T(8,128)(2,1)S(1)}, bf16[2,1,96,384]{3,2,1,0:T(8,128)(2,1)S(1)}, u32[]{:S(2)}, u32[]{:S(2)}) collective-permute-start(bf16[2,1,96,384]{3,2,1,0:T(8,128)(2,1)S(1)} %get-tuple-element.16), channel_id=1, source_target_pairs={{0,1},{1,2},{2,3},{3,4},{4,5},{5,6},{6,7},{7,8},{8,9},{9,10},{10,1... | collective-permute-start | bytes 442376 | tf_op jit(solution)/shard_map/ppermute | solution.py:24
  108.2 1.9 %collective-permute-start.14 = (bf16[2,1,96,384]{3,2,1,0:T(8,128)(2,1)S(1)}, bf16[2,1,96,384]{3,2,1,0:T(8,128)(2,1)S(1)}, u32[]{:S(2)}, u32[]{:S(2)}) collective-permute-start(bf16[2,1,96,384]{3,2,1,0:T(8,128)(2,1)S(1)} %get-tuple-element.17), channel_id=1, source_target_pairs={{1,0},{2,1},{3,2},{4,3},{5,4},{6,5},{7,6},{8,7},{9,8},{10,9},{11,1... | collective-permute-start | bytes 442376 | tf_op jit(solution)/shard_map/ppermute | solution.py:27
  110.2 0.4 collective-permute-done.13
  110.6 8.7 %collective-permute-done.14 = bf16[2,1,96,384]{3,2,1,0:T(8,128)(2,1)S(1)} collective-permute-done((bf16[2,1,96,384]{3,2,1,0:T(8,128)(2,1)S(1)}, bf16[2,1,96,384]{3,2,1,0:T(8,128)(2,1)S(1)}, u32[]{:S(2)}, u32[]{:S(2)}) %collective-permute-start.14) | collective-permute-done | bytes 147488 | tf_op jit(solution)/shard_map/ppermute | solution.py:27
  119.6 2.3 %broadcast_in_dim.5 = bf16[2,6,96,2,384]{4,3,2,1,0:T(2,128)(2,1)} broadcast(bf16[2,6,96,384]{3,2,1,0:T(8,128)(2,1)S(1)} %slice.156), dimensions={0,1,2,4} | broadcast | bytes 2654208 | tf_op jit(solution)/shard_map/broadcast_in_dim | solution.py:180
  121.9 4.0 %reshape.94 = bf16[2,6,192,384]{3,2,1,0:T(8,128)(2,1)S(1)} reshape(bf16[2,6,96,2,384]{4,3,2,1,0:T(2,128)(2,1)} %broadcast_in_dim.5) | data formatting | bytes 3538944 | tf_op jit(solution)/shard_map/reshape | solution.py:180
  125.9 4.0 %pad_slice_fusion = (bf16[2,4,192,384]{3,2,1,0:T(8,128)(2,1)S(1)}, bf16[2,4,192,384]{3,2,1,0:T(8,128)(2,1)S(1)}, bf16[2,4,192,384]{3,2,1,0:T(8,128)(2,1)S(1)}, b...) fusion(bf16[2,6,192,384]{3,2,1,0:T(8,128)(2,1)S(1)} %reshape.94), kind=kLoop, calls=%fused_computation.19 | loop fusion | bytes 15925248 | tf_op jit(solution)/shard_map/slice | solution.py:186
  129.9 0.6 convolution_add_fusion.8
  130.5 0.6 convolution_add_fusion.7
  131.1 0.6 convolution_add_fusion.6
  131.7 0.6 convolution_add_fusion.5
  132.3 0.6 convolution_add_fusion.4
  132.9 0.6 convolution_add_fusion.3
  133.4 0.6 convolution_add_fusion.2
  134.0 0.6 convolution_add_fusion.1
  134.6 0.6 fusion
  135.2 1.2 copy.13
  (56 shorter events, 2.2 us)
Async XLA Ops:
  0.0 89.2 %copy-start = (bf16[384,384]{1,0:T(8,128)(2,1)S(1)}, bf16[384,384]{1,0:T(8,128)(2,1)}, u32[]{:S(2)}) copy-start(bf16[384,384]{1,0:T(8,128)(2,1)} %param.16) | copy-start | bytes 884740
  0.0 13.4 %collective-permute-start = (bf16[192,384]{1,0:T(8,128)(2,1)}, bf16[192,384]{1,0:T(8,128)(2,1)S(1)}, u32[]{:S(2)}, u32[]{:S(2)}) collective-permute-start(bf16[192,384]{1,0:T(8,128)(2,1)} %bitcast.82), channel_id=1, source_target_pairs={{0,2},{1,3},{2,0},{3,1},{4,6},{5,7},{6,4},{7,5},{8,10},{9,11},{10,... | collective-permute-start | bytes 442376 | tf_op jit(solution)/shard_map/ppermute | solution.py:37
  14.4 19.0 %collective-permute-start.1 = (bf16[384,384]{1,0:T(8,128)(2,1)S(1)}, bf16[384,384]{1,0:T(8,128)(2,1)S(1)}, u32[]{:S(2)}, u32[]{:S(2)}) collective-permute-start(bf16[384,384]{1,0:T(8,128)(2,1)S(1)} %pad_maximum_fusion.2), channel_id=1, source_target_pairs={{0,4},{1,5},{2,6},{3,7},{4,8},{5,9},{6,10},{7,11},{8,12},{9,13},{1... | collective-permute-start | bytes 884744 | tf_op jit(solution)/shard_map/ppermute | solution.py:37
  20.0 15.4 %collective-permute-start.2 = (bf16[384,384]{1,0:T(8,128)(2,1)S(1)}, bf16[384,384]{1,0:T(8,128)(2,1)S(1)}, u32[]{:S(2)}, u32[]{:S(2)}) collective-permute-start(bf16[384,384]{1,0:T(8,128)(2,1)S(1)} %pad_maximum_fusion.2), channel_id=1, source_target_pairs={{0,28},{1,29},{2,30},{3,31},{4,0},{5,1},{6,2},{7,3},{8,4},{9,5},{1... | collective-permute-start | bytes 884744 | tf_op jit(solution)/shard_map/ppermute | solution.py:37
  33.4 12.4 %copy-start.5 = (bf16[384,384]{1,0:T(8,128)(2,1)}, bf16[384,384]{1,0:T(8,128)(2,1)S(1)}, u32[]{:S(2)}) copy-start(bf16[384,384]{1,0:T(8,128)(2,1)S(1)} %collective-permute-done.1) | copy-start | bytes 884740
  33.4 10.5 %collective-permute-start.3 = (bf16[384,384]{1,0:T(8,128)(2,1)S(1)}, bf16[384,384]{1,0:T(8,128)(2,1)S(1)}, u32[]{:S(2)}, u32[]{:S(2)}) collective-permute-start(bf16[384,384]{1,0:T(8,128)(2,1)S(1)} %collective-permute-done.1), channel_id=1, source_target_pairs={{0,4},{1,5},{2,6},{3,7},{4,8},{5,9},{6,10},{7,11},{8,12},{9,13},{1... | collective-permute-start | bytes 884744 | tf_op jit(solution)/shard_map/ppermute | solution.py:37
  35.3 10.5 %copy-start.6 = (bf16[384,384]{1,0:T(8,128)(2,1)}, bf16[384,384]{1,0:T(8,128)(2,1)S(1)}, u32[]{:S(2)}) copy-start(bf16[384,384]{1,0:T(8,128)(2,1)S(1)} %collective-permute-done.2) | copy-start | bytes 884740
  35.4 10.5 %collective-permute-start.4 = (bf16[384,384]{1,0:T(8,128)(2,1)S(1)}, bf16[384,384]{1,0:T(8,128)(2,1)S(1)}, u32[]{:S(2)}, u32[]{:S(2)}) collective-permute-start(bf16[384,384]{1,0:T(8,128)(2,1)S(1)} %collective-permute-done.2), channel_id=1, source_target_pairs={{0,28},{1,29},{2,30},{3,31},{4,0},{5,1},{6,2},{7,3},{8,4},{9,5},{1... | collective-permute-start | bytes 884744 | tf_op jit(solution)/shard_map/ppermute | solution.py:37
  43.9 9.6 %collective-permute-start.5 = (bf16[384,384]{1,0:T(8,128)(2,1)S(1)}, bf16[384,384]{1,0:T(8,128)(2,1)S(1)}, u32[]{:S(2)}, u32[]{:S(2)}) collective-permute-start(bf16[384,384]{1,0:T(8,128)(2,1)S(1)} %collective-permute-done.3), channel_id=1, source_target_pairs={{0,4},{1,5},{2,6},{3,7},{4,8},{5,9},{6,10},{7,11},{8,12},{9,13},{1... | collective-permute-start | bytes 884744 | tf_op jit(solution)/shard_map/ppermute | solution.py:37
  45.9 9.7 %collective-permute-start.6 = (bf16[384,384]{1,0:T(8,128)(2,1)S(1)}, bf16[384,384]{1,0:T(8,128)(2,1)S(1)}, u32[]{:S(2)}, u32[]{:S(2)}) collective-permute-start(bf16[384,384]{1,0:T(8,128)(2,1)S(1)} %collective-permute-done.4), channel_id=1, source_target_pairs={{0,28},{1,29},{2,30},{3,31},{4,0},{5,1},{6,2},{7,3},{8,4},{9,5},{1... | collective-permute-start | bytes 884744 | tf_op jit(solution)/shard_map/ppermute | solution.py:37
  51.9 16.3 %copy-start.1 = (bf16[1,2,96,384]{3,2,1,0:T(8,128)(2,1)S(1)}, bf16[1,2,96,384]{3,2,1,0:T(8,128)(2,1)}, u32[]{:S(2)}) copy-start(bf16[1,2,96,384]{3,2,1,0:T(8,128)(2,1)} %param.11) | copy-start | bytes 442372
  53.6 15.3 %copy-start.9 = (bf16[384]{0:T(512)(128)(2,1)S(1)}, bf16[384]{0:T(512)(128)(2,1)}, u32[]{:S(2)}) copy-start(bf16[384]{0:T(512)(128)(2,1)} %param.13) | copy-start | bytes 2308
  53.6 15.9 %copy-start.11 = (bf16[384]{0:T(512)(128)(2,1)S(1)}, bf16[384]{0:T(512)(128)(2,1)}, u32[]{:S(2)}) copy-start(bf16[384]{0:T(512)(128)(2,1)} %param.17) | copy-start | bytes 2308
  53.6 7.1 %collective-permute-start.7 = (bf16[192,384]{1,0:T(8,128)(2,1)S(1)}, bf16[192,384]{1,0:T(8,128)(2,1)S(1)}, u32[]{:S(2)}, u32[]{:S(2)}) collective-permute-start(bf16[192,384]{1,0:T(8,128)(2,1)S(1)} %slice.150), channel_id=1, source_target_pairs={{0,4},{1,5},{2,6},{3,7},{4,8},{5,9},{6,10},{7,11},{8,12},{9,13},{1... | collective-permute-start | bytes 442376 | tf_op jit(solution)/shard_map/ppermute | solution.py:37
  55.5 6.7 %collective-permute-start.8 = (bf16[192,384]{1,0:T(8,128)(2,1)S(1)}, bf16[192,384]{1,0:T(8,128)(2,1)S(1)}, u32[]{:S(2)}, u32[]{:S(2)}) collective-permute-start(bf16[192,384]{1,0:T(8,128)(2,1)S(1)} %slice.151), channel_id=1, source_target_pairs={{0,28},{1,29},{2,30},{3,31},{4,0},{5,1},{6,2},{7,3},{8,4},{9,5},{1... | collective-permute-start | bytes 442376 | tf_op jit(solution)/shard_map/ppermute | solution.py:37
  62.2 14.2 %collective-permute-start.10 = (bf16[1920,384]{1,0:T(8,128)(2,1)S(1)}, bf16[1920,384]{1,0:T(8,128)(2,1)S(1)}, u32[]{:S(2)}, u32[]{:S(2)}) collective-permute-start(bf16[1920,384]{1,0:T(8,128)(2,1)S(1)} %constant_dynamic-update-slice_fusion.refs_7_), channel_id=1, source_target_pairs={{0,1},{1,0},{2,3},{3,2},{4,5},{5,4},{6,7},{7,6},{8,9},{9,8},{10,11... | collective-permute-start | bytes 4423688 | tf_op jit(solution)/shard_map/ppermute | solution.py:37
  69.5 4.6 %copy-start.8 = (f32[384]{0:T(512)S(1)}, f32[384]{0:T(512)}, u32[]{:S(2)}) copy-start(f32[384]{0:T(512)} %convert_element_type.45) | copy-start | bytes 4612
  69.5 4.7 %copy-start.7 = (bf16[2,2,96,384]{3,2,1,0:T(8,128)(2,1)S(1)}, bf16[2,2,96,384]{3,2,1,0:T(8,128)(2,1)}, u32[]{:S(2)}) copy-start(bf16[2,2,96,384]{3,2,1,0:T(8,128)(2,1)} %param.12) | copy-start | bytes 884740
  70.9 3.3 %copy-start.4 = (bf16[384,1152]{1,0:T(8,128)(2,1)S(1)}, bf16[384,1152]{1,0:T(8,128)(2,1)}, u32[]{:S(2)}) copy-start(bf16[384,1152]{1,0:T(8,128)(2,1)} %param.14) | copy-start | bytes 2654212
  70.9 3.3 %copy-start.10 = (f32[384]{0:T(512)S(1)}, f32[384]{0:T(512)}, u32[]{:S(2)}) copy-start(f32[384]{0:T(512)} %get-tuple-element.25) | copy-start | bytes 4612
  72.1 4.3 %collective-permute-start.9 = (bf16[1152,384]{1,0:T(8,128)(2,1)S(1)}, bf16[1152,384]{1,0:T(8,128)(2,1)S(1)}, u32[]{:S(2)}, u32[]{:S(2)}) collective-permute-start(bf16[1152,384]{1,0:T(8,128)(2,1)S(1)} %pad_maximum_fusion.refs_6_), channel_id=1, source_target_pairs={{0,1},{1,0},{2,3},{3,2},{4,5},{5,4},{6,7},{7,6},{8,9},{9,8},{10,11... | collective-permute-start | bytes 2654216 | tf_op jit(solution)/shard_map/ppermute | solution.py:37
  76.4 20.1 %copy-start.2 = (bf16[3,384,768]{2,1,0:T(8,128)(2,1)S(1)}, bf16[3,384,768]{2,1,0:T(8,128)(2,1)}, u32[]{:S(2)}) copy-start(bf16[3,384,768]{2,1,0:T(8,128)(2,1)} %param.18) | copy-start | bytes 5308420
  89.7 9.6 %collective-permute-start.11 = (bf16[192,384]{1,0:T(8,128)(2,1)S(1)}, bf16[192,384]{1,0:T(8,128)(2,1)S(1)}, u32[]{:S(2)}, u32[]{:S(2)}) collective-permute-start(bf16[192,384]{1,0:T(8,128)(2,1)S(1)} %fusion.6), channel_id=1, source_target_pairs={{0,64},{32,96},{64,128},{96,160},{128,192},{160,224},{192,256},{22... | collective-permute-start | bytes 442376 | tf_op jit(solution)/shard_map/ppermute | solution.py:16
  94.3 9.0 %collective-permute-start.12 = (bf16[192,384]{1,0:T(8,128)(2,1)S(1)}, bf16[192,384]{1,0:T(8,128)(2,1)S(1)}, u32[]{:S(2)}, u32[]{:S(2)}) collective-permute-start(bf16[192,384]{1,0:T(8,128)(2,1)S(1)} %fusion.6), channel_id=1, source_target_pairs={{0,32},{32,64},{64,96},{96,128},{128,160},{160,192},{192,224},{224... | collective-permute-start | bytes 442376 | tf_op jit(solution)/shard_map/ppermute | solution.py:16
  103.7 6.4 %copy-start.12 = (bf16[192]{0:T(256)(128)(2,1)S(1)}, bf16[192]{0:T(256)(128)(2,1)}, u32[]{:S(2)}) copy-start(bf16[192]{0:T(256)(128)(2,1)} %param.21) | copy-start | bytes 1156
  104.2 6.5 %collective-permute-start.13 = (bf16[2,1,96,384]{3,2,1,0:T(8,128)(2,1)S(1)}, bf16[2,1,96,384]{3,2,1,0:T(8,128)(2,1)S(1)}, u32[]{:S(2)}, u32[]{:S(2)}) collective-permute-start(bf16[2,1,96,384]{3,2,1,0:T(8,128)(2,1)S(1)} %get-tuple-element.16), channel_id=1, source_target_pairs={{0,1},{1,2},{2,3},{3,4},{4,5},{5,6},{6,7},{7,8},{8,9},{9,10},{10,1... | collective-permute-start | bytes 442376 | tf_op jit(solution)/shard_map/ppermute | solution.py:24
  108.2 11.1 %collective-permute-start.14 = (bf16[2,1,96,384]{3,2,1,0:T(8,128)(2,1)S(1)}, bf16[2,1,96,384]{3,2,1,0:T(8,128)(2,1)S(1)}, u32[]{:S(2)}, u32[]{:S(2)}) collective-permute-start(bf16[2,1,96,384]{3,2,1,0:T(8,128)(2,1)S(1)} %get-tuple-element.17), channel_id=1, source_target_pairs={{1,0},{2,1},{3,2},{4,3},{5,4},{6,5},{7,6},{8,7},{9,8},{10,9},{11,1... | collective-permute-start | bytes 442376 | tf_op jit(solution)/shard_map/ppermute | solution.py:27
  125.9 4.0 %copy-start.3 = (bf16[3,3,384,192]{2,3,1,0:T(8,128)(2,1)S(1)}, bf16[3,3,384,192]{2,3,1,0:T(8,128)(2,1)}, u32[]{:S(2)}) copy-start(bf16[3,3,384,192]{2,3,1,0:T(8,128)(2,1)} %param.20) | copy-start | bytes 3981316

commit v5 on v4

--- a/solution.py
+++ b/solution.py
@@ -177,19 +177,23 @@
     )
     paired = jnp.stack([timed[:, :channels], timed[:, channels:]]).reshape(2, rows, width, channels)
     padded = with_halo(paired, (("space", 1),), 1)
-    upsampled = jnp.repeat(jnp.repeat(padded, 2, axis=1)[:, 1 : 2 * rows + 3], 2, axis=2)
+    upsampled = jnp.repeat(padded, 2, axis=1)[:, 1 : 2 * rows + 3]
     upsampled = jnp.pad(upsampled, ((0, 0), (0, 0), (1, 1), (0, 0)))
     out_channels = w_space.shape[-1]
-    result = jnp.zeros((8 * rows * width, out_channels), jnp.float32) + b_space.astype(jnp.float32)
-    for row_tap in range(3):
-        for col_tap in range(3):
-            window = upsampled[
-                :, row_tap : row_tap + 2 * rows, col_tap : col_tap + 2 * width
-            ].reshape(-1, channels)
-            result = result + jnp.dot(
-                window, w_space[row_tap, col_tap], preferred_element_type=jnp.float32
-            )
-    return result.astype(jnp.bfloat16).reshape(2, 2 * rows, 2 * width, out_channels)
+    phases = []
+    for offsets in ((0, 1, 1), (1, 1, 2)):
+        result = jnp.zeros((4 * rows * width, out_channels), jnp.float32) + b_space.astype(jnp.float32)
+        for row_tap in range(3):
+            for col_tap in range(3):
+                start = offsets[col_tap]
+                window = upsampled[
+                    :, row_tap : row_tap + 2 * rows, start : start + width
+                ].reshape(-1, channels)
+                result = result + jnp.dot(
+                    window, w_space[row_tap, col_tap], preferred_element_type=jnp.float32
+                )
+        phases.append(result.astype(jnp.bfloat16).reshape(2, 2 * rows, width, 1, out_channels))
+    return jnp.concatenate(phases, axis=3).reshape(2, 2 * rows, 2 * width, out_channels)
 
 
 def solution(mesh):

time: 137 us -> 139 us (1.015)
  matrix products: 6.79 us -> 13.6 us
  local copies, waits for them, and re-layouts: 12.1 us -> 7.28 us
    dot_general x9 -> x15, matrix products: 5.18 us -> 11.3 us  [body(): jnp.dot(window, w_space[row_tap, col_tap], preferred_element_type=jnp.flo...]
    broadcast_in_dim x2 -> x1, local copies, waits for them, and re-layouts: 2.41 us -> 0.11 us  [body(): upsampled = jnp.repeat(padded, 2, axis=1)[:, 1:2 * rows + 3]]
    slice x2 -> x3, local copies, waits for them, and re-layouts: 4.09 us -> 1.82 us  [the longest x2 1.73 us: body(): upsampled[:, row_tap:row_tap + 2 * rows, start:start + width]]
    reshape x2 -> x3, local copies, waits for them, and re-layouts: 5.15 us -> 3.25 us  [the longest x2 1.64 us: body(): result.astype(jnp.bfloat16).reshape(2, 2 * rows, width, 1, out_channels)]
    concatenate x0 -> x1, local copies, waits for them, and re-layouts: none -> 1.62 us  [body(): jnp.concatenate(phases, axis=3)]
where the time goes in v5:
time: 139 us; the launch traced here: 138 us
  starting transfers between devices  60.1 us (43%)
  waiting for transfers between devices  36.8 us (26%)
  matrix products  13.6 us (10%)
  Pallas kernels  12.5 us (9%)
  local copies, waits for them, and re-layouts  7.28 us (5%)
  other arithmetic  7.17 us (5%)
    ppermute x11, starting transfers between devices, moved(): return lax.ppermute(value, 'space', [(s, target(s)) for s in range(count)])  47.2 us
    ppermute x11, waiting for transfers between devices, moved(): return lax.ppermute(value, 'space', [(s, target(s)) for s in range(count)])  21.2 us
    pallas_call x1, Pallas kernels, fused_attention(): pl.pallas_call(functools.partial(attention_kernel, sizes=sizes, channels=...  12.5 us
    dot_general x15, matrix products, body(): jnp.dot(window, w_space[row_tap, col_tap], preferred_element_type=jnp.flo...  11.3 us
    ppermute x1, waiting for transfers between devices, with_halo(): lax.ppermute(lax.slice_in_dim(block, 0, width, axis=dim), axis, backward)  8.69 us
    ppermute x2, starting transfers between devices, shifted(): lax.ppermute(value, axis, [(source, source + steps) for source in range(l...  6.86 us
    ppermute x2, waiting for transfers between devices, shifted(): lax.ppermute(value, axis, [(source, source + steps) for source in range(l...  6.45 us
    ppermute x1, starting transfers between devices, with_halo(): lax.ppermute(lax.slice_in_dim(block, block.shape[dim] - width, None, axis...  4.05 us
  transfers between devices with their start and end apart: 15, of which 11 were waited for; matrix products, arithmetic and copies ran while one was open for 5% of the time, Pallas kernels for 0%

profile of v5, /device:TPU:17, one launch (start us, length us, event | category | flops | bytes accessed | tf_op | source)
XLA Modules:
  0.0 138.1 jit_solution(4790448976246297785)
XLA Ops:
  0.0 5.8 %collective-permute-start = (bf16[192,384]{1,0:T(8,128)(2,1)}, bf16[192,384]{1,0:T(8,128)(2,1)S(1)}, u32[]{:S(2)}, u32[]{:S(2)}) collective-permute-start(bf16[192,384]{1,0:T(8,128)(2,1)} %bitcast.105), channel_id=1, source_target_pairs={{0,2},{1,3},{2,0},{3,1},{4,6},{5,7},{6,4},{7,5},{8,10},{9,11},{10,... | collective-permute-start | bytes 442376 | tf_op jit(solution)/shard_map/ppermute | solution.py:37
  5.8 7.7 %collective-permute-done = bf16[192,384]{1,0:T(8,128)(2,1)S(1)} collective-permute-done((bf16[192,384]{1,0:T(8,128)(2,1)}, bf16[192,384]{1,0:T(8,128)(2,1)S(1)}, u32[]{:S(2)}, u32[]{:S(2)}) %collective-permute-start) | collective-permute-done | bytes 147488 | tf_op jit(solution)/shard_map/ppermute | solution.py:37
  13.4 0.9 pad_maximum_fusion.3
  14.4 5.6 %collective-permute-start.1 = (bf16[384,384]{1,0:T(8,128)(2,1)S(1)}, bf16[384,384]{1,0:T(8,128)(2,1)S(1)}, u32[]{:S(2)}, u32[]{:S(2)}) collective-permute-start(bf16[384,384]{1,0:T(8,128)(2,1)S(1)} %pad_maximum_fusion.3), channel_id=1, source_target_pairs={{0,4},{1,5},{2,6},{3,7},{4,8},{5,9},{6,10},{7,11},{8,12},{9,13},{1... | collective-permute-start | bytes 884744 | tf_op jit(solution)/shard_map/ppermute | solution.py:37
  20.0 8.6 %collective-permute-start.2 = (bf16[384,384]{1,0:T(8,128)(2,1)S(1)}, bf16[384,384]{1,0:T(8,128)(2,1)S(1)}, u32[]{:S(2)}, u32[]{:S(2)}) collective-permute-start(bf16[384,384]{1,0:T(8,128)(2,1)S(1)} %pad_maximum_fusion.3), channel_id=1, source_target_pairs={{0,28},{1,29},{2,30},{3,31},{4,0},{5,1},{6,2},{7,3},{8,4},{9,5},{1... | collective-permute-start | bytes 884744 | tf_op jit(solution)/shard_map/ppermute | solution.py:37
  28.6 4.8 %collective-permute-done.1 = bf16[384,384]{1,0:T(8,128)(2,1)S(1)} collective-permute-done((bf16[384,384]{1,0:T(8,128)(2,1)S(1)}, bf16[384,384]{1,0:T(8,128)(2,1)S(1)}, u32[]{:S(2)}, u32[]{:S(2)}) %collective-permute-start.1) | collective-permute-done | bytes 294944 | tf_op jit(solution)/shard_map/ppermute | solution.py:37
  33.4 1.9 %collective-permute-start.3 = (bf16[384,384]{1,0:T(8,128)(2,1)S(1)}, bf16[384,384]{1,0:T(8,128)(2,1)S(1)}, u32[]{:S(2)}, u32[]{:S(2)}) collective-permute-start(bf16[384,384]{1,0:T(8,128)(2,1)S(1)} %collective-permute-done.1), channel_id=1, source_target_pairs={{0,4},{1,5},{2,6},{3,7},{4,8},{5,9},{6,10},{7,11},{8,12},{9,13},{1... | collective-permute-start | bytes 884744 | tf_op jit(solution)/shard_map/ppermute | solution.py:37
  35.4 4.6 %collective-permute-start.4 = (bf16[384,384]{1,0:T(8,128)(2,1)S(1)}, bf16[384,384]{1,0:T(8,128)(2,1)S(1)}, u32[]{:S(2)}, u32[]{:S(2)}) collective-permute-start(bf16[384,384]{1,0:T(8,128)(2,1)S(1)} %collective-permute-done.2), channel_id=1, source_target_pairs={{0,28},{1,29},{2,30},{3,31},{4,0},{5,1},{6,2},{7,3},{8,4},{9,5},{1... | collective-permute-start | bytes 884744 | tf_op jit(solution)/shard_map/ppermute | solution.py:37
  39.9 4.0 %collective-permute-done.3 = bf16[384,384]{1,0:T(8,128)(2,1)S(1)} collective-permute-done((bf16[384,384]{1,0:T(8,128)(2,1)S(1)}, bf16[384,384]{1,0:T(8,128)(2,1)S(1)}, u32[]{:S(2)}, u32[]{:S(2)}) %collective-permute-start.3) | collective-permute-done | bytes 294944 | tf_op jit(solution)/shard_map/ppermute | solution.py:37
  43.9 1.9 %collective-permute-start.5 = (bf16[384,384]{1,0:T(8,128)(2,1)S(1)}, bf16[384,384]{1,0:T(8,128)(2,1)S(1)}, u32[]{:S(2)}, u32[]{:S(2)}) collective-permute-start(bf16[384,384]{1,0:T(8,128)(2,1)S(1)} %collective-permute-done.3), channel_id=1, source_target_pairs={{0,4},{1,5},{2,6},{3,7},{4,8},{5,9},{6,10},{7,11},{8,12},{9,13},{1... | collective-permute-start | bytes 884744 | tf_op jit(solution)/shard_map/ppermute | solution.py:37
  45.9 4.6 %collective-permute-start.6 = (bf16[384,384]{1,0:T(8,128)(2,1)S(1)}, bf16[384,384]{1,0:T(8,128)(2,1)S(1)}, u32[]{:S(2)}, u32[]{:S(2)}) collective-permute-start(bf16[384,384]{1,0:T(8,128)(2,1)S(1)} %collective-permute-done.4), channel_id=1, source_target_pairs={{0,28},{1,29},{2,30},{3,31},{4,0},{5,1},{6,2},{7,3},{8,4},{9,5},{1... | collective-permute-start | bytes 884744 | tf_op jit(solution)/shard_map/ppermute | solution.py:37
  50.4 1.4 slice_convert_fusion
  51.9 1.6 %collective-permute-done.5 = bf16[384,384]{1,0:T(8,128)(2,1)S(1)} collective-permute-done((bf16[384,384]{1,0:T(8,128)(2,1)S(1)}, bf16[384,384]{1,0:T(8,128)(2,1)S(1)}, u32[]{:S(2)}, u32[]{:S(2)}) %collective-permute-start.5) | collective-permute-done | bytes 294944 | tf_op jit(solution)/shard_map/ppermute | solution.py:37
  53.6 1.9 %collective-permute-start.7 = (bf16[192,384]{1,0:T(8,128)(2,1)S(1)}, bf16[192,384]{1,0:T(8,128)(2,1)S(1)}, u32[]{:S(2)}, u32[]{:S(2)}) collective-permute-start(bf16[192,384]{1,0:T(8,128)(2,1)S(1)} %slice.171), channel_id=1, source_target_pairs={{0,4},{1,5},{2,6},{3,7},{4,8},{5,9},{6,10},{7,11},{8,12},{9,13},{1... | collective-permute-start | bytes 442376 | tf_op jit(solution)/shard_map/ppermute | solution.py:37
  55.5 4.6 %collective-permute-start.8 = (bf16[192,384]{1,0:T(8,128)(2,1)S(1)}, bf16[192,384]{1,0:T(8,128)(2,1)S(1)}, u32[]{:S(2)}, u32[]{:S(2)}) collective-permute-start(bf16[192,384]{1,0:T(8,128)(2,1)S(1)} %slice.172), channel_id=1, source_target_pairs={{0,28},{1,29},{2,30},{3,31},{4,0},{5,1},{6,2},{7,3},{8,4},{9,5},{1... | collective-permute-start | bytes 442376 | tf_op jit(solution)/shard_map/ppermute | solution.py:37
  60.2 0.4 collective-permute-done.7
  60.7 1.5 %collective-permute-done.8 = bf16[192,384]{1,0:T(8,128)(2,1)S(1)} collective-permute-done((bf16[192,384]{1,0:T(8,128)(2,1)S(1)}, bf16[192,384]{1,0:T(8,128)(2,1)S(1)}, u32[]{:S(2)}, u32[]{:S(2)}) %collective-permute-start.8) | collective-permute-done | bytes 147488 | tf_op jit(solution)/shard_map/ppermute | solution.py:37
  62.2 5.9 %collective-permute-start.10 = (bf16[1920,384]{1,0:T(8,128)(2,1)S(1)}, bf16[1920,384]{1,0:T(8,128)(2,1)S(1)}, u32[]{:S(2)}, u32[]{:S(2)}) collective-permute-start(bf16[1920,384]{1,0:T(8,128)(2,1)S(1)} %constant_dynamic-update-slice_fusion.refs_7_), channel_id=1, source_target_pairs={{0,1},{1,0},{2,3},{3,2},{4,5},{5,4},{6,7},{7,6},{8,9},{9,8},{10,11... | collective-permute-start | bytes 4423688 | tf_op jit(solution)/shard_map/ppermute | solution.py:37
  68.2 0.7 fusion.22
  68.8 0.6 convert_element_type.49
  69.5 0.8 convert_element_type.46
  70.3 0.7 add_rsqrt_fusion
  71.0 1.1 pad_maximum_fusion.refs_6_
  72.1 1.9 %collective-permute-start.9 = (bf16[1152,384]{1,0:T(8,128)(2,1)S(1)}, bf16[1152,384]{1,0:T(8,128)(2,1)S(1)}, u32[]{:S(2)}, u32[]{:S(2)}) collective-permute-start(bf16[1152,384]{1,0:T(8,128)(2,1)S(1)} %pad_maximum_fusion.refs_6_), channel_id=1, source_target_pairs={{0,1},{1,0},{2,3},{3,2},{4,5},{5,4},{6,7},{7,6},{8,9},{9,8},{10,11... | collective-permute-start | bytes 2654216 | tf_op jit(solution)/shard_map/ppermute | solution.py:37
  74.2 0.9 fusion.12.refs_0_
  75.2 1.2 collective-permute-done.9.refs_8_
  76.4 12.5 %shard_map.109 = bf16[192,384]{1,0:T(8,128)(2,1)S(1)} custom-call(bf16[192,384]{1,0:T(8,128)(2,1)S(1)} %fusion.12.refs_0_, f32[1,384]{1,0:T(1,128)S(1)} %reshape.100.refs_1_, bf16[384,384]{1,0:T(8,128)(2,1)S(1)} %get-tuple-element.15.refs_2_, f32[1,384]{1,0:T(1,128)S(1)} %reshape.119.refs_3_, bf16[384,384]{1,0:T(8,128)(2,1)S(1)} %get-tuple-element.14.refs_4_, ...), custom_call_target="tpu_custom_call" | custom-call | flops 5435817984 | bytes 5603328 | tf_op jit(solution)/shard_map/pallas_call | solution.py:135
  88.9 0.4 fusion.13
  89.3 4.6 %collective-permute-start.11 = (bf16[192,384]{1,0:T(8,128)(2,1)S(1)}, bf16[192,384]{1,0:T(8,128)(2,1)S(1)}, u32[]{:S(2)}, u32[]{:S(2)}) collective-permute-start(bf16[192,384]{1,0:T(8,128)(2,1)S(1)} %fusion.13), channel_id=1, source_target_pairs={{0,64},{32,96},{64,128},{96,160},{128,192},{160,224},{192,256},{22... | collective-permute-start | bytes 442376 | tf_op jit(solution)/shard_map/ppermute | solution.py:16
  94.0 2.2 %collective-permute-start.12 = (bf16[192,384]{1,0:T(8,128)(2,1)S(1)}, bf16[192,384]{1,0:T(8,128)(2,1)S(1)}, u32[]{:S(2)}, u32[]{:S(2)}) collective-permute-start(bf16[192,384]{1,0:T(8,128)(2,1)S(1)} %fusion.13), channel_id=1, source_target_pairs={{0,32},{32,64},{64,96},{96,128},{128,160},{160,192},{192,224},{224... | collective-permute-start | bytes 442376 | tf_op jit(solution)/shard_map/ppermute | solution.py:16
  96.5 2.4 %collective-permute-done.11 = bf16[192,384]{1,0:T(8,128)(2,1)S(1)} collective-permute-done((bf16[192,384]{1,0:T(8,128)(2,1)S(1)}, bf16[192,384]{1,0:T(8,128)(2,1)S(1)}, u32[]{:S(2)}, u32[]{:S(2)}) %collective-permute-start.11) | collective-permute-done | bytes 147488 | tf_op jit(solution)/shard_map/ppermute | solution.py:16
  98.9 4.1 %collective-permute-done.12 = bf16[192,384]{1,0:T(8,128)(2,1)S(1)} collective-permute-done((bf16[192,384]{1,0:T(8,128)(2,1)S(1)}, bf16[192,384]{1,0:T(8,128)(2,1)S(1)}, u32[]{:S(2)}, u32[]{:S(2)}) %collective-permute-start.12) | collective-permute-done | bytes 147488 | tf_op jit(solution)/shard_map/ppermute | solution.py:16
  103.8 4.0 %collective-permute-start.13 = (bf16[2,1,96,384]{3,2,1,0:T(8,128)(2,1)S(1)}, bf16[2,1,96,384]{3,2,1,0:T(8,128)(2,1)S(1)}, u32[]{:S(2)}, u32[]{:S(2)}) collective-permute-start(bf16[2,1,96,384]{3,2,1,0:T(8,128)(2,1)S(1)} %get-tuple-element.16), channel_id=1, source_target_pairs={{0,1},{1,2},{2,3},{3,4},{4,5},{5,6},{6,7},{7,8},{8,9},{9,10},{10,1... | collective-permute-start | bytes 442376 | tf_op jit(solution)/shard_map/ppermute | solution.py:24
  107.9 1.9 %collective-permute-start.14 = (bf16[2,1,96,384]{3,2,1,0:T(8,128)(2,1)S(1)}, bf16[2,1,96,384]{3,2,1,0:T(8,128)(2,1)S(1)}, u32[]{:S(2)}, u32[]{:S(2)}) collective-permute-start(bf16[2,1,96,384]{3,2,1,0:T(8,128)(2,1)S(1)} %get-tuple-element.17), channel_id=1, source_target_pairs={{1,0},{2,1},{3,2},{4,3},{5,4},{6,5},{7,6},{8,7},{9,8},{10,9},{11,1... | collective-permute-start | bytes 442376 | tf_op jit(solution)/shard_map/ppermute | solution.py:27
  109.8 0.5 collective-permute-done.13
  110.3 8.7 %collective-permute-done.14 = bf16[2,1,96,384]{3,2,1,0:T(8,128)(2,1)S(1)} collective-permute-done((bf16[2,1,96,384]{3,2,1,0:T(8,128)(2,1)S(1)}, bf16[2,1,96,384]{3,2,1,0:T(8,128)(2,1)S(1)}, u32[]{:S(2)}, u32[]{:S(2)}) %collective-permute-start.14) | collective-permute-done | bytes 147488 | tf_op jit(solution)/shard_map/ppermute | solution.py:27
  119.5 1.5 %pad_slice_fusion.3 = (bf16[2,4,96,384]{3,2,1,0:T(8,128)(2,1)S(1)}, bf16[2,4,96,384]{3,2,1,0:T(8,128)(2,1)S(1)}, bf16[2,4,96,384]{3,2,1,0:T(8,128)(2,1)}, bf16[2...) fusion(bf16[2,6,96,384]{3,2,1,0:T(8,128)(2,1)S(1)} %slice.177), kind=kLoop, calls=%fused_computation.43 | loop fusion | bytes 4423680 | tf_op jit(solution)/shard_map/slice | solution.py:189
  121.4 1.2 fusion.2
  125.5 1.2 reshape.112
  126.7 1.7 %convolution_add_fusion.4 = f32[768,192]{0,1:T(8,128)S(1)} fusion(f32[768,192]{0,1:T(8,128)} %fusion.2, bf16[768,384]{1,0:T(8,128)(2,1)} %bitcast.114, bf16[3,3,384,192]{2,3,1,0:T(8,128)(2,1)} %param.20), kind=kOutput, calls=%fused_computation.6 | convolution fusion | flops 113393664 | bytes 1916928 | tf_op jit(solution)/shard_map/dot_general | solution.py:192
  128.4 1.3 fusion.1
  129.8 1.3 convolution_add_fusion.2
  131.1 1.3 fusion
  132.4 1.3 fusion.10
  133.7 0.4 reshape.116
  134.2 0.7 pad_maximum_fusion.1
  134.8 1.6 %copy.12 = bf16[2,4,96,2,192]{4,3,2,1,0:T(2,128)(2,1)S(1)} copy(bf16[2,4,96,2,192]{2,1,0,4,3:T(4,128)(2,1)S(1)} %pad_maximum_fusion.1) | data formatting | bytes 1179648 | tf_op jit(solution)/shard_map/concatenate | solution.py:196
  136.4 1.6 %reshape.117 = bf16[2,4,192,192]{3,2,1,0:T(8,128)(2,1)} reshape(bf16[2,4,96,2,192]{4,3,2,1,0:T(2,128)(2,1)S(1)} %copy.12) | data formatting | bytes 1179648 | tf_op jit(solution)/shard_map/reshape | solution.py:196
  (67 shorter events, 5.4 us)
Async XLA Ops:
  0.0 88.9 %copy-start = (bf16[384,384]{1,0:T(8,128)(2,1)S(1)}, bf16[384,384]{1,0:T(8,128)(2,1)}, u32[]{:S(2)}) copy-start(bf16[384,384]{1,0:T(8,128)(2,1)} %param.16) | copy-start | bytes 884740
  0.0 13.4 %collective-permute-start = (bf16[192,384]{1,0:T(8,128)(2,1)}, bf16[192,384]{1,0:T(8,128)(2,1)S(1)}, u32[]{:S(2)}, u32[]{:S(2)}) collective-permute-start(bf16[192,384]{1,0:T(8,128)(2,1)} %bitcast.105), channel_id=1, source_target_pairs={{0,2},{1,3},{2,0},{3,1},{4,6},{5,7},{6,4},{7,5},{8,10},{9,11},{10,... | collective-permute-start | bytes 442376 | tf_op jit(solution)/shard_map/ppermute | solution.py:37
  14.4 19.0 %collective-permute-start.1 = (bf16[384,384]{1,0:T(8,128)(2,1)S(1)}, bf16[384,384]{1,0:T(8,128)(2,1)S(1)}, u32[]{:S(2)}, u32[]{:S(2)}) collective-permute-start(bf16[384,384]{1,0:T(8,128)(2,1)S(1)} %pad_maximum_fusion.3), channel_id=1, source_target_pairs={{0,4},{1,5},{2,6},{3,7},{4,8},{5,9},{6,10},{7,11},{8,12},{9,13},{1... | collective-permute-start | bytes 884744 | tf_op jit(solution)/shard_map/ppermute | solution.py:37
  20.0 15.4 %collective-permute-start.2 = (bf16[384,384]{1,0:T(8,128)(2,1)S(1)}, bf16[384,384]{1,0:T(8,128)(2,1)S(1)}, u32[]{:S(2)}, u32[]{:S(2)}) collective-permute-start(bf16[384,384]{1,0:T(8,128)(2,1)S(1)} %pad_maximum_fusion.3), channel_id=1, source_target_pairs={{0,28},{1,29},{2,30},{3,31},{4,0},{5,1},{6,2},{7,3},{8,4},{9,5},{1... | collective-permute-start | bytes 884744 | tf_op jit(solution)/shard_map/ppermute | solution.py:37
  33.4 12.4 %copy-start.7 = (bf16[384,384]{1,0:T(8,128)(2,1)}, bf16[384,384]{1,0:T(8,128)(2,1)S(1)}, u32[]{:S(2)}) copy-start(bf16[384,384]{1,0:T(8,128)(2,1)S(1)} %collective-permute-done.1) | copy-start | bytes 884740
  33.4 10.5 %collective-permute-start.3 = (bf16[384,384]{1,0:T(8,128)(2,1)S(1)}, bf16[384,384]{1,0:T(8,128)(2,1)S(1)}, u32[]{:S(2)}, u32[]{:S(2)}) collective-permute-start(bf16[384,384]{1,0:T(8,128)(2,1)S(1)} %collective-permute-done.1), channel_id=1, source_target_pairs={{0,4},{1,5},{2,6},{3,7},{4,8},{5,9},{6,10},{7,11},{8,12},{9,13},{1... | collective-permute-start | bytes 884744 | tf_op jit(solution)/shard_map/ppermute | solution.py:37
  35.3 10.5 %copy-start.8 = (bf16[384,384]{1,0:T(8,128)(2,1)}, bf16[384,384]{1,0:T(8,128)(2,1)S(1)}, u32[]{:S(2)}) copy-start(bf16[384,384]{1,0:T(8,128)(2,1)S(1)} %collective-permute-done.2) | copy-start | bytes 884740
  35.4 10.5 %collective-permute-start.4 = (bf16[384,384]{1,0:T(8,128)(2,1)S(1)}, bf16[384,384]{1,0:T(8,128)(2,1)S(1)}, u32[]{:S(2)}, u32[]{:S(2)}) collective-permute-start(bf16[384,384]{1,0:T(8,128)(2,1)S(1)} %collective-permute-done.2), channel_id=1, source_target_pairs={{0,28},{1,29},{2,30},{3,31},{4,0},{5,1},{6,2},{7,3},{8,4},{9,5},{1... | collective-permute-start | bytes 884744 | tf_op jit(solution)/shard_map/ppermute | solution.py:37
  43.9 9.6 %collective-permute-start.5 = (bf16[384,384]{1,0:T(8,128)(2,1)S(1)}, bf16[384,384]{1,0:T(8,128)(2,1)S(1)}, u32[]{:S(2)}, u32[]{:S(2)}) collective-permute-start(bf16[384,384]{1,0:T(8,128)(2,1)S(1)} %collective-permute-done.3), channel_id=1, source_target_pairs={{0,4},{1,5},{2,6},{3,7},{4,8},{5,9},{6,10},{7,11},{8,12},{9,13},{1... | collective-permute-start | bytes 884744 | tf_op jit(solution)/shard_map/ppermute | solution.py:37
  45.9 9.6 %collective-permute-start.6 = (bf16[384,384]{1,0:T(8,128)(2,1)S(1)}, bf16[384,384]{1,0:T(8,128)(2,1)S(1)}, u32[]{:S(2)}, u32[]{:S(2)}) collective-permute-start(bf16[384,384]{1,0:T(8,128)(2,1)S(1)} %collective-permute-done.4), channel_id=1, source_target_pairs={{0,28},{1,29},{2,30},{3,31},{4,0},{5,1},{6,2},{7,3},{8,4},{9,5},{1... | collective-permute-start | bytes 884744 | tf_op jit(solution)/shard_map/ppermute | solution.py:37
  51.8 16.3 %copy-start.2 = (bf16[1,2,96,384]{3,2,1,0:T(8,128)(2,1)S(1)}, bf16[1,2,96,384]{3,2,1,0:T(8,128)(2,1)}, u32[]{:S(2)}) copy-start(bf16[1,2,96,384]{3,2,1,0:T(8,128)(2,1)} %param.11) | copy-start | bytes 442372
  51.9 17.0 %copy-start.11 = (bf16[384]{0:T(512)(128)(2,1)S(1)}, bf16[384]{0:T(512)(128)(2,1)}, u32[]{:S(2)}) copy-start(bf16[384]{0:T(512)(128)(2,1)} %param.13) | copy-start | bytes 2308
  51.9 17.6 %copy-start.12 = (bf16[384]{0:T(512)(128)(2,1)S(1)}, bf16[384]{0:T(512)(128)(2,1)}, u32[]{:S(2)}) copy-start(bf16[384]{0:T(512)(128)(2,1)} %param.17) | copy-start | bytes 2308
  53.6 7.1 %collective-permute-start.7 = (bf16[192,384]{1,0:T(8,128)(2,1)S(1)}, bf16[192,384]{1,0:T(8,128)(2,1)S(1)}, u32[]{:S(2)}, u32[]{:S(2)}) collective-permute-start(bf16[192,384]{1,0:T(8,128)(2,1)S(1)} %slice.171), channel_id=1, source_target_pairs={{0,4},{1,5},{2,6},{3,7},{4,8},{5,9},{6,10},{7,11},{8,12},{9,13},{1... | collective-permute-start | bytes 442376 | tf_op jit(solution)/shard_map/ppermute | solution.py:37
  55.5 6.7 %collective-permute-start.8 = (bf16[192,384]{1,0:T(8,128)(2,1)S(1)}, bf16[192,384]{1,0:T(8,128)(2,1)S(1)}, u32[]{:S(2)}, u32[]{:S(2)}) collective-permute-start(bf16[192,384]{1,0:T(8,128)(2,1)S(1)} %slice.172), channel_id=1, source_target_pairs={{0,28},{1,29},{2,30},{3,31},{4,0},{5,1},{6,2},{7,3},{8,4},{9,5},{1... | collective-permute-start | bytes 442376 | tf_op jit(solution)/shard_map/ppermute | solution.py:37
  62.2 14.2 %collective-permute-start.10 = (bf16[1920,384]{1,0:T(8,128)(2,1)S(1)}, bf16[1920,384]{1,0:T(8,128)(2,1)S(1)}, u32[]{:S(2)}, u32[]{:S(2)}) collective-permute-start(bf16[1920,384]{1,0:T(8,128)(2,1)S(1)} %constant_dynamic-update-slice_fusion.refs_7_), channel_id=1, source_target_pairs={{0,1},{1,0},{2,3},{3,2},{4,5},{5,4},{6,7},{7,6},{8,9},{9,8},{10,11... | collective-permute-start | bytes 4423688 | tf_op jit(solution)/shard_map/ppermute | solution.py:37
  69.5 4.6 %copy-start.10 = (f32[384]{0:T(512)S(1)}, f32[384]{0:T(512)}, u32[]{:S(2)}) copy-start(f32[384]{0:T(512)} %convert_element_type.49) | copy-start | bytes 4612
  69.5 4.7 %copy-start.9 = (bf16[2,2,96,384]{3,2,1,0:T(8,128)(2,1)S(1)}, bf16[2,2,96,384]{3,2,1,0:T(8,128)(2,1)}, u32[]{:S(2)}) copy-start(bf16[2,2,96,384]{3,2,1,0:T(8,128)(2,1)} %param.12) | copy-start | bytes 884740
  69.5 4.7 %copy-start.6 = (bf16[384,1152]{1,0:T(8,128)(2,1)S(1)}, bf16[384,1152]{1,0:T(8,128)(2,1)}, u32[]{:S(2)}) copy-start(bf16[384,1152]{1,0:T(8,128)(2,1)} %param.14) | copy-start | bytes 2654212
  72.1 4.3 %collective-permute-start.9 = (bf16[1152,384]{1,0:T(8,128)(2,1)S(1)}, bf16[1152,384]{1,0:T(8,128)(2,1)S(1)}, u32[]{:S(2)}, u32[]{:S(2)}) collective-permute-start(bf16[1152,384]{1,0:T(8,128)(2,1)S(1)} %pad_maximum_fusion.refs_6_), channel_id=1, source_target_pairs={{0,1},{1,0},{2,3},{3,2},{4,5},{5,4},{6,7},{7,6},{8,9},{9,8},{10,11... | collective-permute-start | bytes 2654216 | tf_op jit(solution)/shard_map/ppermute | solution.py:37
  76.4 19.8 %copy-start.4 = (bf16[3,384,768]{2,1,0:T(8,128)(2,1)S(1)}, bf16[3,384,768]{2,1,0:T(8,128)(2,1)}, u32[]{:S(2)}) copy-start(bf16[3,384,768]{2,1,0:T(8,128)(2,1)} %param.18) | copy-start | bytes 5308420
  89.3 9.6 %collective-permute-start.11 = (bf16[192,384]{1,0:T(8,128)(2,1)S(1)}, bf16[192,384]{1,0:T(8,128)(2,1)S(1)}, u32[]{:S(2)}, u32[]{:S(2)}) collective-permute-start(bf16[192,384]{1,0:T(8,128)(2,1)S(1)} %fusion.13), channel_id=1, source_target_pairs={{0,64},{32,96},{64,128},{96,160},{128,192},{160,224},{192,256},{22... | collective-permute-start | bytes 442376 | tf_op jit(solution)/shard_map/ppermute | solution.py:16
  94.0 9.0 %collective-permute-start.12 = (bf16[192,384]{1,0:T(8,128)(2,1)S(1)}, bf16[192,384]{1,0:T(8,128)(2,1)S(1)}, u32[]{:S(2)}, u32[]{:S(2)}) collective-permute-start(bf16[192,384]{1,0:T(8,128)(2,1)S(1)} %fusion.13), channel_id=1, source_target_pairs={{0,32},{32,64},{64,96},{96,128},{128,160},{160,192},{192,224},{224... | collective-permute-start | bytes 442376 | tf_op jit(solution)/shard_map/ppermute | solution.py:16
  103.4 6.4 %copy-start.13 = (bf16[192]{0:T(256)(128)(2,1)S(1)}, bf16[192]{0:T(256)(128)(2,1)}, u32[]{:S(2)}) copy-start(bf16[192]{0:T(256)(128)(2,1)} %param.21) | copy-start | bytes 1156
  103.8 6.5 %collective-permute-start.13 = (bf16[2,1,96,384]{3,2,1,0:T(8,128)(2,1)S(1)}, bf16[2,1,96,384]{3,2,1,0:T(8,128)(2,1)S(1)}, u32[]{:S(2)}, u32[]{:S(2)}) collective-permute-start(bf16[2,1,96,384]{3,2,1,0:T(8,128)(2,1)S(1)} %get-tuple-element.16), channel_id=1, source_target_pairs={{0,1},{1,2},{2,3},{3,4},{4,5},{5,6},{6,7},{7,8},{8,9},{9,10},{10,1... | collective-permute-start | bytes 442376 | tf_op jit(solution)/shard_map/ppermute | solution.py:24
  107.9 11.1 %collective-permute-start.14 = (bf16[2,1,96,384]{3,2,1,0:T(8,128)(2,1)S(1)}, bf16[2,1,96,384]{3,2,1,0:T(8,128)(2,1)S(1)}, u32[]{:S(2)}, u32[]{:S(2)}) collective-permute-start(bf16[2,1,96,384]{3,2,1,0:T(8,128)(2,1)S(1)} %get-tuple-element.17), channel_id=1, source_target_pairs={{1,0},{2,1},{3,2},{4,3},{5,4},{6,5},{7,6},{8,7},{9,8},{10,9},{11,1... | collective-permute-start | bytes 442376 | tf_op jit(solution)/shard_map/ppermute | solution.py:27
  119.5 1.5 %copy-start.1 = (bf16[3,3,384,192]{2,3,1,0:T(8,128)(2,1)S(1)}, bf16[3,3,384,192]{2,3,1,0:T(8,128)(2,1)}, u32[]{:S(2)}) copy-start(bf16[3,3,384,192]{2,3,1,0:T(8,128)(2,1)} %param.20) | copy-start | bytes 3981316
  128.4 1.4 copy-start.3
  132.4 1.8 %copy-start.5 = (bf16[2,4,96,1,192]{2,1,0,4,3:T(4,128)(2,1)S(1)}, bf16[2,4,96,1,192]{2,1,0,4,3:T(4,128)(2,1)}, u32[]{:S(2)}) copy-start(bf16[2,4,96,1,192]{2,1,0,4,3:T(4,128)(2,1)} %reshape.112) | copy-start | bytes 884740

commit v6 on v4

--- a/solution.py
+++ b/solution.py
@@ -177,19 +177,33 @@
     )
     paired = jnp.stack([timed[:, :channels], timed[:, channels:]]).reshape(2, rows, width, channels)
     padded = with_halo(paired, (("space", 1),), 1)
-    upsampled = jnp.repeat(jnp.repeat(padded, 2, axis=1)[:, 1 : 2 * rows + 3], 2, axis=2)
-    upsampled = jnp.pad(upsampled, ((0, 0), (0, 0), (1, 1), (0, 0)))
     out_channels = w_space.shape[-1]
-    result = jnp.zeros((8 * rows * width, out_channels), jnp.float32) + b_space.astype(jnp.float32)
-    for row_tap in range(3):
-        for col_tap in range(3):
-            window = upsampled[
-                :, row_tap : row_tap + 2 * rows, col_tap : col_tap + 2 * width
-            ].reshape(-1, channels)
-            result = result + jnp.dot(
-                window, w_space[row_tap, col_tap], preferred_element_type=jnp.float32
-            )
-    return result.astype(jnp.bfloat16).reshape(2, 2 * rows, 2 * width, out_channels)
+    row_source = ((0, 1, 1), (1, 1, 2))
+    products = {}
+    for offset in range(3):
+        taps = sorted({row_tap for parity in row_source for row_tap in range(3) if parity[row_tap] == offset})
+        lhs = padded[:, offset : offset + rows].reshape(-1, channels)
+        rhs = jnp.concatenate([w_space[row_tap, col_tap] for row_tap in taps for col_tap in range(3)], axis=1)
+        both = jnp.dot(lhs, rhs, preferred_element_type=jnp.float32)
+        both = both.reshape(2, rows, width, len(taps) * 3, out_channels)
+        for index, row_tap in enumerate(taps):
+            for col_tap in range(3):
+                products[offset, row_tap, col_tap] = both[:, :, :, index * 3 + col_tap]
+
+    def shifted_cols(value, steps):
+        if steps < 0:
+            return jnp.pad(value, ((0, 0), (0, 0), (1, 0), (0, 0)))[:, :, :width]
+        return jnp.pad(value, ((0, 0), (0, 0), (0, 1), (0, 0)))[:, :, 1:]
+
+    bias = b_space.astype(jnp.float32)
+    rows_out = []
+    for parity in row_source:
+        taps = [sum(products[parity[row_tap], row_tap, col_tap] for row_tap in range(3)) for col_tap in range(3)]
+        even = bias + shifted_cols(taps[0], -1) + taps[1] + taps[2]
+        odd = bias + taps[0] + taps[1] + shifted_cols(taps[2], 1)
+        rows_out.append(jnp.stack([even, odd], axis=3).astype(jnp.bfloat16))
+    result = jnp.stack(rows_out, axis=2)
+    return result.reshape(2, 2 * rows, 2 * width, out_channels)
 
 
 def solution(mesh):

time: 137 us -> 123 us (0.90)
  the two profiles are of different devices: /device:TPU:17 before, /device:TPU:260 now
where the time goes in v6:
time: 123 us
  starting transfers between devices  62.2 us (51%)
  waiting for transfers between devices  26.7 us (22%)
  Pallas kernels  14.1 us (11%)
  local copies, waits for them, and re-layouts  8.83 us (7%)
  other arithmetic  6.11 us (5%)
  matrix products  4.18 us (3%)
    ppermute x11, starting transfers between devices, moved(): return lax.ppermute(value, 'space', [(s, target(s)) for s in range(count)])  40.4 us
    pallas_call x1, Pallas kernels, fused_attention(): pl.pallas_call(functools.partial(attention_kernel, sizes=sizes, channels=...  14.1 us
    ppermute x1, starting transfers between devices, with_halo(): lax.ppermute(lax.slice_in_dim(block, 0, width, axis=dim), axis, backward)  12.4 us
    ppermute x11, waiting for transfers between devices, moved(): return lax.ppermute(value, 'space', [(s, target(s)) for s in range(count)])  11.8 us
    ppermute x1, waiting for transfers between devices, with_halo(): lax.ppermute(lax.slice_in_dim(block, block.shape[dim] - width, None, axis...  7.8 us
    ppermute x2, starting transfers between devices, shifted(): lax.ppermute(value, axis, [(source, source + steps) for source in range(l...  7.49 us
    unnamed x39, local copies, waits for them, and re-layouts  5.03 us
    ppermute x2, waiting for transfers between devices, shifted(): lax.ppermute(value, axis, [(source, source + steps) for source in range(l...  4.48 us
  transfers between devices with their start and end apart: 15, of which 9 were waited for; matrix products, arithmetic and copies ran while one was open for 12% of the time, Pallas kernels for 0%

profile of v6, /device:TPU:260, one launch (start us, length us, event | category | flops | bytes accessed | tf_op | source)
XLA Modules:
  0.0 122.8 jit_solution(11644417706660183558)
XLA Ops:
  0.0 7.9 %collective-permute-start = (bf16[192,384]{1,0:T(8,128)(2,1)}, bf16[192,384]{1,0:T(8,128)(2,1)S(1)}, u32[]{:S(2)}, u32[]{:S(2)}) collective-permute-start(bf16[192,384]{1,0:T(8,128)(2,1)} %bitcast.212), channel_id=1, source_target_pairs={{0,2},{1,3},{2,0},{3,1},{4,6},{5,7},{6,4},{7,5},{8,10},{9,11},{10,... | collective-permute-start | bytes 442376 | tf_op jit(solution)/shard_map/ppermute | solution.py:37
  7.9 0.9 constant_dynamic-update-slice_fusion.11
  8.8 0.9 constant_dynamic-update-slice_fusion.10
  9.8 0.9 constant_dynamic-update-slice_fusion.9
  10.7 0.9 bitcast_dynamic-update-slice_fusion.2
  11.7 0.9 bitcast_dynamic-update-slice_fusion.1
  12.8 3.4 %collective-permute-start.1 = (bf16[384,384]{1,0:T(8,128)(2,1)S(1)}, bf16[384,384]{1,0:T(8,128)(2,1)S(1)}, u32[]{:S(2)}, u32[]{:S(2)}) collective-permute-start(bf16[384,384]{1,0:T(8,128)(2,1)S(1)} %pad_maximum_fusion.10), channel_id=1, source_target_pairs={{0,4},{1,5},{2,6},{3,7},{4,8},{5,9},{6,10},{7,11},{8,12},{9,13},{1... | collective-permute-start | bytes 884744 | tf_op jit(solution)/shard_map/ppermute | solution.py:37
  16.2 3.7 %collective-permute-start.2 = (bf16[384,384]{1,0:T(8,128)(2,1)S(1)}, bf16[384,384]{1,0:T(8,128)(2,1)S(1)}, u32[]{:S(2)}, u32[]{:S(2)}) collective-permute-start(bf16[384,384]{1,0:T(8,128)(2,1)S(1)} %pad_maximum_fusion.10), channel_id=1, source_target_pairs={{0,28},{1,29},{2,30},{3,31},{4,0},{5,1},{6,2},{7,3},{8,4},{9,5},{1... | collective-permute-start | bytes 884744 | tf_op jit(solution)/shard_map/ppermute | solution.py:37
  20.0 4.3 %collective-permute-done.1 = bf16[384,384]{1,0:T(8,128)(2,1)S(1)} collective-permute-done((bf16[384,384]{1,0:T(8,128)(2,1)S(1)}, bf16[384,384]{1,0:T(8,128)(2,1)S(1)}, u32[]{:S(2)}, u32[]{:S(2)}) %collective-permute-start.1) | collective-permute-done | bytes 294944 | tf_op jit(solution)/shard_map/ppermute | solution.py:37
  24.4 2.2 %collective-permute-start.3 = (bf16[384,384]{1,0:T(8,128)(2,1)S(1)}, bf16[384,384]{1,0:T(8,128)(2,1)S(1)}, u32[]{:S(2)}, u32[]{:S(2)}) collective-permute-start(bf16[384,384]{1,0:T(8,128)(2,1)S(1)} %collective-permute-done.1), channel_id=1, source_target_pairs={{0,4},{1,5},{2,6},{3,7},{4,8},{5,9},{6,10},{7,11},{8,12},{9,13},{1... | collective-permute-start | bytes 884744 | tf_op jit(solution)/shard_map/ppermute | solution.py:37
  26.5 4.9 %collective-permute-start.4 = (bf16[384,384]{1,0:T(8,128)(2,1)S(1)}, bf16[384,384]{1,0:T(8,128)(2,1)S(1)}, u32[]{:S(2)}, u32[]{:S(2)}) collective-permute-start(bf16[384,384]{1,0:T(8,128)(2,1)S(1)} %collective-permute-done.2), channel_id=1, source_target_pairs={{0,28},{1,29},{2,30},{3,31},{4,0},{5,1},{6,2},{7,3},{8,4},{9,5},{1... | collective-permute-start | bytes 884744 | tf_op jit(solution)/shard_map/ppermute | solution.py:37
  31.5 0.8 fusion.41
  32.2 2.8 %collective-permute-done.3 = bf16[384,384]{1,0:T(8,128)(2,1)S(1)} collective-permute-done((bf16[384,384]{1,0:T(8,128)(2,1)S(1)}, bf16[384,384]{1,0:T(8,128)(2,1)S(1)}, u32[]{:S(2)}, u32[]{:S(2)}) %collective-permute-start.3) | collective-permute-done | bytes 294944 | tf_op jit(solution)/shard_map/ppermute | solution.py:37
  35.1 1.9 %collective-permute-start.5 = (bf16[384,384]{1,0:T(8,128)(2,1)S(1)}, bf16[384,384]{1,0:T(8,128)(2,1)S(1)}, u32[]{:S(2)}, u32[]{:S(2)}) collective-permute-start(bf16[384,384]{1,0:T(8,128)(2,1)S(1)} %collective-permute-done.3), channel_id=1, source_target_pairs={{0,4},{1,5},{2,6},{3,7},{4,8},{5,9},{6,10},{7,11},{8,12},{9,13},{1... | collective-permute-start | bytes 884744 | tf_op jit(solution)/shard_map/ppermute | solution.py:37
  37.0 5.1 %collective-permute-start.6 = (bf16[384,384]{1,0:T(8,128)(2,1)S(1)}, bf16[384,384]{1,0:T(8,128)(2,1)S(1)}, u32[]{:S(2)}, u32[]{:S(2)}) collective-permute-start(bf16[384,384]{1,0:T(8,128)(2,1)S(1)} %collective-permute-done.4), channel_id=1, source_target_pairs={{0,28},{1,29},{2,30},{3,31},{4,0},{5,1},{6,2},{7,3},{8,4},{9,5},{1... | collective-permute-start | bytes 884744 | tf_op jit(solution)/shard_map/ppermute | solution.py:37
  42.1 0.6 slice_convert_fusion
  42.8 2.1 %collective-permute-done.5 = bf16[384,384]{1,0:T(8,128)(2,1)S(1)} collective-permute-done((bf16[384,384]{1,0:T(8,128)(2,1)S(1)}, bf16[384,384]{1,0:T(8,128)(2,1)S(1)}, u32[]{:S(2)}, u32[]{:S(2)}) %collective-permute-start.5) | collective-permute-done | bytes 294944 | tf_op jit(solution)/shard_map/ppermute | solution.py:37
  44.9 1.9 %collective-permute-start.7 = (bf16[192,384]{1,0:T(8,128)(2,1)S(1)}, bf16[192,384]{1,0:T(8,128)(2,1)S(1)}, u32[]{:S(2)}, u32[]{:S(2)}) collective-permute-start(bf16[192,384]{1,0:T(8,128)(2,1)S(1)} %slice.199), channel_id=1, source_target_pairs={{0,4},{1,5},{2,6},{3,7},{4,8},{5,9},{6,10},{7,11},{8,12},{9,13},{1... | collective-permute-start | bytes 442376 | tf_op jit(solution)/shard_map/ppermute | solution.py:37
  46.9 5.1 %collective-permute-start.8 = (bf16[192,384]{1,0:T(8,128)(2,1)S(1)}, bf16[192,384]{1,0:T(8,128)(2,1)S(1)}, u32[]{:S(2)}, u32[]{:S(2)}) collective-permute-start(bf16[192,384]{1,0:T(8,128)(2,1)S(1)} %slice.200), channel_id=1, source_target_pairs={{0,28},{1,29},{2,30},{3,31},{4,0},{5,1},{6,2},{7,3},{8,4},{9,5},{1... | collective-permute-start | bytes 442376 | tf_op jit(solution)/shard_map/ppermute | solution.py:37
  52.2 1.0 collective-permute-done.7
  53.2 1.5 %collective-permute-done.8 = bf16[192,384]{1,0:T(8,128)(2,1)S(1)} collective-permute-done((bf16[192,384]{1,0:T(8,128)(2,1)S(1)}, bf16[192,384]{1,0:T(8,128)(2,1)S(1)}, u32[]{:S(2)}, u32[]{:S(2)}) %collective-permute-start.8) | collective-permute-done | bytes 147488 | tf_op jit(solution)/shard_map/ppermute | solution.py:37
  54.7 1.9 %collective-permute-start.10 = (bf16[1920,384]{1,0:T(8,128)(2,1)S(1)}, bf16[1920,384]{1,0:T(8,128)(2,1)}, u32[]{:S(2)}, u32[]{:S(2)}) collective-permute-start(bf16[1920,384]{1,0:T(8,128)(2,1)S(1)} %constant_dynamic-update-slice_fusion.refs_7_), channel_id=1, source_target_pairs={{0,1},{1,0},{2,3},{3,2},{4,5},{5,4},{6,7},{7,6},{8,9},{9,8},{10,11... | collective-permute-start | bytes 4423688 | tf_op jit(solution)/shard_map/ppermute | solution.py:37
  56.6 0.8 slice_bitcast_fusion.14
  57.6 2.4 %collective-permute-start.9 = (bf16[1152,384]{1,0:T(8,128)(2,1)S(1)}, bf16[1152,384]{1,0:T(8,128)(2,1)S(1)}, u32[]{:S(2)}, u32[]{:S(2)}) collective-permute-start(bf16[1152,384]{1,0:T(8,128)(2,1)S(1)} %pad_maximum_fusion.refs_6_), channel_id=1, source_target_pairs={{0,1},{1,0},{2,3},{3,2},{4,5},{5,4},{6,7},{7,6},{8,9},{9,8},{10,11... | collective-permute-start | bytes 2654216 | tf_op jit(solution)/shard_map/ppermute | solution.py:37
  60.0 0.8 pad_maximum_fusion.2
  60.8 0.8 convert_element_type.59
  61.6 0.7 convert_element_type.58
  62.3 1.1 pad_maximum_fusion.1
  63.4 1.0 fusion.68
  64.4 0.9 fusion.4.refs_0_
  65.4 14.1 %shard_map.109 = bf16[192,384]{1,0:T(8,128)(2,1)S(1)} custom-call(bf16[192,384]{1,0:T(8,128)(2,1)S(1)} %fusion.4.refs_0_, f32[1,384]{1,0:T(1,128)S(1)} %reshape.151.refs_1_, bf16[384,384]{1,0:T(8,128)(2,1)S(1)} %get-tuple-element.19.refs_2_, f32[1,384]{1,0:T(1,128)S(1)} %reshape.158.refs_3_, bf16[384,384]{1,0:T(8,128)(2,1)S(1)} %get-tuple-element.18.refs_4_, ...), custom_call_target="tpu_custom_call" | custom-call | flops 5435817984 | bytes 5603328 | tf_op jit(solution)/shard_map/pallas_call | solution.py:135
  79.8 3.5 %collective-permute-start.11 = (bf16[192,384]{1,0:T(8,128)(2,1)S(1)}, bf16[192,384]{1,0:T(8,128)(2,1)S(1)}, u32[]{:S(2)}, u32[]{:S(2)}) collective-permute-start(bf16[192,384]{1,0:T(8,128)(2,1)S(1)} %fusion.5), channel_id=1, source_target_pairs={{0,64},{32,96},{64,128},{96,160},{128,192},{160,224},{192,256},{22... | collective-permute-start | bytes 442376 | tf_op jit(solution)/shard_map/ppermute | solution.py:16
  83.4 4.0 %collective-permute-start.12 = (bf16[192,384]{1,0:T(8,128)(2,1)S(1)}, bf16[192,384]{1,0:T(8,128)(2,1)S(1)}, u32[]{:S(2)}, u32[]{:S(2)}) collective-permute-start(bf16[192,384]{1,0:T(8,128)(2,1)S(1)} %fusion.5), channel_id=1, source_target_pairs={{0,32},{32,64},{64,96},{96,128},{128,160},{160,192},{192,224},{224... | collective-permute-start | bytes 442376 | tf_op jit(solution)/shard_map/ppermute | solution.py:16
  87.4 0.3 fusion.6
  87.7 2.2 %collective-permute-done.11 = bf16[192,384]{1,0:T(8,128)(2,1)S(1)} collective-permute-done((bf16[192,384]{1,0:T(8,128)(2,1)S(1)}, bf16[192,384]{1,0:T(8,128)(2,1)S(1)}, u32[]{:S(2)}, u32[]{:S(2)}) %collective-permute-start.11) | collective-permute-done | bytes 147488 | tf_op jit(solution)/shard_map/ppermute | solution.py:16
  89.9 2.3 %collective-permute-done.12 = bf16[192,384]{1,0:T(8,128)(2,1)S(1)} collective-permute-done((bf16[192,384]{1,0:T(8,128)(2,1)S(1)}, bf16[192,384]{1,0:T(8,128)(2,1)S(1)}, u32[]{:S(2)}, u32[]{:S(2)}) %collective-permute-start.12) | collective-permute-done | bytes 147488 | tf_op jit(solution)/shard_map/ppermute | solution.py:16
  92.3 0.3 fusion.8
  92.6 0.3 fusion.2
  93.0 12.4 %collective-permute-start.14 = (bf16[2,1,96,384]{3,2,1,0:T(8,128)(2,1)S(1)}, bf16[2,1,96,384]{3,2,1,0:T(8,128)(2,1)S(1)}, u32[]{:S(2)}, u32[]{:S(2)}) collective-permute-start(bf16[2,1,96,384]{3,2,1,0:T(8,128)(2,1)S(1)} %get-tuple-element.21), channel_id=1, source_target_pairs={{1,0},{2,1},{3,2},{4,3},{5,4},{6,5},{7,6},{8,7},{9,8},{10,9},{11,1... | collective-permute-start | bytes 442376 | tf_op jit(solution)/shard_map/ppermute | solution.py:27
  105.4 1.9 %collective-permute-start.13 = (bf16[2,1,96,384]{3,2,1,0:T(8,128)(2,1)S(1)}, bf16[2,1,96,384]{3,2,1,0:T(8,128)(2,1)S(1)}, u32[]{:S(2)}, u32[]{:S(2)}) collective-permute-start(bf16[2,1,96,384]{3,2,1,0:T(8,128)(2,1)S(1)} %get-tuple-element.20), channel_id=1, source_target_pairs={{0,1},{1,2},{2,3},{3,4},{4,5},{5,6},{6,7},{7,8},{8,9},{9,10},{10,1... | collective-permute-start | bytes 442376 | tf_op jit(solution)/shard_map/ppermute | solution.py:24
  107.4 1.1 fusion.43
  108.5 2.6 %collective-permute-done.14 = bf16[2,1,96,384]{3,2,1,0:T(8,128)(2,1)S(1)} collective-permute-done((bf16[2,1,96,384]{3,2,1,0:T(8,128)(2,1)S(1)}, bf16[2,1,96,384]{3,2,1,0:T(8,128)(2,1)S(1)}, u32[]{:S(2)}, u32[]{:S(2)}) %collective-permute-start.14) | collective-permute-done | bytes 147488 | tf_op jit(solution)/shard_map/ppermute | solution.py:27
  111.1 0.5 fusion.46
  111.6 7.8 %collective-permute-done.13 = bf16[2,1,96,384]{3,2,1,0:T(8,128)(2,1)S(1)} collective-permute-done((bf16[2,1,96,384]{3,2,1,0:T(8,128)(2,1)S(1)}, bf16[2,1,96,384]{3,2,1,0:T(8,128)(2,1)S(1)}, u32[]{:S(2)}, u32[]{:S(2)}) %collective-permute-start.13) | collective-permute-done | bytes 147488 | tf_op jit(solution)/shard_map/ppermute | solution.py:24
  119.4 0.5 fusion.50
  120.2 0.4 fusion.55
  120.9 0.8 copy.40
  121.8 1.0 copy.41
  (62 shorter events, 1.8 us)
Async XLA Ops:
  0.0 79.6 %copy-start = (bf16[384,384]{1,0:T(8,128)(2,1)S(1)}, bf16[384,384]{1,0:T(8,128)(2,1)}, u32[]{:S(2)}) copy-start(bf16[384,384]{1,0:T(8,128)(2,1)} %param.16) | copy-start | bytes 884740
  0.0 12.7 %copy-start.1 = (bf16[1,2,96,384]{3,2,1,0:T(8,128)(2,1)S(1)}, bf16[1,2,96,384]{3,2,1,0:T(8,128)(2,1)}, u32[]{:S(2)}) copy-start(bf16[1,2,96,384]{3,2,1,0:T(8,128)(2,1)} %param.11) | copy-start | bytes 442372
  0.0 12.6 %copy-start.3 = (bf16[3,3,384,192]{2,3,1,0:T(8,128)(2,1)S(1)}, bf16[3,3,384,192]{2,3,1,0:T(8,128)(2,1)}, u32[]{:S(2)}) copy-start(bf16[3,3,384,192]{2,3,1,0:T(8,128)(2,1)} %param.20) | copy-start | bytes 3981316
  0.0 12.7 %collective-permute-start = (bf16[192,384]{1,0:T(8,128)(2,1)}, bf16[192,384]{1,0:T(8,128)(2,1)S(1)}, u32[]{:S(2)}, u32[]{:S(2)}) collective-permute-start(bf16[192,384]{1,0:T(8,128)(2,1)} %bitcast.212), channel_id=1, source_target_pairs={{0,2},{1,3},{2,0},{3,1},{4,6},{5,7},{6,4},{7,5},{8,10},{9,11},{10,... | collective-permute-start | bytes 442376 | tf_op jit(solution)/shard_map/ppermute | solution.py:37
  10.7 20.7 %copy-start.10 = (bf16[384]{0:T(512)(128)(2,1)S(1)}, bf16[384]{0:T(512)(128)(2,1)}, u32[]{:S(2)}) copy-start(bf16[384]{0:T(512)(128)(2,1)} %param.13) | copy-start | bytes 2308
  11.7 30.5 %copy-start.11 = (bf16[1152]{0:T(1024)(128)(2,1)S(1)}, bf16[1152]{0:T(1024)(128)(2,1)}, u32[]{:S(2)}) copy-start(bf16[1152]{0:T(1024)(128)(2,1)} %param.15) | copy-start | bytes 6916
  12.8 11.6 %collective-permute-start.1 = (bf16[384,384]{1,0:T(8,128)(2,1)S(1)}, bf16[384,384]{1,0:T(8,128)(2,1)S(1)}, u32[]{:S(2)}, u32[]{:S(2)}) collective-permute-start(bf16[384,384]{1,0:T(8,128)(2,1)S(1)} %pad_maximum_fusion.10), channel_id=1, source_target_pairs={{0,4},{1,5},{2,6},{3,7},{4,8},{5,9},{6,10},{7,11},{8,12},{9,13},{1... | collective-permute-start | bytes 884744 | tf_op jit(solution)/shard_map/ppermute | solution.py:37
  16.2 10.4 %collective-permute-start.2 = (bf16[384,384]{1,0:T(8,128)(2,1)S(1)}, bf16[384,384]{1,0:T(8,128)(2,1)S(1)}, u32[]{:S(2)}, u32[]{:S(2)}) collective-permute-start(bf16[384,384]{1,0:T(8,128)(2,1)S(1)} %pad_maximum_fusion.10), channel_id=1, source_target_pairs={{0,28},{1,29},{2,30},{3,31},{4,0},{5,1},{6,2},{7,3},{8,4},{9,5},{1... | collective-permute-start | bytes 884744 | tf_op jit(solution)/shard_map/ppermute | solution.py:37
  20.0 32.1 %copy-start.6 = (bf16[384,1728]{0,1:T(8,128)(2,1)}, bf16[384,1728]{0,1:T(8,128)(2,1)S(1)}, u32[]{:S(2)}) copy-start(bf16[384,1728]{0,1:T(8,128)(2,1)S(1)} %constant_dynamic-update-slice_fusion.6) | copy-start | bytes 3981316
  24.4 10.7 %collective-permute-start.3 = (bf16[384,384]{1,0:T(8,128)(2,1)S(1)}, bf16[384,384]{1,0:T(8,128)(2,1)S(1)}, u32[]{:S(2)}, u32[]{:S(2)}) collective-permute-start(bf16[384,384]{1,0:T(8,128)(2,1)S(1)} %collective-permute-done.1), channel_id=1, source_target_pairs={{0,4},{1,5},{2,6},{3,7},{4,8},{5,9},{6,10},{7,11},{8,12},{9,13},{1... | collective-permute-start | bytes 884744 | tf_op jit(solution)/shard_map/ppermute | solution.py:37
  26.5 10.4 %collective-permute-start.4 = (bf16[384,384]{1,0:T(8,128)(2,1)S(1)}, bf16[384,384]{1,0:T(8,128)(2,1)S(1)}, u32[]{:S(2)}, u32[]{:S(2)}) collective-permute-start(bf16[384,384]{1,0:T(8,128)(2,1)S(1)} %collective-permute-done.2), channel_id=1, source_target_pairs={{0,28},{1,29},{2,30},{3,31},{4,0},{5,1},{6,2},{7,3},{8,4},{9,5},{1... | collective-permute-start | bytes 884744 | tf_op jit(solution)/shard_map/ppermute | solution.py:37
  35.1 9.8 %collective-permute-start.5 = (bf16[384,384]{1,0:T(8,128)(2,1)S(1)}, bf16[384,384]{1,0:T(8,128)(2,1)S(1)}, u32[]{:S(2)}, u32[]{:S(2)}) collective-permute-start(bf16[384,384]{1,0:T(8,128)(2,1)S(1)} %collective-permute-done.3), channel_id=1, source_target_pairs={{0,4},{1,5},{2,6},{3,7},{4,8},{5,9},{6,10},{7,11},{8,12},{9,13},{1... | collective-permute-start | bytes 884744 | tf_op jit(solution)/shard_map/ppermute | solution.py:37
  37.0 9.9 %collective-permute-start.6 = (bf16[384,384]{1,0:T(8,128)(2,1)S(1)}, bf16[384,384]{1,0:T(8,128)(2,1)S(1)}, u32[]{:S(2)}, u32[]{:S(2)}) collective-permute-start(bf16[384,384]{1,0:T(8,128)(2,1)S(1)} %collective-permute-done.4), channel_id=1, source_target_pairs={{0,28},{1,29},{2,30},{3,31},{4,0},{5,1},{6,2},{7,3},{8,4},{9,5},{1... | collective-permute-start | bytes 884744 | tf_op jit(solution)/shard_map/ppermute | solution.py:37
  44.9 8.2 %collective-permute-start.7 = (bf16[192,384]{1,0:T(8,128)(2,1)S(1)}, bf16[192,384]{1,0:T(8,128)(2,1)S(1)}, u32[]{:S(2)}, u32[]{:S(2)}) collective-permute-start(bf16[192,384]{1,0:T(8,128)(2,1)S(1)} %slice.199), channel_id=1, source_target_pairs={{0,4},{1,5},{2,6},{3,7},{4,8},{5,9},{6,10},{7,11},{8,12},{9,13},{1... | collective-permute-start | bytes 442376 | tf_op jit(solution)/shard_map/ppermute | solution.py:37
  46.9 7.8 %collective-permute-start.8 = (bf16[192,384]{1,0:T(8,128)(2,1)S(1)}, bf16[192,384]{1,0:T(8,128)(2,1)S(1)}, u32[]{:S(2)}, u32[]{:S(2)}) collective-permute-start(bf16[192,384]{1,0:T(8,128)(2,1)S(1)} %slice.200), channel_id=1, source_target_pairs={{0,28},{1,29},{2,30},{3,31},{4,0},{5,1},{6,2},{7,3},{8,4},{9,5},{1... | collective-permute-start | bytes 442376 | tf_op jit(solution)/shard_map/ppermute | solution.py:37
  54.7 10.7 %collective-permute-start.10 = (bf16[1920,384]{1,0:T(8,128)(2,1)S(1)}, bf16[1920,384]{1,0:T(8,128)(2,1)}, u32[]{:S(2)}, u32[]{:S(2)}) collective-permute-start(bf16[1920,384]{1,0:T(8,128)(2,1)S(1)} %constant_dynamic-update-slice_fusion.refs_7_), channel_id=1, source_target_pairs={{0,1},{1,0},{2,3},{3,2},{4,5},{5,4},{6,7},{7,6},{8,9},{9,8},{10,11... | collective-permute-start | bytes 4423688 | tf_op jit(solution)/shard_map/ppermute | solution.py:37
  57.5 3.3 %copy-start.12 = (bf16[384]{0:T(512)(128)(2,1)S(1)}, bf16[384]{0:T(512)(128)(2,1)}, u32[]{:S(2)}) copy-start(bf16[384]{0:T(512)(128)(2,1)} %param.17) | copy-start | bytes 2308
  57.6 7.8 %collective-permute-start.9 = (bf16[1152,384]{1,0:T(8,128)(2,1)S(1)}, bf16[1152,384]{1,0:T(8,128)(2,1)S(1)}, u32[]{:S(2)}, u32[]{:S(2)}) collective-permute-start(bf16[1152,384]{1,0:T(8,128)(2,1)S(1)} %pad_maximum_fusion.refs_6_), channel_id=1, source_target_pairs={{0,1},{1,0},{2,3},{3,2},{4,5},{5,4},{6,7},{7,6},{8,9},{9,8},{10,11... | collective-permute-start | bytes 2654216 | tf_op jit(solution)/shard_map/ppermute | solution.py:37
  60.8 3.6 %copy-start.8 = (bf16[384,1152]{1,0:T(8,128)(2,1)S(1)}, bf16[384,1152]{1,0:T(8,128)(2,1)}, u32[]{:S(2)}) copy-start(bf16[384,1152]{1,0:T(8,128)(2,1)} %param.14) | copy-start | bytes 2654212
  60.8 3.6 %copy-start.9 = (bf16[1,2,96,384]{3,2,1,0:T(8,128)(2,1)S(1)}, bf16[1,2,96,384]{3,2,1,0:T(8,128)(2,1)}, u32[]{:S(2)}) copy-start(bf16[1,2,96,384]{3,2,1,0:T(8,128)(2,1)} %fusion.41) | copy-start | bytes 442372
  65.4 14.2 %copy-start.2 = (bf16[1,2,96,384]{3,2,1,0:T(8,128)(2,1)S(1)}, bf16[1,2,96,384]{3,2,1,0:T(8,128)(2,1)}, u32[]{:S(2)}) copy-start(bf16[1,2,96,384]{3,2,1,0:T(8,128)(2,1)} %param.11) | copy-start | bytes 442372
  65.4 21.9 %copy-start.4 = (bf16[3,384,768]{2,1,0:T(8,128)(2,1)S(1)}, bf16[3,384,768]{2,1,0:T(8,128)(2,1)}, u32[]{:S(2)}) copy-start(bf16[3,384,768]{2,1,0:T(8,128)(2,1)} %param.18) | copy-start | bytes 5308420
  79.8 10.1 %collective-permute-start.11 = (bf16[192,384]{1,0:T(8,128)(2,1)S(1)}, bf16[192,384]{1,0:T(8,128)(2,1)S(1)}, u32[]{:S(2)}, u32[]{:S(2)}) collective-permute-start(bf16[192,384]{1,0:T(8,128)(2,1)S(1)} %fusion.5), channel_id=1, source_target_pairs={{0,64},{32,96},{64,128},{96,160},{128,192},{160,224},{192,256},{22... | collective-permute-start | bytes 442376 | tf_op jit(solution)/shard_map/ppermute | solution.py:16
  83.4 8.8 %collective-permute-start.12 = (bf16[192,384]{1,0:T(8,128)(2,1)S(1)}, bf16[192,384]{1,0:T(8,128)(2,1)S(1)}, u32[]{:S(2)}, u32[]{:S(2)}) collective-permute-start(bf16[192,384]{1,0:T(8,128)(2,1)S(1)} %fusion.5), channel_id=1, source_target_pairs={{0,32},{32,64},{64,96},{96,128},{128,160},{160,192},{192,224},{224... | collective-permute-start | bytes 442376 | tf_op jit(solution)/shard_map/ppermute | solution.py:16
  92.6 14.8 %copy-start.7 = (bf16[384,1728]{0,1:T(8,128)(2,1)S(1)}, bf16[384,1728]{0,1:T(8,128)(2,1)}, u32[]{:S(2)}) copy-start(bf16[384,1728]{0,1:T(8,128)(2,1)} %copy-done.6) | copy-start | bytes 3981316
  93.0 18.1 %collective-permute-start.14 = (bf16[2,1,96,384]{3,2,1,0:T(8,128)(2,1)S(1)}, bf16[2,1,96,384]{3,2,1,0:T(8,128)(2,1)S(1)}, u32[]{:S(2)}, u32[]{:S(2)}) collective-permute-start(bf16[2,1,96,384]{3,2,1,0:T(8,128)(2,1)S(1)} %get-tuple-element.21), channel_id=1, source_target_pairs={{1,0},{2,1},{3,2},{4,3},{5,4},{6,5},{7,6},{8,7},{9,8},{10,9},{11,1... | collective-permute-start | bytes 442376 | tf_op jit(solution)/shard_map/ppermute | solution.py:27
  105.4 14.0 %collective-permute-start.13 = (bf16[2,1,96,384]{3,2,1,0:T(8,128)(2,1)S(1)}, bf16[2,1,96,384]{3,2,1,0:T(8,128)(2,1)S(1)}, u32[]{:S(2)}, u32[]{:S(2)}) collective-permute-start(bf16[2,1,96,384]{3,2,1,0:T(8,128)(2,1)S(1)} %get-tuple-element.20), channel_id=1, source_target_pairs={{0,1},{1,2},{2,3},{3,4},{4,5},{5,6},{6,7},{7,8},{8,9},{9,10},{10,1... | collective-permute-start | bytes 442376 | tf_op jit(solution)/shard_map/ppermute | solution.py:24
  107.3 3.7 %copy-start.5 = (bf16[384,576]{0,1:T(8,128)(2,1)S(1)}, bf16[384,576]{0,1:T(8,128)(2,1)}, u32[]{:S(2)}) copy-start(bf16[384,576]{0,1:T(8,128)(2,1)} %pad_maximum_fusion.2) | copy-start | bytes 1327108

commit v7 on v6

--- a/solution.py
+++ b/solution.py
@@ -85,10 +85,10 @@
 BLOCK = 384
 
 
-def attention_kernel(*refs, sizes, channels):
+def attention_kernel(*refs, sizes, channels, resume, finish):
     q_ref, gain_ref, wk_ref, bk_ref, wv_ref, bv_ref = refs[:6]
     chunk_refs = refs[6:6 + len(sizes)]
-    out_ref = refs[6 + len(sizes)]
+    rest = refs[6 + len(sizes):]
     queries = q_ref[...]
     gain = gain_ref[...]
     wk = wk_ref[...]
@@ -96,9 +96,13 @@
     bk = bk_ref[...]
     bv = bv_ref[...]
     count = queries.shape[0]
-    best = jnp.full((count, 1), -jnp.inf, jnp.float32)
-    mass = jnp.zeros((count, 1), jnp.float32)
-    total = jnp.zeros((count, channels), jnp.float32)
+    if resume:
+        best, mass, total = rest[0][...], rest[1][...], rest[2][...]
+        rest = rest[3:]
+    else:
+        best = jnp.full((count, 1), -jnp.inf, jnp.float32)
+        mass = jnp.zeros((count, 1), jnp.float32)
+        total = jnp.zeros((count, channels), jnp.float32)
     for chunk_ref, size in zip(chunk_refs, sizes):
         for start in range(0, size, BLOCK):
             rows = chunk_ref[start:start + BLOCK, :].astype(jnp.float32)
@@ -117,33 +121,51 @@
                 weights.astype(jnp.bfloat16), values, preferred_element_type=jnp.float32
             )
             best = new_best
-    out_ref[...] = (total / mass).astype(out_ref.dtype)
-
-
-def fused_attention(queries, chunks, norm_gain, w_qkv, b_qkv):
+    if finish:
+        rest[0][...] = (total / mass).astype(rest[0].dtype)
+    else:
+        rest[0][...] = best
+        rest[1][...] = mass
+        rest[2][...] = total
+
+
+def fused_attention(queries, chunks, norm_gain, w_qkv, b_qkv, state=None, finish=True):
     channels = queries.shape[1]
+    count = queries.shape[0]
     sizes = tuple(c.shape[0] for c in chunks)
     gain = norm_gain.astype(jnp.float32).reshape(1, channels)
     wk = w_qkv[:, channels:2 * channels]
     wv = w_qkv[:, 2 * channels:]
     bk = b_qkv[channels:2 * channels].astype(jnp.float32).reshape(1, channels)
     bv = b_qkv[2 * channels:].astype(jnp.float32).reshape(1, channels)
-    vmem = pltpu.MemorySpace.VMEM
-    spec = pl.BlockSpec(memory_space=vmem)
+    spec = pl.BlockSpec(memory_space=pltpu.MemorySpace.VMEM)
     total_rows = sum(sizes)
-    flops = 2 * total_rows * channels * (2 * channels + 2 * queries.shape[0])
+    flops = 2 * total_rows * channels * (2 * channels + 2 * count)
+    extra = tuple(state) if state is not None else ()
+    if finish:
+        out_shape = jax.ShapeDtypeStruct(queries.shape, jnp.bfloat16)
+        out_specs = spec
+    else:
+        out_shape = (
+            jax.ShapeDtypeStruct((count, 1), jnp.float32),
+            jax.ShapeDtypeStruct((count, 1), jnp.float32),
+            jax.ShapeDtypeStruct((count, channels), jnp.float32),
+        )
+        out_specs = (spec, spec, spec)
     return pl.pallas_call(
-        functools.partial(attention_kernel, sizes=sizes, channels=channels),
-        out_shape=jax.ShapeDtypeStruct(queries.shape, jnp.bfloat16),
-        in_specs=[spec] * (6 + len(chunks)),
-        out_specs=spec,
+        functools.partial(
+            attention_kernel, sizes=sizes, channels=channels, resume=state is not None, finish=finish
+        ),
+        out_shape=out_shape,
+        in_specs=[spec] * (6 + len(chunks) + len(extra)),
+        out_specs=out_specs,
         compiler_params=pltpu.CompilerParams(vmem_limit_bytes=48 * 1024 * 1024),
         cost_estimate=pl.CostEstimate(
             flops=flops,
-            transcendentals=total_rows * queries.shape[0],
+            transcendentals=total_rows * count,
             bytes_accessed=2 * total_rows * channels + 4 * channels * channels + 4 * queries.size,
         ),
-    )(queries, gain, wk, bk, wv, bv, *chunks)
+    )(queries, gain, wk, bk, wv, bv, *chunks, *extra)
 
 
 def body(
@@ -155,7 +177,9 @@
     chunks = gather_space(frames.reshape(-1, channels))
     normed = normalize(frames, norm_gain).reshape(-1, channels)
     queries = project(normed, w_qkv[:, :channels], b_qkv[:channels])
-    mixed = fused_attention(queries, chunks, norm_gain, w_qkv, b_qkv)
+    half = len(chunks) // 2
+    state = fused_attention(queries, chunks[:half], norm_gain, w_qkv, b_qkv, finish=False)
+    mixed = fused_attention(queries, chunks[half:], norm_gain, w_qkv, b_qkv, state=state)
     hidden = (
         frames.reshape(-1, channels).astype(jnp.float32)
         + jnp.dot(mixed, w_proj, preferred_element_type=jnp.float32)

time: 123 us -> 124 us (level)
  starting transfers between devices: 62.2 us -> 58.6 us
  other arithmetic: 6.11 us -> 7.7 us
  Pallas kernels: 14.1 us -> 15.5 us
    ppermute x1, starting transfers between devices: 12.4 us -> 9.99 us  [with_halo(): lax.ppermute(lax.slice_in_dim(block, 0, width, axis=dim), axis, backward)]
    pallas_call x1 -> x2, Pallas kernels: 14.1 us -> 15.5 us  [fused_attention(): pl.pallas_call(functools.partial(attention_kernel, sizes=sizes, channels=...]
    unnamed x39 -> x43, local copies, waits for them, and re-layouts: 5.03 us -> 5.07 us
  transfers between devices with their start and end apart: 15 -> 15, of which waited for: 9 -> 9; matrix products, arithmetic and copies ran while one was open for 12% -> 13% of each run, Pallas kernels for 0% -> 5%
where the time goes in v7:
time: 124 us; the launch traced here: 123 us
  starting transfers between devices  58.6 us (47%)
  waiting for transfers between devices  27.7 us (22%)
  Pallas kernels  15.5 us (12%)
  local copies, waits for them, and re-layouts  8.59 us (7%)
  other arithmetic  7.7 us (6%)
  matrix products  4.51 us (4%)
    ppermute x11, starting transfers between devices, moved(): return lax.ppermute(value, 'space', [(s, target(s)) for s in range(count)])  40.4 us
    pallas_call x2, Pallas kernels, fused_attention(): pl.pallas_call(functools.partial(attention_kernel, sizes=sizes, channels=...  15.5 us
    ppermute x11, waiting for transfers between devices, moved(): return lax.ppermute(value, 'space', [(s, target(s)) for s in range(count)])  11.7 us
    ppermute x1, starting transfers between devices, with_halo(): lax.ppermute(lax.slice_in_dim(block, 0, width, axis=dim), axis, backward)  9.99 us
    ppermute x1, waiting for transfers between devices, with_halo(): lax.ppermute(lax.slice_in_dim(block, block.shape[dim] - width, None, axis...  7.59 us
    ppermute x2, starting transfers between devices, shifted(): lax.ppermute(value, axis, [(source, source + steps) for source in range(l...  6.32 us
    ppermute x2, waiting for transfers between devices, shifted(): lax.ppermute(value, axis, [(source, source + steps) for source in range(l...  5.66 us
    unnamed x43, local copies, waits for them, and re-layouts  5.07 us
  transfers between devices with their start and end apart: 15, of which 9 were waited for; matrix products, arithmetic and copies ran while one was open for 13% of the time, Pallas kernels for 5%

profile of v7, /device:TPU:260, one launch (start us, length us, event | category | flops | bytes accessed | tf_op | source)
XLA Modules:
  0.0 123.2 jit_solution(10500752024568896296)
XLA Ops:
  0.0 7.9 %collective-permute-start = (bf16[192,384]{1,0:T(8,128)(2,1)}, bf16[192,384]{1,0:T(8,128)(2,1)S(1)}, u32[]{:S(2)}, u32[]{:S(2)}) collective-permute-start(bf16[192,384]{1,0:T(8,128)(2,1)} %bitcast.212), channel_id=1, source_target_pairs={{0,2},{1,3},{2,0},{3,1},{4,6},{5,7},{6,4},{7,5},{8,10},{9,11},{10,... | collective-permute-start | bytes 442376 | tf_op jit(solution)/shard_map/ppermute | solution.py:37
  7.9 1.0 fusion.39
  8.9 0.7 convert_element_type.65
  9.6 0.9 constant_dynamic-update-slice_fusion.11
  10.6 1.0 constant_dynamic-update-slice_fusion.10
  11.5 0.9 constant_dynamic-update-slice_fusion.9
  12.5 0.9 bitcast_dynamic-update-slice_fusion.2
  13.4 0.9 bitcast_dynamic-update-slice_fusion.1
  14.4 0.8 fusion.41
  15.2 3.4 %collective-permute-start.1 = (bf16[384,384]{1,0:T(8,128)(2,1)S(1)}, bf16[384,384]{1,0:T(8,128)(2,1)S(1)}, u32[]{:S(2)}, u32[]{:S(2)}) collective-permute-start(bf16[384,384]{1,0:T(8,128)(2,1)S(1)} %pad_maximum_fusion.10), channel_id=1, source_target_pairs={{0,4},{1,5},{2,6},{3,7},{4,8},{5,9},{6,10},{7,11},{8,12},{9,13},{1... | collective-permute-start | bytes 884744 | tf_op jit(solution)/shard_map/ppermute | solution.py:37
  18.6 3.7 %collective-permute-start.2 = (bf16[384,384]{1,0:T(8,128)(2,1)S(1)}, bf16[384,384]{1,0:T(8,128)(2,1)S(1)}, u32[]{:S(2)}, u32[]{:S(2)}) collective-permute-start(bf16[384,384]{1,0:T(8,128)(2,1)S(1)} %pad_maximum_fusion.10), channel_id=1, source_target_pairs={{0,28},{1,29},{2,30},{3,31},{4,0},{5,1},{6,2},{7,3},{8,4},{9,5},{1... | collective-permute-start | bytes 884744 | tf_op jit(solution)/shard_map/ppermute | solution.py:37
  22.3 0.8 fusion.68
  23.1 3.7 %collective-permute-done.1 = bf16[384,384]{1,0:T(8,128)(2,1)S(1)} collective-permute-done((bf16[384,384]{1,0:T(8,128)(2,1)S(1)}, bf16[384,384]{1,0:T(8,128)(2,1)S(1)}, u32[]{:S(2)}, u32[]{:S(2)}) %collective-permute-start.1) | collective-permute-done | bytes 294944 | tf_op jit(solution)/shard_map/ppermute | solution.py:37
  26.8 2.2 %collective-permute-start.4 = (bf16[384,384]{1,0:T(8,128)(2,1)S(1)}, bf16[384,384]{1,0:T(8,128)(2,1)S(1)}, u32[]{:S(2)}, u32[]{:S(2)}) collective-permute-start(bf16[384,384]{1,0:T(8,128)(2,1)S(1)} %collective-permute-done.1), channel_id=1, source_target_pairs={{0,4},{1,5},{2,6},{3,7},{4,8},{5,9},{6,10},{7,11},{8,12},{9,13},{1... | collective-permute-start | bytes 884744 | tf_op jit(solution)/shard_map/ppermute | solution.py:37
  29.0 4.9 %collective-permute-start.5 = (bf16[384,384]{1,0:T(8,128)(2,1)S(1)}, bf16[384,384]{1,0:T(8,128)(2,1)S(1)}, u32[]{:S(2)}, u32[]{:S(2)}) collective-permute-start(bf16[384,384]{1,0:T(8,128)(2,1)S(1)} %collective-permute-done.2), channel_id=1, source_target_pairs={{0,28},{1,29},{2,30},{3,31},{4,0},{5,1},{6,2},{7,3},{8,4},{9,5},{1... | collective-permute-start | bytes 884744 | tf_op jit(solution)/shard_map/ppermute | solution.py:37
  33.9 0.8 slice_bitcast_fusion.14
  34.7 2.8 %collective-permute-done.4 = bf16[384,384]{1,0:T(8,128)(2,1)S(1)} collective-permute-done((bf16[384,384]{1,0:T(8,128)(2,1)S(1)}, bf16[384,384]{1,0:T(8,128)(2,1)S(1)}, u32[]{:S(2)}, u32[]{:S(2)}) %collective-permute-start.4) | collective-permute-done | bytes 294944 | tf_op jit(solution)/shard_map/ppermute | solution.py:37
  37.5 1.9 %collective-permute-start.6 = (bf16[384,384]{1,0:T(8,128)(2,1)S(1)}, bf16[384,384]{1,0:T(8,128)(2,1)S(1)}, u32[]{:S(2)}, u32[]{:S(2)}) collective-permute-start(bf16[384,384]{1,0:T(8,128)(2,1)S(1)} %collective-permute-done.4), channel_id=1, source_target_pairs={{0,4},{1,5},{2,6},{3,7},{4,8},{5,9},{6,10},{7,11},{8,12},{9,13},{1... | collective-permute-start | bytes 884744 | tf_op jit(solution)/shard_map/ppermute | solution.py:37
  39.4 5.1 %collective-permute-start.7 = (bf16[384,384]{1,0:T(8,128)(2,1)S(1)}, bf16[384,384]{1,0:T(8,128)(2,1)S(1)}, u32[]{:S(2)}, u32[]{:S(2)}) collective-permute-start(bf16[384,384]{1,0:T(8,128)(2,1)S(1)} %collective-permute-done.5), channel_id=1, source_target_pairs={{0,28},{1,29},{2,30},{3,31},{4,0},{5,1},{6,2},{7,3},{8,4},{9,5},{1... | collective-permute-start | bytes 884744 | tf_op jit(solution)/shard_map/ppermute | solution.py:37
  44.7 2.6 %collective-permute-done.6 = bf16[384,384]{1,0:T(8,128)(2,1)S(1)} collective-permute-done((bf16[384,384]{1,0:T(8,128)(2,1)S(1)}, bf16[384,384]{1,0:T(8,128)(2,1)S(1)}, u32[]{:S(2)}, u32[]{:S(2)}) %collective-permute-start.6) | collective-permute-done | bytes 294944 | tf_op jit(solution)/shard_map/ppermute | solution.py:37
  47.4 1.9 %collective-permute-start.8 = (bf16[192,384]{1,0:T(8,128)(2,1)S(1)}, bf16[192,384]{1,0:T(8,128)(2,1)S(1)}, u32[]{:S(2)}, u32[]{:S(2)}) collective-permute-start(bf16[192,384]{1,0:T(8,128)(2,1)S(1)} %slice.203), channel_id=1, source_target_pairs={{0,4},{1,5},{2,6},{3,7},{4,8},{5,9},{6,10},{7,11},{8,12},{9,13},{1... | collective-permute-start | bytes 442376 | tf_op jit(solution)/shard_map/ppermute | solution.py:37
  49.3 5.1 %collective-permute-start.9 = (bf16[192,384]{1,0:T(8,128)(2,1)S(1)}, bf16[192,384]{1,0:T(8,128)(2,1)S(1)}, u32[]{:S(2)}, u32[]{:S(2)}) collective-permute-start(bf16[192,384]{1,0:T(8,128)(2,1)S(1)} %slice.204), channel_id=1, source_target_pairs={{0,28},{1,29},{2,30},{3,31},{4,0},{5,1},{6,2},{7,3},{8,4},{9,5},{1... | collective-permute-start | bytes 442376 | tf_op jit(solution)/shard_map/ppermute | solution.py:37
  54.6 1.0 collective-permute-done.8
  55.6 1.5 %collective-permute-done.9 = bf16[192,384]{1,0:T(8,128)(2,1)S(1)} collective-permute-done((bf16[192,384]{1,0:T(8,128)(2,1)S(1)}, bf16[192,384]{1,0:T(8,128)(2,1)S(1)}, u32[]{:S(2)}, u32[]{:S(2)}) %collective-permute-start.9) | collective-permute-done | bytes 147488 | tf_op jit(solution)/shard_map/ppermute | solution.py:37
  57.2 1.9 %collective-permute-start.10 = (bf16[1920,384]{1,0:T(8,128)(2,1)S(1)}, bf16[1920,384]{1,0:T(8,128)(2,1)}, u32[]{:S(2)}, u32[]{:S(2)}) collective-permute-start(bf16[1920,384]{1,0:T(8,128)(2,1)S(1)} %constant_dynamic-update-slice_fusion.refs_7_), channel_id=1, source_target_pairs={{0,1},{1,0},{2,3},{3,2},{4,5},{5,4},{6,7},{7,6},{8,9},{9,8},{10,11... | collective-permute-start | bytes 4423688 | tf_op jit(solution)/shard_map/ppermute | solution.py:37
  59.1 0.6 slice_convert_fusion
  59.8 2.4 %collective-permute-start.3 = (bf16[1152,384]{1,0:T(8,128)(2,1)S(1)}, bf16[1152,384]{1,0:T(8,128)(2,1)S(1)}, u32[]{:S(2)}, u32[]{:S(2)}) collective-permute-start(bf16[1152,384]{1,0:T(8,128)(2,1)S(1)} %pad_maximum_fusion.refs_6_), channel_id=1, source_target_pairs={{0,1},{1,0},{2,3},{3,2},{4,5},{5,4},{6,7},{7,6},{8,9},{9,8},{10,11... | collective-permute-start | bytes 2654216 | tf_op jit(solution)/shard_map/ppermute | solution.py:37
  62.2 0.8 pad_maximum_fusion.2
  63.1 0.8 convert_element_type.62
  63.8 0.7 convert_element_type.61
  64.5 1.1 pad_maximum_fusion.1
  65.6 1.2 %fusion.4.refs_0_ = bf16[192,384]{1,0:T(8,128)(2,1)S(1)} fusion(bf16[192,384]{1,0:T(8,128)(2,1)} %bitcast.220, bf16[384,1152]{1,0:T(8,128)(2,1)} %param.14, f32[384]{0:T(512)} %get-tuple-element.35), kind=kOutput, calls=%fused_computation.7 | convolution fusion | flops 56770560 | bytes 591872 | tf_op jit(solution)/shard_map/dot_general | solution.py:67
  66.9 6.3 %shard_map.109 = (f32[192,1]{1,0:T(8,128)S(1)}, f32[192,1]{1,0:T(8,128)S(1)}, f32[192,384]{1,0:T(8,128)S(1)}) custom-call(bf16[192,384]{1,0:T(8,128)(2,1)S(1)} %fusion.4.refs_0_, f32[1,384]{1,0:T(1,128)S(1)} %reshape.154.refs_1_, bf16[384,384]{1,0:T(8,128)(2,1)S(1)} %get-tuple-element.25.refs_2_, f32[1,384]{1,0:T(1,128)S(1)} %reshape.161.refs_3_, ...), custom_call_target="tpu_custom_call" | custom-call | flops 2717908992 | bytes 3244032 | tf_op jit(solution)/shard_map/pallas_call | solution.py:155
  73.2 9.2 %shard_map.110 = bf16[192,384]{1,0:T(8,128)(2,1)S(1)} custom-call(bf16[192,384]{1,0:T(8,128)(2,1)S(1)} %fusion.4.refs_0_, f32[1,384]{1,0:T(1,128)S(1)} %reshape.154.refs_1_, bf16[384,384]{1,0:T(8,128)(2,1)S(1)} %get-tuple-element.25.refs_2_, f32[1,384]{1,0:T(1,128)S(1)} %reshape.161.refs_3_, bf16[384,384]{1,0:T(8,128)(2,1)S(1)} %get-tuple-element.24.refs_4_, ...), custom_call_target="tpu_custom_call" | custom-call | flops 2717908992 | bytes 3244032 | tf_op jit(solution)/shard_map/pallas_call | solution.py:155
  82.7 2.3 %collective-permute-start.11 = (bf16[192,384]{1,0:T(8,128)(2,1)S(1)}, bf16[192,384]{1,0:T(8,128)(2,1)S(1)}, u32[]{:S(2)}, u32[]{:S(2)}) collective-permute-start(bf16[192,384]{1,0:T(8,128)(2,1)S(1)} %fusion.5), channel_id=1, source_target_pairs={{0,64},{32,96},{64,128},{96,160},{128,192},{160,224},{192,256},{22... | collective-permute-start | bytes 442376 | tf_op jit(solution)/shard_map/ppermute | solution.py:16
  85.0 4.0 %collective-permute-start.12 = (bf16[192,384]{1,0:T(8,128)(2,1)S(1)}, bf16[192,384]{1,0:T(8,128)(2,1)S(1)}, u32[]{:S(2)}, u32[]{:S(2)}) collective-permute-start(bf16[192,384]{1,0:T(8,128)(2,1)S(1)} %fusion.5), channel_id=1, source_target_pairs={{0,32},{32,64},{64,96},{96,128},{128,160},{160,192},{192,224},{224... | collective-permute-start | bytes 442376 | tf_op jit(solution)/shard_map/ppermute | solution.py:16
  89.4 3.4 %collective-permute-done.11 = bf16[192,384]{1,0:T(8,128)(2,1)S(1)} collective-permute-done((bf16[192,384]{1,0:T(8,128)(2,1)S(1)}, bf16[192,384]{1,0:T(8,128)(2,1)S(1)}, u32[]{:S(2)}, u32[]{:S(2)}) %collective-permute-start.11) | collective-permute-done | bytes 147488 | tf_op jit(solution)/shard_map/ppermute | solution.py:16
  92.8 2.2 %collective-permute-done.12 = bf16[192,384]{1,0:T(8,128)(2,1)S(1)} collective-permute-done((bf16[192,384]{1,0:T(8,128)(2,1)S(1)}, bf16[192,384]{1,0:T(8,128)(2,1)S(1)}, u32[]{:S(2)}, u32[]{:S(2)}) %collective-permute-start.12) | collective-permute-done | bytes 147488 | tf_op jit(solution)/shard_map/ppermute | solution.py:16
  95.9 10.0 %collective-permute-start.14 = (bf16[2,1,96,384]{3,2,1,0:T(8,128)(2,1)S(1)}, bf16[2,1,96,384]{3,2,1,0:T(8,128)(2,1)S(1)}, u32[]{:S(2)}, u32[]{:S(2)}) collective-permute-start(bf16[2,1,96,384]{3,2,1,0:T(8,128)(2,1)S(1)} %get-tuple-element.27), channel_id=1, source_target_pairs={{1,0},{2,1},{3,2},{4,3},{5,4},{6,5},{7,6},{8,7},{9,8},{10,9},{11,1... | collective-permute-start | bytes 442376 | tf_op jit(solution)/shard_map/ppermute | solution.py:27
  105.9 1.9 %collective-permute-start.13 = (bf16[2,1,96,384]{3,2,1,0:T(8,128)(2,1)S(1)}, bf16[2,1,96,384]{3,2,1,0:T(8,128)(2,1)S(1)}, u32[]{:S(2)}, u32[]{:S(2)}) collective-permute-start(bf16[2,1,96,384]{3,2,1,0:T(8,128)(2,1)S(1)} %get-tuple-element.26), channel_id=1, source_target_pairs={{0,1},{1,2},{2,3},{3,4},{4,5},{5,6},{6,7},{7,8},{8,9},{9,10},{10,1... | collective-permute-start | bytes 442376 | tf_op jit(solution)/shard_map/ppermute | solution.py:24
  107.8 1.1 fusion.43
  108.9 2.8 %collective-permute-done.14 = bf16[2,1,96,384]{3,2,1,0:T(8,128)(2,1)S(1)} collective-permute-done((bf16[2,1,96,384]{3,2,1,0:T(8,128)(2,1)S(1)}, bf16[2,1,96,384]{3,2,1,0:T(8,128)(2,1)S(1)}, u32[]{:S(2)}, u32[]{:S(2)}) %collective-permute-start.14) | collective-permute-done | bytes 147488 | tf_op jit(solution)/shard_map/ppermute | solution.py:27
  111.8 0.5 fusion.46
  112.2 7.6 %collective-permute-done.13 = bf16[2,1,96,384]{3,2,1,0:T(8,128)(2,1)S(1)} collective-permute-done((bf16[2,1,96,384]{3,2,1,0:T(8,128)(2,1)S(1)}, bf16[2,1,96,384]{3,2,1,0:T(8,128)(2,1)S(1)}, u32[]{:S(2)}, u32[]{:S(2)}) %collective-permute-start.13) | collective-permute-done | bytes 147488 | tf_op jit(solution)/shard_map/ppermute | solution.py:24
  119.8 0.5 fusion.50
  120.7 0.4 fusion.55
  121.4 0.8 copy.40
  122.2 1.0 copy.41
  (67 shorter events, 2.7 us)
Async XLA Ops:
  0.0 82.4 %copy-start = (bf16[384,384]{1,0:T(8,128)(2,1)S(1)}, bf16[384,384]{1,0:T(8,128)(2,1)}, u32[]{:S(2)}) copy-start(bf16[384,384]{1,0:T(8,128)(2,1)} %param.16) | copy-start | bytes 884740
  0.0 14.4 %copy-start.1 = (bf16[1,2,96,384]{3,2,1,0:T(8,128)(2,1)S(1)}, bf16[1,2,96,384]{3,2,1,0:T(8,128)(2,1)}, u32[]{:S(2)}) copy-start(bf16[1,2,96,384]{3,2,1,0:T(8,128)(2,1)} %param.11) | copy-start | bytes 442372
  0.0 15.1 %copy-start.3 = (bf16[3,3,384,192]{2,3,1,0:T(8,128)(2,1)S(1)}, bf16[3,3,384,192]{2,3,1,0:T(8,128)(2,1)}, u32[]{:S(2)}) copy-start(bf16[3,3,384,192]{2,3,1,0:T(8,128)(2,1)} %param.20) | copy-start | bytes 3981316
  0.0 15.2 %collective-permute-start = (bf16[192,384]{1,0:T(8,128)(2,1)}, bf16[192,384]{1,0:T(8,128)(2,1)S(1)}, u32[]{:S(2)}, u32[]{:S(2)}) collective-permute-start(bf16[192,384]{1,0:T(8,128)(2,1)} %bitcast.212), channel_id=1, source_target_pairs={{0,2},{1,3},{2,0},{3,1},{4,6},{5,7},{6,4},{7,5},{8,10},{9,11},{10,... | collective-permute-start | bytes 442376 | tf_op jit(solution)/shard_map/ppermute | solution.py:37
  10.5 11.8 %copy-start.11 = (bf16[2,2,96,384]{3,2,1,0:T(8,128)(2,1)S(1)}, bf16[2,2,96,384]{3,2,1,0:T(8,128)(2,1)}, u32[]{:S(2)}) copy-start(bf16[2,2,96,384]{3,2,1,0:T(8,128)(2,1)} %param.12) | copy-start | bytes 884740
  15.2 11.6 %collective-permute-start.1 = (bf16[384,384]{1,0:T(8,128)(2,1)S(1)}, bf16[384,384]{1,0:T(8,128)(2,1)S(1)}, u32[]{:S(2)}, u32[]{:S(2)}) collective-permute-start(bf16[384,384]{1,0:T(8,128)(2,1)S(1)} %pad_maximum_fusion.10), channel_id=1, source_target_pairs={{0,4},{1,5},{2,6},{3,7},{4,8},{5,9},{6,10},{7,11},{8,12},{9,13},{1... | collective-permute-start | bytes 884744 | tf_op jit(solution)/shard_map/ppermute | solution.py:37
  18.6 10.4 %collective-permute-start.2 = (bf16[384,384]{1,0:T(8,128)(2,1)S(1)}, bf16[384,384]{1,0:T(8,128)(2,1)S(1)}, u32[]{:S(2)}, u32[]{:S(2)}) collective-permute-start(bf16[384,384]{1,0:T(8,128)(2,1)S(1)} %pad_maximum_fusion.10), channel_id=1, source_target_pairs={{0,28},{1,29},{2,30},{3,31},{4,0},{5,1},{6,2},{7,3},{8,4},{9,5},{1... | collective-permute-start | bytes 884744 | tf_op jit(solution)/shard_map/ppermute | solution.py:37
  26.8 10.7 %collective-permute-start.4 = (bf16[384,384]{1,0:T(8,128)(2,1)S(1)}, bf16[384,384]{1,0:T(8,128)(2,1)S(1)}, u32[]{:S(2)}, u32[]{:S(2)}) collective-permute-start(bf16[384,384]{1,0:T(8,128)(2,1)S(1)} %collective-permute-done.1), channel_id=1, source_target_pairs={{0,4},{1,5},{2,6},{3,7},{4,8},{5,9},{6,10},{7,11},{8,12},{9,13},{1... | collective-permute-start | bytes 884744 | tf_op jit(solution)/shard_map/ppermute | solution.py:37
  29.0 10.4 %collective-permute-start.5 = (bf16[384,384]{1,0:T(8,128)(2,1)S(1)}, bf16[384,384]{1,0:T(8,128)(2,1)S(1)}, u32[]{:S(2)}, u32[]{:S(2)}) collective-permute-start(bf16[384,384]{1,0:T(8,128)(2,1)S(1)} %collective-permute-done.2), channel_id=1, source_target_pairs={{0,28},{1,29},{2,30},{3,31},{4,0},{5,1},{6,2},{7,3},{8,4},{9,5},{1... | collective-permute-start | bytes 884744 | tf_op jit(solution)/shard_map/ppermute | solution.py:37
  37.5 9.8 %collective-permute-start.6 = (bf16[384,384]{1,0:T(8,128)(2,1)S(1)}, bf16[384,384]{1,0:T(8,128)(2,1)S(1)}, u32[]{:S(2)}, u32[]{:S(2)}) collective-permute-start(bf16[384,384]{1,0:T(8,128)(2,1)S(1)} %collective-permute-done.4), channel_id=1, source_target_pairs={{0,4},{1,5},{2,6},{3,7},{4,8},{5,9},{6,10},{7,11},{8,12},{9,13},{1... | collective-permute-start | bytes 884744 | tf_op jit(solution)/shard_map/ppermute | solution.py:37
  39.4 9.9 %collective-permute-start.7 = (bf16[384,384]{1,0:T(8,128)(2,1)S(1)}, bf16[384,384]{1,0:T(8,128)(2,1)S(1)}, u32[]{:S(2)}, u32[]{:S(2)}) collective-permute-start(bf16[384,384]{1,0:T(8,128)(2,1)S(1)} %collective-permute-done.5), channel_id=1, source_target_pairs={{0,28},{1,29},{2,30},{3,31},{4,0},{5,1},{6,2},{7,3},{8,4},{9,5},{1... | collective-permute-start | bytes 884744 | tf_op jit(solution)/shard_map/ppermute | solution.py:37
  44.6 10.0 %copy-start.6 = (bf16[384,1728]{0,1:T(8,128)(2,1)}, bf16[384,1728]{0,1:T(8,128)(2,1)S(1)}, u32[]{:S(2)}) copy-start(bf16[384,1728]{0,1:T(8,128)(2,1)S(1)} %constant_dynamic-update-slice_fusion.6) | copy-start | bytes 3981316
  44.7 14.4 %copy-start.13 = (bf16[1152]{0:T(1024)(128)(2,1)S(1)}, bf16[1152]{0:T(1024)(128)(2,1)}, u32[]{:S(2)}) copy-start(bf16[1152]{0:T(1024)(128)(2,1)} %param.15) | copy-start | bytes 6916
  47.4 8.2 %collective-permute-start.8 = (bf16[192,384]{1,0:T(8,128)(2,1)S(1)}, bf16[192,384]{1,0:T(8,128)(2,1)S(1)}, u32[]{:S(2)}, u32[]{:S(2)}) collective-permute-start(bf16[192,384]{1,0:T(8,128)(2,1)S(1)} %slice.203), channel_id=1, source_target_pairs={{0,4},{1,5},{2,6},{3,7},{4,8},{5,9},{6,10},{7,11},{8,12},{9,13},{1... | collective-permute-start | bytes 442376 | tf_op jit(solution)/shard_map/ppermute | solution.py:37
  49.3 7.8 %collective-permute-start.9 = (bf16[192,384]{1,0:T(8,128)(2,1)S(1)}, bf16[192,384]{1,0:T(8,128)(2,1)S(1)}, u32[]{:S(2)}, u32[]{:S(2)}) collective-permute-start(bf16[192,384]{1,0:T(8,128)(2,1)S(1)} %slice.204), channel_id=1, source_target_pairs={{0,28},{1,29},{2,30},{3,31},{4,0},{5,1},{6,2},{7,3},{8,4},{9,5},{1... | collective-permute-start | bytes 442376 | tf_op jit(solution)/shard_map/ppermute | solution.py:37
  57.2 16.1 %collective-permute-start.10 = (bf16[1920,384]{1,0:T(8,128)(2,1)S(1)}, bf16[1920,384]{1,0:T(8,128)(2,1)}, u32[]{:S(2)}, u32[]{:S(2)}) collective-permute-start(bf16[1920,384]{1,0:T(8,128)(2,1)S(1)} %constant_dynamic-update-slice_fusion.refs_7_), channel_id=1, source_target_pairs={{0,1},{1,0},{2,3},{3,2},{4,5},{5,4},{6,7},{7,6},{8,9},{9,8},{10,11... | collective-permute-start | bytes 4423688 | tf_op jit(solution)/shard_map/ppermute | solution.py:37
  59.7 3.3 %copy-start.12 = (bf16[384]{0:T(512)(128)(2,1)S(1)}, bf16[384]{0:T(512)(128)(2,1)}, u32[]{:S(2)}) copy-start(bf16[384]{0:T(512)(128)(2,1)} %param.13) | copy-start | bytes 2308
  59.7 3.3 %copy-start.14 = (bf16[384]{0:T(512)(128)(2,1)S(1)}, bf16[384]{0:T(512)(128)(2,1)}, u32[]{:S(2)}) copy-start(bf16[384]{0:T(512)(128)(2,1)} %param.17) | copy-start | bytes 2308
  59.8 13.4 %collective-permute-start.3 = (bf16[1152,384]{1,0:T(8,128)(2,1)S(1)}, bf16[1152,384]{1,0:T(8,128)(2,1)S(1)}, u32[]{:S(2)}, u32[]{:S(2)}) collective-permute-start(bf16[1152,384]{1,0:T(8,128)(2,1)S(1)} %pad_maximum_fusion.refs_6_), channel_id=1, source_target_pairs={{0,1},{1,0},{2,3},{3,2},{4,5},{5,4},{6,7},{7,6},{8,9},{9,8},{10,11... | collective-permute-start | bytes 2654216 | tf_op jit(solution)/shard_map/ppermute | solution.py:37
  63.0 3.8 %copy-start.10 = (bf16[384,1152]{1,0:T(8,128)(2,1)S(1)}, bf16[384,1152]{1,0:T(8,128)(2,1)}, u32[]{:S(2)}) copy-start(bf16[384,1152]{1,0:T(8,128)(2,1)} %param.14) | copy-start | bytes 2654212
  73.2 9.2 %copy-start.2 = (bf16[1,2,96,384]{3,2,1,0:T(8,128)(2,1)S(1)}, bf16[1,2,96,384]{3,2,1,0:T(8,128)(2,1)}, u32[]{:S(2)}) copy-start(bf16[1,2,96,384]{3,2,1,0:T(8,128)(2,1)} %param.11) | copy-start | bytes 442372
  73.2 15.8 %copy-start.4 = (bf16[3,384,768]{2,1,0:T(8,128)(2,1)S(1)}, bf16[3,384,768]{2,1,0:T(8,128)(2,1)}, u32[]{:S(2)}) copy-start(bf16[3,384,768]{2,1,0:T(8,128)(2,1)} %param.18) | copy-start | bytes 5308420
  82.4 12.6 %copy-start.8 = (bf16[1,2,96,384]{3,2,1,0:T(8,128)(2,1)S(1)}, bf16[1,2,96,384]{3,2,1,0:T(8,128)(2,1)}, u32[]{:S(2)}) copy-start(bf16[1,2,96,384]{3,2,1,0:T(8,128)(2,1)} %get-tuple-element.30) | copy-start | bytes 442372
  82.5 12.6 %copy-start.9 = (bf16[1,2,96,384]{3,2,1,0:T(8,128)(2,1)S(1)}, bf16[1,2,96,384]{3,2,1,0:T(8,128)(2,1)}, u32[]{:S(2)}) copy-start(bf16[1,2,96,384]{3,2,1,0:T(8,128)(2,1)} %get-tuple-element.31) | copy-start | bytes 442372
  82.7 10.1 %collective-permute-start.11 = (bf16[192,384]{1,0:T(8,128)(2,1)S(1)}, bf16[192,384]{1,0:T(8,128)(2,1)S(1)}, u32[]{:S(2)}, u32[]{:S(2)}) collective-permute-start(bf16[192,384]{1,0:T(8,128)(2,1)S(1)} %fusion.5), channel_id=1, source_target_pairs={{0,64},{32,96},{64,128},{96,160},{128,192},{160,224},{192,256},{22... | collective-permute-start | bytes 442376 | tf_op jit(solution)/shard_map/ppermute | solution.py:16
  85.0 10.0 %collective-permute-start.12 = (bf16[192,384]{1,0:T(8,128)(2,1)S(1)}, bf16[192,384]{1,0:T(8,128)(2,1)S(1)}, u32[]{:S(2)}, u32[]{:S(2)}) collective-permute-start(bf16[192,384]{1,0:T(8,128)(2,1)S(1)} %fusion.5), channel_id=1, source_target_pairs={{0,32},{32,64},{64,96},{96,128},{128,160},{160,192},{192,224},{224... | collective-permute-start | bytes 442376 | tf_op jit(solution)/shard_map/ppermute | solution.py:16
  95.5 12.3 %copy-start.7 = (bf16[384,1728]{0,1:T(8,128)(2,1)S(1)}, bf16[384,1728]{0,1:T(8,128)(2,1)}, u32[]{:S(2)}) copy-start(bf16[384,1728]{0,1:T(8,128)(2,1)} %copy-done.6) | copy-start | bytes 3981316
  95.9 15.9 %collective-permute-start.14 = (bf16[2,1,96,384]{3,2,1,0:T(8,128)(2,1)S(1)}, bf16[2,1,96,384]{3,2,1,0:T(8,128)(2,1)S(1)}, u32[]{:S(2)}, u32[]{:S(2)}) collective-permute-start(bf16[2,1,96,384]{3,2,1,0:T(8,128)(2,1)S(1)} %get-tuple-element.27), channel_id=1, source_target_pairs={{1,0},{2,1},{3,2},{4,3},{5,4},{6,5},{7,6},{8,7},{9,8},{10,9},{11,1... | collective-permute-start | bytes 442376 | tf_op jit(solution)/shard_map/ppermute | solution.py:27
  105.9 14.0 %collective-permute-start.13 = (bf16[2,1,96,384]{3,2,1,0:T(8,128)(2,1)S(1)}, bf16[2,1,96,384]{3,2,1,0:T(8,128)(2,1)S(1)}, u32[]{:S(2)}, u32[]{:S(2)}) collective-permute-start(bf16[2,1,96,384]{3,2,1,0:T(8,128)(2,1)S(1)} %get-tuple-element.26), channel_id=1, source_target_pairs={{0,1},{1,2},{2,3},{3,4},{4,5},{5,6},{6,7},{7,8},{8,9},{9,10},{10,1... | collective-permute-start | bytes 442376 | tf_op jit(solution)/shard_map/ppermute | solution.py:24
  107.8 3.9 %copy-start.5 = (bf16[384,576]{0,1:T(8,128)(2,1)S(1)}, bf16[384,576]{0,1:T(8,128)(2,1)}, u32[]{:S(2)}) copy-start(bf16[384,576]{0,1:T(8,128)(2,1)} %pad_maximum_fusion.2) | copy-start | bytes 1327108

commit v8 on v7

--- a/solution.py
+++ b/solution.py
@@ -29,7 +29,7 @@
     return block
 
 
-def gather_space(block):
+def gather_space(block, riders):
     count = lax.axis_size("space")
     rings = count // 4
 
@@ -45,6 +45,8 @@
     for step in range(rings // 2 - 1):
         ahead = moved(ahead, forward)
         behind = moved(behind, backward)
+        if step == 0:
+            ahead, behind, riders = lax.optimization_barrier((ahead, behind, riders))
         batches[-1] += [ahead, behind]
         if step == 0:
             batches.append([])
@@ -53,7 +55,7 @@
     batches[-1].append(moved(behind[half:], backward))
     mine = [jnp.concatenate(batch, axis=0) for batch in batches]
     other = [moved(chunk, lambda s: s ^ 1) for chunk in mine]
-    return mine + other
+    return mine + other, riders
 
 
 def normalize(frames, norm_gain):
@@ -82,19 +84,17 @@
     )
     return (new_best, mass, total_sum)
 
-BLOCK = 384
+BLOCK = 768
 
 
 def attention_kernel(*refs, sizes, channels, resume, finish):
-    q_ref, gain_ref, wk_ref, bk_ref, wv_ref, bv_ref = refs[:6]
-    chunk_refs = refs[6:6 + len(sizes)]
-    rest = refs[6 + len(sizes):]
+    q_ref, gain_ref, wkv_ref, bkv_ref = refs[:4]
+    chunk_refs = refs[4:4 + len(sizes)]
+    rest = refs[4 + len(sizes):]
     queries = q_ref[...]
     gain = gain_ref[...]
-    wk = wk_ref[...]
-    wv = wv_ref[...]
-    bk = bk_ref[...]
-    bv = bv_ref[...]
+    wkv = wkv_ref[...]
+    bkv = bkv_ref[...]
     count = queries.shape[0]
     if resume:
         best, mass, total = rest[0][...], rest[1][...], rest[2][...]
@@ -105,11 +105,12 @@
         total = jnp.zeros((count, channels), jnp.float32)
     for chunk_ref, size in zip(chunk_refs, sizes):
         for start in range(0, size, BLOCK):
-            rows = chunk_ref[start:start + BLOCK, :].astype(jnp.float32)
+            rows = chunk_ref[start:min(start + BLOCK, size), :].astype(jnp.float32)
             inverse = lax.rsqrt(jnp.mean(rows * rows, axis=-1, keepdims=True) + EPSILON)
             normed = (rows * inverse * gain).astype(jnp.bfloat16)
-            keys = (jnp.dot(normed, wk, preferred_element_type=jnp.float32) + bk).astype(jnp.bfloat16)
-            values = (jnp.dot(normed, wv, preferred_element_type=jnp.float32) + bv).astype(jnp.bfloat16)
+            both = (jnp.dot(normed, wkv, preferred_element_type=jnp.float32) + bkv).astype(jnp.bfloat16)
+            keys = both[:, :channels]
+            values = both[:, channels:]
             scores = lax.dot_general(
                 queries, keys, (((1,), (1,)), ((), ())), preferred_element_type=jnp.float32
             ) * channels ** (-0.5)
@@ -129,15 +130,19 @@
         rest[2][...] = total
 
 
-def fused_attention(queries, chunks, norm_gain, w_qkv, b_qkv, state=None, finish=True):
+def attention_weights(norm_gain, w_qkv, b_qkv):
+    channels = w_qkv.shape[0]
+    gain = norm_gain.astype(jnp.float32).reshape(1, channels)
+    wkv = w_qkv[:, channels:]
+    bkv = b_qkv[channels:].astype(jnp.float32).reshape(1, 2 * channels)
+    return gain, wkv, bkv
+
+
+def fused_attention(queries, chunks, weights, state=None, finish=True):
     channels = queries.shape[1]
     count = queries.shape[0]
     sizes = tuple(c.shape[0] for c in chunks)
-    gain = norm_gain.astype(jnp.float32).reshape(1, channels)
-    wk = w_qkv[:, channels:2 * channels]
-    wv = w_qkv[:, 2 * channels:]
-    bk = b_qkv[channels:2 * channels].astype(jnp.float32).reshape(1, channels)
-    bv = b_qkv[2 * channels:].astype(jnp.float32).reshape(1, channels)
+    gain, wkv, bkv = weights
     spec = pl.BlockSpec(memory_space=pltpu.MemorySpace.VMEM)
     total_rows = sum(sizes)
     flops = 2 * total_rows * channels * (2 * channels + 2 * count)
@@ -157,7 +162,7 @@
             attention_kernel, sizes=sizes, channels=channels, resume=state is not None, finish=finish
         ),
         out_shape=out_shape,
-        in_specs=[spec] * (6 + len(chunks) + len(extra)),
+        in_specs=[spec] * (4 + len(chunks) + len(extra)),
         out_specs=out_specs,
         compiler_params=pltpu.CompilerParams(vmem_limit_bytes=48 * 1024 * 1024),
         cost_estimate=pl.CostEstimate(
@@ -165,7 +170,7 @@
             transcendentals=total_rows * count,
             bytes_accessed=2 * total_rows * channels + 4 * channels * channels + 4 * queries.size,
         ),
-    )(queries, gain, wk, bk, wv, bv, *chunks, *extra)
+    )(queries, gain, wkv, bkv, *chunks, *extra)
 
 
 def body(
@@ -174,16 +179,33 @@
     channels = frames.shape[-1]
     rows = frames.shape[1]
     width = frames.shape[2]
-    chunks = gather_space(frames.reshape(-1, channels))
+    out_channels = w_space.shape[-1]
+    row_source = ((0, 1, 1), (1, 1, 2))
+    tap_lists = [
+        sorted({row_tap for parity in row_source for row_tap in range(3) if parity[row_tap] == offset})
+        for offset in range(3)
+    ]
     normed = normalize(frames, norm_gain).reshape(-1, channels)
-    queries = project(normed, w_qkv[:, :channels], b_qkv[:channels])
+    riders = dict(
+        queries=project(normed, w_qkv[:, :channels], b_qkv[:channels]),
+        weights=attention_weights(norm_gain, w_qkv, b_qkv),
+        conv=[
+            jnp.concatenate([w_space[row_tap, col_tap] for row_tap in taps for col_tap in range(3)], axis=1)
+            for taps in tap_lists
+        ],
+        b_proj=b_proj.astype(jnp.float32),
+        b_time=b_time.astype(jnp.float32),
+        b_space=b_space.astype(jnp.float32),
+    )
+    chunks, riders = gather_space(frames.reshape(-1, channels), riders)
+    queries = riders["queries"]
     half = len(chunks) // 2
-    state = fused_attention(queries, chunks[:half], norm_gain, w_qkv, b_qkv, finish=False)
-    mixed = fused_attention(queries, chunks[half:], norm_gain, w_qkv, b_qkv, state=state)
+    state = fused_attention(queries, chunks[:half], riders["weights"], finish=False)
+    mixed = fused_attention(queries, chunks[half:], riders["weights"], state=state)
     hidden = (
         frames.reshape(-1, channels).astype(jnp.float32)
         + jnp.dot(mixed, w_proj, preferred_element_type=jnp.float32)
-        + b_proj.astype(jnp.float32)
+        + riders["b_proj"]
     ).astype(jnp.bfloat16)
     position = lax.axis_index("tm")
     carried = cache_in.reshape(2, -1, channels)
@@ -192,7 +214,7 @@
     far_frame = shifted(hidden, "tm", 2)
     far_frame = jnp.where(position == 1, carried[1], far_frame)
     far_frame = jnp.where(position == 0, carried[0], far_frame)
-    timed = b_time.astype(jnp.float32) + jnp.dot(
+    timed = riders["b_time"] + jnp.dot(
         far_frame, w_time[0], preferred_element_type=jnp.float32
     )
     timed = timed + jnp.dot(near_frame, w_time[1], preferred_element_type=jnp.float32)
@@ -201,14 +223,11 @@
     )
     paired = jnp.stack([timed[:, :channels], timed[:, channels:]]).reshape(2, rows, width, channels)
     padded = with_halo(paired, (("space", 1),), 1)
-    out_channels = w_space.shape[-1]
-    row_source = ((0, 1, 1), (1, 1, 2))
     products = {}
     for offset in range(3):
-        taps = sorted({row_tap for parity in row_source for row_tap in range(3) if parity[row_tap] == offset})
+        taps = tap_lists[offset]
         lhs = padded[:, offset : offset + rows].reshape(-1, channels)
-        rhs = jnp.concatenate([w_space[row_tap, col_tap] for row_tap in taps for col_tap in range(3)], axis=1)
-        both = jnp.dot(lhs, rhs, preferred_element_type=jnp.float32)
+        both = jnp.dot(lhs, riders["conv"][offset], preferred_element_type=jnp.float32)
         both = both.reshape(2, rows, width, len(taps) * 3, out_channels)
         for index, row_tap in enumerate(taps):
             for col_tap in range(3):
@@ -219,7 +238,7 @@
             return jnp.pad(value, ((0, 0), (0, 0), (1, 0), (0, 0)))[:, :, :width]
         return jnp.pad(value, ((0, 0), (0, 0), (0, 1), (0, 0)))[:, :, 1:]
 
-    bias = b_space.astype(jnp.float32)
+    bias = riders["b_space"]
     rows_out = []
     for parity in row_source:
         taps = [sum(products[parity[row_tap], row_tap, col_tap] for row_tap in range(3)) for col_tap in range(3)]

time: 124 us -> 119 us (0.960)
  starting transfers between devices: 58.6 us -> 66.3 us
  other arithmetic: 7.7 us -> 3.13 us
  local copies, waits for them, and re-layouts: 8.59 us -> 5.05 us
  Pallas kernels: 15.5 us -> 13.2 us
    ppermute x2, starting transfers between devices: 6.32 us -> 10.9 us  [shifted(): lax.ppermute(value, axis, [(source, source + steps) for source in range(l...]
    unnamed x43, local copies, waits for them, and re-layouts: 5.07 us -> 0.74 us
    ppermute x1, starting transfers between devices: 9.99 us -> 12.7 us  [with_halo(): lax.ppermute(lax.slice_in_dim(block, 0, width, axis=dim), axis, backward)]
    ppermute x2, waiting for transfers between devices: 5.66 us -> 3.03 us  [shifted(): lax.ppermute(value, axis, [(source, source + steps) for source in range(l...]
    ppermute x11, waiting for transfers between devices: 11.7 us -> 13.9 us  [moved(): return lax.ppermute(value, 'space', [(s, target(s)) for s in range(count)])]
    pallas_call x2, Pallas kernels: 15.5 us -> 13.2 us  [fused_attention(): pl.pallas_call(functools.partial(attention_kernel, sizes=sizes, channels=...]
  transfers between devices with their start and end apart: 15 -> 15, of which waited for: 9 -> 10; matrix products, arithmetic and copies ran while one was open for 13% -> 6% of each run, Pallas kernels for 5% -> 5%
where the time goes in v8:
time: 119 us
  starting transfers between devices  66.3 us (56%)
  waiting for transfers between devices  26.8 us (23%)
  Pallas kernels  13.2 us (11%)
  local copies, waits for them, and re-layouts  5.05 us (4%)
  matrix products  3.48 us (3%)
  other arithmetic  3.13 us (3%)
    ppermute x11, starting transfers between devices, moved(): return lax.ppermute(value, 'space', [(s, target(s)) for s in range(count)])  40.6 us
    ppermute x11, waiting for transfers between devices, moved(): return lax.ppermute(value, 'space', [(s, target(s)) for s in range(count)])  13.9 us
    pallas_call x2, Pallas kernels, fused_attention(): pl.pallas_call(functools.partial(attention_kernel, sizes=sizes, channels=...  13.2 us
    ppermute x1, starting transfers between devices, with_halo(): lax.ppermute(lax.slice_in_dim(block, 0, width, axis=dim), axis, backward)  12.7 us
    ppermute x2, starting transfers between devices, shifted(): lax.ppermute(value, axis, [(source, source + steps) for source in range(l...  10.9 us
    ppermute x1, waiting for transfers between devices, with_halo(): lax.ppermute(lax.slice_in_dim(block, block.shape[dim] - width, None, axis...  7.46 us
    ppermute x2, waiting for transfers between devices, shifted(): lax.ppermute(value, axis, [(source, source + steps) for source in range(l...  3.03 us
    ppermute x1, waiting for transfers between devices, with_halo(): lax.ppermute(lax.slice_in_dim(block, 0, width, axis=dim), axis, backward)  2.4 us
  transfers between devices with their start and end apart: 15, of which 10 were waited for; matrix products, arithmetic and copies ran while one was open for 6% of the time, Pallas kernels for 5%

profile of v8, /device:TPU:260, one launch (start us, length us, event | category | flops | bytes accessed | tf_op | source)
XLA Modules:
  0.0 118.6 jit_solution(1093878368081065189)
XLA Ops:
  0.0 7.9 %collective-permute-start = (bf16[192,384]{1,0:T(8,128)(2,1)}, bf16[192,384]{1,0:T(8,128)(2,1)S(1)}, u32[]{:S(2)}, u32[]{:S(2)}) collective-permute-start(bf16[192,384]{1,0:T(8,128)(2,1)} %bitcast.214), channel_id=1, source_target_pairs={{0,2},{1,3},{2,0},{3,1},{4,6},{5,7},{6,4},{7,5},{8,10},{9,11},{10,... | collective-permute-start | bytes 442376 | tf_op jit(solution)/shard_map/ppermute | solution.py:37
  7.9 1.3 %slice_bitcast_fusion.11 = (bf16[384,192]{0,1:T(8,128)(2,1)S(1)}, bf16[384,192]{0,1:T(8,128)(2,1)S(1)}, bf16[384,192]{0,1:T(8,128)(2,1)S(1)}, bf16[384,192]{0,1:...) fusion(bf16[3,3,384,192]{2,3,1,0:T(8,128)(2,1)} %param.20), kind=kLoop, calls=%fused_computation.100 | loop fusion | bytes 1769472 | tf_op jit(solution)/shard_map/squeeze | solution.py:193
  9.3 0.1 fusion.37
  9.7 0.2 copy-done.10
  10.1 1.9 %collective-permute-done = bf16[192,384]{1,0:T(8,128)(2,1)S(1)} collective-permute-done((bf16[192,384]{1,0:T(8,128)(2,1)}, bf16[192,384]{1,0:T(8,128)(2,1)S(1)}, u32[]{:S(2)}, u32[]{:S(2)}) %collective-permute-start) | collective-permute-done | bytes 147488 | tf_op jit(solution)/shard_map/ppermute | solution.py:37
  12.1 3.4 %collective-permute-start.1 = (bf16[384,384]{1,0:T(8,128)(2,1)S(1)}, bf16[384,384]{1,0:T(8,128)(2,1)S(1)}, u32[]{:S(2)}, u32[]{:S(2)}) collective-permute-start(bf16[384,384]{1,0:T(8,128)(2,1)S(1)} %pad_maximum_fusion.10), channel_id=1, source_target_pairs={{0,4},{1,5},{2,6},{3,7},{4,8},{5,9},{6,10},{7,11},{8,12},{9,13},{1... | collective-permute-start | bytes 884744 | tf_op jit(solution)/shard_map/ppermute | solution.py:37
  15.4 3.7 %collective-permute-start.2 = (bf16[384,384]{1,0:T(8,128)(2,1)S(1)}, bf16[384,384]{1,0:T(8,128)(2,1)S(1)}, u32[]{:S(2)}, u32[]{:S(2)}) collective-permute-start(bf16[384,384]{1,0:T(8,128)(2,1)S(1)} %pad_maximum_fusion.10), channel_id=1, source_target_pairs={{0,28},{1,29},{2,30},{3,31},{4,0},{5,1},{6,2},{7,3},{8,4},{9,5},{1... | collective-permute-start | bytes 884744 | tf_op jit(solution)/shard_map/ppermute | solution.py:37
  19.2 1.0 pad_maximum_fusion.1
  20.3 0.6 convert_element_type.57
  20.9 0.2 fusion.1.refs_0_
  21.1 2.0 %collective-permute-done.1 = bf16[384,384]{1,0:T(8,128)(2,1)S(1)} collective-permute-done((bf16[384,384]{1,0:T(8,128)(2,1)S(1)}, bf16[384,384]{1,0:T(8,128)(2,1)S(1)}, u32[]{:S(2)}, u32[]{:S(2)}) %collective-permute-start.1) | collective-permute-done | bytes 294944 | tf_op jit(solution)/shard_map/ppermute | solution.py:37
  23.1 1.9 %collective-permute-done.2 = bf16[384,384]{1,0:T(8,128)(2,1)S(1)} collective-permute-done((bf16[384,384]{1,0:T(8,128)(2,1)S(1)}, bf16[384,384]{1,0:T(8,128)(2,1)S(1)}, u32[]{:S(2)}, u32[]{:S(2)}) %collective-permute-start.2) | collective-permute-done | bytes 294944 | tf_op jit(solution)/shard_map/ppermute | solution.py:37
  25.0 3.4 %collective-permute-start.4 = (bf16[384,384]{1,0:T(8,128)(2,1)S(1)}, bf16[384,384]{1,0:T(8,128)(2,1)S(1)}, u32[]{:S(2)}, u32[]{:S(2)}) collective-permute-start(bf16[384,384]{1,0:T(8,128)(2,1)S(1)} %collective-permute-done.1), channel_id=1, source_target_pairs={{0,4},{1,5},{2,6},{3,7},{4,8},{5,9},{6,10},{7,11},{8,12},{9,13},{1... | collective-permute-start | bytes 884744 | tf_op jit(solution)/shard_map/ppermute | solution.py:37
  28.4 3.7 %collective-permute-start.5 = (bf16[384,384]{1,0:T(8,128)(2,1)S(1)}, bf16[384,384]{1,0:T(8,128)(2,1)S(1)}, u32[]{:S(2)}, u32[]{:S(2)}) collective-permute-start(bf16[384,384]{1,0:T(8,128)(2,1)S(1)} %collective-permute-done.2), channel_id=1, source_target_pairs={{0,28},{1,29},{2,30},{3,31},{4,0},{5,1},{6,2},{7,3},{8,4},{9,5},{1... | collective-permute-start | bytes 884744 | tf_op jit(solution)/shard_map/ppermute | solution.py:37
  32.1 2.9 %collective-permute-done.4 = bf16[384,384]{1,0:T(8,128)(2,1)S(1)} collective-permute-done((bf16[384,384]{1,0:T(8,128)(2,1)S(1)}, bf16[384,384]{1,0:T(8,128)(2,1)S(1)}, u32[]{:S(2)}, u32[]{:S(2)}) %collective-permute-start.4) | collective-permute-done | bytes 294944 | tf_op jit(solution)/shard_map/ppermute | solution.py:37
  35.0 2.1 %collective-permute-start.6 = (bf16[384,384]{1,0:T(8,128)(2,1)S(1)}, bf16[384,384]{1,0:T(8,128)(2,1)S(1)}, u32[]{:S(2)}, u32[]{:S(2)}) collective-permute-start(bf16[384,384]{1,0:T(8,128)(2,1)S(1)} %collective-permute-done.4), channel_id=1, source_target_pairs={{0,4},{1,5},{2,6},{3,7},{4,8},{5,9},{6,10},{7,11},{8,12},{9,13},{1... | collective-permute-start | bytes 884744 | tf_op jit(solution)/shard_map/ppermute | solution.py:37
  37.1 4.9 %collective-permute-start.7 = (bf16[384,384]{1,0:T(8,128)(2,1)S(1)}, bf16[384,384]{1,0:T(8,128)(2,1)S(1)}, u32[]{:S(2)}, u32[]{:S(2)}) collective-permute-start(bf16[384,384]{1,0:T(8,128)(2,1)S(1)} %collective-permute-done.5), channel_id=1, source_target_pairs={{0,28},{1,29},{2,30},{3,31},{4,0},{5,1},{6,2},{7,3},{8,4},{9,5},{1... | collective-permute-start | bytes 884744 | tf_op jit(solution)/shard_map/ppermute | solution.py:37
  42.2 2.7 %collective-permute-done.6 = bf16[384,384]{1,0:T(8,128)(2,1)S(1)} collective-permute-done((bf16[384,384]{1,0:T(8,128)(2,1)S(1)}, bf16[384,384]{1,0:T(8,128)(2,1)S(1)}, u32[]{:S(2)}, u32[]{:S(2)}) %collective-permute-start.6) | collective-permute-done | bytes 294944 | tf_op jit(solution)/shard_map/ppermute | solution.py:37
  44.8 1.9 %collective-permute-start.8 = (bf16[192,384]{1,0:T(8,128)(2,1)S(1)}, bf16[192,384]{1,0:T(8,128)(2,1)S(1)}, u32[]{:S(2)}, u32[]{:S(2)}) collective-permute-start(bf16[192,384]{1,0:T(8,128)(2,1)S(1)} %slice.191), channel_id=1, source_target_pairs={{0,4},{1,5},{2,6},{3,7},{4,8},{5,9},{6,10},{7,11},{8,12},{9,13},{1... | collective-permute-start | bytes 442376 | tf_op jit(solution)/shard_map/ppermute | solution.py:37
  46.8 5.1 %collective-permute-start.9 = (bf16[192,384]{1,0:T(8,128)(2,1)S(1)}, bf16[192,384]{1,0:T(8,128)(2,1)S(1)}, u32[]{:S(2)}, u32[]{:S(2)}) collective-permute-start(bf16[192,384]{1,0:T(8,128)(2,1)S(1)} %slice.192), channel_id=1, source_target_pairs={{0,28},{1,29},{2,30},{3,31},{4,0},{5,1},{6,2},{7,3},{8,4},{9,5},{1... | collective-permute-start | bytes 442376 | tf_op jit(solution)/shard_map/ppermute | solution.py:37
  52.1 1.0 collective-permute-done.8
  53.1 1.5 %collective-permute-done.9 = bf16[192,384]{1,0:T(8,128)(2,1)S(1)} collective-permute-done((bf16[192,384]{1,0:T(8,128)(2,1)S(1)}, bf16[192,384]{1,0:T(8,128)(2,1)S(1)}, u32[]{:S(2)}, u32[]{:S(2)}) %collective-permute-start.9) | collective-permute-done | bytes 147488 | tf_op jit(solution)/shard_map/ppermute | solution.py:37
  54.6 1.9 %collective-permute-start.10 = (bf16[1920,384]{1,0:T(8,128)(2,1)S(1)}, bf16[1920,384]{1,0:T(8,128)(2,1)}, u32[]{:S(2)}, u32[]{:S(2)}) collective-permute-start(bf16[1920,384]{1,0:T(8,128)(2,1)S(1)} %constant_dynamic-update-slice_fusion.6.refs_5_), channel_id=1, source_target_pairs={{0,1},{1,0},{2,3},{3,2},{4,5},{5,4},{6,7},{7,6},{8,9},{9,8},{10,11... | collective-permute-start | bytes 4423688 | tf_op jit(solution)/shard_map/ppermute | solution.py:37
  56.7 2.6 %collective-permute-start.3 = (bf16[1152,384]{1,0:T(8,128)(2,1)S(1)}, bf16[1152,384]{1,0:T(8,128)(2,1)}, u32[]{:S(2)}, u32[]{:S(2)}) collective-permute-start(bf16[1152,384]{1,0:T(8,128)(2,1)S(1)} %pad_maximum_fusion.refs_4_), channel_id=1, source_target_pairs={{0,1},{1,0},{2,3},{3,2},{4,5},{5,4},{6,7},{7,6},{8,9},{9,8},{10,11... | collective-permute-start | bytes 2654216 | tf_op jit(solution)/shard_map/ppermute | solution.py:37
  59.3 1.0 fusion.65
  60.3 5.4 %shard_map.109 = (f32[192,1]{1,0:T(8,128)S(1)}, f32[192,1]{1,0:T(8,128)S(1)}, f32[192,384]{1,0:T(8,128)S(1)}) custom-call(bf16[192,384]{1,0:T(8,128)(2,1)S(1)} %fusion.1.refs_0_, f32[1,384]{1,0:T(1,128)S(1)} %reshape.147.refs_1_, bf16[384,768]{1,0:T(8,128)(2,1)S(1)} %slice.157.refs_2_, f32[1,768]{1,0:T(1,128)S(1)} %reshape.152.refs_3_, ...), custom_call_target="tpu_custom_call" | custom-call | flops 2717908992 | bytes 3244032 | tf_op jit(solution)/shard_map/pallas_call | solution.py:160
  65.8 7.8 %shard_map.110 = bf16[192,384]{1,0:T(8,128)(2,1)S(1)} custom-call(bf16[192,384]{1,0:T(8,128)(2,1)S(1)} %fusion.1.refs_0_, f32[1,384]{1,0:T(1,128)S(1)} %reshape.147.refs_1_, bf16[384,768]{1,0:T(8,128)(2,1)S(1)} %slice.157.refs_2_, f32[1,768]{1,0:T(1,128)S(1)} %reshape.152.refs_3_, bf16[1152,384]{1,0:T(8,128)(2,1)} %collective-permute-done.3.refs_4_, ...), custom_call_target="tpu_custom_call" | custom-call | flops 2717908992 | bytes 3244032 | tf_op jit(solution)/shard_map/pallas_call | solution.py:160
  73.6 0.2 fusion.2
  73.8 6.9 %collective-permute-start.11 = (bf16[192,384]{1,0:T(8,128)(2,1)S(1)}, bf16[192,384]{1,0:T(8,128)(2,1)S(1)}, u32[]{:S(2)}, u32[]{:S(2)}) collective-permute-start(bf16[192,384]{1,0:T(8,128)(2,1)S(1)} %fusion.2), channel_id=1, source_target_pairs={{0,64},{32,96},{64,128},{96,160},{128,192},{160,224},{192,256},{22... | collective-permute-start | bytes 442376 | tf_op jit(solution)/shard_map/ppermute | solution.py:16
  80.7 4.0 %collective-permute-start.12 = (bf16[192,384]{1,0:T(8,128)(2,1)S(1)}, bf16[192,384]{1,0:T(8,128)(2,1)S(1)}, u32[]{:S(2)}, u32[]{:S(2)}) collective-permute-start(bf16[192,384]{1,0:T(8,128)(2,1)S(1)} %fusion.2), channel_id=1, source_target_pairs={{0,32},{32,64},{64,96},{96,128},{128,160},{160,192},{192,224},{224... | collective-permute-start | bytes 442376 | tf_op jit(solution)/shard_map/ppermute | solution.py:16
  84.7 0.3 fusion.3
  85.0 3.0 %collective-permute-done.12 = bf16[192,384]{1,0:T(8,128)(2,1)S(1)} collective-permute-done((bf16[192,384]{1,0:T(8,128)(2,1)S(1)}, bf16[192,384]{1,0:T(8,128)(2,1)S(1)}, u32[]{:S(2)}, u32[]{:S(2)}) %collective-permute-start.12) | collective-permute-done | bytes 147488 | tf_op jit(solution)/shard_map/ppermute | solution.py:16
  88.2 0.3 fusion.7
  88.5 0.3 add_convert_fusion
  88.9 12.7 %collective-permute-start.14 = (bf16[2,1,96,384]{3,2,1,0:T(8,128)(2,1)S(1)}, bf16[2,1,96,384]{3,2,1,0:T(8,128)(2,1)S(1)}, u32[]{:S(2)}, u32[]{:S(2)}) collective-permute-start(bf16[2,1,96,384]{3,2,1,0:T(8,128)(2,1)S(1)} %get-tuple-element.49), channel_id=1, source_target_pairs={{1,0},{2,1},{3,2},{4,3},{5,4},{6,5},{7,6},{8,7},{9,8},{10,9},{11,1... | collective-permute-start | bytes 442376 | tf_op jit(solution)/shard_map/ppermute | solution.py:27
  101.6 2.1 %collective-permute-start.13 = (bf16[2,1,96,384]{3,2,1,0:T(8,128)(2,1)S(1)}, bf16[2,1,96,384]{3,2,1,0:T(8,128)(2,1)S(1)}, u32[]{:S(2)}, u32[]{:S(2)}) collective-permute-start(bf16[2,1,96,384]{3,2,1,0:T(8,128)(2,1)S(1)} %get-tuple-element.48), channel_id=1, source_target_pairs={{0,1},{1,2},{2,3},{3,4},{4,5},{5,6},{6,7},{7,8},{8,9},{9,10},{10,1... | collective-permute-start | bytes 442376 | tf_op jit(solution)/shard_map/ppermute | solution.py:24
  103.7 1.1 fusion.41
  104.9 2.4 %collective-permute-done.14 = bf16[2,1,96,384]{3,2,1,0:T(8,128)(2,1)S(1)} collective-permute-done((bf16[2,1,96,384]{3,2,1,0:T(8,128)(2,1)S(1)}, bf16[2,1,96,384]{3,2,1,0:T(8,128)(2,1)S(1)}, u32[]{:S(2)}, u32[]{:S(2)}) %collective-permute-start.14) | collective-permute-done | bytes 147488 | tf_op jit(solution)/shard_map/ppermute | solution.py:27
  107.3 0.5 fusion.44
  107.8 7.5 %collective-permute-done.13 = bf16[2,1,96,384]{3,2,1,0:T(8,128)(2,1)S(1)} collective-permute-done((bf16[2,1,96,384]{3,2,1,0:T(8,128)(2,1)S(1)}, bf16[2,1,96,384]{3,2,1,0:T(8,128)(2,1)S(1)}, u32[]{:S(2)}, u32[]{:S(2)}) %collective-permute-start.13) | collective-permute-done | bytes 147488 | tf_op jit(solution)/shard_map/ppermute | solution.py:24
  115.2 0.5 fusion.48
  115.7 0.1 fusion.35
  115.8 0.2 fusion.55
  116.1 0.4 fusion.53
  116.4 0.1 fusion.52
  116.6 0.2 maximum_maximum_fusion
  116.8 0.8 copy.40
  117.6 1.0 copy.41
  (66 shorter events, 1.0 us)
Async XLA Ops:
  0.0 73.5 %copy-start = (bf16[384,384]{1,0:T(8,128)(2,1)S(1)}, bf16[384,384]{1,0:T(8,128)(2,1)}, u32[]{:S(2)}) copy-start(bf16[384,384]{1,0:T(8,128)(2,1)} %param.16) | copy-start | bytes 884740
  0.0 9.3 %copy-start.1 = (bf16[1,2,96,384]{3,2,1,0:T(8,128)(2,1)S(1)}, bf16[1,2,96,384]{3,2,1,0:T(8,128)(2,1)}, u32[]{:S(2)}) copy-start(bf16[1,2,96,384]{3,2,1,0:T(8,128)(2,1)} %param.11) | copy-start | bytes 442372
  0.0 9.2 %copy-start.2 = (bf16[3,3,384,192]{2,3,1,0:T(8,128)(2,1)S(1)}, bf16[3,3,384,192]{2,3,1,0:T(8,128)(2,1)}, u32[]{:S(2)}) copy-start(bf16[3,3,384,192]{2,3,1,0:T(8,128)(2,1)} %param.20) | copy-start | bytes 3981316
  0.0 12.0 %collective-permute-start = (bf16[192,384]{1,0:T(8,128)(2,1)}, bf16[192,384]{1,0:T(8,128)(2,1)S(1)}, u32[]{:S(2)}, u32[]{:S(2)}) collective-permute-start(bf16[192,384]{1,0:T(8,128)(2,1)} %bitcast.214), channel_id=1, source_target_pairs={{0,2},{1,3},{2,0},{3,1},{4,6},{5,7},{6,4},{7,5},{8,10},{9,11},{10,... | collective-permute-start | bytes 442376 | tf_op jit(solution)/shard_map/ppermute | solution.py:37
  9.3 0.7 copy-start.10
  9.3 0.7 copy-start.11
  9.7 10.5 %copy-start.6 = (bf16[384,1728]{0,1:T(8,128)(2,1)}, bf16[384,1728]{0,1:T(8,128)(2,1)S(1)}, u32[]{:S(2)}) copy-start(bf16[384,1728]{0,1:T(8,128)(2,1)S(1)} %constant_dynamic-update-slice_fusion) | copy-start | bytes 3981316
  10.0 10.2 %copy-start.8 = (bf16[384,1152]{1,0:T(8,128)(2,1)S(1)}, bf16[384,1152]{1,0:T(8,128)(2,1)}, u32[]{:S(2)}) copy-start(bf16[384,1152]{1,0:T(8,128)(2,1)} %param.14) | copy-start | bytes 2654212
  12.1 11.1 %collective-permute-start.1 = (bf16[384,384]{1,0:T(8,128)(2,1)S(1)}, bf16[384,384]{1,0:T(8,128)(2,1)S(1)}, u32[]{:S(2)}, u32[]{:S(2)}) collective-permute-start(bf16[384,384]{1,0:T(8,128)(2,1)S(1)} %pad_maximum_fusion.10), channel_id=1, source_target_pairs={{0,4},{1,5},{2,6},{3,7},{4,8},{5,9},{6,10},{7,11},{8,12},{9,13},{1... | collective-permute-start | bytes 884744 | tf_op jit(solution)/shard_map/ppermute | solution.py:37
  15.4 9.6 %collective-permute-start.2 = (bf16[384,384]{1,0:T(8,128)(2,1)S(1)}, bf16[384,384]{1,0:T(8,128)(2,1)S(1)}, u32[]{:S(2)}, u32[]{:S(2)}) collective-permute-start(bf16[384,384]{1,0:T(8,128)(2,1)S(1)} %pad_maximum_fusion.10), channel_id=1, source_target_pairs={{0,28},{1,29},{2,30},{3,31},{4,0},{5,1},{6,2},{7,3},{8,4},{9,5},{1... | collective-permute-start | bytes 884744 | tf_op jit(solution)/shard_map/ppermute | solution.py:37
  19.1 1.1 copy-start.12
  19.1 1.1 copy-start.13
  19.2 1.7 %copy-start.14 = (bf16[192]{0:T(256)(128)(2,1)S(1)}, bf16[192]{0:T(256)(128)(2,1)}, u32[]{:S(2)}) copy-start(bf16[192]{0:T(256)(128)(2,1)} %param.21) | copy-start | bytes 1156
  25.0 10.0 %collective-permute-start.4 = (bf16[384,384]{1,0:T(8,128)(2,1)S(1)}, bf16[384,384]{1,0:T(8,128)(2,1)S(1)}, u32[]{:S(2)}, u32[]{:S(2)}) collective-permute-start(bf16[384,384]{1,0:T(8,128)(2,1)S(1)} %collective-permute-done.1), channel_id=1, source_target_pairs={{0,4},{1,5},{2,6},{3,7},{4,8},{5,9},{6,10},{7,11},{8,12},{9,13},{1... | collective-permute-start | bytes 884744 | tf_op jit(solution)/shard_map/ppermute | solution.py:37
  28.4 8.7 %collective-permute-start.5 = (bf16[384,384]{1,0:T(8,128)(2,1)S(1)}, bf16[384,384]{1,0:T(8,128)(2,1)S(1)}, u32[]{:S(2)}, u32[]{:S(2)}) collective-permute-start(bf16[384,384]{1,0:T(8,128)(2,1)S(1)} %collective-permute-done.2), channel_id=1, source_target_pairs={{0,28},{1,29},{2,30},{3,31},{4,0},{5,1},{6,2},{7,3},{8,4},{9,5},{1... | collective-permute-start | bytes 884744 | tf_op jit(solution)/shard_map/ppermute | solution.py:37
  35.0 9.8 %collective-permute-start.6 = (bf16[384,384]{1,0:T(8,128)(2,1)S(1)}, bf16[384,384]{1,0:T(8,128)(2,1)S(1)}, u32[]{:S(2)}, u32[]{:S(2)}) collective-permute-start(bf16[384,384]{1,0:T(8,128)(2,1)S(1)} %collective-permute-done.4), channel_id=1, source_target_pairs={{0,4},{1,5},{2,6},{3,7},{4,8},{5,9},{6,10},{7,11},{8,12},{9,13},{1... | collective-permute-start | bytes 884744 | tf_op jit(solution)/shard_map/ppermute | solution.py:37
  37.1 9.6 %collective-permute-start.7 = (bf16[384,384]{1,0:T(8,128)(2,1)S(1)}, bf16[384,384]{1,0:T(8,128)(2,1)S(1)}, u32[]{:S(2)}, u32[]{:S(2)}) collective-permute-start(bf16[384,384]{1,0:T(8,128)(2,1)S(1)} %collective-permute-done.5), channel_id=1, source_target_pairs={{0,28},{1,29},{2,30},{3,31},{4,0},{5,1},{6,2},{7,3},{8,4},{9,5},{1... | collective-permute-start | bytes 884744 | tf_op jit(solution)/shard_map/ppermute | solution.py:37
  44.8 8.2 %collective-permute-start.8 = (bf16[192,384]{1,0:T(8,128)(2,1)S(1)}, bf16[192,384]{1,0:T(8,128)(2,1)S(1)}, u32[]{:S(2)}, u32[]{:S(2)}) collective-permute-start(bf16[192,384]{1,0:T(8,128)(2,1)S(1)} %slice.191), channel_id=1, source_target_pairs={{0,4},{1,5},{2,6},{3,7},{4,8},{5,9},{6,10},{7,11},{8,12},{9,13},{1... | collective-permute-start | bytes 442376 | tf_op jit(solution)/shard_map/ppermute | solution.py:37
  46.8 7.8 %collective-permute-start.9 = (bf16[192,384]{1,0:T(8,128)(2,1)S(1)}, bf16[192,384]{1,0:T(8,128)(2,1)S(1)}, u32[]{:S(2)}, u32[]{:S(2)}) collective-permute-start(bf16[192,384]{1,0:T(8,128)(2,1)S(1)} %slice.192), channel_id=1, source_target_pairs={{0,28},{1,29},{2,30},{3,31},{4,0},{5,1},{6,2},{7,3},{8,4},{9,5},{1... | collective-permute-start | bytes 442376 | tf_op jit(solution)/shard_map/ppermute | solution.py:37
  54.6 11.1 %collective-permute-start.10 = (bf16[1920,384]{1,0:T(8,128)(2,1)S(1)}, bf16[1920,384]{1,0:T(8,128)(2,1)}, u32[]{:S(2)}, u32[]{:S(2)}) collective-permute-start(bf16[1920,384]{1,0:T(8,128)(2,1)S(1)} %constant_dynamic-update-slice_fusion.6.refs_5_), channel_id=1, source_target_pairs={{0,1},{1,0},{2,3},{3,2},{4,5},{5,4},{6,7},{7,6},{8,9},{9,8},{10,11... | collective-permute-start | bytes 4423688 | tf_op jit(solution)/shard_map/ppermute | solution.py:37
  56.7 9.1 %collective-permute-start.3 = (bf16[1152,384]{1,0:T(8,128)(2,1)S(1)}, bf16[1152,384]{1,0:T(8,128)(2,1)}, u32[]{:S(2)}, u32[]{:S(2)}) collective-permute-start(bf16[1152,384]{1,0:T(8,128)(2,1)S(1)} %pad_maximum_fusion.refs_4_), channel_id=1, source_target_pairs={{0,1},{1,0},{2,3},{3,2},{4,5},{5,4},{6,7},{7,6},{8,9},{9,8},{10,11... | collective-permute-start | bytes 2654216 | tf_op jit(solution)/shard_map/ppermute | solution.py:37
  65.7 7.8 %copy-start.9 = (f32[384]{0:T(512)S(1)}, f32[384]{0:T(512)}, u32[]{:S(2)}) copy-start(f32[384]{0:T(512)} %convert_element_type.57) | copy-start | bytes 4612
  65.8 18.9 %copy-start.5 = (bf16[3,384,768]{2,1,0:T(8,128)(2,1)S(1)}, bf16[3,384,768]{2,1,0:T(8,128)(2,1)}, u32[]{:S(2)}) copy-start(bf16[3,384,768]{2,1,0:T(8,128)(2,1)} %param.18) | copy-start | bytes 5308420
  73.8 11.2 %collective-permute-start.11 = (bf16[192,384]{1,0:T(8,128)(2,1)S(1)}, bf16[192,384]{1,0:T(8,128)(2,1)S(1)}, u32[]{:S(2)}, u32[]{:S(2)}) collective-permute-start(bf16[192,384]{1,0:T(8,128)(2,1)S(1)} %fusion.2), channel_id=1, source_target_pairs={{0,64},{32,96},{64,128},{96,160},{128,192},{160,224},{192,256},{22... | collective-permute-start | bytes 442376 | tf_op jit(solution)/shard_map/ppermute | solution.py:16
  80.7 7.4 %collective-permute-start.12 = (bf16[192,384]{1,0:T(8,128)(2,1)S(1)}, bf16[192,384]{1,0:T(8,128)(2,1)S(1)}, u32[]{:S(2)}, u32[]{:S(2)}) collective-permute-start(bf16[192,384]{1,0:T(8,128)(2,1)S(1)} %fusion.2), channel_id=1, source_target_pairs={{0,32},{32,64},{64,96},{96,128},{128,160},{160,192},{192,224},{224... | collective-permute-start | bytes 442376 | tf_op jit(solution)/shard_map/ppermute | solution.py:16
  88.5 15.3 %copy-start.7 = (bf16[384,1728]{0,1:T(8,128)(2,1)S(1)}, bf16[384,1728]{0,1:T(8,128)(2,1)}, u32[]{:S(2)}) copy-start(bf16[384,1728]{0,1:T(8,128)(2,1)} %copy-done.6) | copy-start | bytes 3981316
  88.9 18.4 %collective-permute-start.14 = (bf16[2,1,96,384]{3,2,1,0:T(8,128)(2,1)S(1)}, bf16[2,1,96,384]{3,2,1,0:T(8,128)(2,1)S(1)}, u32[]{:S(2)}, u32[]{:S(2)}) collective-permute-start(bf16[2,1,96,384]{3,2,1,0:T(8,128)(2,1)S(1)} %get-tuple-element.49), channel_id=1, source_target_pairs={{1,0},{2,1},{3,2},{4,3},{5,4},{6,5},{7,6},{8,7},{9,8},{10,9},{11,1... | collective-permute-start | bytes 442376 | tf_op jit(solution)/shard_map/ppermute | solution.py:27
  101.6 13.6 %collective-permute-start.13 = (bf16[2,1,96,384]{3,2,1,0:T(8,128)(2,1)S(1)}, bf16[2,1,96,384]{3,2,1,0:T(8,128)(2,1)S(1)}, u32[]{:S(2)}, u32[]{:S(2)}) collective-permute-start(bf16[2,1,96,384]{3,2,1,0:T(8,128)(2,1)S(1)} %get-tuple-element.48), channel_id=1, source_target_pairs={{0,1},{1,2},{2,3},{3,4},{4,5},{5,6},{6,7},{7,8},{8,9},{9,10},{10,1... | collective-permute-start | bytes 442376 | tf_op jit(solution)/shard_map/ppermute | solution.py:24
  103.7 3.5 %copy-start.4 = (bf16[384,576]{0,1:T(8,128)(2,1)S(1)}, bf16[384,576]{0,1:T(8,128)(2,1)}, u32[]{:S(2)}) copy-start(bf16[384,576]{0,1:T(8,128)(2,1)} %get-tuple-element.34) | copy-start | bytes 1327108
  104.8 10.4 %copy-start.3 = (bf16[384,576]{0,1:T(8,128)(2,1)S(1)}, bf16[384,576]{0,1:T(8,128)(2,1)}, u32[]{:S(2)}) copy-start(bf16[384,576]{0,1:T(8,128)(2,1)} %get-tuple-element.32) | copy-start | bytes 1327108

commit v9 on v8

--- a/solution.py
+++ b/solution.py
@@ -47,15 +47,17 @@
         behind = moved(behind, backward)
         if step == 0:
             ahead, behind, riders = lax.optimization_barrier((ahead, behind, riders))
+        if step == 1:
+            ahead, behind, early = lax.optimization_barrier((ahead, behind, early))
         batches[-1] += [ahead, behind]
         if step == 0:
+            early = moved(jnp.concatenate(batches[0], axis=0), lambda s: s ^ 1)
             batches.append([])
     half = own.shape[0] // 2
     batches[-1].append(moved(ahead[:half], forward))
     batches[-1].append(moved(behind[half:], backward))
     mine = [jnp.concatenate(batch, axis=0) for batch in batches]
-    other = [moved(chunk, lambda s: s ^ 1) for chunk in mine]
-    return mine + other, riders
+    return mine + [early, moved(mine[1], lambda s: s ^ 1)], riders
 
 
 def normalize(frames, norm_gain):
@@ -199,9 +201,8 @@
     )
     chunks, riders = gather_space(frames.reshape(-1, channels), riders)
     queries = riders["queries"]
-    half = len(chunks) // 2
-    state = fused_attention(queries, chunks[:half], riders["weights"], finish=False)
-    mixed = fused_attention(queries, chunks[half:], riders["weights"], state=state)
+    state = fused_attention(queries, chunks[:-1], riders["weights"], finish=False)
+    mixed = fused_attention(queries, chunks[-1:], riders["weights"], state=state)
     hidden = (
         frames.reshape(-1, channels).astype(jnp.float32)
         + jnp.dot(mixed, w_proj, preferred_element_type=jnp.float32)

time: 119 us -> 125 us (1.050)
  waiting for transfers between devices: 26.8 us -> 34.1 us
  starting transfers between devices: 66.3 us -> 63.3 us
  local copies, waits for them, and re-layouts: 5.05 us -> 7.14 us
    ppermute x11, waiting for transfers between devices: 13.9 us -> 20 us  [moved(): return lax.ppermute(value, 'space', [(s, target(s)) for s in range(count)])]
    unnamed x43 -> x47, local copies, waits for them, and re-layouts: 0.74 us -> 2.83 us
    ppermute x2, starting transfers between devices: 10.9 us -> 8.88 us  [shifted(): lax.ppermute(value, axis, [(source, source + steps) for source in range(l...]
    ppermute x1, waiting for transfers between devices: 7.46 us -> 9.16 us  [with_halo(): lax.ppermute(lax.slice_in_dim(block, block.shape[dim] - width, None, axis...]
    ppermute x1, waiting for transfers between devices: 2.4 us -> 1.08 us  [with_halo(): lax.ppermute(lax.slice_in_dim(block, 0, width, axis=dim), axis, backward)]
  transfers between devices with their start and end apart: 15 -> 15, of which waited for: 10 -> 12; matrix products, arithmetic and copies ran while one was open for 6% -> 5% of each run, Pallas kernels for 5% -> 6%
where the time goes in v9:
time: 125 us; the launch traced here: 124 us
  starting transfers between devices  63.3 us (51%)
  waiting for transfers between devices  34.1 us (27%)
  Pallas kernels  12.7 us (10%)
  local copies, waits for them, and re-layouts  7.14 us (6%)
  matrix products  3.49 us (3%)
  other arithmetic  3.12 us (2%)
    ppermute x11, starting transfers between devices, moved(): return lax.ppermute(value, 'space', [(s, target(s)) for s in range(count)])  40.1 us
    ppermute x11, waiting for transfers between devices, moved(): return lax.ppermute(value, 'space', [(s, target(s)) for s in range(count)])  20 us
    pallas_call x2, Pallas kernels, fused_attention(): pl.pallas_call(functools.partial(attention_kernel, sizes=sizes, channels=...  12.7 us
    ppermute x1, starting transfers between devices, with_halo(): lax.ppermute(lax.slice_in_dim(block, 0, width, axis=dim), axis, backward)  12.2 us
    ppermute x1, waiting for transfers between devices, with_halo(): lax.ppermute(lax.slice_in_dim(block, block.shape[dim] - width, None, axis...  9.16 us
    ppermute x2, starting transfers between devices, shifted(): lax.ppermute(value, axis, [(source, source + steps) for source in range(l...  8.88 us
    ppermute x2, waiting for transfers between devices, shifted(): lax.ppermute(value, axis, [(source, source + steps) for source in range(l...  3.79 us
    unnamed x47, local copies, waits for them, and re-layouts  2.83 us
  transfers between devices with their start and end apart: 15, of which 12 were waited for; matrix products, arithmetic and copies ran while one was open for 5% of the time, Pallas kernels for 6%

profile of v9, /device:TPU:260, one launch (start us, length us, event | category | flops | bytes accessed | tf_op | source)
XLA Modules:
  0.0 124.4 jit_solution(3090853868589760158)
XLA Ops:
  0.0 7.9 %collective-permute-start = (bf16[192,384]{1,0:T(8,128)(2,1)}, bf16[192,384]{1,0:T(8,128)(2,1)S(1)}, u32[]{:S(2)}, u32[]{:S(2)}) collective-permute-start(bf16[192,384]{1,0:T(8,128)(2,1)} %bitcast.214), channel_id=1, source_target_pairs={{0,2},{1,3},{2,0},{3,1},{4,6},{5,7},{6,4},{7,5},{8,10},{9,11},{10,... | collective-permute-start | bytes 442376 | tf_op jit(solution)/shard_map/ppermute | solution.py:37
  7.9 1.3 %slice_bitcast_fusion.11 = (bf16[384,192]{0,1:T(8,128)(2,1)S(1)}, bf16[384,192]{0,1:T(8,128)(2,1)S(1)}, bf16[384,192]{0,1:T(8,128)(2,1)S(1)}, bf16[384,192]{0,1:...) fusion(bf16[3,3,384,192]{2,3,1,0:T(8,128)(2,1)} %param.20), kind=kLoop, calls=%fused_computation.100 | loop fusion | bytes 1769472 | tf_op jit(solution)/shard_map/squeeze | solution.py:195
  9.7 0.2 copy-done.12
  10.1 1.9 %collective-permute-done = bf16[192,384]{1,0:T(8,128)(2,1)S(1)} collective-permute-done((bf16[192,384]{1,0:T(8,128)(2,1)}, bf16[192,384]{1,0:T(8,128)(2,1)S(1)}, u32[]{:S(2)}, u32[]{:S(2)}) %collective-permute-start) | collective-permute-done | bytes 147488 | tf_op jit(solution)/shard_map/ppermute | solution.py:37
  12.1 3.4 %collective-permute-start.1 = (bf16[384,384]{1,0:T(8,128)(2,1)S(1)}, bf16[384,384]{1,0:T(8,128)(2,1)S(1)}, u32[]{:S(2)}, u32[]{:S(2)}) collective-permute-start(bf16[384,384]{1,0:T(8,128)(2,1)S(1)} %pad_maximum_fusion.10), channel_id=1, source_target_pairs={{0,4},{1,5},{2,6},{3,7},{4,8},{5,9},{6,10},{7,11},{8,12},{9,13},{1... | collective-permute-start | bytes 884744 | tf_op jit(solution)/shard_map/ppermute | solution.py:37
  15.4 3.7 %collective-permute-start.2 = (bf16[384,384]{1,0:T(8,128)(2,1)S(1)}, bf16[384,384]{1,0:T(8,128)(2,1)S(1)}, u32[]{:S(2)}, u32[]{:S(2)}) collective-permute-start(bf16[384,384]{1,0:T(8,128)(2,1)S(1)} %pad_maximum_fusion.10), channel_id=1, source_target_pairs={{0,28},{1,29},{2,30},{3,31},{4,0},{5,1},{6,2},{7,3},{8,4},{9,5},{1... | collective-permute-start | bytes 884744 | tf_op jit(solution)/shard_map/ppermute | solution.py:37
  19.2 1.0 pad_maximum_fusion.1
  20.3 0.6 convert_element_type.57
  20.8 0.2 fusion.1.refs_0_
  21.1 2.0 %collective-permute-done.1 = bf16[384,384]{1,0:T(8,128)(2,1)S(1)} collective-permute-done((bf16[384,384]{1,0:T(8,128)(2,1)S(1)}, bf16[384,384]{1,0:T(8,128)(2,1)S(1)}, u32[]{:S(2)}, u32[]{:S(2)}) %collective-permute-start.1) | collective-permute-done | bytes 294944 | tf_op jit(solution)/shard_map/ppermute | solution.py:37
  23.1 1.9 %collective-permute-done.2 = bf16[384,384]{1,0:T(8,128)(2,1)S(1)} collective-permute-done((bf16[384,384]{1,0:T(8,128)(2,1)S(1)}, bf16[384,384]{1,0:T(8,128)(2,1)S(1)}, u32[]{:S(2)}, u32[]{:S(2)}) %collective-permute-start.2) | collective-permute-done | bytes 294944 | tf_op jit(solution)/shard_map/ppermute | solution.py:37
  25.1 1.9 %collective-permute-start.5 = (bf16[1152,384]{1,0:T(8,128)(2,1)S(1)}, bf16[1152,384]{1,0:T(8,128)(2,1)S(1)}, u32[]{:S(2)}, u32[]{:S(2)}) collective-permute-start(bf16[1152,384]{1,0:T(8,128)(2,1)S(1)} %pad_maximum_fusion.refs_4_), channel_id=1, source_target_pairs={{0,1},{1,0},{2,3},{3,2},{4,5},{5,4},{6,7},{7,6},{8,9},{9,8},{10,11... | collective-permute-start | bytes 2654216 | tf_op jit(solution)/shard_map/ppermute | solution.py:37
  27.1 3.4 %collective-permute-start.3 = (bf16[384,384]{1,0:T(8,128)(2,1)S(1)}, bf16[384,384]{1,0:T(8,128)(2,1)S(1)}, u32[]{:S(2)}, u32[]{:S(2)}) collective-permute-start(bf16[384,384]{1,0:T(8,128)(2,1)S(1)} %collective-permute-done.1), channel_id=1, source_target_pairs={{0,4},{1,5},{2,6},{3,7},{4,8},{5,9},{6,10},{7,11},{8,12},{9,13},{1... | collective-permute-start | bytes 884744 | tf_op jit(solution)/shard_map/ppermute | solution.py:37
  30.4 3.7 %collective-permute-start.4 = (bf16[384,384]{1,0:T(8,128)(2,1)S(1)}, bf16[384,384]{1,0:T(8,128)(2,1)S(1)}, u32[]{:S(2)}, u32[]{:S(2)}) collective-permute-start(bf16[384,384]{1,0:T(8,128)(2,1)S(1)} %collective-permute-done.2), channel_id=1, source_target_pairs={{0,28},{1,29},{2,30},{3,31},{4,0},{5,1},{6,2},{7,3},{8,4},{9,5},{1... | collective-permute-start | bytes 884744 | tf_op jit(solution)/shard_map/ppermute | solution.py:37
  34.1 5.5 %collective-permute-done.3 = bf16[384,384]{1,0:T(8,128)(2,1)S(1)} collective-permute-done((bf16[384,384]{1,0:T(8,128)(2,1)S(1)}, bf16[384,384]{1,0:T(8,128)(2,1)S(1)}, u32[]{:S(2)}, u32[]{:S(2)}) %collective-permute-start.3) | collective-permute-done | bytes 294944 | tf_op jit(solution)/shard_map/ppermute | solution.py:37
  39.6 1.9 %collective-permute-done.4 = bf16[384,384]{1,0:T(8,128)(2,1)S(1)} collective-permute-done((bf16[384,384]{1,0:T(8,128)(2,1)S(1)}, bf16[384,384]{1,0:T(8,128)(2,1)S(1)}, u32[]{:S(2)}, u32[]{:S(2)}) %collective-permute-start.4) | collective-permute-done | bytes 294944 | tf_op jit(solution)/shard_map/ppermute | solution.py:37
  41.5 0.9 copy-done.1
  42.4 3.4 %collective-permute-start.6 = (bf16[384,384]{1,0:T(8,128)(2,1)S(1)}, bf16[384,384]{1,0:T(8,128)(2,1)S(1)}, u32[]{:S(2)}, u32[]{:S(2)}) collective-permute-start(bf16[384,384]{1,0:T(8,128)(2,1)S(1)} %collective-permute-done.3), channel_id=1, source_target_pairs={{0,4},{1,5},{2,6},{3,7},{4,8},{5,9},{6,10},{7,11},{8,12},{9,13},{1... | collective-permute-start | bytes 884744 | tf_op jit(solution)/shard_map/ppermute | solution.py:37
  45.8 3.7 %collective-permute-start.7 = (bf16[384,384]{1,0:T(8,128)(2,1)S(1)}, bf16[384,384]{1,0:T(8,128)(2,1)S(1)}, u32[]{:S(2)}, u32[]{:S(2)}) collective-permute-start(bf16[384,384]{1,0:T(8,128)(2,1)S(1)} %collective-permute-done.4), channel_id=1, source_target_pairs={{0,28},{1,29},{2,30},{3,31},{4,0},{5,1},{6,2},{7,3},{8,4},{9,5},{1... | collective-permute-start | bytes 884744 | tf_op jit(solution)/shard_map/ppermute | solution.py:37
  49.6 4.3 %collective-permute-done.6 = bf16[384,384]{1,0:T(8,128)(2,1)S(1)} collective-permute-done((bf16[384,384]{1,0:T(8,128)(2,1)S(1)}, bf16[384,384]{1,0:T(8,128)(2,1)S(1)}, u32[]{:S(2)}, u32[]{:S(2)}) %collective-permute-start.6) | collective-permute-done | bytes 294944 | tf_op jit(solution)/shard_map/ppermute | solution.py:37
  53.9 2.1 %collective-permute-start.8 = (bf16[192,384]{1,0:T(8,128)(2,1)S(1)}, bf16[192,384]{1,0:T(8,128)(2,1)S(1)}, u32[]{:S(2)}, u32[]{:S(2)}) collective-permute-start(bf16[192,384]{1,0:T(8,128)(2,1)S(1)} %slice.191), channel_id=1, source_target_pairs={{0,4},{1,5},{2,6},{3,7},{4,8},{5,9},{6,10},{7,11},{8,12},{9,13},{1... | collective-permute-start | bytes 442376 | tf_op jit(solution)/shard_map/ppermute | solution.py:37
  56.0 5.0 %collective-permute-start.9 = (bf16[192,384]{1,0:T(8,128)(2,1)S(1)}, bf16[192,384]{1,0:T(8,128)(2,1)S(1)}, u32[]{:S(2)}, u32[]{:S(2)}) collective-permute-start(bf16[192,384]{1,0:T(8,128)(2,1)S(1)} %slice.192), channel_id=1, source_target_pairs={{0,28},{1,29},{2,30},{3,31},{4,0},{5,1},{6,2},{7,3},{8,4},{9,5},{1... | collective-permute-start | bytes 442376 | tf_op jit(solution)/shard_map/ppermute | solution.py:37
  61.1 1.0 collective-permute-done.8
  62.2 1.5 %collective-permute-done.9 = bf16[192,384]{1,0:T(8,128)(2,1)S(1)} collective-permute-done((bf16[192,384]{1,0:T(8,128)(2,1)S(1)}, bf16[192,384]{1,0:T(8,128)(2,1)S(1)}, u32[]{:S(2)}, u32[]{:S(2)}) %collective-permute-start.9) | collective-permute-done | bytes 147488 | tf_op jit(solution)/shard_map/ppermute | solution.py:37
  63.7 2.1 %collective-permute-start.10 = (bf16[1920,384]{1,0:T(8,128)(2,1)S(1)}, bf16[1920,384]{1,0:T(8,128)(2,1)}, u32[]{:S(2)}, u32[]{:S(2)}) collective-permute-start(bf16[1920,384]{1,0:T(8,128)(2,1)S(1)} %constant_dynamic-update-slice_fusion.6.refs_5_), channel_id=1, source_target_pairs={{0,1},{1,0},{2,3},{3,2},{4,5},{5,4},{6,7},{7,6},{8,9},{9,8},{10,11... | collective-permute-start | bytes 4423688 | tf_op jit(solution)/shard_map/ppermute | solution.py:37
  65.8 1.0 fusion.65
  66.8 1.2 copy-done.2
  68.0 7.4 %shard_map.109 = (f32[192,1]{1,0:T(8,128)S(1)}, f32[192,1]{1,0:T(8,128)S(1)}, f32[192,384]{1,0:T(8,128)S(1)}) custom-call(bf16[192,384]{1,0:T(8,128)(2,1)S(1)} %fusion.1.refs_0_, f32[1,384]{1,0:T(1,128)S(1)} %reshape.147.refs_1_, bf16[384,768]{1,0:T(8,128)(2,1)S(1)} %slice.157.refs_2_, f32[1,768]{1,0:T(1,128)S(1)} %reshape.152.refs_3_, ...), custom_call_target="tpu_custom_call" | custom-call | flops 3737124864 | bytes 4128768 | tf_op jit(solution)/shard_map/pallas_call | solution.py:162
  75.4 5.3 %shard_map.110 = bf16[192,384]{1,0:T(8,128)(2,1)S(1)} custom-call(bf16[192,384]{1,0:T(8,128)(2,1)S(1)} %fusion.1.refs_0_, f32[1,384]{1,0:T(1,128)S(1)} %reshape.147.refs_1_, bf16[384,768]{1,0:T(8,128)(2,1)S(1)} %slice.157.refs_2_, f32[1,768]{1,0:T(1,128)S(1)} %reshape.152.refs_3_, bf16[1920,384]{1,0:T(8,128)(2,1)} %collective-permute-done.10.refs_4_, ...), custom_call_target="tpu_custom_call" | custom-call | flops 1698693120 | bytes 2359296 | tf_op jit(solution)/shard_map/pallas_call | solution.py:162
  80.8 0.2 fusion.2
  81.0 4.9 %collective-permute-start.11 = (bf16[192,384]{1,0:T(8,128)(2,1)S(1)}, bf16[192,384]{1,0:T(8,128)(2,1)S(1)}, u32[]{:S(2)}, u32[]{:S(2)}) collective-permute-start(bf16[192,384]{1,0:T(8,128)(2,1)S(1)} %fusion.2), channel_id=1, source_target_pairs={{0,64},{32,96},{64,128},{96,160},{128,192},{160,224},{192,256},{22... | collective-permute-start | bytes 442376 | tf_op jit(solution)/shard_map/ppermute | solution.py:16
  85.9 4.0 %collective-permute-start.12 = (bf16[192,384]{1,0:T(8,128)(2,1)S(1)}, bf16[192,384]{1,0:T(8,128)(2,1)S(1)}, u32[]{:S(2)}, u32[]{:S(2)}) collective-permute-start(bf16[192,384]{1,0:T(8,128)(2,1)S(1)} %fusion.2), channel_id=1, source_target_pairs={{0,32},{32,64},{64,96},{96,128},{128,160},{160,192},{192,224},{224... | collective-permute-start | bytes 442376 | tf_op jit(solution)/shard_map/ppermute | solution.py:16
  89.9 0.3 fusion.3
  90.2 0.9 collective-permute-done.11
  91.1 2.9 %collective-permute-done.12 = bf16[192,384]{1,0:T(8,128)(2,1)S(1)} collective-permute-done((bf16[192,384]{1,0:T(8,128)(2,1)S(1)}, bf16[192,384]{1,0:T(8,128)(2,1)S(1)}, u32[]{:S(2)}, u32[]{:S(2)}) %collective-permute-start.12) | collective-permute-done | bytes 147488 | tf_op jit(solution)/shard_map/ppermute | solution.py:16
  94.1 0.3 fusion.7
  94.4 0.3 add_convert_fusion
  94.8 12.2 %collective-permute-start.14 = (bf16[2,1,96,384]{3,2,1,0:T(8,128)(2,1)S(1)}, bf16[2,1,96,384]{3,2,1,0:T(8,128)(2,1)S(1)}, u32[]{:S(2)}, u32[]{:S(2)}) collective-permute-start(bf16[2,1,96,384]{3,2,1,0:T(8,128)(2,1)S(1)} %get-tuple-element.55), channel_id=1, source_target_pairs={{1,0},{2,1},{3,2},{4,3},{5,4},{6,5},{7,6},{8,7},{9,8},{10,9},{11,1... | collective-permute-start | bytes 442376 | tf_op jit(solution)/shard_map/ppermute | solution.py:27
  107.0 2.1 %collective-permute-start.13 = (bf16[2,1,96,384]{3,2,1,0:T(8,128)(2,1)S(1)}, bf16[2,1,96,384]{3,2,1,0:T(8,128)(2,1)S(1)}, u32[]{:S(2)}, u32[]{:S(2)}) collective-permute-start(bf16[2,1,96,384]{3,2,1,0:T(8,128)(2,1)S(1)} %get-tuple-element.54), channel_id=1, source_target_pairs={{0,1},{1,2},{2,3},{3,4},{4,5},{5,6},{6,7},{7,8},{8,9},{9,10},{10,1... | collective-permute-start | bytes 442376 | tf_op jit(solution)/shard_map/ppermute | solution.py:24
  109.2 1.1 fusion.41
  110.3 1.1 collective-permute-done.14
  111.4 0.5 fusion.44
  111.9 9.2 %collective-permute-done.13 = bf16[2,1,96,384]{3,2,1,0:T(8,128)(2,1)S(1)} collective-permute-done((bf16[2,1,96,384]{3,2,1,0:T(8,128)(2,1)S(1)}, bf16[2,1,96,384]{3,2,1,0:T(8,128)(2,1)S(1)}, u32[]{:S(2)}, u32[]{:S(2)}) %collective-permute-start.13) | collective-permute-done | bytes 147488 | tf_op jit(solution)/shard_map/ppermute | solution.py:24
  121.1 0.5 fusion.48
  121.7 0.2 fusion.55
  121.9 0.4 fusion.53
  122.6 0.8 copy.40
  123.4 1.0 copy.41
  (70 shorter events, 1.6 us)
Async XLA Ops:
  0.0 80.7 %copy-start = (bf16[384,384]{1,0:T(8,128)(2,1)S(1)}, bf16[384,384]{1,0:T(8,128)(2,1)}, u32[]{:S(2)}) copy-start(bf16[384,384]{1,0:T(8,128)(2,1)} %param.16) | copy-start | bytes 884740
  0.0 9.3 %copy-start.3 = (bf16[1,2,96,384]{3,2,1,0:T(8,128)(2,1)S(1)}, bf16[1,2,96,384]{3,2,1,0:T(8,128)(2,1)}, u32[]{:S(2)}) copy-start(bf16[1,2,96,384]{3,2,1,0:T(8,128)(2,1)} %param.11) | copy-start | bytes 442372
  0.0 9.2 %copy-start.4 = (bf16[3,3,384,192]{2,3,1,0:T(8,128)(2,1)S(1)}, bf16[3,3,384,192]{2,3,1,0:T(8,128)(2,1)}, u32[]{:S(2)}) copy-start(bf16[3,3,384,192]{2,3,1,0:T(8,128)(2,1)} %param.20) | copy-start | bytes 3981316
  0.0 12.0 %collective-permute-start = (bf16[192,384]{1,0:T(8,128)(2,1)}, bf16[192,384]{1,0:T(8,128)(2,1)S(1)}, u32[]{:S(2)}, u32[]{:S(2)}) collective-permute-start(bf16[192,384]{1,0:T(8,128)(2,1)} %bitcast.214), channel_id=1, source_target_pairs={{0,2},{1,3},{2,0},{3,1},{4,6},{5,7},{6,4},{7,5},{8,10},{9,11},{10,... | collective-permute-start | bytes 442376 | tf_op jit(solution)/shard_map/ppermute | solution.py:37
  9.3 0.7 copy-start.12
  9.3 0.7 copy-start.13
  9.7 10.5 %copy-start.8 = (bf16[384,1728]{0,1:T(8,128)(2,1)}, bf16[384,1728]{0,1:T(8,128)(2,1)S(1)}, u32[]{:S(2)}) copy-start(bf16[384,1728]{0,1:T(8,128)(2,1)S(1)} %constant_dynamic-update-slice_fusion) | copy-start | bytes 3981316
  10.0 10.2 %copy-start.10 = (bf16[384,1152]{1,0:T(8,128)(2,1)S(1)}, bf16[384,1152]{1,0:T(8,128)(2,1)}, u32[]{:S(2)}) copy-start(bf16[384,1152]{1,0:T(8,128)(2,1)} %param.14) | copy-start | bytes 2654212
  12.1 11.1 %collective-permute-start.1 = (bf16[384,384]{1,0:T(8,128)(2,1)S(1)}, bf16[384,384]{1,0:T(8,128)(2,1)S(1)}, u32[]{:S(2)}, u32[]{:S(2)}) collective-permute-start(bf16[384,384]{1,0:T(8,128)(2,1)S(1)} %pad_maximum_fusion.10), channel_id=1, source_target_pairs={{0,4},{1,5},{2,6},{3,7},{4,8},{5,9},{6,10},{7,11},{8,12},{9,13},{1... | collective-permute-start | bytes 884744 | tf_op jit(solution)/shard_map/ppermute | solution.py:37
  15.4 9.6 %collective-permute-start.2 = (bf16[384,384]{1,0:T(8,128)(2,1)S(1)}, bf16[384,384]{1,0:T(8,128)(2,1)S(1)}, u32[]{:S(2)}, u32[]{:S(2)}) collective-permute-start(bf16[384,384]{1,0:T(8,128)(2,1)S(1)} %pad_maximum_fusion.10), channel_id=1, source_target_pairs={{0,28},{1,29},{2,30},{3,31},{4,0},{5,1},{6,2},{7,3},{8,4},{9,5},{1... | collective-permute-start | bytes 884744 | tf_op jit(solution)/shard_map/ppermute | solution.py:37
  19.1 1.1 copy-start.14
  19.1 1.1 copy-start.15
  19.2 1.7 %copy-start.16 = (bf16[192]{0:T(256)(128)(2,1)S(1)}, bf16[192]{0:T(256)(128)(2,1)}, u32[]{:S(2)}) copy-start(bf16[192]{0:T(256)(128)(2,1)} %param.21) | copy-start | bytes 1156
  25.1 16.3 %collective-permute-start.5 = (bf16[1152,384]{1,0:T(8,128)(2,1)S(1)}, bf16[1152,384]{1,0:T(8,128)(2,1)S(1)}, u32[]{:S(2)}, u32[]{:S(2)}) collective-permute-start(bf16[1152,384]{1,0:T(8,128)(2,1)S(1)} %pad_maximum_fusion.refs_4_), channel_id=1, source_target_pairs={{0,1},{1,0},{2,3},{3,2},{4,5},{5,4},{6,7},{7,6},{8,9},{9,8},{10,11... | collective-permute-start | bytes 2654216 | tf_op jit(solution)/shard_map/ppermute | solution.py:37
  27.1 12.5 %collective-permute-start.3 = (bf16[384,384]{1,0:T(8,128)(2,1)S(1)}, bf16[384,384]{1,0:T(8,128)(2,1)S(1)}, u32[]{:S(2)}, u32[]{:S(2)}) collective-permute-start(bf16[384,384]{1,0:T(8,128)(2,1)S(1)} %collective-permute-done.1), channel_id=1, source_target_pairs={{0,4},{1,5},{2,6},{3,7},{4,8},{5,9},{6,10},{7,11},{8,12},{9,13},{1... | collective-permute-start | bytes 884744 | tf_op jit(solution)/shard_map/ppermute | solution.py:37
  30.4 11.0 %collective-permute-start.4 = (bf16[384,384]{1,0:T(8,128)(2,1)S(1)}, bf16[384,384]{1,0:T(8,128)(2,1)S(1)}, u32[]{:S(2)}, u32[]{:S(2)}) collective-permute-start(bf16[384,384]{1,0:T(8,128)(2,1)S(1)} %collective-permute-done.2), channel_id=1, source_target_pairs={{0,28},{1,29},{2,30},{3,31},{4,0},{5,1},{6,2},{7,3},{8,4},{9,5},{1... | collective-permute-start | bytes 884744 | tf_op jit(solution)/shard_map/ppermute | solution.py:37
  41.5 0.9 copy-start.1
  42.4 11.5 %collective-permute-start.6 = (bf16[384,384]{1,0:T(8,128)(2,1)S(1)}, bf16[384,384]{1,0:T(8,128)(2,1)S(1)}, u32[]{:S(2)}, u32[]{:S(2)}) collective-permute-start(bf16[384,384]{1,0:T(8,128)(2,1)S(1)} %collective-permute-done.3), channel_id=1, source_target_pairs={{0,4},{1,5},{2,6},{3,7},{4,8},{5,9},{6,10},{7,11},{8,12},{9,13},{1... | collective-permute-start | bytes 884744 | tf_op jit(solution)/shard_map/ppermute | solution.py:37
  45.8 10.2 %collective-permute-start.7 = (bf16[384,384]{1,0:T(8,128)(2,1)S(1)}, bf16[384,384]{1,0:T(8,128)(2,1)S(1)}, u32[]{:S(2)}, u32[]{:S(2)}) collective-permute-start(bf16[384,384]{1,0:T(8,128)(2,1)S(1)} %collective-permute-done.4), channel_id=1, source_target_pairs={{0,28},{1,29},{2,30},{3,31},{4,0},{5,1},{6,2},{7,3},{8,4},{9,5},{1... | collective-permute-start | bytes 884744 | tf_op jit(solution)/shard_map/ppermute | solution.py:37
  53.9 8.2 %collective-permute-start.8 = (bf16[192,384]{1,0:T(8,128)(2,1)S(1)}, bf16[192,384]{1,0:T(8,128)(2,1)S(1)}, u32[]{:S(2)}, u32[]{:S(2)}) collective-permute-start(bf16[192,384]{1,0:T(8,128)(2,1)S(1)} %slice.191), channel_id=1, source_target_pairs={{0,4},{1,5},{2,6},{3,7},{4,8},{5,9},{6,10},{7,11},{8,12},{9,13},{1... | collective-permute-start | bytes 442376 | tf_op jit(solution)/shard_map/ppermute | solution.py:37
  56.0 7.6 %collective-permute-start.9 = (bf16[192,384]{1,0:T(8,128)(2,1)S(1)}, bf16[192,384]{1,0:T(8,128)(2,1)S(1)}, u32[]{:S(2)}, u32[]{:S(2)}) collective-permute-start(bf16[192,384]{1,0:T(8,128)(2,1)S(1)} %slice.192), channel_id=1, source_target_pairs={{0,28},{1,29},{2,30},{3,31},{4,0},{5,1},{6,2},{7,3},{8,4},{9,5},{1... | collective-permute-start | bytes 442376 | tf_op jit(solution)/shard_map/ppermute | solution.py:37
  63.7 11.7 %collective-permute-start.10 = (bf16[1920,384]{1,0:T(8,128)(2,1)S(1)}, bf16[1920,384]{1,0:T(8,128)(2,1)}, u32[]{:S(2)}, u32[]{:S(2)}) collective-permute-start(bf16[1920,384]{1,0:T(8,128)(2,1)S(1)} %constant_dynamic-update-slice_fusion.6.refs_5_), channel_id=1, source_target_pairs={{0,1},{1,0},{2,3},{3,2},{4,5},{5,4},{6,7},{7,6},{8,9},{9,8},{10,11... | collective-permute-start | bytes 4423688 | tf_op jit(solution)/shard_map/ppermute | solution.py:37
  66.8 1.2 copy-start.2
  75.4 5.4 %copy-start.11 = (f32[384]{0:T(512)S(1)}, f32[384]{0:T(512)}, u32[]{:S(2)}) copy-start(f32[384]{0:T(512)} %convert_element_type.57) | copy-start | bytes 4612
  75.4 14.5 %copy-start.7 = (bf16[3,384,768]{2,1,0:T(8,128)(2,1)S(1)}, bf16[3,384,768]{2,1,0:T(8,128)(2,1)}, u32[]{:S(2)}) copy-start(bf16[3,384,768]{2,1,0:T(8,128)(2,1)} %param.18) | copy-start | bytes 5308420
  81.0 10.1 %collective-permute-start.11 = (bf16[192,384]{1,0:T(8,128)(2,1)S(1)}, bf16[192,384]{1,0:T(8,128)(2,1)S(1)}, u32[]{:S(2)}, u32[]{:S(2)}) collective-permute-start(bf16[192,384]{1,0:T(8,128)(2,1)S(1)} %fusion.2), channel_id=1, source_target_pairs={{0,64},{32,96},{64,128},{96,160},{128,192},{160,224},{192,256},{22... | collective-permute-start | bytes 442376 | tf_op jit(solution)/shard_map/ppermute | solution.py:16
  85.9 8.1 %collective-permute-start.12 = (bf16[192,384]{1,0:T(8,128)(2,1)S(1)}, bf16[192,384]{1,0:T(8,128)(2,1)S(1)}, u32[]{:S(2)}, u32[]{:S(2)}) collective-permute-start(bf16[192,384]{1,0:T(8,128)(2,1)S(1)} %fusion.2), channel_id=1, source_target_pairs={{0,32},{32,64},{64,96},{96,128},{128,160},{160,192},{192,224},{224... | collective-permute-start | bytes 442376 | tf_op jit(solution)/shard_map/ppermute | solution.py:16
  94.4 14.8 %copy-start.9 = (bf16[384,1728]{0,1:T(8,128)(2,1)S(1)}, bf16[384,1728]{0,1:T(8,128)(2,1)}, u32[]{:S(2)}) copy-start(bf16[384,1728]{0,1:T(8,128)(2,1)} %copy-done.8) | copy-start | bytes 3981316
  94.8 16.6 %collective-permute-start.14 = (bf16[2,1,96,384]{3,2,1,0:T(8,128)(2,1)S(1)}, bf16[2,1,96,384]{3,2,1,0:T(8,128)(2,1)S(1)}, u32[]{:S(2)}, u32[]{:S(2)}) collective-permute-start(bf16[2,1,96,384]{3,2,1,0:T(8,128)(2,1)S(1)} %get-tuple-element.55), channel_id=1, source_target_pairs={{1,0},{2,1},{3,2},{4,3},{5,4},{6,5},{7,6},{8,7},{9,8},{10,9},{11,1... | collective-permute-start | bytes 442376 | tf_op jit(solution)/shard_map/ppermute | solution.py:27
  107.0 14.0 %collective-permute-start.13 = (bf16[2,1,96,384]{3,2,1,0:T(8,128)(2,1)S(1)}, bf16[2,1,96,384]{3,2,1,0:T(8,128)(2,1)S(1)}, u32[]{:S(2)}, u32[]{:S(2)}) collective-permute-start(bf16[2,1,96,384]{3,2,1,0:T(8,128)(2,1)S(1)} %get-tuple-element.54), channel_id=1, source_target_pairs={{0,1},{1,2},{2,3},{3,4},{4,5},{5,6},{6,7},{7,8},{8,9},{9,10},{10,1... | collective-permute-start | bytes 442376 | tf_op jit(solution)/shard_map/ppermute | solution.py:24
  109.2 2.2 %copy-start.6 = (bf16[384,576]{0,1:T(8,128)(2,1)S(1)}, bf16[384,576]{0,1:T(8,128)(2,1)}, u32[]{:S(2)}) copy-start(bf16[384,576]{0,1:T(8,128)(2,1)} %get-tuple-element.40) | copy-start | bytes 1327108
  110.3 10.8 %copy-start.5 = (bf16[384,576]{0,1:T(8,128)(2,1)S(1)}, bf16[384,576]{0,1:T(8,128)(2,1)}, u32[]{:S(2)}) copy-start(bf16[384,576]{0,1:T(8,128)(2,1)} %get-tuple-element.38) | copy-start | bytes 1327108

commit v10 on v8

--- a/solution.py
+++ b/solution.py
@@ -185,7 +185,11 @@
         sorted({row_tap for parity in row_source for row_tap in range(3) if parity[row_tap] == offset})
         for offset in range(3)
     ]
-    normed = normalize(frames, norm_gain).reshape(-1, channels)
+    stacked = jnp.concatenate([frames, cache_in], axis=0)
+    stacked = with_halo(stacked, (("space", 1),), 1)
+    extended = stacked[0].reshape(-1, channels)
+    carried = stacked[1:].reshape(2, -1, channels)
+    normed = normalize(extended, norm_gain)
     riders = dict(
         queries=project(normed, w_qkv[:, :channels], b_qkv[:channels]),
         weights=attention_weights(norm_gain, w_qkv, b_qkv),
@@ -203,12 +207,11 @@
     state = fused_attention(queries, chunks[:half], riders["weights"], finish=False)
     mixed = fused_attention(queries, chunks[half:], riders["weights"], state=state)
     hidden = (
-        frames.reshape(-1, channels).astype(jnp.float32)
+        extended.astype(jnp.float32)
         + jnp.dot(mixed, w_proj, preferred_element_type=jnp.float32)
         + riders["b_proj"]
     ).astype(jnp.bfloat16)
     position = lax.axis_index("tm")
-    carried = cache_in.reshape(2, -1, channels)
     near_frame = shifted(hidden, "tm", 1)
     near_frame = jnp.where(position == 0, carried[1], near_frame)
     far_frame = shifted(hidden, "tm", 2)
@@ -221,8 +224,11 @@
     timed = (timed + jnp.dot(hidden, w_time[2], preferred_element_type=jnp.float32)).astype(
         jnp.bfloat16
     )
-    paired = jnp.stack([timed[:, :channels], timed[:, channels:]]).reshape(2, rows, width, channels)
-    padded = with_halo(paired, (("space", 1),), 1)
+    paired = jnp.stack([timed[:, :channels], timed[:, channels:]]).reshape(2, rows + 2, width, channels)
+    place = lax.axis_index("space")
+    line = lax.broadcasted_iota(jnp.int32, (1, rows + 2, 1, 1), 1)
+    outside = ((place == 0) & (line == 0)) | ((place == lax.axis_size("space") - 1) & (line == rows + 1))
+    padded = jnp.where(outside, jnp.zeros_like(paired), paired)
     products = {}
     for offset in range(3):
         taps = tap_lists[offset]

time: 119 us -> 130 us (1.092)
  the two profiles are of different devices: /device:TPU:260 before, /device:TPU:5 now
where the time goes in v10:
time: 130 us; the launch traced here: 129 us
  starting transfers between devices  65.1 us (50%)
  waiting for transfers between devices  29 us (22%)
  Pallas kernels  16.7 us (13%)
  local copies, waits for them, and re-layouts  6.72 us (5%)
  other arithmetic  5.65 us (4%)
  matrix products  4.82 us (4%)
    ppermute x11, starting transfers between devices, moved(): return lax.ppermute(value, 'space', [(s, target(s)) for s in range(count)])  50.3 us
    pallas_call x2, Pallas kernels, fused_attention(): pl.pallas_call(functools.partial(attention_kernel, sizes=sizes, channels=...  16.7 us
    ppermute x11, waiting for transfers between devices, moved(): return lax.ppermute(value, 'space', [(s, target(s)) for s in range(count)])  15.7 us
    ppermute x2, waiting for transfers between devices, shifted(): lax.ppermute(value, axis, [(source, source + steps) for source in range(l...  13.4 us
    ppermute x1, starting transfers between devices, with_halo(): lax.ppermute(lax.slice_in_dim(block, block.shape[dim] - width, None, axis...  8.01 us
    ppermute x2, starting transfers between devices, shifted(): lax.ppermute(value, axis, [(source, source + steps) for source in range(l...  4.88 us
    unnamed x68, local copies, waits for them, and re-layouts  3.5 us
  transfers between devices with their start and end apart: 15, of which 8 were waited for; matrix products, arithmetic and copies ran while one was open for 5% of the time, Pallas kernels for 5%

profile of v10, /device:TPU:5, one launch (start us, length us, event | category | flops | bytes accessed | tf_op | source)
XLA Modules:
  0.0 128.9 jit_solution(6579590675772454159)
XLA Ops:
  0.0 1.1 constant_dynamic-update-slice_fusion.7
  1.1 1.0 constant_dynamic-update-slice_fusion.6
  2.1 8.0 %collective-permute-start.3 = (bf16[3,1,96,384]{3,2,1,0:T(8,128)(2,1)S(1)}, bf16[3,1,96,384]{3,2,1,0:T(8,128)(2,1)S(1)}, u32[]{:S(2)}, u32[]{:S(2)}) collective-permute-start(bf16[3,1,96,384]{3,2,1,0:T(8,128)(2,1)S(1)} %get-tuple-element.53), channel_id=1, source_target_pairs={{0,1},{1,2},{2,3},{3,4},{4,5},{5,6},{6,7},{7,8},{8,9},{9,10},{10,1... | collective-permute-start | bytes 663560 | tf_op jit(solution)/shard_map/ppermute | solution.py:24
  10.2 1.9 %collective-permute-start.4 = (bf16[3,1,96,384]{3,2,1,0:T(8,128)(2,1)S(1)}, bf16[3,1,96,384]{3,2,1,0:T(8,128)(2,1)S(1)}, u32[]{:S(2)}, u32[]{:S(2)}) collective-permute-start(bf16[3,1,96,384]{3,2,1,0:T(8,128)(2,1)S(1)} %get-tuple-element.54), channel_id=1, source_target_pairs={{1,0},{2,1},{3,2},{4,3},{5,4},{6,5},{7,6},{8,7},{9,8},{10,9},{11,1... | collective-permute-start | bytes 663560 | tf_op jit(solution)/shard_map/ppermute | solution.py:27
  12.1 3.5 %collective-permute-start = (bf16[192,384]{1,0:T(8,128)(2,1)S(1)}, bf16[192,384]{1,0:T(8,128)(2,1)S(1)}, u32[]{:S(2)}, u32[]{:S(2)}) collective-permute-start(bf16[192,384]{1,0:T(8,128)(2,1)S(1)} %bitcast.216), channel_id=1, source_target_pairs={{0,2},{1,3},{2,0},{3,1},{4,6},{5,7},{6,4},{7,5},{8,10},{9,11},{10,... | collective-permute-start | bytes 442376 | tf_op jit(solution)/shard_map/ppermute | solution.py:37
  16.1 0.3 copy-done.23
  16.5 0.6 slice_convert_fusion.2
  17.1 0.6 convert_element_type.67
  17.8 0.6 convert_element_type.61
  18.4 1.0 pad_maximum_fusion.2
  19.4 6.0 %collective-permute-done = bf16[192,384]{1,0:T(8,128)(2,1)S(1)} collective-permute-done((bf16[192,384]{1,0:T(8,128)(2,1)S(1)}, bf16[192,384]{1,0:T(8,128)(2,1)S(1)}, u32[]{:S(2)}, u32[]{:S(2)}) %collective-permute-start) | collective-permute-done | bytes 147488 | tf_op jit(solution)/shard_map/ppermute | solution.py:37
  25.4 7.0 %collective-permute-start.1 = (bf16[384,384]{1,0:T(8,128)(2,1)S(1)}, bf16[384,384]{1,0:T(8,128)(2,1)S(1)}, u32[]{:S(2)}, u32[]{:S(2)}) collective-permute-start(bf16[384,384]{1,0:T(8,128)(2,1)S(1)} %pad_maximum_fusion.4), channel_id=1, source_target_pairs={{0,4},{1,5},{2,6},{3,7},{4,8},{5,9},{6,10},{7,11},{8,12},{9,13},{1... | collective-permute-start | bytes 884744 | tf_op jit(solution)/shard_map/ppermute | solution.py:37
  32.5 6.2 %collective-permute-start.2 = (bf16[384,384]{1,0:T(8,128)(2,1)S(1)}, bf16[384,384]{1,0:T(8,128)(2,1)S(1)}, u32[]{:S(2)}, u32[]{:S(2)}) collective-permute-start(bf16[384,384]{1,0:T(8,128)(2,1)S(1)} %pad_maximum_fusion.4), channel_id=1, source_target_pairs={{0,28},{1,29},{2,30},{3,31},{4,0},{5,1},{6,2},{7,3},{8,4},{9,5},{1... | collective-permute-start | bytes 884744 | tf_op jit(solution)/shard_map/ppermute | solution.py:37
  38.8 1.0 fusion.52
  40.2 1.0 fusion.1.refs_0_
  41.2 1.1 collective-permute-done.2
  42.3 1.9 %collective-permute-start.6 = (bf16[384,384]{1,0:T(8,128)(2,1)S(1)}, bf16[384,384]{1,0:T(8,128)(2,1)S(1)}, u32[]{:S(2)}, u32[]{:S(2)}) collective-permute-start(bf16[384,384]{1,0:T(8,128)(2,1)S(1)} %collective-permute-done.1), channel_id=1, source_target_pairs={{0,4},{1,5},{2,6},{3,7},{4,8},{5,9},{6,10},{7,11},{8,12},{9,13},{1... | collective-permute-start | bytes 884744 | tf_op jit(solution)/shard_map/ppermute | solution.py:37
  44.2 5.0 %collective-permute-start.7 = (bf16[384,384]{1,0:T(8,128)(2,1)S(1)}, bf16[384,384]{1,0:T(8,128)(2,1)S(1)}, u32[]{:S(2)}, u32[]{:S(2)}) collective-permute-start(bf16[384,384]{1,0:T(8,128)(2,1)S(1)} %collective-permute-done.2), channel_id=1, source_target_pairs={{0,28},{1,29},{2,30},{3,31},{4,0},{5,1},{6,2},{7,3},{8,4},{9,5},{1... | collective-permute-start | bytes 884744 | tf_op jit(solution)/shard_map/ppermute | solution.py:37
  49.3 2.2 %collective-permute-done.6 = bf16[384,384]{1,0:T(8,128)(2,1)S(1)} collective-permute-done((bf16[384,384]{1,0:T(8,128)(2,1)S(1)}, bf16[384,384]{1,0:T(8,128)(2,1)S(1)}, u32[]{:S(2)}, u32[]{:S(2)}) %collective-permute-start.6) | collective-permute-done | bytes 294944 | tf_op jit(solution)/shard_map/ppermute | solution.py:37
  51.4 1.9 %collective-permute-start.8 = (bf16[384,384]{1,0:T(8,128)(2,1)S(1)}, bf16[384,384]{1,0:T(8,128)(2,1)S(1)}, u32[]{:S(2)}, u32[]{:S(2)}) collective-permute-start(bf16[384,384]{1,0:T(8,128)(2,1)S(1)} %collective-permute-done.6), channel_id=1, source_target_pairs={{0,4},{1,5},{2,6},{3,7},{4,8},{5,9},{6,10},{7,11},{8,12},{9,13},{1... | collective-permute-start | bytes 884744 | tf_op jit(solution)/shard_map/ppermute | solution.py:37
  53.4 4.6 %collective-permute-start.9 = (bf16[384,384]{1,0:T(8,128)(2,1)S(1)}, bf16[384,384]{1,0:T(8,128)(2,1)S(1)}, u32[]{:S(2)}, u32[]{:S(2)}) collective-permute-start(bf16[384,384]{1,0:T(8,128)(2,1)S(1)} %collective-permute-done.7), channel_id=1, source_target_pairs={{0,28},{1,29},{2,30},{3,31},{4,0},{5,1},{6,2},{7,3},{8,4},{9,5},{1... | collective-permute-start | bytes 884744 | tf_op jit(solution)/shard_map/ppermute | solution.py:37
  58.1 2.9 %collective-permute-done.8 = bf16[384,384]{1,0:T(8,128)(2,1)S(1)} collective-permute-done((bf16[384,384]{1,0:T(8,128)(2,1)S(1)}, bf16[384,384]{1,0:T(8,128)(2,1)S(1)}, u32[]{:S(2)}, u32[]{:S(2)}) %collective-permute-start.8) | collective-permute-done | bytes 294944 | tf_op jit(solution)/shard_map/ppermute | solution.py:37
  61.0 1.9 %collective-permute-start.10 = (bf16[192,384]{1,0:T(8,128)(2,1)S(1)}, bf16[192,384]{1,0:T(8,128)(2,1)S(1)}, u32[]{:S(2)}, u32[]{:S(2)}) collective-permute-start(bf16[192,384]{1,0:T(8,128)(2,1)S(1)} %slice.205), channel_id=1, source_target_pairs={{0,4},{1,5},{2,6},{3,7},{4,8},{5,9},{6,10},{7,11},{8,12},{9,13},{1... | collective-permute-start | bytes 442376 | tf_op jit(solution)/shard_map/ppermute | solution.py:37
  63.0 4.8 %collective-permute-start.11 = (bf16[192,384]{1,0:T(8,128)(2,1)S(1)}, bf16[192,384]{1,0:T(8,128)(2,1)S(1)}, u32[]{:S(2)}, u32[]{:S(2)}) collective-permute-start(bf16[192,384]{1,0:T(8,128)(2,1)S(1)} %slice.206), channel_id=1, source_target_pairs={{0,28},{1,29},{2,30},{3,31},{4,0},{5,1},{6,2},{7,3},{8,4},{9,5},{1... | collective-permute-start | bytes 442376 | tf_op jit(solution)/shard_map/ppermute | solution.py:37
  67.9 2.1 %collective-permute-done.10 = bf16[192,384]{1,0:T(8,128)(2,1)S(1)} collective-permute-done((bf16[192,384]{1,0:T(8,128)(2,1)S(1)}, bf16[192,384]{1,0:T(8,128)(2,1)S(1)}, u32[]{:S(2)}, u32[]{:S(2)}) %collective-permute-start.10) | collective-permute-done | bytes 147488 | tf_op jit(solution)/shard_map/ppermute | solution.py:37
  70.0 1.4 %collective-permute-done.11 = bf16[192,384]{1,0:T(8,128)(2,1)S(1)} collective-permute-done((bf16[192,384]{1,0:T(8,128)(2,1)S(1)}, bf16[192,384]{1,0:T(8,128)(2,1)S(1)}, u32[]{:S(2)}, u32[]{:S(2)}) %collective-permute-start.11) | collective-permute-done | bytes 147488 | tf_op jit(solution)/shard_map/ppermute | solution.py:37
  71.5 11.3 %collective-permute-start.12 = (bf16[1920,384]{1,0:T(8,128)(2,1)S(1)}, bf16[1920,384]{1,0:T(8,128)(2,1)}, u32[]{:S(2)}, u32[]{:S(2)}) collective-permute-start(bf16[1920,384]{1,0:T(8,128)(2,1)S(1)} %constant_dynamic-update-slice_fusion.8.refs_5_), channel_id=1, source_target_pairs={{0,1},{1,0},{2,3},{3,2},{4,5},{5,4},{6,7},{7,6},{8,9},{9,8},{10,11... | collective-permute-start | bytes 4423688 | tf_op jit(solution)/shard_map/ppermute | solution.py:37
  82.9 2.1 %collective-permute-start.5 = (bf16[1152,384]{1,0:T(8,128)(2,1)S(1)}, bf16[1152,384]{1,0:T(8,128)(2,1)}, u32[]{:S(2)}, u32[]{:S(2)}) collective-permute-start(bf16[1152,384]{1,0:T(8,128)(2,1)S(1)} %pad_maximum_fusion.1.refs_4_), channel_id=1, source_target_pairs={{0,1},{1,0},{2,3},{3,2},{4,5},{5,4},{6,7},{7,6},{8,9},{9,8},{10,11... | collective-permute-start | bytes 2654216 | tf_op jit(solution)/shard_map/ppermute | solution.py:37
  85.0 6.8 %shard_map.109 = (f32[384,1]{1,0:T(8,128)S(1)}, f32[384,1]{1,0:T(8,128)S(1)}, f32[384,384]{1,0:T(8,128)S(1)}) custom-call(bf16[384,384]{1,0:T(8,128)(2,1)S(1)} %fusion.1.refs_0_, f32[1,384]{1,0:T(1,128)S(1)} %broadcast_in_dim.12.refs_1_, bf16[384,768]{1,0:T(8,128)(2,1)S(1)} %slice.167.refs_2_, f32[1,768]{1,0:T(1,128)S(1)} %reshape.161.refs_3_, ...), custom_call_target="tpu_custom_call" | custom-call | flops 3623878656 | bytes 3538944 | tf_op jit(solution)/shard_map/pallas_call | solution.py:160
  91.9 9.9 %shard_map.110 = bf16[384,384]{1,0:T(8,128)(2,1)S(1)} custom-call(bf16[384,384]{1,0:T(8,128)(2,1)S(1)} %fusion.1.refs_0_, f32[1,384]{1,0:T(1,128)S(1)} %broadcast_in_dim.12.refs_1_, bf16[384,768]{1,0:T(8,128)(2,1)S(1)} %slice.167.refs_2_, f32[1,768]{1,0:T(1,128)S(1)} %reshape.161.refs_3_, bf16[1152,384]{1,0:T(8,128)(2,1)} %collective-permute-done.5.refs_4_, ...), custom_call_target="tpu_custom_call" | custom-call | flops 3623878656 | bytes 3538944 | tf_op jit(solution)/shard_map/pallas_call | solution.py:160
  101.8 0.3 fusion.2
  102.2 2.1 %collective-permute-start.13 = (bf16[384,384]{1,0:T(8,128)(2,1)S(1)}, bf16[384,384]{1,0:T(8,128)(2,1)S(1)}, u32[]{:S(2)}, u32[]{:S(2)}) collective-permute-start(bf16[384,384]{1,0:T(8,128)(2,1)S(1)} %fusion.2), channel_id=1, source_target_pairs={{0,64},{32,96},{64,128},{96,160},{128,192},{160,224},{192,256},{22... | collective-permute-start | bytes 884744 | tf_op jit(solution)/shard_map/ppermute | solution.py:16
  104.2 2.8 %collective-permute-start.14 = (bf16[384,384]{1,0:T(8,128)(2,1)S(1)}, bf16[384,384]{1,0:T(8,128)(2,1)S(1)}, u32[]{:S(2)}, u32[]{:S(2)}) collective-permute-start(bf16[384,384]{1,0:T(8,128)(2,1)S(1)} %fusion.2), channel_id=1, source_target_pairs={{0,32},{32,64},{64,96},{96,128},{128,160},{160,192},{192,224},{224... | collective-permute-start | bytes 884744 | tf_op jit(solution)/shard_map/ppermute | solution.py:16
  107.1 0.5 fusion.3
  107.6 6.2 %collective-permute-done.13 = bf16[384,384]{1,0:T(8,128)(2,1)S(1)} collective-permute-done((bf16[384,384]{1,0:T(8,128)(2,1)S(1)}, bf16[384,384]{1,0:T(8,128)(2,1)S(1)}, u32[]{:S(2)}, u32[]{:S(2)}) %collective-permute-start.13) | collective-permute-done | bytes 294944 | tf_op jit(solution)/shard_map/ppermute | solution.py:16
  113.8 7.1 %collective-permute-done.14 = bf16[384,384]{1,0:T(8,128)(2,1)S(1)} collective-permute-done((bf16[384,384]{1,0:T(8,128)(2,1)S(1)}, bf16[384,384]{1,0:T(8,128)(2,1)S(1)}, u32[]{:S(2)}, u32[]{:S(2)}) %collective-permute-start.14) | collective-permute-done | bytes 294944 | tf_op jit(solution)/shard_map/ppermute | solution.py:16
  121.1 0.5 fusion.9
  121.6 0.5 add_convert_fusion
  122.3 0.8 copy-done.5
  123.1 0.5 fusion.41
  123.6 0.5 fusion.43
  124.1 0.8 copy-done.8
  124.9 1.1 fusion.42
  126.1 0.2 fusion.49
  126.4 0.4 fusion.47
  126.9 0.2 maximum_maximum_fusion
  127.1 0.8 copy.40
  127.9 1.0 copy.41
  (96 shorter events, 2.1 us)
Async XLA Ops:
  0.0 101.8 %copy-start = (bf16[384,384]{1,0:T(8,128)(2,1)S(1)}, bf16[384,384]{1,0:T(8,128)(2,1)}, u32[]{:S(2)}) copy-start(bf16[384,384]{1,0:T(8,128)(2,1)} %param.16) | copy-start | bytes 884740
  0.0 12.1 %copy-start.9 = (bf16[1,2,96,384]{3,2,1,0:T(8,128)(2,1)S(1)}, bf16[1,2,96,384]{3,2,1,0:T(8,128)(2,1)}, u32[]{:S(2)}) copy-start(bf16[1,2,96,384]{3,2,1,0:T(8,128)(2,1)} %param.11) | copy-start | bytes 442372
  0.0 15.6 %copy-start.3 = (bf16[3,3,384,192]{2,3,1,0:T(8,128)(2,1)S(1)}, bf16[3,3,384,192]{2,3,1,0:T(8,128)(2,1)}, u32[]{:S(2)}) copy-start(bf16[3,3,384,192]{2,3,1,0:T(8,128)(2,1)} %param.20) | copy-start | bytes 3981316
  2.1 36.5 %collective-permute-start.3 = (bf16[3,1,96,384]{3,2,1,0:T(8,128)(2,1)S(1)}, bf16[3,1,96,384]{3,2,1,0:T(8,128)(2,1)S(1)}, u32[]{:S(2)}, u32[]{:S(2)}) collective-permute-start(bf16[3,1,96,384]{3,2,1,0:T(8,128)(2,1)S(1)} %get-tuple-element.53), channel_id=1, source_target_pairs={{0,1},{1,2},{2,3},{3,4},{4,5},{5,6},{6,7},{7,8},{8,9},{9,10},{10,1... | collective-permute-start | bytes 663560 | tf_op jit(solution)/shard_map/ppermute | solution.py:24
  10.2 28.5 %collective-permute-start.4 = (bf16[3,1,96,384]{3,2,1,0:T(8,128)(2,1)S(1)}, bf16[3,1,96,384]{3,2,1,0:T(8,128)(2,1)S(1)}, u32[]{:S(2)}, u32[]{:S(2)}) collective-permute-start(bf16[3,1,96,384]{3,2,1,0:T(8,128)(2,1)S(1)} %get-tuple-element.54), channel_id=1, source_target_pairs={{1,0},{2,1},{3,2},{4,3},{5,4},{6,5},{7,6},{8,7},{9,8},{10,9},{11,1... | collective-permute-start | bytes 663560 | tf_op jit(solution)/shard_map/ppermute | solution.py:27
  12.1 13.3 %collective-permute-start = (bf16[192,384]{1,0:T(8,128)(2,1)S(1)}, bf16[192,384]{1,0:T(8,128)(2,1)S(1)}, u32[]{:S(2)}, u32[]{:S(2)}) collective-permute-start(bf16[192,384]{1,0:T(8,128)(2,1)S(1)} %bitcast.216), channel_id=1, source_target_pairs={{0,2},{1,3},{2,0},{3,1},{4,6},{5,7},{6,4},{7,5},{8,10},{9,11},{10,... | collective-permute-start | bytes 442376 | tf_op jit(solution)/shard_map/ppermute | solution.py:37
  15.8 0.7 copy-start.23
  15.8 1.3 %copy-start.22 = (bf16[384]{0:T(512)(128)(2,1)S(1)}, bf16[384]{0:T(512)(128)(2,1)}, u32[]{:S(2)}) copy-start(bf16[384]{0:T(512)(128)(2,1)} %param.13) | copy-start | bytes 2308
  15.8 1.9 %copy-start.15 = (bf16[384,1152]{1,0:T(8,128)(2,1)S(1)}, bf16[384,1152]{1,0:T(8,128)(2,1)}, u32[]{:S(2)}) copy-start(bf16[384,1152]{1,0:T(8,128)(2,1)} %param.14) | copy-start | bytes 2654212
  15.9 1.8 %copy-start.24 = (bf16[768]{0:T(1024)(128)(2,1)S(1)}, bf16[768]{0:T(1024)(128)(2,1)}, u32[]{:S(2)}) copy-start(bf16[768]{0:T(1024)(128)(2,1)} %param.19) | copy-start | bytes 4612
  15.9 1.8 %copy-start.25 = (bf16[384]{0:T(512)(128)(2,1)S(1)}, bf16[384]{0:T(512)(128)(2,1)}, u32[]{:S(2)}) copy-start(bf16[384]{0:T(512)(128)(2,1)} %param.17) | copy-start | bytes 2308
  15.9 2.4 %copy-start.26 = (bf16[192]{0:T(256)(128)(2,1)S(1)}, bf16[192]{0:T(256)(128)(2,1)}, u32[]{:S(2)}) copy-start(bf16[192]{0:T(256)(128)(2,1)} %param.21) | copy-start | bytes 1156
  16.5 1.2 copy-start.7
  25.4 14.4 %copy-start.13 = (bf16[192,384]{1,0:T(8,128)(2,1)}, bf16[192,384]{1,0:T(8,128)(2,1)S(1)}, u32[]{:S(2)}) copy-start(bf16[192,384]{1,0:T(8,128)(2,1)S(1)} %collective-permute-done) | copy-start | bytes 442372
  25.4 15.8 %collective-permute-start.1 = (bf16[384,384]{1,0:T(8,128)(2,1)S(1)}, bf16[384,384]{1,0:T(8,128)(2,1)S(1)}, u32[]{:S(2)}, u32[]{:S(2)}) collective-permute-start(bf16[384,384]{1,0:T(8,128)(2,1)S(1)} %pad_maximum_fusion.4), channel_id=1, source_target_pairs={{0,4},{1,5},{2,6},{3,7},{4,8},{5,9},{6,10},{7,11},{8,12},{9,13},{1... | collective-permute-start | bytes 884744 | tf_op jit(solution)/shard_map/ppermute | solution.py:37
  32.5 9.9 %collective-permute-start.2 = (bf16[384,384]{1,0:T(8,128)(2,1)S(1)}, bf16[384,384]{1,0:T(8,128)(2,1)S(1)}, u32[]{:S(2)}, u32[]{:S(2)}) collective-permute-start(bf16[384,384]{1,0:T(8,128)(2,1)S(1)} %pad_maximum_fusion.4), channel_id=1, source_target_pairs={{0,28},{1,29},{2,30},{3,31},{4,0},{5,1},{6,2},{7,3},{8,4},{9,5},{1... | collective-permute-start | bytes 884744 | tf_op jit(solution)/shard_map/ppermute | solution.py:37
  38.8 1.2 copy-start.21
  39.8 18.2 %copy-start.1 = (f32[1,4,96,384]{3,2,1,0:T(8,128)}, f32[1,4,96,384]{3,2,1,0:T(8,128)S(1)}, u32[]{:S(2)}) copy-start(f32[1,4,96,384]{3,2,1,0:T(8,128)S(1)} %get-tuple-element.50) | copy-start | bytes 1769476
  41.2 12.1 %copy-start.16 = (bf16[384,384]{1,0:T(8,128)(2,1)}, bf16[384,384]{1,0:T(8,128)(2,1)S(1)}, u32[]{:S(2)}) copy-start(bf16[384,384]{1,0:T(8,128)(2,1)S(1)} %collective-permute-done.1) | copy-start | bytes 884740
  42.3 11.1 %copy-start.18 = (bf16[384,384]{1,0:T(8,128)(2,1)}, bf16[384,384]{1,0:T(8,128)(2,1)S(1)}, u32[]{:S(2)}) copy-start(bf16[384,384]{1,0:T(8,128)(2,1)S(1)} %collective-permute-done.2) | copy-start | bytes 884740
  42.3 9.1 %collective-permute-start.6 = (bf16[384,384]{1,0:T(8,128)(2,1)S(1)}, bf16[384,384]{1,0:T(8,128)(2,1)S(1)}, u32[]{:S(2)}, u32[]{:S(2)}) collective-permute-start(bf16[384,384]{1,0:T(8,128)(2,1)S(1)} %collective-permute-done.1), channel_id=1, source_target_pairs={{0,4},{1,5},{2,6},{3,7},{4,8},{5,9},{6,10},{7,11},{8,12},{9,13},{1... | collective-permute-start | bytes 884744 | tf_op jit(solution)/shard_map/ppermute | solution.py:37
  44.2 9.1 %collective-permute-start.7 = (bf16[384,384]{1,0:T(8,128)(2,1)S(1)}, bf16[384,384]{1,0:T(8,128)(2,1)S(1)}, u32[]{:S(2)}, u32[]{:S(2)}) collective-permute-start(bf16[384,384]{1,0:T(8,128)(2,1)S(1)} %collective-permute-done.2), channel_id=1, source_target_pairs={{0,28},{1,29},{2,30},{3,31},{4,0},{5,1},{6,2},{7,3},{8,4},{9,5},{1... | collective-permute-start | bytes 884744 | tf_op jit(solution)/shard_map/ppermute | solution.py:37
  51.4 9.6 %collective-permute-start.8 = (bf16[384,384]{1,0:T(8,128)(2,1)S(1)}, bf16[384,384]{1,0:T(8,128)(2,1)S(1)}, u32[]{:S(2)}, u32[]{:S(2)}) collective-permute-start(bf16[384,384]{1,0:T(8,128)(2,1)S(1)} %collective-permute-done.6), channel_id=1, source_target_pairs={{0,4},{1,5},{2,6},{3,7},{4,8},{5,9},{6,10},{7,11},{8,12},{9,13},{1... | collective-permute-start | bytes 884744 | tf_op jit(solution)/shard_map/ppermute | solution.py:37
  53.4 9.6 %collective-permute-start.9 = (bf16[384,384]{1,0:T(8,128)(2,1)S(1)}, bf16[384,384]{1,0:T(8,128)(2,1)S(1)}, u32[]{:S(2)}, u32[]{:S(2)}) collective-permute-start(bf16[384,384]{1,0:T(8,128)(2,1)S(1)} %collective-permute-done.7), channel_id=1, source_target_pairs={{0,28},{1,29},{2,30},{3,31},{4,0},{5,1},{6,2},{7,3},{8,4},{9,5},{1... | collective-permute-start | bytes 884744 | tf_op jit(solution)/shard_map/ppermute | solution.py:37
  58.1 24.7 %copy-start.10 = (bf16[1,2,96,384]{3,2,1,0:T(8,128)(2,1)S(1)}, bf16[1,2,96,384]{3,2,1,0:T(8,128)(2,1)}, u32[]{:S(2)}) copy-start(bf16[1,2,96,384]{3,2,1,0:T(8,128)(2,1)} %param.11) | copy-start | bytes 442372
  58.1 24.7 %copy-start.14 = (bf16[192,384]{1,0:T(8,128)(2,1)S(1)}, bf16[192,384]{1,0:T(8,128)(2,1)}, u32[]{:S(2)}) copy-start(bf16[192,384]{1,0:T(8,128)(2,1)} %copy-done.13) | copy-start | bytes 442372
  58.1 24.7 %copy-start.17 = (bf16[384,384]{1,0:T(8,128)(2,1)S(1)}, bf16[384,384]{1,0:T(8,128)(2,1)}, u32[]{:S(2)}) copy-start(bf16[384,384]{1,0:T(8,128)(2,1)} %copy-done.16) | copy-start | bytes 884740
  58.1 24.7 %copy-start.19 = (bf16[384,384]{1,0:T(8,128)(2,1)S(1)}, bf16[384,384]{1,0:T(8,128)(2,1)}, u32[]{:S(2)}) copy-start(bf16[384,384]{1,0:T(8,128)(2,1)} %copy-done.18) | copy-start | bytes 884740
  61.0 9.0 %collective-permute-start.10 = (bf16[192,384]{1,0:T(8,128)(2,1)S(1)}, bf16[192,384]{1,0:T(8,128)(2,1)S(1)}, u32[]{:S(2)}, u32[]{:S(2)}) collective-permute-start(bf16[192,384]{1,0:T(8,128)(2,1)S(1)} %slice.205), channel_id=1, source_target_pairs={{0,4},{1,5},{2,6},{3,7},{4,8},{5,9},{6,10},{7,11},{8,12},{9,13},{1... | collective-permute-start | bytes 442376 | tf_op jit(solution)/shard_map/ppermute | solution.py:37
  63.0 8.5 %collective-permute-start.11 = (bf16[192,384]{1,0:T(8,128)(2,1)S(1)}, bf16[192,384]{1,0:T(8,128)(2,1)S(1)}, u32[]{:S(2)}, u32[]{:S(2)}) collective-permute-start(bf16[192,384]{1,0:T(8,128)(2,1)S(1)} %slice.206), channel_id=1, source_target_pairs={{0,28},{1,29},{2,30},{3,31},{4,0},{5,1},{6,2},{7,3},{8,4},{9,5},{1... | collective-permute-start | bytes 442376 | tf_op jit(solution)/shard_map/ppermute | solution.py:37
  71.5 20.4 %collective-permute-start.12 = (bf16[1920,384]{1,0:T(8,128)(2,1)S(1)}, bf16[1920,384]{1,0:T(8,128)(2,1)}, u32[]{:S(2)}, u32[]{:S(2)}) collective-permute-start(bf16[1920,384]{1,0:T(8,128)(2,1)S(1)} %constant_dynamic-update-slice_fusion.8.refs_5_), channel_id=1, source_target_pairs={{0,1},{1,0},{2,3},{3,2},{4,5},{5,4},{6,7},{7,6},{8,9},{9,8},{10,11... | collective-permute-start | bytes 4423688 | tf_op jit(solution)/shard_map/ppermute | solution.py:37
  82.9 8.9 %collective-permute-start.5 = (bf16[1152,384]{1,0:T(8,128)(2,1)S(1)}, bf16[1152,384]{1,0:T(8,128)(2,1)}, u32[]{:S(2)}, u32[]{:S(2)}) collective-permute-start(bf16[1152,384]{1,0:T(8,128)(2,1)S(1)} %pad_maximum_fusion.1.refs_4_), channel_id=1, source_target_pairs={{0,1},{1,0},{2,3},{3,2},{4,5},{5,4},{6,7},{7,6},{8,9},{9,8},{10,11... | collective-permute-start | bytes 2654216 | tf_op jit(solution)/shard_map/ppermute | solution.py:37
  91.8 10.0 %copy-start.2 = (f32[1,4,96,384]{3,2,1,0:T(8,128)S(1)}, f32[1,4,96,384]{3,2,1,0:T(8,128)}, u32[]{:S(2)}) copy-start(f32[1,4,96,384]{3,2,1,0:T(8,128)} %copy-done.1) | copy-start | bytes 1769476
  91.8 10.0 %copy-start.20 = (f32[384]{0:T(512)S(1)}, f32[384]{0:T(512)}, u32[]{:S(2)}) copy-start(f32[384]{0:T(512)} %convert_element_type.61) | copy-start | bytes 4612
  91.9 15.2 %copy-start.6 = (bf16[3,384,768]{2,1,0:T(8,128)(2,1)S(1)}, bf16[3,384,768]{2,1,0:T(8,128)(2,1)}, u32[]{:S(2)}) copy-start(bf16[3,384,768]{2,1,0:T(8,128)(2,1)} %param.18) | copy-start | bytes 5308420
  102.1 18.8 %copy-start.11 = (bf16[1,4,96,384]{3,2,1,0:T(8,128)(2,1)S(1)}, bf16[1,4,96,384]{3,2,1,0:T(8,128)(2,1)}, u32[]{:S(2)}) copy-start(bf16[1,4,96,384]{3,2,1,0:T(8,128)(2,1)} %get-tuple-element.48) | copy-start | bytes 884740
  102.2 18.8 %copy-start.12 = (bf16[1,4,96,384]{3,2,1,0:T(8,128)(2,1)S(1)}, bf16[1,4,96,384]{3,2,1,0:T(8,128)(2,1)}, u32[]{:S(2)}) copy-start(bf16[1,4,96,384]{3,2,1,0:T(8,128)(2,1)} %get-tuple-element.49) | copy-start | bytes 884740
  102.2 11.6 %collective-permute-start.13 = (bf16[384,384]{1,0:T(8,128)(2,1)S(1)}, bf16[384,384]{1,0:T(8,128)(2,1)S(1)}, u32[]{:S(2)}, u32[]{:S(2)}) collective-permute-start(bf16[384,384]{1,0:T(8,128)(2,1)S(1)} %fusion.2), channel_id=1, source_target_pairs={{0,64},{32,96},{64,128},{96,160},{128,192},{160,224},{192,256},{22... | collective-permute-start | bytes 884744 | tf_op jit(solution)/shard_map/ppermute | solution.py:16
  104.2 16.7 %collective-permute-start.14 = (bf16[384,384]{1,0:T(8,128)(2,1)S(1)}, bf16[384,384]{1,0:T(8,128)(2,1)S(1)}, u32[]{:S(2)}, u32[]{:S(2)}) collective-permute-start(bf16[384,384]{1,0:T(8,128)(2,1)S(1)} %fusion.2), channel_id=1, source_target_pairs={{0,32},{32,64},{64,96},{96,128},{128,160},{160,192},{192,224},{224... | collective-permute-start | bytes 884744 | tf_op jit(solution)/shard_map/ppermute | solution.py:16
  122.1 1.0 copy-start.5
  122.1 1.4 %copy-start.4 = (bf16[384,576]{0,1:T(8,128)(2,1)S(1)}, bf16[384,576]{0,1:T(8,128)(2,1)}, u32[]{:S(2)}) copy-start(bf16[384,576]{0,1:T(8,128)(2,1)} %get-tuple-element.32) | copy-start | bytes 1327108
  123.6 1.3 %copy-start.8 = (bf16[384,1728]{0,1:T(8,128)(2,1)S(1)}, bf16[384,1728]{0,1:T(8,128)(2,1)}, u32[]{:S(2)}) copy-start(bf16[384,1728]{0,1:T(8,128)(2,1)} %copy-done.7) | copy-start | bytes 3981316

commit v11 on v8

--- a/solution.py
+++ b/solution.py
@@ -84,7 +84,7 @@
     )
     return (new_best, mass, total_sum)
 
-BLOCK = 768
+BLOCK = 1152
 
 
 def attention_kernel(*refs, sizes, channels, resume, finish):
@@ -104,8 +104,10 @@
         mass = jnp.zeros((count, 1), jnp.float32)
         total = jnp.zeros((count, channels), jnp.float32)
     for chunk_ref, size in zip(chunk_refs, sizes):
-        for start in range(0, size, BLOCK):
-            rows = chunk_ref[start:min(start + BLOCK, size), :].astype(jnp.float32)
+        pieces = -(-size // BLOCK)
+        step = size // pieces
+        for start in range(0, size, step):
+            rows = chunk_ref[start:start + step, :].astype(jnp.float32)
             inverse = lax.rsqrt(jnp.mean(rows * rows, axis=-1, keepdims=True) + EPSILON)
             normed = (rows * inverse * gain).astype(jnp.bfloat16)
             both = (jnp.dot(normed, wkv, preferred_element_type=jnp.float32) + bkv).astype(jnp.bfloat16)

time: 119 us -> 118 us (level)
  Pallas kernels: 13.2 us -> 12 us
    pallas_call x2, Pallas kernels: 13.2 us -> 12 us  [fused_attention(): pl.pallas_call(functools.partial(attention_kernel, sizes=sizes, channels=...]
  transfers between devices with their start and end apart: 15 -> 15, of which waited for: 10 -> 10; matrix products, arithmetic and copies ran while one was open for 6% -> 6% of each run, Pallas kernels for 5% -> 4%
where the time goes in v11:
time: 118 us; the launch traced here: 117 us
  starting transfers between devices  66.3 us (56%)
  waiting for transfers between devices  26.8 us (23%)
  Pallas kernels  12 us (10%)
  local copies, waits for them, and re-layouts  5.05 us (4%)
  matrix products  3.49 us (3%)
  other arithmetic  3.13 us (3%)
    ppermute x11, starting transfers between devices, moved(): return lax.ppermute(value, 'space', [(s, target(s)) for s in range(count)])  40.6 us
    ppermute x11, waiting for transfers between devices, moved(): return lax.ppermute(value, 'space', [(s, target(s)) for s in range(count)])  13.9 us
    ppermute x1, starting transfers between devices, with_halo(): lax.ppermute(lax.slice_in_dim(block, 0, width, axis=dim), axis, backward)  12.7 us
    pallas_call x2, Pallas kernels, fused_attention(): pl.pallas_call(functools.partial(attention_kernel, sizes=sizes, channels=...  12 us
    ppermute x2, starting transfers between devices, shifted(): lax.ppermute(value, axis, [(source, source + steps) for source in range(l...  10.9 us
    ppermute x1, waiting for transfers between devices, with_halo(): lax.ppermute(lax.slice_in_dim(block, block.shape[dim] - width, None, axis...  7.45 us
    ppermute x2, waiting for transfers between devices, shifted(): lax.ppermute(value, axis, [(source, source + steps) for source in range(l...  3.03 us
    ppermute x1, waiting for transfers between devices, with_halo(): lax.ppermute(lax.slice_in_dim(block, 0, width, axis=dim), axis, backward)  2.38 us
  transfers between devices with their start and end apart: 15, of which 10 were waited for; matrix products, arithmetic and copies ran while one was open for 6% of the time, Pallas kernels for 4%

profile of v11, /device:TPU:260, one launch (start us, length us, event | category | flops | bytes accessed | tf_op | source)
XLA Modules:
  0.0 117.4 jit_solution(9972451416162019089)
XLA Ops:
  0.0 7.9 %collective-permute-start = (bf16[192,384]{1,0:T(8,128)(2,1)}, bf16[192,384]{1,0:T(8,128)(2,1)S(1)}, u32[]{:S(2)}, u32[]{:S(2)}) collective-permute-start(bf16[192,384]{1,0:T(8,128)(2,1)} %bitcast.214), channel_id=1, source_target_pairs={{0,2},{1,3},{2,0},{3,1},{4,6},{5,7},{6,4},{7,5},{8,10},{9,11},{10,... | collective-permute-start | bytes 442376 | tf_op jit(solution)/shard_map/ppermute | solution.py:37
  7.9 1.3 %slice_bitcast_fusion.11 = (bf16[384,192]{0,1:T(8,128)(2,1)S(1)}, bf16[384,192]{0,1:T(8,128)(2,1)S(1)}, bf16[384,192]{0,1:T(8,128)(2,1)S(1)}, bf16[384,192]{0,1:...) fusion(bf16[3,3,384,192]{2,3,1,0:T(8,128)(2,1)} %param.20), kind=kLoop, calls=%fused_computation.100 | loop fusion | bytes 1769472 | tf_op jit(solution)/shard_map/squeeze | solution.py:195
  9.3 0.1 fusion.37
  9.7 0.2 copy-done.10
  10.1 1.9 %collective-permute-done = bf16[192,384]{1,0:T(8,128)(2,1)S(1)} collective-permute-done((bf16[192,384]{1,0:T(8,128)(2,1)}, bf16[192,384]{1,0:T(8,128)(2,1)S(1)}, u32[]{:S(2)}, u32[]{:S(2)}) %collective-permute-start) | collective-permute-done | bytes 147488 | tf_op jit(solution)/shard_map/ppermute | solution.py:37
  12.1 3.4 %collective-permute-start.1 = (bf16[384,384]{1,0:T(8,128)(2,1)S(1)}, bf16[384,384]{1,0:T(8,128)(2,1)S(1)}, u32[]{:S(2)}, u32[]{:S(2)}) collective-permute-start(bf16[384,384]{1,0:T(8,128)(2,1)S(1)} %pad_maximum_fusion.10), channel_id=1, source_target_pairs={{0,4},{1,5},{2,6},{3,7},{4,8},{5,9},{6,10},{7,11},{8,12},{9,13},{1... | collective-permute-start | bytes 884744 | tf_op jit(solution)/shard_map/ppermute | solution.py:37
  15.4 3.7 %collective-permute-start.2 = (bf16[384,384]{1,0:T(8,128)(2,1)S(1)}, bf16[384,384]{1,0:T(8,128)(2,1)S(1)}, u32[]{:S(2)}, u32[]{:S(2)}) collective-permute-start(bf16[384,384]{1,0:T(8,128)(2,1)S(1)} %pad_maximum_fusion.10), channel_id=1, source_target_pairs={{0,28},{1,29},{2,30},{3,31},{4,0},{5,1},{6,2},{7,3},{8,4},{9,5},{1... | collective-permute-start | bytes 884744 | tf_op jit(solution)/shard_map/ppermute | solution.py:37
  19.2 1.0 pad_maximum_fusion.1
  20.3 0.6 convert_element_type.57
  20.9 0.2 fusion.1.refs_0_
  21.1 2.0 %collective-permute-done.1 = bf16[384,384]{1,0:T(8,128)(2,1)S(1)} collective-permute-done((bf16[384,384]{1,0:T(8,128)(2,1)S(1)}, bf16[384,384]{1,0:T(8,128)(2,1)S(1)}, u32[]{:S(2)}, u32[]{:S(2)}) %collective-permute-start.1) | collective-permute-done | bytes 294944 | tf_op jit(solution)/shard_map/ppermute | solution.py:37
  23.1 1.9 %collective-permute-done.2 = bf16[384,384]{1,0:T(8,128)(2,1)S(1)} collective-permute-done((bf16[384,384]{1,0:T(8,128)(2,1)S(1)}, bf16[384,384]{1,0:T(8,128)(2,1)S(1)}, u32[]{:S(2)}, u32[]{:S(2)}) %collective-permute-start.2) | collective-permute-done | bytes 294944 | tf_op jit(solution)/shard_map/ppermute | solution.py:37
  25.0 3.4 %collective-permute-start.4 = (bf16[384,384]{1,0:T(8,128)(2,1)S(1)}, bf16[384,384]{1,0:T(8,128)(2,1)S(1)}, u32[]{:S(2)}, u32[]{:S(2)}) collective-permute-start(bf16[384,384]{1,0:T(8,128)(2,1)S(1)} %collective-permute-done.1), channel_id=1, source_target_pairs={{0,4},{1,5},{2,6},{3,7},{4,8},{5,9},{6,10},{7,11},{8,12},{9,13},{1... | collective-permute-start | bytes 884744 | tf_op jit(solution)/shard_map/ppermute | solution.py:37
  28.4 3.7 %collective-permute-start.5 = (bf16[384,384]{1,0:T(8,128)(2,1)S(1)}, bf16[384,384]{1,0:T(8,128)(2,1)S(1)}, u32[]{:S(2)}, u32[]{:S(2)}) collective-permute-start(bf16[384,384]{1,0:T(8,128)(2,1)S(1)} %collective-permute-done.2), channel_id=1, source_target_pairs={{0,28},{1,29},{2,30},{3,31},{4,0},{5,1},{6,2},{7,3},{8,4},{9,5},{1... | collective-permute-start | bytes 884744 | tf_op jit(solution)/shard_map/ppermute | solution.py:37
  32.1 2.9 %collective-permute-done.4 = bf16[384,384]{1,0:T(8,128)(2,1)S(1)} collective-permute-done((bf16[384,384]{1,0:T(8,128)(2,1)S(1)}, bf16[384,384]{1,0:T(8,128)(2,1)S(1)}, u32[]{:S(2)}, u32[]{:S(2)}) %collective-permute-start.4) | collective-permute-done | bytes 294944 | tf_op jit(solution)/shard_map/ppermute | solution.py:37
  35.0 2.1 %collective-permute-start.6 = (bf16[384,384]{1,0:T(8,128)(2,1)S(1)}, bf16[384,384]{1,0:T(8,128)(2,1)S(1)}, u32[]{:S(2)}, u32[]{:S(2)}) collective-permute-start(bf16[384,384]{1,0:T(8,128)(2,1)S(1)} %collective-permute-done.4), channel_id=1, source_target_pairs={{0,4},{1,5},{2,6},{3,7},{4,8},{5,9},{6,10},{7,11},{8,12},{9,13},{1... | collective-permute-start | bytes 884744 | tf_op jit(solution)/shard_map/ppermute | solution.py:37
  37.1 4.9 %collective-permute-start.7 = (bf16[384,384]{1,0:T(8,128)(2,1)S(1)}, bf16[384,384]{1,0:T(8,128)(2,1)S(1)}, u32[]{:S(2)}, u32[]{:S(2)}) collective-permute-start(bf16[384,384]{1,0:T(8,128)(2,1)S(1)} %collective-permute-done.5), channel_id=1, source_target_pairs={{0,28},{1,29},{2,30},{3,31},{4,0},{5,1},{6,2},{7,3},{8,4},{9,5},{1... | collective-permute-start | bytes 884744 | tf_op jit(solution)/shard_map/ppermute | solution.py:37
  42.2 2.7 %collective-permute-done.6 = bf16[384,384]{1,0:T(8,128)(2,1)S(1)} collective-permute-done((bf16[384,384]{1,0:T(8,128)(2,1)S(1)}, bf16[384,384]{1,0:T(8,128)(2,1)S(1)}, u32[]{:S(2)}, u32[]{:S(2)}) %collective-permute-start.6) | collective-permute-done | bytes 294944 | tf_op jit(solution)/shard_map/ppermute | solution.py:37
  44.8 1.9 %collective-permute-start.8 = (bf16[192,384]{1,0:T(8,128)(2,1)S(1)}, bf16[192,384]{1,0:T(8,128)(2,1)S(1)}, u32[]{:S(2)}, u32[]{:S(2)}) collective-permute-start(bf16[192,384]{1,0:T(8,128)(2,1)S(1)} %slice.191), channel_id=1, source_target_pairs={{0,4},{1,5},{2,6},{3,7},{4,8},{5,9},{6,10},{7,11},{8,12},{9,13},{1... | collective-permute-start | bytes 442376 | tf_op jit(solution)/shard_map/ppermute | solution.py:37
  46.8 5.1 %collective-permute-start.9 = (bf16[192,384]{1,0:T(8,128)(2,1)S(1)}, bf16[192,384]{1,0:T(8,128)(2,1)S(1)}, u32[]{:S(2)}, u32[]{:S(2)}) collective-permute-start(bf16[192,384]{1,0:T(8,128)(2,1)S(1)} %slice.192), channel_id=1, source_target_pairs={{0,28},{1,29},{2,30},{3,31},{4,0},{5,1},{6,2},{7,3},{8,4},{9,5},{1... | collective-permute-start | bytes 442376 | tf_op jit(solution)/shard_map/ppermute | solution.py:37
  52.1 1.0 collective-permute-done.8
  53.1 1.5 %collective-permute-done.9 = bf16[192,384]{1,0:T(8,128)(2,1)S(1)} collective-permute-done((bf16[192,384]{1,0:T(8,128)(2,1)S(1)}, bf16[192,384]{1,0:T(8,128)(2,1)S(1)}, u32[]{:S(2)}, u32[]{:S(2)}) %collective-permute-start.9) | collective-permute-done | bytes 147488 | tf_op jit(solution)/shard_map/ppermute | solution.py:37
  54.6 1.9 %collective-permute-start.10 = (bf16[1920,384]{1,0:T(8,128)(2,1)S(1)}, bf16[1920,384]{1,0:T(8,128)(2,1)}, u32[]{:S(2)}, u32[]{:S(2)}) collective-permute-start(bf16[1920,384]{1,0:T(8,128)(2,1)S(1)} %constant_dynamic-update-slice_fusion.6.refs_5_), channel_id=1, source_target_pairs={{0,1},{1,0},{2,3},{3,2},{4,5},{5,4},{6,7},{7,6},{8,9},{9,8},{10,11... | collective-permute-start | bytes 4423688 | tf_op jit(solution)/shard_map/ppermute | solution.py:37
  56.7 2.6 %collective-permute-start.3 = (bf16[1152,384]{1,0:T(8,128)(2,1)S(1)}, bf16[1152,384]{1,0:T(8,128)(2,1)}, u32[]{:S(2)}, u32[]{:S(2)}) collective-permute-start(bf16[1152,384]{1,0:T(8,128)(2,1)S(1)} %pad_maximum_fusion.refs_4_), channel_id=1, source_target_pairs={{0,1},{1,0},{2,3},{3,2},{4,5},{5,4},{6,7},{7,6},{8,9},{9,8},{10,11... | collective-permute-start | bytes 2654216 | tf_op jit(solution)/shard_map/ppermute | solution.py:37
  59.3 1.0 fusion.65
  60.3 5.0 %shard_map.109 = (f32[192,1]{1,0:T(8,128)S(1)}, f32[192,1]{1,0:T(8,128)S(1)}, f32[192,384]{1,0:T(8,128)S(1)}) custom-call(bf16[192,384]{1,0:T(8,128)(2,1)S(1)} %fusion.1.refs_0_, f32[1,384]{1,0:T(1,128)S(1)} %reshape.147.refs_1_, bf16[384,768]{1,0:T(8,128)(2,1)S(1)} %slice.157.refs_2_, f32[1,768]{1,0:T(1,128)S(1)} %reshape.152.refs_3_, ...), custom_call_target="tpu_custom_call" | custom-call | flops 2717908992 | bytes 3244032 | tf_op jit(solution)/shard_map/pallas_call | solution.py:162
  65.3 7.0 %shard_map.110 = bf16[192,384]{1,0:T(8,128)(2,1)S(1)} custom-call(bf16[192,384]{1,0:T(8,128)(2,1)S(1)} %fusion.1.refs_0_, f32[1,384]{1,0:T(1,128)S(1)} %reshape.147.refs_1_, bf16[384,768]{1,0:T(8,128)(2,1)S(1)} %slice.157.refs_2_, f32[1,768]{1,0:T(1,128)S(1)} %reshape.152.refs_3_, bf16[1152,384]{1,0:T(8,128)(2,1)} %collective-permute-done.3.refs_4_, ...), custom_call_target="tpu_custom_call" | custom-call | flops 2717908992 | bytes 3244032 | tf_op jit(solution)/shard_map/pallas_call | solution.py:162
  72.4 0.2 fusion.2
  72.6 6.9 %collective-permute-start.11 = (bf16[192,384]{1,0:T(8,128)(2,1)S(1)}, bf16[192,384]{1,0:T(8,128)(2,1)S(1)}, u32[]{:S(2)}, u32[]{:S(2)}) collective-permute-start(bf16[192,384]{1,0:T(8,128)(2,1)S(1)} %fusion.2), channel_id=1, source_target_pairs={{0,64},{32,96},{64,128},{96,160},{128,192},{160,224},{192,256},{22... | collective-permute-start | bytes 442376 | tf_op jit(solution)/shard_map/ppermute | solution.py:16
  79.5 4.0 %collective-permute-start.12 = (bf16[192,384]{1,0:T(8,128)(2,1)S(1)}, bf16[192,384]{1,0:T(8,128)(2,1)S(1)}, u32[]{:S(2)}, u32[]{:S(2)}) collective-permute-start(bf16[192,384]{1,0:T(8,128)(2,1)S(1)} %fusion.2), channel_id=1, source_target_pairs={{0,32},{32,64},{64,96},{96,128},{128,160},{160,192},{192,224},{224... | collective-permute-start | bytes 442376 | tf_op jit(solution)/shard_map/ppermute | solution.py:16
  83.5 0.3 fusion.3
  83.8 3.0 %collective-permute-done.12 = bf16[192,384]{1,0:T(8,128)(2,1)S(1)} collective-permute-done((bf16[192,384]{1,0:T(8,128)(2,1)S(1)}, bf16[192,384]{1,0:T(8,128)(2,1)S(1)}, u32[]{:S(2)}, u32[]{:S(2)}) %collective-permute-start.12) | collective-permute-done | bytes 147488 | tf_op jit(solution)/shard_map/ppermute | solution.py:16
  86.9 0.3 fusion.7
  87.3 0.3 add_convert_fusion
  87.7 12.7 %collective-permute-start.14 = (bf16[2,1,96,384]{3,2,1,0:T(8,128)(2,1)S(1)}, bf16[2,1,96,384]{3,2,1,0:T(8,128)(2,1)S(1)}, u32[]{:S(2)}, u32[]{:S(2)}) collective-permute-start(bf16[2,1,96,384]{3,2,1,0:T(8,128)(2,1)S(1)} %get-tuple-element.49), channel_id=1, source_target_pairs={{1,0},{2,1},{3,2},{4,3},{5,4},{6,5},{7,6},{8,7},{9,8},{10,9},{11,1... | collective-permute-start | bytes 442376 | tf_op jit(solution)/shard_map/ppermute | solution.py:27
  100.4 2.1 %collective-permute-start.13 = (bf16[2,1,96,384]{3,2,1,0:T(8,128)(2,1)S(1)}, bf16[2,1,96,384]{3,2,1,0:T(8,128)(2,1)S(1)}, u32[]{:S(2)}, u32[]{:S(2)}) collective-permute-start(bf16[2,1,96,384]{3,2,1,0:T(8,128)(2,1)S(1)} %get-tuple-element.48), channel_id=1, source_target_pairs={{0,1},{1,2},{2,3},{3,4},{4,5},{5,6},{6,7},{7,8},{8,9},{9,10},{10,1... | collective-permute-start | bytes 442376 | tf_op jit(solution)/shard_map/ppermute | solution.py:24
  102.6 1.1 fusion.41
  103.7 2.4 %collective-permute-done.14 = bf16[2,1,96,384]{3,2,1,0:T(8,128)(2,1)S(1)} collective-permute-done((bf16[2,1,96,384]{3,2,1,0:T(8,128)(2,1)S(1)}, bf16[2,1,96,384]{3,2,1,0:T(8,128)(2,1)S(1)}, u32[]{:S(2)}, u32[]{:S(2)}) %collective-permute-start.14) | collective-permute-done | bytes 147488 | tf_op jit(solution)/shard_map/ppermute | solution.py:27
  106.1 0.5 fusion.44
  106.6 7.4 %collective-permute-done.13 = bf16[2,1,96,384]{3,2,1,0:T(8,128)(2,1)S(1)} collective-permute-done((bf16[2,1,96,384]{3,2,1,0:T(8,128)(2,1)S(1)}, bf16[2,1,96,384]{3,2,1,0:T(8,128)(2,1)S(1)}, u32[]{:S(2)}, u32[]{:S(2)}) %collective-permute-start.13) | collective-permute-done | bytes 147488 | tf_op jit(solution)/shard_map/ppermute | solution.py:24
  114.0 0.5 fusion.48
  114.5 0.1 fusion.35
  114.6 0.2 fusion.55
  114.8 0.4 fusion.53
  115.2 0.1 fusion.52
  115.4 0.2 maximum_maximum_fusion
  115.6 0.8 copy.40
  116.4 1.0 copy.41
  (66 shorter events, 1.0 us)
Async XLA Ops:
  0.0 72.3 %copy-start = (bf16[384,384]{1,0:T(8,128)(2,1)S(1)}, bf16[384,384]{1,0:T(8,128)(2,1)}, u32[]{:S(2)}) copy-start(bf16[384,384]{1,0:T(8,128)(2,1)} %param.16) | copy-start | bytes 884740
  0.0 9.3 %copy-start.1 = (bf16[1,2,96,384]{3,2,1,0:T(8,128)(2,1)S(1)}, bf16[1,2,96,384]{3,2,1,0:T(8,128)(2,1)}, u32[]{:S(2)}) copy-start(bf16[1,2,96,384]{3,2,1,0:T(8,128)(2,1)} %param.11) | copy-start | bytes 442372
  0.0 9.2 %copy-start.2 = (bf16[3,3,384,192]{2,3,1,0:T(8,128)(2,1)S(1)}, bf16[3,3,384,192]{2,3,1,0:T(8,128)(2,1)}, u32[]{:S(2)}) copy-start(bf16[3,3,384,192]{2,3,1,0:T(8,128)(2,1)} %param.20) | copy-start | bytes 3981316
  0.0 12.0 %collective-permute-start = (bf16[192,384]{1,0:T(8,128)(2,1)}, bf16[192,384]{1,0:T(8,128)(2,1)S(1)}, u32[]{:S(2)}, u32[]{:S(2)}) collective-permute-start(bf16[192,384]{1,0:T(8,128)(2,1)} %bitcast.214), channel_id=1, source_target_pairs={{0,2},{1,3},{2,0},{3,1},{4,6},{5,7},{6,4},{7,5},{8,10},{9,11},{10,... | collective-permute-start | bytes 442376 | tf_op jit(solution)/shard_map/ppermute | solution.py:37
  9.3 0.7 copy-start.10
  9.3 0.7 copy-start.11
  9.7 10.5 %copy-start.6 = (bf16[384,1728]{0,1:T(8,128)(2,1)}, bf16[384,1728]{0,1:T(8,128)(2,1)S(1)}, u32[]{:S(2)}) copy-start(bf16[384,1728]{0,1:T(8,128)(2,1)S(1)} %constant_dynamic-update-slice_fusion) | copy-start | bytes 3981316
  10.0 10.2 %copy-start.8 = (bf16[384,1152]{1,0:T(8,128)(2,1)S(1)}, bf16[384,1152]{1,0:T(8,128)(2,1)}, u32[]{:S(2)}) copy-start(bf16[384,1152]{1,0:T(8,128)(2,1)} %param.14) | copy-start | bytes 2654212
  12.1 11.1 %collective-permute-start.1 = (bf16[384,384]{1,0:T(8,128)(2,1)S(1)}, bf16[384,384]{1,0:T(8,128)(2,1)S(1)}, u32[]{:S(2)}, u32[]{:S(2)}) collective-permute-start(bf16[384,384]{1,0:T(8,128)(2,1)S(1)} %pad_maximum_fusion.10), channel_id=1, source_target_pairs={{0,4},{1,5},{2,6},{3,7},{4,8},{5,9},{6,10},{7,11},{8,12},{9,13},{1... | collective-permute-start | bytes 884744 | tf_op jit(solution)/shard_map/ppermute | solution.py:37
  15.4 9.6 %collective-permute-start.2 = (bf16[384,384]{1,0:T(8,128)(2,1)S(1)}, bf16[384,384]{1,0:T(8,128)(2,1)S(1)}, u32[]{:S(2)}, u32[]{:S(2)}) collective-permute-start(bf16[384,384]{1,0:T(8,128)(2,1)S(1)} %pad_maximum_fusion.10), channel_id=1, source_target_pairs={{0,28},{1,29},{2,30},{3,31},{4,0},{5,1},{6,2},{7,3},{8,4},{9,5},{1... | collective-permute-start | bytes 884744 | tf_op jit(solution)/shard_map/ppermute | solution.py:37
  19.1 1.1 copy-start.12
  19.1 1.1 copy-start.13
  19.2 1.7 %copy-start.14 = (bf16[192]{0:T(256)(128)(2,1)S(1)}, bf16[192]{0:T(256)(128)(2,1)}, u32[]{:S(2)}) copy-start(bf16[192]{0:T(256)(128)(2,1)} %param.21) | copy-start | bytes 1156
  25.0 10.0 %collective-permute-start.4 = (bf16[384,384]{1,0:T(8,128)(2,1)S(1)}, bf16[384,384]{1,0:T(8,128)(2,1)S(1)}, u32[]{:S(2)}, u32[]{:S(2)}) collective-permute-start(bf16[384,384]{1,0:T(8,128)(2,1)S(1)} %collective-permute-done.1), channel_id=1, source_target_pairs={{0,4},{1,5},{2,6},{3,7},{4,8},{5,9},{6,10},{7,11},{8,12},{9,13},{1... | collective-permute-start | bytes 884744 | tf_op jit(solution)/shard_map/ppermute | solution.py:37
  28.4 8.7 %collective-permute-start.5 = (bf16[384,384]{1,0:T(8,128)(2,1)S(1)}, bf16[384,384]{1,0:T(8,128)(2,1)S(1)}, u32[]{:S(2)}, u32[]{:S(2)}) collective-permute-start(bf16[384,384]{1,0:T(8,128)(2,1)S(1)} %collective-permute-done.2), channel_id=1, source_target_pairs={{0,28},{1,29},{2,30},{3,31},{4,0},{5,1},{6,2},{7,3},{8,4},{9,5},{1... | collective-permute-start | bytes 884744 | tf_op jit(solution)/shard_map/ppermute | solution.py:37
  35.0 9.8 %collective-permute-start.6 = (bf16[384,384]{1,0:T(8,128)(2,1)S(1)}, bf16[384,384]{1,0:T(8,128)(2,1)S(1)}, u32[]{:S(2)}, u32[]{:S(2)}) collective-permute-start(bf16[384,384]{1,0:T(8,128)(2,1)S(1)} %collective-permute-done.4), channel_id=1, source_target_pairs={{0,4},{1,5},{2,6},{3,7},{4,8},{5,9},{6,10},{7,11},{8,12},{9,13},{1... | collective-permute-start | bytes 884744 | tf_op jit(solution)/shard_map/ppermute | solution.py:37
  37.1 9.6 %collective-permute-start.7 = (bf16[384,384]{1,0:T(8,128)(2,1)S(1)}, bf16[384,384]{1,0:T(8,128)(2,1)S(1)}, u32[]{:S(2)}, u32[]{:S(2)}) collective-permute-start(bf16[384,384]{1,0:T(8,128)(2,1)S(1)} %collective-permute-done.5), channel_id=1, source_target_pairs={{0,28},{1,29},{2,30},{3,31},{4,0},{5,1},{6,2},{7,3},{8,4},{9,5},{1... | collective-permute-start | bytes 884744 | tf_op jit(solution)/shard_map/ppermute | solution.py:37
  44.8 8.2 %collective-permute-start.8 = (bf16[192,384]{1,0:T(8,128)(2,1)S(1)}, bf16[192,384]{1,0:T(8,128)(2,1)S(1)}, u32[]{:S(2)}, u32[]{:S(2)}) collective-permute-start(bf16[192,384]{1,0:T(8,128)(2,1)S(1)} %slice.191), channel_id=1, source_target_pairs={{0,4},{1,5},{2,6},{3,7},{4,8},{5,9},{6,10},{7,11},{8,12},{9,13},{1... | collective-permute-start | bytes 442376 | tf_op jit(solution)/shard_map/ppermute | solution.py:37
  46.8 7.8 %collective-permute-start.9 = (bf16[192,384]{1,0:T(8,128)(2,1)S(1)}, bf16[192,384]{1,0:T(8,128)(2,1)S(1)}, u32[]{:S(2)}, u32[]{:S(2)}) collective-permute-start(bf16[192,384]{1,0:T(8,128)(2,1)S(1)} %slice.192), channel_id=1, source_target_pairs={{0,28},{1,29},{2,30},{3,31},{4,0},{5,1},{6,2},{7,3},{8,4},{9,5},{1... | collective-permute-start | bytes 442376 | tf_op jit(solution)/shard_map/ppermute | solution.py:37
  54.6 10.6 %collective-permute-start.10 = (bf16[1920,384]{1,0:T(8,128)(2,1)S(1)}, bf16[1920,384]{1,0:T(8,128)(2,1)}, u32[]{:S(2)}, u32[]{:S(2)}) collective-permute-start(bf16[1920,384]{1,0:T(8,128)(2,1)S(1)} %constant_dynamic-update-slice_fusion.6.refs_5_), channel_id=1, source_target_pairs={{0,1},{1,0},{2,3},{3,2},{4,5},{5,4},{6,7},{7,6},{8,9},{9,8},{10,11... | collective-permute-start | bytes 4423688 | tf_op jit(solution)/shard_map/ppermute | solution.py:37
  56.7 8.6 %collective-permute-start.3 = (bf16[1152,384]{1,0:T(8,128)(2,1)S(1)}, bf16[1152,384]{1,0:T(8,128)(2,1)}, u32[]{:S(2)}, u32[]{:S(2)}) collective-permute-start(bf16[1152,384]{1,0:T(8,128)(2,1)S(1)} %pad_maximum_fusion.refs_4_), channel_id=1, source_target_pairs={{0,1},{1,0},{2,3},{3,2},{4,5},{5,4},{6,7},{7,6},{8,9},{9,8},{10,11... | collective-permute-start | bytes 2654216 | tf_op jit(solution)/shard_map/ppermute | solution.py:37
  65.3 7.1 %copy-start.9 = (f32[384]{0:T(512)S(1)}, f32[384]{0:T(512)}, u32[]{:S(2)}) copy-start(f32[384]{0:T(512)} %convert_element_type.57) | copy-start | bytes 4612
  65.3 18.2 %copy-start.5 = (bf16[3,384,768]{2,1,0:T(8,128)(2,1)S(1)}, bf16[3,384,768]{2,1,0:T(8,128)(2,1)}, u32[]{:S(2)}) copy-start(bf16[3,384,768]{2,1,0:T(8,128)(2,1)} %param.18) | copy-start | bytes 5308420
  72.6 11.2 %collective-permute-start.11 = (bf16[192,384]{1,0:T(8,128)(2,1)S(1)}, bf16[192,384]{1,0:T(8,128)(2,1)S(1)}, u32[]{:S(2)}, u32[]{:S(2)}) collective-permute-start(bf16[192,384]{1,0:T(8,128)(2,1)S(1)} %fusion.2), channel_id=1, source_target_pairs={{0,64},{32,96},{64,128},{96,160},{128,192},{160,224},{192,256},{22... | collective-permute-start | bytes 442376 | tf_op jit(solution)/shard_map/ppermute | solution.py:16
  79.5 7.4 %collective-permute-start.12 = (bf16[192,384]{1,0:T(8,128)(2,1)S(1)}, bf16[192,384]{1,0:T(8,128)(2,1)S(1)}, u32[]{:S(2)}, u32[]{:S(2)}) collective-permute-start(bf16[192,384]{1,0:T(8,128)(2,1)S(1)} %fusion.2), channel_id=1, source_target_pairs={{0,32},{32,64},{64,96},{96,128},{128,160},{160,192},{192,224},{224... | collective-permute-start | bytes 442376 | tf_op jit(solution)/shard_map/ppermute | solution.py:16
  87.3 15.3 %copy-start.7 = (bf16[384,1728]{0,1:T(8,128)(2,1)S(1)}, bf16[384,1728]{0,1:T(8,128)(2,1)}, u32[]{:S(2)}) copy-start(bf16[384,1728]{0,1:T(8,128)(2,1)} %copy-done.6) | copy-start | bytes 3981316
  87.7 18.4 %collective-permute-start.14 = (bf16[2,1,96,384]{3,2,1,0:T(8,128)(2,1)S(1)}, bf16[2,1,96,384]{3,2,1,0:T(8,128)(2,1)S(1)}, u32[]{:S(2)}, u32[]{:S(2)}) collective-permute-start(bf16[2,1,96,384]{3,2,1,0:T(8,128)(2,1)S(1)} %get-tuple-element.49), channel_id=1, source_target_pairs={{1,0},{2,1},{3,2},{4,3},{5,4},{6,5},{7,6},{8,7},{9,8},{10,9},{11,1... | collective-permute-start | bytes 442376 | tf_op jit(solution)/shard_map/ppermute | solution.py:27
  100.4 13.6 %collective-permute-start.13 = (bf16[2,1,96,384]{3,2,1,0:T(8,128)(2,1)S(1)}, bf16[2,1,96,384]{3,2,1,0:T(8,128)(2,1)S(1)}, u32[]{:S(2)}, u32[]{:S(2)}) collective-permute-start(bf16[2,1,96,384]{3,2,1,0:T(8,128)(2,1)S(1)} %get-tuple-element.48), channel_id=1, source_target_pairs={{0,1},{1,2},{2,3},{3,4},{4,5},{5,6},{6,7},{7,8},{8,9},{9,10},{10,1... | collective-permute-start | bytes 442376 | tf_op jit(solution)/shard_map/ppermute | solution.py:24
  102.6 3.5 %copy-start.4 = (bf16[384,576]{0,1:T(8,128)(2,1)S(1)}, bf16[384,576]{0,1:T(8,128)(2,1)}, u32[]{:S(2)}) copy-start(bf16[384,576]{0,1:T(8,128)(2,1)} %get-tuple-element.34) | copy-start | bytes 1327108
  103.7 10.3 %copy-start.3 = (bf16[384,576]{0,1:T(8,128)(2,1)S(1)}, bf16[384,576]{0,1:T(8,128)(2,1)}, u32[]{:S(2)}) copy-start(bf16[384,576]{0,1:T(8,128)(2,1)} %get-tuple-element.32) | copy-start | bytes 1327108

commit v12 on v11

--- a/solution.py
+++ b/solution.py
@@ -84,7 +84,7 @@
     )
     return (new_best, mass, total_sum)
 
-BLOCK = 1152
+BLOCK = 1920
 
 
 def attention_kernel(*refs, sizes, channels, resume, finish):

time: 118 us -> 118 us (level)
  no operation moved by 1% of the time
where the time goes in v12:
time: 118 us; the launch traced here: 117 us
  starting transfers between devices  66.3 us (56%)
  waiting for transfers between devices  26.8 us (23%)
  Pallas kernels  11.8 us (10%)
  local copies, waits for them, and re-layouts  5.05 us (4%)
  matrix products  3.49 us (3%)
  other arithmetic  3.13 us (3%)
    ppermute x11, starting transfers between devices, moved(): return lax.ppermute(value, 'space', [(s, target(s)) for s in range(count)])  40.6 us
    ppermute x11, waiting for transfers between devices, moved(): return lax.ppermute(value, 'space', [(s, target(s)) for s in range(count)])  13.9 us
    ppermute x1, starting transfers between devices, with_halo(): lax.ppermute(lax.slice_in_dim(block, 0, width, axis=dim), axis, backward)  12.7 us
    pallas_call x2, Pallas kernels, fused_attention(): pl.pallas_call(functools.partial(attention_kernel, sizes=sizes, channels=...  11.8 us
    ppermute x2, starting transfers between devices, shifted(): lax.ppermute(value, axis, [(source, source + steps) for source in range(l...  10.9 us
    ppermute x1, waiting for transfers between devices, with_halo(): lax.ppermute(lax.slice_in_dim(block, block.shape[dim] - width, None, axis...  7.47 us
    ppermute x2, waiting for transfers between devices, shifted(): lax.ppermute(value, axis, [(source, source + steps) for source in range(l...  3.05 us
  transfers between devices with their start and end apart: 15, of which 10 were waited for; matrix products, arithmetic and copies ran while one was open for 6% of the time, Pallas kernels for 4%

profile of v12, /device:TPU:260, one launch (start us, length us, event | category | flops | bytes accessed | tf_op | source)
XLA Modules:
  0.0 117.2 jit_solution(6653805626335197014)
XLA Ops:
  0.0 7.9 %collective-permute-start = (bf16[192,384]{1,0:T(8,128)(2,1)}, bf16[192,384]{1,0:T(8,128)(2,1)S(1)}, u32[]{:S(2)}, u32[]{:S(2)}) collective-permute-start(bf16[192,384]{1,0:T(8,128)(2,1)} %bitcast.214), channel_id=1, source_target_pairs={{0,2},{1,3},{2,0},{3,1},{4,6},{5,7},{6,4},{7,5},{8,10},{9,11},{10,... | collective-permute-start | bytes 442376 | tf_op jit(solution)/shard_map/ppermute | solution.py:37
  7.9 1.3 %slice_bitcast_fusion.11 = (bf16[384,192]{0,1:T(8,128)(2,1)S(1)}, bf16[384,192]{0,1:T(8,128)(2,1)S(1)}, bf16[384,192]{0,1:T(8,128)(2,1)S(1)}, bf16[384,192]{0,1:...) fusion(bf16[3,3,384,192]{2,3,1,0:T(8,128)(2,1)} %param.20), kind=kLoop, calls=%fused_computation.100 | loop fusion | bytes 1769472 | tf_op jit(solution)/shard_map/squeeze | solution.py:195
  9.3 0.1 fusion.37
  9.7 0.2 copy-done.10
  10.1 1.9 %collective-permute-done = bf16[192,384]{1,0:T(8,128)(2,1)S(1)} collective-permute-done((bf16[192,384]{1,0:T(8,128)(2,1)}, bf16[192,384]{1,0:T(8,128)(2,1)S(1)}, u32[]{:S(2)}, u32[]{:S(2)}) %collective-permute-start) | collective-permute-done | bytes 147488 | tf_op jit(solution)/shard_map/ppermute | solution.py:37
  12.1 3.4 %collective-permute-start.1 = (bf16[384,384]{1,0:T(8,128)(2,1)S(1)}, bf16[384,384]{1,0:T(8,128)(2,1)S(1)}, u32[]{:S(2)}, u32[]{:S(2)}) collective-permute-start(bf16[384,384]{1,0:T(8,128)(2,1)S(1)} %pad_maximum_fusion.10), channel_id=1, source_target_pairs={{0,4},{1,5},{2,6},{3,7},{4,8},{5,9},{6,10},{7,11},{8,12},{9,13},{1... | collective-permute-start | bytes 884744 | tf_op jit(solution)/shard_map/ppermute | solution.py:37
  15.4 3.7 %collective-permute-start.2 = (bf16[384,384]{1,0:T(8,128)(2,1)S(1)}, bf16[384,384]{1,0:T(8,128)(2,1)S(1)}, u32[]{:S(2)}, u32[]{:S(2)}) collective-permute-start(bf16[384,384]{1,0:T(8,128)(2,1)S(1)} %pad_maximum_fusion.10), channel_id=1, source_target_pairs={{0,28},{1,29},{2,30},{3,31},{4,0},{5,1},{6,2},{7,3},{8,4},{9,5},{1... | collective-permute-start | bytes 884744 | tf_op jit(solution)/shard_map/ppermute | solution.py:37
  19.2 1.0 pad_maximum_fusion.1
  20.3 0.6 convert_element_type.57
  20.9 0.2 fusion.1.refs_0_
  21.1 2.0 %collective-permute-done.1 = bf16[384,384]{1,0:T(8,128)(2,1)S(1)} collective-permute-done((bf16[384,384]{1,0:T(8,128)(2,1)S(1)}, bf16[384,384]{1,0:T(8,128)(2,1)S(1)}, u32[]{:S(2)}, u32[]{:S(2)}) %collective-permute-start.1) | collective-permute-done | bytes 294944 | tf_op jit(solution)/shard_map/ppermute | solution.py:37
  23.1 1.9 %collective-permute-done.2 = bf16[384,384]{1,0:T(8,128)(2,1)S(1)} collective-permute-done((bf16[384,384]{1,0:T(8,128)(2,1)S(1)}, bf16[384,384]{1,0:T(8,128)(2,1)S(1)}, u32[]{:S(2)}, u32[]{:S(2)}) %collective-permute-start.2) | collective-permute-done | bytes 294944 | tf_op jit(solution)/shard_map/ppermute | solution.py:37
  25.0 3.4 %collective-permute-start.4 = (bf16[384,384]{1,0:T(8,128)(2,1)S(1)}, bf16[384,384]{1,0:T(8,128)(2,1)S(1)}, u32[]{:S(2)}, u32[]{:S(2)}) collective-permute-start(bf16[384,384]{1,0:T(8,128)(2,1)S(1)} %collective-permute-done.1), channel_id=1, source_target_pairs={{0,4},{1,5},{2,6},{3,7},{4,8},{5,9},{6,10},{7,11},{8,12},{9,13},{1... | collective-permute-start | bytes 884744 | tf_op jit(solution)/shard_map/ppermute | solution.py:37
  28.4 3.7 %collective-permute-start.5 = (bf16[384,384]{1,0:T(8,128)(2,1)S(1)}, bf16[384,384]{1,0:T(8,128)(2,1)S(1)}, u32[]{:S(2)}, u32[]{:S(2)}) collective-permute-start(bf16[384,384]{1,0:T(8,128)(2,1)S(1)} %collective-permute-done.2), channel_id=1, source_target_pairs={{0,28},{1,29},{2,30},{3,31},{4,0},{5,1},{6,2},{7,3},{8,4},{9,5},{1... | collective-permute-start | bytes 884744 | tf_op jit(solution)/shard_map/ppermute | solution.py:37
  32.1 2.9 %collective-permute-done.4 = bf16[384,384]{1,0:T(8,128)(2,1)S(1)} collective-permute-done((bf16[384,384]{1,0:T(8,128)(2,1)S(1)}, bf16[384,384]{1,0:T(8,128)(2,1)S(1)}, u32[]{:S(2)}, u32[]{:S(2)}) %collective-permute-start.4) | collective-permute-done | bytes 294944 | tf_op jit(solution)/shard_map/ppermute | solution.py:37
  35.0 2.1 %collective-permute-start.6 = (bf16[384,384]{1,0:T(8,128)(2,1)S(1)}, bf16[384,384]{1,0:T(8,128)(2,1)S(1)}, u32[]{:S(2)}, u32[]{:S(2)}) collective-permute-start(bf16[384,384]{1,0:T(8,128)(2,1)S(1)} %collective-permute-done.4), channel_id=1, source_target_pairs={{0,4},{1,5},{2,6},{3,7},{4,8},{5,9},{6,10},{7,11},{8,12},{9,13},{1... | collective-permute-start | bytes 884744 | tf_op jit(solution)/shard_map/ppermute | solution.py:37
  37.1 4.9 %collective-permute-start.7 = (bf16[384,384]{1,0:T(8,128)(2,1)S(1)}, bf16[384,384]{1,0:T(8,128)(2,1)S(1)}, u32[]{:S(2)}, u32[]{:S(2)}) collective-permute-start(bf16[384,384]{1,0:T(8,128)(2,1)S(1)} %collective-permute-done.5), channel_id=1, source_target_pairs={{0,28},{1,29},{2,30},{3,31},{4,0},{5,1},{6,2},{7,3},{8,4},{9,5},{1... | collective-permute-start | bytes 884744 | tf_op jit(solution)/shard_map/ppermute | solution.py:37
  42.2 2.7 %collective-permute-done.6 = bf16[384,384]{1,0:T(8,128)(2,1)S(1)} collective-permute-done((bf16[384,384]{1,0:T(8,128)(2,1)S(1)}, bf16[384,384]{1,0:T(8,128)(2,1)S(1)}, u32[]{:S(2)}, u32[]{:S(2)}) %collective-permute-start.6) | collective-permute-done | bytes 294944 | tf_op jit(solution)/shard_map/ppermute | solution.py:37
  44.8 1.9 %collective-permute-start.8 = (bf16[192,384]{1,0:T(8,128)(2,1)S(1)}, bf16[192,384]{1,0:T(8,128)(2,1)S(1)}, u32[]{:S(2)}, u32[]{:S(2)}) collective-permute-start(bf16[192,384]{1,0:T(8,128)(2,1)S(1)} %slice.191), channel_id=1, source_target_pairs={{0,4},{1,5},{2,6},{3,7},{4,8},{5,9},{6,10},{7,11},{8,12},{9,13},{1... | collective-permute-start | bytes 442376 | tf_op jit(solution)/shard_map/ppermute | solution.py:37
  46.8 5.1 %collective-permute-start.9 = (bf16[192,384]{1,0:T(8,128)(2,1)S(1)}, bf16[192,384]{1,0:T(8,128)(2,1)S(1)}, u32[]{:S(2)}, u32[]{:S(2)}) collective-permute-start(bf16[192,384]{1,0:T(8,128)(2,1)S(1)} %slice.192), channel_id=1, source_target_pairs={{0,28},{1,29},{2,30},{3,31},{4,0},{5,1},{6,2},{7,3},{8,4},{9,5},{1... | collective-permute-start | bytes 442376 | tf_op jit(solution)/shard_map/ppermute | solution.py:37
  52.1 1.0 collective-permute-done.8
  53.1 1.5 %collective-permute-done.9 = bf16[192,384]{1,0:T(8,128)(2,1)S(1)} collective-permute-done((bf16[192,384]{1,0:T(8,128)(2,1)S(1)}, bf16[192,384]{1,0:T(8,128)(2,1)S(1)}, u32[]{:S(2)}, u32[]{:S(2)}) %collective-permute-start.9) | collective-permute-done | bytes 147488 | tf_op jit(solution)/shard_map/ppermute | solution.py:37
  54.6 1.9 %collective-permute-start.10 = (bf16[1920,384]{1,0:T(8,128)(2,1)S(1)}, bf16[1920,384]{1,0:T(8,128)(2,1)}, u32[]{:S(2)}, u32[]{:S(2)}) collective-permute-start(bf16[1920,384]{1,0:T(8,128)(2,1)S(1)} %constant_dynamic-update-slice_fusion.6.refs_5_), channel_id=1, source_target_pairs={{0,1},{1,0},{2,3},{3,2},{4,5},{5,4},{6,7},{7,6},{8,9},{9,8},{10,11... | collective-permute-start | bytes 4423688 | tf_op jit(solution)/shard_map/ppermute | solution.py:37
  56.7 2.6 %collective-permute-start.3 = (bf16[1152,384]{1,0:T(8,128)(2,1)S(1)}, bf16[1152,384]{1,0:T(8,128)(2,1)}, u32[]{:S(2)}, u32[]{:S(2)}) collective-permute-start(bf16[1152,384]{1,0:T(8,128)(2,1)S(1)} %pad_maximum_fusion.refs_4_), channel_id=1, source_target_pairs={{0,1},{1,0},{2,3},{3,2},{4,5},{5,4},{6,7},{7,6},{8,9},{9,8},{10,11... | collective-permute-start | bytes 2654216 | tf_op jit(solution)/shard_map/ppermute | solution.py:37
  59.3 1.0 fusion.65
  60.3 4.9 %shard_map.109 = (f32[192,1]{1,0:T(8,128)S(1)}, f32[192,1]{1,0:T(8,128)S(1)}, f32[192,384]{1,0:T(8,128)S(1)}) custom-call(bf16[192,384]{1,0:T(8,128)(2,1)S(1)} %fusion.1.refs_0_, f32[1,384]{1,0:T(1,128)S(1)} %reshape.147.refs_1_, bf16[384,768]{1,0:T(8,128)(2,1)S(1)} %slice.157.refs_2_, f32[1,768]{1,0:T(1,128)S(1)} %reshape.152.refs_3_, ...), custom_call_target="tpu_custom_call" | custom-call | flops 2717908992 | bytes 3244032 | tf_op jit(solution)/shard_map/pallas_call | solution.py:162
  65.2 6.9 %shard_map.110 = bf16[192,384]{1,0:T(8,128)(2,1)S(1)} custom-call(bf16[192,384]{1,0:T(8,128)(2,1)S(1)} %fusion.1.refs_0_, f32[1,384]{1,0:T(1,128)S(1)} %reshape.147.refs_1_, bf16[384,768]{1,0:T(8,128)(2,1)S(1)} %slice.157.refs_2_, f32[1,768]{1,0:T(1,128)S(1)} %reshape.152.refs_3_, bf16[1152,384]{1,0:T(8,128)(2,1)} %collective-permute-done.3.refs_4_, ...), custom_call_target="tpu_custom_call" | custom-call | flops 2717908992 | bytes 3244032 | tf_op jit(solution)/shard_map/pallas_call | solution.py:162
  72.1 0.2 fusion.2
  72.4 6.9 %collective-permute-start.11 = (bf16[192,384]{1,0:T(8,128)(2,1)S(1)}, bf16[192,384]{1,0:T(8,128)(2,1)S(1)}, u32[]{:S(2)}, u32[]{:S(2)}) collective-permute-start(bf16[192,384]{1,0:T(8,128)(2,1)S(1)} %fusion.2), channel_id=1, source_target_pairs={{0,64},{32,96},{64,128},{96,160},{128,192},{160,224},{192,256},{22... | collective-permute-start | bytes 442376 | tf_op jit(solution)/shard_map/ppermute | solution.py:16
  79.2 4.0 %collective-permute-start.12 = (bf16[192,384]{1,0:T(8,128)(2,1)S(1)}, bf16[192,384]{1,0:T(8,128)(2,1)S(1)}, u32[]{:S(2)}, u32[]{:S(2)}) collective-permute-start(bf16[192,384]{1,0:T(8,128)(2,1)S(1)} %fusion.2), channel_id=1, source_target_pairs={{0,32},{32,64},{64,96},{96,128},{128,160},{160,192},{192,224},{224... | collective-permute-start | bytes 442376 | tf_op jit(solution)/shard_map/ppermute | solution.py:16
  83.3 0.3 fusion.3
  83.6 3.0 %collective-permute-done.12 = bf16[192,384]{1,0:T(8,128)(2,1)S(1)} collective-permute-done((bf16[192,384]{1,0:T(8,128)(2,1)S(1)}, bf16[192,384]{1,0:T(8,128)(2,1)S(1)}, u32[]{:S(2)}, u32[]{:S(2)}) %collective-permute-start.12) | collective-permute-done | bytes 147488 | tf_op jit(solution)/shard_map/ppermute | solution.py:16
  86.7 0.3 fusion.7
  87.1 0.3 add_convert_fusion
  87.5 12.7 %collective-permute-start.14 = (bf16[2,1,96,384]{3,2,1,0:T(8,128)(2,1)S(1)}, bf16[2,1,96,384]{3,2,1,0:T(8,128)(2,1)S(1)}, u32[]{:S(2)}, u32[]{:S(2)}) collective-permute-start(bf16[2,1,96,384]{3,2,1,0:T(8,128)(2,1)S(1)} %get-tuple-element.49), channel_id=1, source_target_pairs={{1,0},{2,1},{3,2},{4,3},{5,4},{6,5},{7,6},{8,7},{9,8},{10,9},{11,1... | collective-permute-start | bytes 442376 | tf_op jit(solution)/shard_map/ppermute | solution.py:27
  100.2 2.1 %collective-permute-start.13 = (bf16[2,1,96,384]{3,2,1,0:T(8,128)(2,1)S(1)}, bf16[2,1,96,384]{3,2,1,0:T(8,128)(2,1)S(1)}, u32[]{:S(2)}, u32[]{:S(2)}) collective-permute-start(bf16[2,1,96,384]{3,2,1,0:T(8,128)(2,1)S(1)} %get-tuple-element.48), channel_id=1, source_target_pairs={{0,1},{1,2},{2,3},{3,4},{4,5},{5,6},{6,7},{7,8},{8,9},{9,10},{10,1... | collective-permute-start | bytes 442376 | tf_op jit(solution)/shard_map/ppermute | solution.py:24
  102.3 1.1 fusion.41
  103.5 2.4 %collective-permute-done.14 = bf16[2,1,96,384]{3,2,1,0:T(8,128)(2,1)S(1)} collective-permute-done((bf16[2,1,96,384]{3,2,1,0:T(8,128)(2,1)S(1)}, bf16[2,1,96,384]{3,2,1,0:T(8,128)(2,1)S(1)}, u32[]{:S(2)}, u32[]{:S(2)}) %collective-permute-start.14) | collective-permute-done | bytes 147488 | tf_op jit(solution)/shard_map/ppermute | solution.py:27
  105.8 0.5 fusion.44
  106.3 7.5 %collective-permute-done.13 = bf16[2,1,96,384]{3,2,1,0:T(8,128)(2,1)S(1)} collective-permute-done((bf16[2,1,96,384]{3,2,1,0:T(8,128)(2,1)S(1)}, bf16[2,1,96,384]{3,2,1,0:T(8,128)(2,1)S(1)}, u32[]{:S(2)}, u32[]{:S(2)}) %collective-permute-start.13) | collective-permute-done | bytes 147488 | tf_op jit(solution)/shard_map/ppermute | solution.py:24
  113.8 0.5 fusion.48
  114.3 0.1 fusion.35
  114.4 0.2 fusion.55
  114.6 0.4 fusion.53
  115.0 0.1 fusion.52
  115.1 0.2 maximum_maximum_fusion
  115.3 0.8 copy.40
  116.2 1.0 copy.41
  (66 shorter events, 1.0 us)
Async XLA Ops:
  0.0 72.1 %copy-start = (bf16[384,384]{1,0:T(8,128)(2,1)S(1)}, bf16[384,384]{1,0:T(8,128)(2,1)}, u32[]{:S(2)}) copy-start(bf16[384,384]{1,0:T(8,128)(2,1)} %param.16) | copy-start | bytes 884740
  0.0 9.3 %copy-start.1 = (bf16[1,2,96,384]{3,2,1,0:T(8,128)(2,1)S(1)}, bf16[1,2,96,384]{3,2,1,0:T(8,128)(2,1)}, u32[]{:S(2)}) copy-start(bf16[1,2,96,384]{3,2,1,0:T(8,128)(2,1)} %param.11) | copy-start | bytes 442372
  0.0 9.2 %copy-start.2 = (bf16[3,3,384,192]{2,3,1,0:T(8,128)(2,1)S(1)}, bf16[3,3,384,192]{2,3,1,0:T(8,128)(2,1)}, u32[]{:S(2)}) copy-start(bf16[3,3,384,192]{2,3,1,0:T(8,128)(2,1)} %param.20) | copy-start | bytes 3981316
  0.0 12.0 %collective-permute-start = (bf16[192,384]{1,0:T(8,128)(2,1)}, bf16[192,384]{1,0:T(8,128)(2,1)S(1)}, u32[]{:S(2)}, u32[]{:S(2)}) collective-permute-start(bf16[192,384]{1,0:T(8,128)(2,1)} %bitcast.214), channel_id=1, source_target_pairs={{0,2},{1,3},{2,0},{3,1},{4,6},{5,7},{6,4},{7,5},{8,10},{9,11},{10,... | collective-permute-start | bytes 442376 | tf_op jit(solution)/shard_map/ppermute | solution.py:37
  9.3 0.7 copy-start.10
  9.3 0.7 copy-start.11
  9.7 10.5 %copy-start.6 = (bf16[384,1728]{0,1:T(8,128)(2,1)}, bf16[384,1728]{0,1:T(8,128)(2,1)S(1)}, u32[]{:S(2)}) copy-start(bf16[384,1728]{0,1:T(8,128)(2,1)S(1)} %constant_dynamic-update-slice_fusion) | copy-start | bytes 3981316
  10.0 10.2 %copy-start.8 = (bf16[384,1152]{1,0:T(8,128)(2,1)S(1)}, bf16[384,1152]{1,0:T(8,128)(2,1)}, u32[]{:S(2)}) copy-start(bf16[384,1152]{1,0:T(8,128)(2,1)} %param.14) | copy-start | bytes 2654212
  12.1 11.1 %collective-permute-start.1 = (bf16[384,384]{1,0:T(8,128)(2,1)S(1)}, bf16[384,384]{1,0:T(8,128)(2,1)S(1)}, u32[]{:S(2)}, u32[]{:S(2)}) collective-permute-start(bf16[384,384]{1,0:T(8,128)(2,1)S(1)} %pad_maximum_fusion.10), channel_id=1, source_target_pairs={{0,4},{1,5},{2,6},{3,7},{4,8},{5,9},{6,10},{7,11},{8,12},{9,13},{1... | collective-permute-start | bytes 884744 | tf_op jit(solution)/shard_map/ppermute | solution.py:37
  15.4 9.6 %collective-permute-start.2 = (bf16[384,384]{1,0:T(8,128)(2,1)S(1)}, bf16[384,384]{1,0:T(8,128)(2,1)S(1)}, u32[]{:S(2)}, u32[]{:S(2)}) collective-permute-start(bf16[384,384]{1,0:T(8,128)(2,1)S(1)} %pad_maximum_fusion.10), channel_id=1, source_target_pairs={{0,28},{1,29},{2,30},{3,31},{4,0},{5,1},{6,2},{7,3},{8,4},{9,5},{1... | collective-permute-start | bytes 884744 | tf_op jit(solution)/shard_map/ppermute | solution.py:37
  19.1 1.1 copy-start.12
  19.1 1.1 copy-start.13
  19.2 1.7 %copy-start.14 = (bf16[192]{0:T(256)(128)(2,1)S(1)}, bf16[192]{0:T(256)(128)(2,1)}, u32[]{:S(2)}) copy-start(bf16[192]{0:T(256)(128)(2,1)} %param.21) | copy-start | bytes 1156
  25.0 10.0 %collective-permute-start.4 = (bf16[384,384]{1,0:T(8,128)(2,1)S(1)}, bf16[384,384]{1,0:T(8,128)(2,1)S(1)}, u32[]{:S(2)}, u32[]{:S(2)}) collective-permute-start(bf16[384,384]{1,0:T(8,128)(2,1)S(1)} %collective-permute-done.1), channel_id=1, source_target_pairs={{0,4},{1,5},{2,6},{3,7},{4,8},{5,9},{6,10},{7,11},{8,12},{9,13},{1... | collective-permute-start | bytes 884744 | tf_op jit(solution)/shard_map/ppermute | solution.py:37
  28.4 8.7 %collective-permute-start.5 = (bf16[384,384]{1,0:T(8,128)(2,1)S(1)}, bf16[384,384]{1,0:T(8,128)(2,1)S(1)}, u32[]{:S(2)}, u32[]{:S(2)}) collective-permute-start(bf16[384,384]{1,0:T(8,128)(2,1)S(1)} %collective-permute-done.2), channel_id=1, source_target_pairs={{0,28},{1,29},{2,30},{3,31},{4,0},{5,1},{6,2},{7,3},{8,4},{9,5},{1... | collective-permute-start | bytes 884744 | tf_op jit(solution)/shard_map/ppermute | solution.py:37
  35.0 9.8 %collective-permute-start.6 = (bf16[384,384]{1,0:T(8,128)(2,1)S(1)}, bf16[384,384]{1,0:T(8,128)(2,1)S(1)}, u32[]{:S(2)}, u32[]{:S(2)}) collective-permute-start(bf16[384,384]{1,0:T(8,128)(2,1)S(1)} %collective-permute-done.4), channel_id=1, source_target_pairs={{0,4},{1,5},{2,6},{3,7},{4,8},{5,9},{6,10},{7,11},{8,12},{9,13},{1... | collective-permute-start | bytes 884744 | tf_op jit(solution)/shard_map/ppermute | solution.py:37
  37.1 9.6 %collective-permute-start.7 = (bf16[384,384]{1,0:T(8,128)(2,1)S(1)}, bf16[384,384]{1,0:T(8,128)(2,1)S(1)}, u32[]{:S(2)}, u32[]{:S(2)}) collective-permute-start(bf16[384,384]{1,0:T(8,128)(2,1)S(1)} %collective-permute-done.5), channel_id=1, source_target_pairs={{0,28},{1,29},{2,30},{3,31},{4,0},{5,1},{6,2},{7,3},{8,4},{9,5},{1... | collective-permute-start | bytes 884744 | tf_op jit(solution)/shard_map/ppermute | solution.py:37
  44.8 8.2 %collective-permute-start.8 = (bf16[192,384]{1,0:T(8,128)(2,1)S(1)}, bf16[192,384]{1,0:T(8,128)(2,1)S(1)}, u32[]{:S(2)}, u32[]{:S(2)}) collective-permute-start(bf16[192,384]{1,0:T(8,128)(2,1)S(1)} %slice.191), channel_id=1, source_target_pairs={{0,4},{1,5},{2,6},{3,7},{4,8},{5,9},{6,10},{7,11},{8,12},{9,13},{1... | collective-permute-start | bytes 442376 | tf_op jit(solution)/shard_map/ppermute | solution.py:37
  46.8 7.8 %collective-permute-start.9 = (bf16[192,384]{1,0:T(8,128)(2,1)S(1)}, bf16[192,384]{1,0:T(8,128)(2,1)S(1)}, u32[]{:S(2)}, u32[]{:S(2)}) collective-permute-start(bf16[192,384]{1,0:T(8,128)(2,1)S(1)} %slice.192), channel_id=1, source_target_pairs={{0,28},{1,29},{2,30},{3,31},{4,0},{5,1},{6,2},{7,3},{8,4},{9,5},{1... | collective-permute-start | bytes 442376 | tf_op jit(solution)/shard_map/ppermute | solution.py:37
  54.6 10.6 %collective-permute-start.10 = (bf16[1920,384]{1,0:T(8,128)(2,1)S(1)}, bf16[1920,384]{1,0:T(8,128)(2,1)}, u32[]{:S(2)}, u32[]{:S(2)}) collective-permute-start(bf16[1920,384]{1,0:T(8,128)(2,1)S(1)} %constant_dynamic-update-slice_fusion.6.refs_5_), channel_id=1, source_target_pairs={{0,1},{1,0},{2,3},{3,2},{4,5},{5,4},{6,7},{7,6},{8,9},{9,8},{10,11... | collective-permute-start | bytes 4423688 | tf_op jit(solution)/shard_map/ppermute | solution.py:37
  56.7 8.5 %collective-permute-start.3 = (bf16[1152,384]{1,0:T(8,128)(2,1)S(1)}, bf16[1152,384]{1,0:T(8,128)(2,1)}, u32[]{:S(2)}, u32[]{:S(2)}) collective-permute-start(bf16[1152,384]{1,0:T(8,128)(2,1)S(1)} %pad_maximum_fusion.refs_4_), channel_id=1, source_target_pairs={{0,1},{1,0},{2,3},{3,2},{4,5},{5,4},{6,7},{7,6},{8,9},{9,8},{10,11... | collective-permute-start | bytes 2654216 | tf_op jit(solution)/shard_map/ppermute | solution.py:37
  65.2 6.9 %copy-start.9 = (f32[384]{0:T(512)S(1)}, f32[384]{0:T(512)}, u32[]{:S(2)}) copy-start(f32[384]{0:T(512)} %convert_element_type.57) | copy-start | bytes 4612
  65.2 18.0 %copy-start.5 = (bf16[3,384,768]{2,1,0:T(8,128)(2,1)S(1)}, bf16[3,384,768]{2,1,0:T(8,128)(2,1)}, u32[]{:S(2)}) copy-start(bf16[3,384,768]{2,1,0:T(8,128)(2,1)} %param.18) | copy-start | bytes 5308420
  72.4 11.2 %collective-permute-start.11 = (bf16[192,384]{1,0:T(8,128)(2,1)S(1)}, bf16[192,384]{1,0:T(8,128)(2,1)S(1)}, u32[]{:S(2)}, u32[]{:S(2)}) collective-permute-start(bf16[192,384]{1,0:T(8,128)(2,1)S(1)} %fusion.2), channel_id=1, source_target_pairs={{0,64},{32,96},{64,128},{96,160},{128,192},{160,224},{192,256},{22... | collective-permute-start | bytes 442376 | tf_op jit(solution)/shard_map/ppermute | solution.py:16
  79.2 7.4 %collective-permute-start.12 = (bf16[192,384]{1,0:T(8,128)(2,1)S(1)}, bf16[192,384]{1,0:T(8,128)(2,1)S(1)}, u32[]{:S(2)}, u32[]{:S(2)}) collective-permute-start(bf16[192,384]{1,0:T(8,128)(2,1)S(1)} %fusion.2), channel_id=1, source_target_pairs={{0,32},{32,64},{64,96},{96,128},{128,160},{160,192},{192,224},{224... | collective-permute-start | bytes 442376 | tf_op jit(solution)/shard_map/ppermute | solution.py:16
  87.1 15.3 %copy-start.7 = (bf16[384,1728]{0,1:T(8,128)(2,1)S(1)}, bf16[384,1728]{0,1:T(8,128)(2,1)}, u32[]{:S(2)}) copy-start(bf16[384,1728]{0,1:T(8,128)(2,1)} %copy-done.6) | copy-start | bytes 3981316
  87.5 18.3 %collective-permute-start.14 = (bf16[2,1,96,384]{3,2,1,0:T(8,128)(2,1)S(1)}, bf16[2,1,96,384]{3,2,1,0:T(8,128)(2,1)S(1)}, u32[]{:S(2)}, u32[]{:S(2)}) collective-permute-start(bf16[2,1,96,384]{3,2,1,0:T(8,128)(2,1)S(1)} %get-tuple-element.49), channel_id=1, source_target_pairs={{1,0},{2,1},{3,2},{4,3},{5,4},{6,5},{7,6},{8,7},{9,8},{10,9},{11,1... | collective-permute-start | bytes 442376 | tf_op jit(solution)/shard_map/ppermute | solution.py:27
  100.2 13.6 %collective-permute-start.13 = (bf16[2,1,96,384]{3,2,1,0:T(8,128)(2,1)S(1)}, bf16[2,1,96,384]{3,2,1,0:T(8,128)(2,1)S(1)}, u32[]{:S(2)}, u32[]{:S(2)}) collective-permute-start(bf16[2,1,96,384]{3,2,1,0:T(8,128)(2,1)S(1)} %get-tuple-element.48), channel_id=1, source_target_pairs={{0,1},{1,2},{2,3},{3,4},{4,5},{5,6},{6,7},{7,8},{8,9},{9,10},{10,1... | collective-permute-start | bytes 442376 | tf_op jit(solution)/shard_map/ppermute | solution.py:24
  102.3 3.5 %copy-start.4 = (bf16[384,576]{0,1:T(8,128)(2,1)S(1)}, bf16[384,576]{0,1:T(8,128)(2,1)}, u32[]{:S(2)}) copy-start(bf16[384,576]{0,1:T(8,128)(2,1)} %get-tuple-element.34) | copy-start | bytes 1327108
  103.4 10.3 %copy-start.3 = (bf16[384,576]{0,1:T(8,128)(2,1)S(1)}, bf16[384,576]{0,1:T(8,128)(2,1)}, u32[]{:S(2)}) copy-start(bf16[384,576]{0,1:T(8,128)(2,1)} %get-tuple-element.32) | copy-start | bytes 1327108

commit v13 on v12

--- a/solution.py
+++ b/solution.py
@@ -246,7 +246,7 @@
         taps = [sum(products[parity[row_tap], row_tap, col_tap] for row_tap in range(3)) for col_tap in range(3)]
         even = bias + shifted_cols(taps[0], -1) + taps[1] + taps[2]
         odd = bias + taps[0] + taps[1] + shifted_cols(taps[2], 1)
-        rows_out.append(jnp.stack([even, odd], axis=3).astype(jnp.bfloat16))
+        rows_out.append(jnp.concatenate([even, odd], axis=-1).astype(jnp.bfloat16))
     result = jnp.stack(rows_out, axis=2)
     return result.reshape(2, 2 * rows, 2 * width, out_channels)
 

time: 118 us -> 117 us (level)
  no operation moved by 1% of the time
where the time goes in v13:
time: 117 us
  starting transfers between devices  66.3 us (57%)
  waiting for transfers between devices  26.8 us (23%)
  Pallas kernels  11.8 us (10%)
  local copies, waits for them, and re-layouts  4.63 us (4%)
  matrix products  3.49 us (3%)
  other arithmetic  3.17 us (3%)
    ppermute x11, starting transfers between devices, moved(): return lax.ppermute(value, 'space', [(s, target(s)) for s in range(count)])  40.6 us
    ppermute x11, waiting for transfers between devices, moved(): return lax.ppermute(value, 'space', [(s, target(s)) for s in range(count)])  13.9 us
    ppermute x1, starting transfers between devices, with_halo(): lax.ppermute(lax.slice_in_dim(block, 0, width, axis=dim), axis, backward)  12.7 us
    pallas_call x2, Pallas kernels, fused_attention(): pl.pallas_call(functools.partial(attention_kernel, sizes=sizes, channels=...  11.8 us
    ppermute x2, starting transfers between devices, shifted(): lax.ppermute(value, axis, [(source, source + steps) for source in range(l...  10.9 us
    ppermute x1, waiting for transfers between devices, with_halo(): lax.ppermute(lax.slice_in_dim(block, block.shape[dim] - width, None, axis...  7.47 us
    ppermute x2, waiting for transfers between devices, shifted(): lax.ppermute(value, axis, [(source, source + steps) for source in range(l...  3.05 us
    ppermute x1, waiting for transfers between devices, with_halo(): lax.ppermute(lax.slice_in_dim(block, 0, width, axis=dim), axis, backward)  2.36 us
  transfers between devices with their start and end apart: 15, of which 10 were waited for; matrix products, arithmetic and copies ran while one was open for 6% of the time, Pallas kernels for 4%

profile of v13, /device:TPU:260, one launch (start us, length us, event | category | flops | bytes accessed | tf_op | source)
XLA Modules:
  0.0 116.8 jit_solution(13748650735711076031)
XLA Ops:
  0.0 7.9 %collective-permute-start = (bf16[192,384]{1,0:T(8,128)(2,1)}, bf16[192,384]{1,0:T(8,128)(2,1)S(1)}, u32[]{:S(2)}, u32[]{:S(2)}) collective-permute-start(bf16[192,384]{1,0:T(8,128)(2,1)} %bitcast.215), channel_id=1, source_target_pairs={{0,2},{1,3},{2,0},{3,1},{4,6},{5,7},{6,4},{7,5},{8,10},{9,11},{10,... | collective-permute-start | bytes 442376 | tf_op jit(solution)/shard_map/ppermute | solution.py:37
  7.9 1.3 %slice_bitcast_fusion.11 = (bf16[384,192]{0,1:T(8,128)(2,1)S(1)}, bf16[384,192]{0,1:T(8,128)(2,1)S(1)}, bf16[384,192]{0,1:T(8,128)(2,1)S(1)}, bf16[384,192]{0,1:...) fusion(bf16[3,3,384,192]{2,3,1,0:T(8,128)(2,1)} %param.20), kind=kLoop, calls=%fused_computation.100 | loop fusion | bytes 1769472 | tf_op jit(solution)/shard_map/squeeze | solution.py:195
  9.3 0.1 fusion.37
  9.7 0.2 copy-done.10
  10.0 0.1 fusion.39
  10.1 1.9 %collective-permute-done = bf16[192,384]{1,0:T(8,128)(2,1)S(1)} collective-permute-done((bf16[192,384]{1,0:T(8,128)(2,1)}, bf16[192,384]{1,0:T(8,128)(2,1)S(1)}, u32[]{:S(2)}, u32[]{:S(2)}) %collective-permute-start) | collective-permute-done | bytes 147488 | tf_op jit(solution)/shard_map/ppermute | solution.py:37
  12.1 3.4 %collective-permute-start.1 = (bf16[384,384]{1,0:T(8,128)(2,1)S(1)}, bf16[384,384]{1,0:T(8,128)(2,1)S(1)}, u32[]{:S(2)}, u32[]{:S(2)}) collective-permute-start(bf16[384,384]{1,0:T(8,128)(2,1)S(1)} %pad_maximum_fusion.10), channel_id=1, source_target_pairs={{0,4},{1,5},{2,6},{3,7},{4,8},{5,9},{6,10},{7,11},{8,12},{9,13},{1... | collective-permute-start | bytes 884744 | tf_op jit(solution)/shard_map/ppermute | solution.py:37
  15.4 3.7 %collective-permute-start.2 = (bf16[384,384]{1,0:T(8,128)(2,1)S(1)}, bf16[384,384]{1,0:T(8,128)(2,1)S(1)}, u32[]{:S(2)}, u32[]{:S(2)}) collective-permute-start(bf16[384,384]{1,0:T(8,128)(2,1)S(1)} %pad_maximum_fusion.10), channel_id=1, source_target_pairs={{0,28},{1,29},{2,30},{3,31},{4,0},{5,1},{6,2},{7,3},{8,4},{9,5},{1... | collective-permute-start | bytes 884744 | tf_op jit(solution)/shard_map/ppermute | solution.py:37
  19.2 1.0 pad_maximum_fusion.1
  20.3 0.6 convert_element_type.57
  20.9 0.2 fusion.1.refs_0_
  21.1 2.0 %collective-permute-done.1 = bf16[384,384]{1,0:T(8,128)(2,1)S(1)} collective-permute-done((bf16[384,384]{1,0:T(8,128)(2,1)S(1)}, bf16[384,384]{1,0:T(8,128)(2,1)S(1)}, u32[]{:S(2)}, u32[]{:S(2)}) %collective-permute-start.1) | collective-permute-done | bytes 294944 | tf_op jit(solution)/shard_map/ppermute | solution.py:37
  23.1 1.9 %collective-permute-done.2 = bf16[384,384]{1,0:T(8,128)(2,1)S(1)} collective-permute-done((bf16[384,384]{1,0:T(8,128)(2,1)S(1)}, bf16[384,384]{1,0:T(8,128)(2,1)S(1)}, u32[]{:S(2)}, u32[]{:S(2)}) %collective-permute-start.2) | collective-permute-done | bytes 294944 | tf_op jit(solution)/shard_map/ppermute | solution.py:37
  25.0 3.4 %collective-permute-start.4 = (bf16[384,384]{1,0:T(8,128)(2,1)S(1)}, bf16[384,384]{1,0:T(8,128)(2,1)S(1)}, u32[]{:S(2)}, u32[]{:S(2)}) collective-permute-start(bf16[384,384]{1,0:T(8,128)(2,1)S(1)} %collective-permute-done.1), channel_id=1, source_target_pairs={{0,4},{1,5},{2,6},{3,7},{4,8},{5,9},{6,10},{7,11},{8,12},{9,13},{1... | collective-permute-start | bytes 884744 | tf_op jit(solution)/shard_map/ppermute | solution.py:37
  28.4 3.7 %collective-permute-start.5 = (bf16[384,384]{1,0:T(8,128)(2,1)S(1)}, bf16[384,384]{1,0:T(8,128)(2,1)S(1)}, u32[]{:S(2)}, u32[]{:S(2)}) collective-permute-start(bf16[384,384]{1,0:T(8,128)(2,1)S(1)} %collective-permute-done.2), channel_id=1, source_target_pairs={{0,28},{1,29},{2,30},{3,31},{4,0},{5,1},{6,2},{7,3},{8,4},{9,5},{1... | collective-permute-start | bytes 884744 | tf_op jit(solution)/shard_map/ppermute | solution.py:37
  32.1 2.9 %collective-permute-done.4 = bf16[384,384]{1,0:T(8,128)(2,1)S(1)} collective-permute-done((bf16[384,384]{1,0:T(8,128)(2,1)S(1)}, bf16[384,384]{1,0:T(8,128)(2,1)S(1)}, u32[]{:S(2)}, u32[]{:S(2)}) %collective-permute-start.4) | collective-permute-done | bytes 294944 | tf_op jit(solution)/shard_map/ppermute | solution.py:37
  35.0 2.1 %collective-permute-start.6 = (bf16[384,384]{1,0:T(8,128)(2,1)S(1)}, bf16[384,384]{1,0:T(8,128)(2,1)S(1)}, u32[]{:S(2)}, u32[]{:S(2)}) collective-permute-start(bf16[384,384]{1,0:T(8,128)(2,1)S(1)} %collective-permute-done.4), channel_id=1, source_target_pairs={{0,4},{1,5},{2,6},{3,7},{4,8},{5,9},{6,10},{7,11},{8,12},{9,13},{1... | collective-permute-start | bytes 884744 | tf_op jit(solution)/shard_map/ppermute | solution.py:37
  37.1 4.9 %collective-permute-start.7 = (bf16[384,384]{1,0:T(8,128)(2,1)S(1)}, bf16[384,384]{1,0:T(8,128)(2,1)S(1)}, u32[]{:S(2)}, u32[]{:S(2)}) collective-permute-start(bf16[384,384]{1,0:T(8,128)(2,1)S(1)} %collective-permute-done.5), channel_id=1, source_target_pairs={{0,28},{1,29},{2,30},{3,31},{4,0},{5,1},{6,2},{7,3},{8,4},{9,5},{1... | collective-permute-start | bytes 884744 | tf_op jit(solution)/shard_map/ppermute | solution.py:37
  42.2 2.7 %collective-permute-done.6 = bf16[384,384]{1,0:T(8,128)(2,1)S(1)} collective-permute-done((bf16[384,384]{1,0:T(8,128)(2,1)S(1)}, bf16[384,384]{1,0:T(8,128)(2,1)S(1)}, u32[]{:S(2)}, u32[]{:S(2)}) %collective-permute-start.6) | collective-permute-done | bytes 294944 | tf_op jit(solution)/shard_map/ppermute | solution.py:37
  44.8 1.9 %collective-permute-start.8 = (bf16[192,384]{1,0:T(8,128)(2,1)S(1)}, bf16[192,384]{1,0:T(8,128)(2,1)S(1)}, u32[]{:S(2)}, u32[]{:S(2)}) collective-permute-start(bf16[192,384]{1,0:T(8,128)(2,1)S(1)} %slice.191), channel_id=1, source_target_pairs={{0,4},{1,5},{2,6},{3,7},{4,8},{5,9},{6,10},{7,11},{8,12},{9,13},{1... | collective-permute-start | bytes 442376 | tf_op jit(solution)/shard_map/ppermute | solution.py:37
  46.8 5.1 %collective-permute-start.9 = (bf16[192,384]{1,0:T(8,128)(2,1)S(1)}, bf16[192,384]{1,0:T(8,128)(2,1)S(1)}, u32[]{:S(2)}, u32[]{:S(2)}) collective-permute-start(bf16[192,384]{1,0:T(8,128)(2,1)S(1)} %slice.192), channel_id=1, source_target_pairs={{0,28},{1,29},{2,30},{3,31},{4,0},{5,1},{6,2},{7,3},{8,4},{9,5},{1... | collective-permute-start | bytes 442376 | tf_op jit(solution)/shard_map/ppermute | solution.py:37
  52.1 1.0 collective-permute-done.8
  53.1 1.5 %collective-permute-done.9 = bf16[192,384]{1,0:T(8,128)(2,1)S(1)} collective-permute-done((bf16[192,384]{1,0:T(8,128)(2,1)S(1)}, bf16[192,384]{1,0:T(8,128)(2,1)S(1)}, u32[]{:S(2)}, u32[]{:S(2)}) %collective-permute-start.9) | collective-permute-done | bytes 147488 | tf_op jit(solution)/shard_map/ppermute | solution.py:37
  54.6 1.9 %collective-permute-start.10 = (bf16[1920,384]{1,0:T(8,128)(2,1)S(1)}, bf16[1920,384]{1,0:T(8,128)(2,1)}, u32[]{:S(2)}, u32[]{:S(2)}) collective-permute-start(bf16[1920,384]{1,0:T(8,128)(2,1)S(1)} %constant_dynamic-update-slice_fusion.6.refs_5_), channel_id=1, source_target_pairs={{0,1},{1,0},{2,3},{3,2},{4,5},{5,4},{6,7},{7,6},{8,9},{9,8},{10,11... | collective-permute-start | bytes 4423688 | tf_op jit(solution)/shard_map/ppermute | solution.py:37
  56.7 2.6 %collective-permute-start.3 = (bf16[1152,384]{1,0:T(8,128)(2,1)S(1)}, bf16[1152,384]{1,0:T(8,128)(2,1)}, u32[]{:S(2)}, u32[]{:S(2)}) collective-permute-start(bf16[1152,384]{1,0:T(8,128)(2,1)S(1)} %pad_maximum_fusion.refs_4_), channel_id=1, source_target_pairs={{0,1},{1,0},{2,3},{3,2},{4,5},{5,4},{6,7},{7,6},{8,9},{9,8},{10,11... | collective-permute-start | bytes 2654216 | tf_op jit(solution)/shard_map/ppermute | solution.py:37
  59.3 1.0 fusion.65
  60.3 4.9 %shard_map.109 = (f32[192,1]{1,0:T(8,128)S(1)}, f32[192,1]{1,0:T(8,128)S(1)}, f32[192,384]{1,0:T(8,128)S(1)}) custom-call(bf16[192,384]{1,0:T(8,128)(2,1)S(1)} %fusion.1.refs_0_, f32[1,384]{1,0:T(1,128)S(1)} %reshape.143.refs_1_, bf16[384,768]{1,0:T(8,128)(2,1)S(1)} %slice.157.refs_2_, f32[1,768]{1,0:T(1,128)S(1)} %reshape.148.refs_3_, ...), custom_call_target="tpu_custom_call" | custom-call | flops 2717908992 | bytes 3244032 | tf_op jit(solution)/shard_map/pallas_call | solution.py:162
  65.2 6.9 %shard_map.110 = bf16[192,384]{1,0:T(8,128)(2,1)S(1)} custom-call(bf16[192,384]{1,0:T(8,128)(2,1)S(1)} %fusion.1.refs_0_, f32[1,384]{1,0:T(1,128)S(1)} %reshape.143.refs_1_, bf16[384,768]{1,0:T(8,128)(2,1)S(1)} %slice.157.refs_2_, f32[1,768]{1,0:T(1,128)S(1)} %reshape.148.refs_3_, bf16[1152,384]{1,0:T(8,128)(2,1)} %collective-permute-done.3.refs_4_, ...), custom_call_target="tpu_custom_call" | custom-call | flops 2717908992 | bytes 3244032 | tf_op jit(solution)/shard_map/pallas_call | solution.py:162
  72.1 0.2 fusion.2
  72.4 6.9 %collective-permute-start.11 = (bf16[192,384]{1,0:T(8,128)(2,1)S(1)}, bf16[192,384]{1,0:T(8,128)(2,1)S(1)}, u32[]{:S(2)}, u32[]{:S(2)}) collective-permute-start(bf16[192,384]{1,0:T(8,128)(2,1)S(1)} %fusion.2), channel_id=1, source_target_pairs={{0,64},{32,96},{64,128},{96,160},{128,192},{160,224},{192,256},{22... | collective-permute-start | bytes 442376 | tf_op jit(solution)/shard_map/ppermute | solution.py:16
  79.2 4.0 %collective-permute-start.12 = (bf16[192,384]{1,0:T(8,128)(2,1)S(1)}, bf16[192,384]{1,0:T(8,128)(2,1)S(1)}, u32[]{:S(2)}, u32[]{:S(2)}) collective-permute-start(bf16[192,384]{1,0:T(8,128)(2,1)S(1)} %fusion.2), channel_id=1, source_target_pairs={{0,32},{32,64},{64,96},{96,128},{128,160},{160,192},{192,224},{224... | collective-permute-start | bytes 442376 | tf_op jit(solution)/shard_map/ppermute | solution.py:16
  83.3 0.3 fusion.3
  83.6 3.0 %collective-permute-done.12 = bf16[192,384]{1,0:T(8,128)(2,1)S(1)} collective-permute-done((bf16[192,384]{1,0:T(8,128)(2,1)S(1)}, bf16[192,384]{1,0:T(8,128)(2,1)S(1)}, u32[]{:S(2)}, u32[]{:S(2)}) %collective-permute-start.12) | collective-permute-done | bytes 147488 | tf_op jit(solution)/shard_map/ppermute | solution.py:16
  86.7 0.3 fusion.7
  87.1 0.3 add_convert_fusion
  87.5 12.7 %collective-permute-start.14 = (bf16[2,1,96,384]{3,2,1,0:T(8,128)(2,1)S(1)}, bf16[2,1,96,384]{3,2,1,0:T(8,128)(2,1)S(1)}, u32[]{:S(2)}, u32[]{:S(2)}) collective-permute-start(bf16[2,1,96,384]{3,2,1,0:T(8,128)(2,1)S(1)} %get-tuple-element.49), channel_id=1, source_target_pairs={{1,0},{2,1},{3,2},{4,3},{5,4},{6,5},{7,6},{8,7},{9,8},{10,9},{11,1... | collective-permute-start | bytes 442376 | tf_op jit(solution)/shard_map/ppermute | solution.py:27
  100.2 2.1 %collective-permute-start.13 = (bf16[2,1,96,384]{3,2,1,0:T(8,128)(2,1)S(1)}, bf16[2,1,96,384]{3,2,1,0:T(8,128)(2,1)S(1)}, u32[]{:S(2)}, u32[]{:S(2)}) collective-permute-start(bf16[2,1,96,384]{3,2,1,0:T(8,128)(2,1)S(1)} %get-tuple-element.48), channel_id=1, source_target_pairs={{0,1},{1,2},{2,3},{3,4},{4,5},{5,6},{6,7},{7,8},{8,9},{9,10},{10,1... | collective-permute-start | bytes 442376 | tf_op jit(solution)/shard_map/ppermute | solution.py:24
  102.3 1.1 fusion.41
  103.5 2.4 %collective-permute-done.14 = bf16[2,1,96,384]{3,2,1,0:T(8,128)(2,1)S(1)} collective-permute-done((bf16[2,1,96,384]{3,2,1,0:T(8,128)(2,1)S(1)}, bf16[2,1,96,384]{3,2,1,0:T(8,128)(2,1)S(1)}, u32[]{:S(2)}, u32[]{:S(2)}) %collective-permute-start.14) | collective-permute-done | bytes 147488 | tf_op jit(solution)/shard_map/ppermute | solution.py:27
  105.8 0.5 fusion.44
  106.3 7.5 %collective-permute-done.13 = bf16[2,1,96,384]{3,2,1,0:T(8,128)(2,1)S(1)} collective-permute-done((bf16[2,1,96,384]{3,2,1,0:T(8,128)(2,1)S(1)}, bf16[2,1,96,384]{3,2,1,0:T(8,128)(2,1)S(1)}, u32[]{:S(2)}, u32[]{:S(2)}) %collective-permute-start.13) | collective-permute-done | bytes 147488 | tf_op jit(solution)/shard_map/ppermute | solution.py:24
  113.8 0.5 fusion.48
  114.3 0.1 fusion.35
  114.4 0.2 fusion.55
  114.6 0.4 fusion.53
  115.0 0.1 fusion.52
  115.1 0.2 maximum_maximum_fusion
  115.4 1.3 %reshape.146 = bf16[2,4,192,192]{3,2,1,0:T(8,128)(2,1)} reshape(bf16[2,2,2,96,384]{4,3,2,1,0:T(8,128)(2,1)S(1)} %copy.40) | data formatting | bytes 1179648 | tf_op jit(solution)/shard_map/reshape | solution.py:251
  (66 shorter events, 1.0 us)
Async XLA Ops:
  0.0 72.1 %copy-start = (bf16[384,384]{1,0:T(8,128)(2,1)S(1)}, bf16[384,384]{1,0:T(8,128)(2,1)}, u32[]{:S(2)}) copy-start(bf16[384,384]{1,0:T(8,128)(2,1)} %param.16) | copy-start | bytes 884740
  0.0 9.3 %copy-start.1 = (bf16[1,2,96,384]{3,2,1,0:T(8,128)(2,1)S(1)}, bf16[1,2,96,384]{3,2,1,0:T(8,128)(2,1)}, u32[]{:S(2)}) copy-start(bf16[1,2,96,384]{3,2,1,0:T(8,128)(2,1)} %param.11) | copy-start | bytes 442372
  0.0 9.2 %copy-start.2 = (bf16[3,3,384,192]{2,3,1,0:T(8,128)(2,1)S(1)}, bf16[3,3,384,192]{2,3,1,0:T(8,128)(2,1)}, u32[]{:S(2)}) copy-start(bf16[3,3,384,192]{2,3,1,0:T(8,128)(2,1)} %param.20) | copy-start | bytes 3981316
  0.0 12.0 %collective-permute-start = (bf16[192,384]{1,0:T(8,128)(2,1)}, bf16[192,384]{1,0:T(8,128)(2,1)S(1)}, u32[]{:S(2)}, u32[]{:S(2)}) collective-permute-start(bf16[192,384]{1,0:T(8,128)(2,1)} %bitcast.215), channel_id=1, source_target_pairs={{0,2},{1,3},{2,0},{3,1},{4,6},{5,7},{6,4},{7,5},{8,10},{9,11},{10,... | collective-permute-start | bytes 442376 | tf_op jit(solution)/shard_map/ppermute | solution.py:37
  9.3 0.7 copy-start.10
  9.3 0.7 copy-start.11
  9.7 10.5 %copy-start.6 = (bf16[384,1728]{0,1:T(8,128)(2,1)}, bf16[384,1728]{0,1:T(8,128)(2,1)S(1)}, u32[]{:S(2)}) copy-start(bf16[384,1728]{0,1:T(8,128)(2,1)S(1)} %constant_dynamic-update-slice_fusion) | copy-start | bytes 3981316
  10.0 10.2 %copy-start.8 = (bf16[384,1152]{1,0:T(8,128)(2,1)S(1)}, bf16[384,1152]{1,0:T(8,128)(2,1)}, u32[]{:S(2)}) copy-start(bf16[384,1152]{1,0:T(8,128)(2,1)} %param.14) | copy-start | bytes 2654212
  12.1 11.1 %collective-permute-start.1 = (bf16[384,384]{1,0:T(8,128)(2,1)S(1)}, bf16[384,384]{1,0:T(8,128)(2,1)S(1)}, u32[]{:S(2)}, u32[]{:S(2)}) collective-permute-start(bf16[384,384]{1,0:T(8,128)(2,1)S(1)} %pad_maximum_fusion.10), channel_id=1, source_target_pairs={{0,4},{1,5},{2,6},{3,7},{4,8},{5,9},{6,10},{7,11},{8,12},{9,13},{1... | collective-permute-start | bytes 884744 | tf_op jit(solution)/shard_map/ppermute | solution.py:37
  15.4 9.6 %collective-permute-start.2 = (bf16[384,384]{1,0:T(8,128)(2,1)S(1)}, bf16[384,384]{1,0:T(8,128)(2,1)S(1)}, u32[]{:S(2)}, u32[]{:S(2)}) collective-permute-start(bf16[384,384]{1,0:T(8,128)(2,1)S(1)} %pad_maximum_fusion.10), channel_id=1, source_target_pairs={{0,28},{1,29},{2,30},{3,31},{4,0},{5,1},{6,2},{7,3},{8,4},{9,5},{1... | collective-permute-start | bytes 884744 | tf_op jit(solution)/shard_map/ppermute | solution.py:37
  19.1 1.1 copy-start.12
  19.1 1.1 copy-start.13
  19.2 1.7 %copy-start.14 = (bf16[192]{0:T(256)(128)(2,1)S(1)}, bf16[192]{0:T(256)(128)(2,1)}, u32[]{:S(2)}) copy-start(bf16[192]{0:T(256)(128)(2,1)} %param.21) | copy-start | bytes 1156
  25.0 10.0 %collective-permute-start.4 = (bf16[384,384]{1,0:T(8,128)(2,1)S(1)}, bf16[384,384]{1,0:T(8,128)(2,1)S(1)}, u32[]{:S(2)}, u32[]{:S(2)}) collective-permute-start(bf16[384,384]{1,0:T(8,128)(2,1)S(1)} %collective-permute-done.1), channel_id=1, source_target_pairs={{0,4},{1,5},{2,6},{3,7},{4,8},{5,9},{6,10},{7,11},{8,12},{9,13},{1... | collective-permute-start | bytes 884744 | tf_op jit(solution)/shard_map/ppermute | solution.py:37
  28.4 8.7 %collective-permute-start.5 = (bf16[384,384]{1,0:T(8,128)(2,1)S(1)}, bf16[384,384]{1,0:T(8,128)(2,1)S(1)}, u32[]{:S(2)}, u32[]{:S(2)}) collective-permute-start(bf16[384,384]{1,0:T(8,128)(2,1)S(1)} %collective-permute-done.2), channel_id=1, source_target_pairs={{0,28},{1,29},{2,30},{3,31},{4,0},{5,1},{6,2},{7,3},{8,4},{9,5},{1... | collective-permute-start | bytes 884744 | tf_op jit(solution)/shard_map/ppermute | solution.py:37
  35.0 9.8 %collective-permute-start.6 = (bf16[384,384]{1,0:T(8,128)(2,1)S(1)}, bf16[384,384]{1,0:T(8,128)(2,1)S(1)}, u32[]{:S(2)}, u32[]{:S(2)}) collective-permute-start(bf16[384,384]{1,0:T(8,128)(2,1)S(1)} %collective-permute-done.4), channel_id=1, source_target_pairs={{0,4},{1,5},{2,6},{3,7},{4,8},{5,9},{6,10},{7,11},{8,12},{9,13},{1... | collective-permute-start | bytes 884744 | tf_op jit(solution)/shard_map/ppermute | solution.py:37
  37.1 9.6 %collective-permute-start.7 = (bf16[384,384]{1,0:T(8,128)(2,1)S(1)}, bf16[384,384]{1,0:T(8,128)(2,1)S(1)}, u32[]{:S(2)}, u32[]{:S(2)}) collective-permute-start(bf16[384,384]{1,0:T(8,128)(2,1)S(1)} %collective-permute-done.5), channel_id=1, source_target_pairs={{0,28},{1,29},{2,30},{3,31},{4,0},{5,1},{6,2},{7,3},{8,4},{9,5},{1... | collective-permute-start | bytes 884744 | tf_op jit(solution)/shard_map/ppermute | solution.py:37
  44.8 8.2 %collective-permute-start.8 = (bf16[192,384]{1,0:T(8,128)(2,1)S(1)}, bf16[192,384]{1,0:T(8,128)(2,1)S(1)}, u32[]{:S(2)}, u32[]{:S(2)}) collective-permute-start(bf16[192,384]{1,0:T(8,128)(2,1)S(1)} %slice.191), channel_id=1, source_target_pairs={{0,4},{1,5},{2,6},{3,7},{4,8},{5,9},{6,10},{7,11},{8,12},{9,13},{1... | collective-permute-start | bytes 442376 | tf_op jit(solution)/shard_map/ppermute | solution.py:37
  46.8 7.8 %collective-permute-start.9 = (bf16[192,384]{1,0:T(8,128)(2,1)S(1)}, bf16[192,384]{1,0:T(8,128)(2,1)S(1)}, u32[]{:S(2)}, u32[]{:S(2)}) collective-permute-start(bf16[192,384]{1,0:T(8,128)(2,1)S(1)} %slice.192), channel_id=1, source_target_pairs={{0,28},{1,29},{2,30},{3,31},{4,0},{5,1},{6,2},{7,3},{8,4},{9,5},{1... | collective-permute-start | bytes 442376 | tf_op jit(solution)/shard_map/ppermute | solution.py:37
  54.6 10.6 %collective-permute-start.10 = (bf16[1920,384]{1,0:T(8,128)(2,1)S(1)}, bf16[1920,384]{1,0:T(8,128)(2,1)}, u32[]{:S(2)}, u32[]{:S(2)}) collective-permute-start(bf16[1920,384]{1,0:T(8,128)(2,1)S(1)} %constant_dynamic-update-slice_fusion.6.refs_5_), channel_id=1, source_target_pairs={{0,1},{1,0},{2,3},{3,2},{4,5},{5,4},{6,7},{7,6},{8,9},{9,8},{10,11... | collective-permute-start | bytes 4423688 | tf_op jit(solution)/shard_map/ppermute | solution.py:37
  56.7 8.5 %collective-permute-start.3 = (bf16[1152,384]{1,0:T(8,128)(2,1)S(1)}, bf16[1152,384]{1,0:T(8,128)(2,1)}, u32[]{:S(2)}, u32[]{:S(2)}) collective-permute-start(bf16[1152,384]{1,0:T(8,128)(2,1)S(1)} %pad_maximum_fusion.refs_4_), channel_id=1, source_target_pairs={{0,1},{1,0},{2,3},{3,2},{4,5},{5,4},{6,7},{7,6},{8,9},{9,8},{10,11... | collective-permute-start | bytes 2654216 | tf_op jit(solution)/shard_map/ppermute | solution.py:37
  65.2 6.9 %copy-start.9 = (f32[384]{0:T(512)S(1)}, f32[384]{0:T(512)}, u32[]{:S(2)}) copy-start(f32[384]{0:T(512)} %convert_element_type.57) | copy-start | bytes 4612
  65.2 18.0 %copy-start.5 = (bf16[3,384,768]{2,1,0:T(8,128)(2,1)S(1)}, bf16[3,384,768]{2,1,0:T(8,128)(2,1)}, u32[]{:S(2)}) copy-start(bf16[3,384,768]{2,1,0:T(8,128)(2,1)} %param.18) | copy-start | bytes 5308420
  72.4 11.2 %collective-permute-start.11 = (bf16[192,384]{1,0:T(8,128)(2,1)S(1)}, bf16[192,384]{1,0:T(8,128)(2,1)S(1)}, u32[]{:S(2)}, u32[]{:S(2)}) collective-permute-start(bf16[192,384]{1,0:T(8,128)(2,1)S(1)} %fusion.2), channel_id=1, source_target_pairs={{0,64},{32,96},{64,128},{96,160},{128,192},{160,224},{192,256},{22... | collective-permute-start | bytes 442376 | tf_op jit(solution)/shard_map/ppermute | solution.py:16
  79.2 7.4 %collective-permute-start.12 = (bf16[192,384]{1,0:T(8,128)(2,1)S(1)}, bf16[192,384]{1,0:T(8,128)(2,1)S(1)}, u32[]{:S(2)}, u32[]{:S(2)}) collective-permute-start(bf16[192,384]{1,0:T(8,128)(2,1)S(1)} %fusion.2), channel_id=1, source_target_pairs={{0,32},{32,64},{64,96},{96,128},{128,160},{160,192},{192,224},{224... | collective-permute-start | bytes 442376 | tf_op jit(solution)/shard_map/ppermute | solution.py:16
  87.1 15.3 %copy-start.7 = (bf16[384,1728]{0,1:T(8,128)(2,1)S(1)}, bf16[384,1728]{0,1:T(8,128)(2,1)}, u32[]{:S(2)}) copy-start(bf16[384,1728]{0,1:T(8,128)(2,1)} %copy-done.6) | copy-start | bytes 3981316
  87.5 18.3 %collective-permute-start.14 = (bf16[2,1,96,384]{3,2,1,0:T(8,128)(2,1)S(1)}, bf16[2,1,96,384]{3,2,1,0:T(8,128)(2,1)S(1)}, u32[]{:S(2)}, u32[]{:S(2)}) collective-permute-start(bf16[2,1,96,384]{3,2,1,0:T(8,128)(2,1)S(1)} %get-tuple-element.49), channel_id=1, source_target_pairs={{1,0},{2,1},{3,2},{4,3},{5,4},{6,5},{7,6},{8,7},{9,8},{10,9},{11,1... | collective-permute-start | bytes 442376 | tf_op jit(solution)/shard_map/ppermute | solution.py:27
  100.2 13.6 %collective-permute-start.13 = (bf16[2,1,96,384]{3,2,1,0:T(8,128)(2,1)S(1)}, bf16[2,1,96,384]{3,2,1,0:T(8,128)(2,1)S(1)}, u32[]{:S(2)}, u32[]{:S(2)}) collective-permute-start(bf16[2,1,96,384]{3,2,1,0:T(8,128)(2,1)S(1)} %get-tuple-element.48), channel_id=1, source_target_pairs={{0,1},{1,2},{2,3},{3,4},{4,5},{5,6},{6,7},{7,8},{8,9},{9,10},{10,1... | collective-permute-start | bytes 442376 | tf_op jit(solution)/shard_map/ppermute | solution.py:24
  102.3 3.5 %copy-start.4 = (bf16[384,576]{0,1:T(8,128)(2,1)S(1)}, bf16[384,576]{0,1:T(8,128)(2,1)}, u32[]{:S(2)}) copy-start(bf16[384,576]{0,1:T(8,128)(2,1)} %get-tuple-element.34) | copy-start | bytes 1327108
  103.4 10.3 %copy-start.3 = (bf16[384,576]{0,1:T(8,128)(2,1)S(1)}, bf16[384,576]{0,1:T(8,128)(2,1)}, u32[]{:S(2)}) copy-start(bf16[384,576]{0,1:T(8,128)(2,1)} %get-tuple-element.32) | copy-start | bytes 1327108

commit v14 on v13

--- a/solution.py
+++ b/solution.py
@@ -125,7 +125,13 @@
             )
             best = new_best
     if finish:
-        rest[0][...] = (total / mass).astype(rest[0].dtype)
+        mixed = (total / mass).astype(jnp.bfloat16)
+        residual_ref, proj_ref, bproj_ref, out_ref = rest
+        out_ref[...] = (
+            residual_ref[...].astype(jnp.float32)
+            + jnp.dot(mixed, proj_ref[...], preferred_element_type=jnp.float32)
+            + bproj_ref[...]
+        ).astype(out_ref.dtype)
     else:
         rest[0][...] = best
         rest[1][...] = mass
@@ -140,7 +146,7 @@
     return gain, wkv, bkv
 
 
-def fused_attention(queries, chunks, weights, state=None, finish=True):
+def fused_attention(queries, chunks, weights, state=None, finish=True, epilogue=()):
     channels = queries.shape[1]
     count = queries.shape[0]
     sizes = tuple(c.shape[0] for c in chunks)
@@ -148,7 +154,7 @@
     spec = pl.BlockSpec(memory_space=pltpu.MemorySpace.VMEM)
     total_rows = sum(sizes)
     flops = 2 * total_rows * channels * (2 * channels + 2 * count)
-    extra = tuple(state) if state is not None else ()
+    extra = (tuple(state) if state is not None else ()) + tuple(epilogue)
     if finish:
         out_shape = jax.ShapeDtypeStruct(queries.shape, jnp.bfloat16)
         out_specs = spec
@@ -203,12 +209,8 @@
     queries = riders["queries"]
     half = len(chunks) // 2
     state = fused_attention(queries, chunks[:half], riders["weights"], finish=False)
-    mixed = fused_attention(queries, chunks[half:], riders["weights"], state=state)
-    hidden = (
-        frames.reshape(-1, channels).astype(jnp.float32)
-        + jnp.dot(mixed, w_proj, preferred_element_type=jnp.float32)
-        + riders["b_proj"]
-    ).astype(jnp.bfloat16)
+    epilogue = (frames.reshape(-1, channels), w_proj, riders["b_proj"].reshape(1, channels))
+    hidden = fused_attention(queries, chunks[half:], riders["weights"], state=state, epilogue=epilogue)
     position = lax.axis_index("tm")
     carried = cache_in.reshape(2, -1, channels)
     near_frame = shifted(hidden, "tm", 1)

time: 117 us -> 116 us (level)
  transfers between devices with their start and end apart: 15 -> 15, of which waited for: 10 -> 10; matrix products, arithmetic and copies ran while one was open for 6% -> 4% of each run, Pallas kernels for 4% -> 4%
where the time goes in v14:
time: 116 us
  starting transfers between devices  66.3 us (57%)
  waiting for transfers between devices  26.8 us (23%)
  Pallas kernels  11.9 us (10%)
  local copies, waits for them, and re-layouts  4.46 us (4%)
  matrix products  3.26 us (3%)
  other arithmetic  2.58 us (2%)
    ppermute x11, starting transfers between devices, moved(): return lax.ppermute(value, 'space', [(s, target(s)) for s in range(count)])  40.6 us
    ppermute x11, waiting for transfers between devices, moved(): return lax.ppermute(value, 'space', [(s, target(s)) for s in range(count)])  13.7 us
    ppermute x1, starting transfers between devices, with_halo(): lax.ppermute(lax.slice_in_dim(block, 0, width, axis=dim), axis, backward)  12.7 us
    pallas_call x2, Pallas kernels, fused_attention(): pl.pallas_call(functools.partial(attention_kernel, sizes=sizes, channels=...  11.9 us
    ppermute x2, starting transfers between devices, shifted(): lax.ppermute(value, axis, [(source, source + steps) for source in range(l...  10.9 us
    ppermute x1, waiting for transfers between devices, with_halo(): lax.ppermute(lax.slice_in_dim(block, block.shape[dim] - width, None, axis...  7.48 us
    ppermute x2, waiting for transfers between devices, shifted(): lax.ppermute(value, axis, [(source, source + steps) for source in range(l...  3.3 us
    ppermute x1, waiting for transfers between devices, with_halo(): lax.ppermute(lax.slice_in_dim(block, 0, width, axis=dim), axis, backward)  2.38 us
  transfers between devices with their start and end apart: 15, of which 10 were waited for; matrix products, arithmetic and copies ran while one was open for 4% of the time, Pallas kernels for 4%

profile of v14, /device:TPU:260, one launch (start us, length us, event | category | flops | bytes accessed | tf_op | source)
XLA Modules:
  0.0 115.9 jit_solution(15076599823452430281)
XLA Ops:
  0.0 7.9 %collective-permute-start = (bf16[192,384]{1,0:T(8,128)(2,1)}, bf16[192,384]{1,0:T(8,128)(2,1)S(1)}, u32[]{:S(2)}, u32[]{:S(2)}) collective-permute-start(bf16[192,384]{1,0:T(8,128)(2,1)} %bitcast.205), channel_id=1, source_target_pairs={{0,2},{1,3},{2,0},{3,1},{4,6},{5,7},{6,4},{7,5},{8,10},{9,11},{10,... | collective-permute-start | bytes 442376 | tf_op jit(solution)/shard_map/ppermute | solution.py:37
  7.9 1.3 %slice_bitcast_fusion.11 = (bf16[384,192]{0,1:T(8,128)(2,1)S(1)}, bf16[384,192]{0,1:T(8,128)(2,1)S(1)}, bf16[384,192]{0,1:T(8,128)(2,1)S(1)}, bf16[384,192]{0,1:...) fusion(bf16[3,3,384,192]{2,3,1,0:T(8,128)(2,1)} %param.20), kind=kLoop, calls=%fused_computation.97 | loop fusion | bytes 1769472 | tf_op jit(solution)/shard_map/squeeze | solution.py:201
  9.3 0.1 fusion.35
  9.7 1.1 copy-done.6
  10.8 0.1 fusion.37
  10.9 1.1 collective-permute-done
  12.0 3.4 %collective-permute-start.1 = (bf16[384,384]{1,0:T(8,128)(2,1)S(1)}, bf16[384,384]{1,0:T(8,128)(2,1)S(1)}, u32[]{:S(2)}, u32[]{:S(2)}) collective-permute-start(bf16[384,384]{1,0:T(8,128)(2,1)S(1)} %pad_maximum_fusion.10), channel_id=1, source_target_pairs={{0,4},{1,5},{2,6},{3,7},{4,8},{5,9},{6,10},{7,11},{8,12},{9,13},{1... | collective-permute-start | bytes 884744 | tf_op jit(solution)/shard_map/ppermute | solution.py:37
  15.4 3.7 %collective-permute-start.2 = (bf16[384,384]{1,0:T(8,128)(2,1)S(1)}, bf16[384,384]{1,0:T(8,128)(2,1)S(1)}, u32[]{:S(2)}, u32[]{:S(2)}) collective-permute-start(bf16[384,384]{1,0:T(8,128)(2,1)S(1)} %pad_maximum_fusion.10), channel_id=1, source_target_pairs={{0,28},{1,29},{2,30},{3,31},{4,0},{5,1},{6,2},{7,3},{8,4},{9,5},{1... | collective-permute-start | bytes 884744 | tf_op jit(solution)/shard_map/ppermute | solution.py:37
  19.1 1.0 pad_maximum_fusion.1
  20.3 0.2 fusion.refs_0_
  20.5 2.6 %collective-permute-done.1 = bf16[384,384]{1,0:T(8,128)(2,1)S(1)} collective-permute-done((bf16[384,384]{1,0:T(8,128)(2,1)S(1)}, bf16[384,384]{1,0:T(8,128)(2,1)S(1)}, u32[]{:S(2)}, u32[]{:S(2)}) %collective-permute-start.1) | collective-permute-done | bytes 294944 | tf_op jit(solution)/shard_map/ppermute | solution.py:37
  23.1 1.9 %collective-permute-done.2 = bf16[384,384]{1,0:T(8,128)(2,1)S(1)} collective-permute-done((bf16[384,384]{1,0:T(8,128)(2,1)S(1)}, bf16[384,384]{1,0:T(8,128)(2,1)S(1)}, u32[]{:S(2)}, u32[]{:S(2)}) %collective-permute-start.2) | collective-permute-done | bytes 294944 | tf_op jit(solution)/shard_map/ppermute | solution.py:37
  25.0 3.4 %collective-permute-start.4 = (bf16[384,384]{1,0:T(8,128)(2,1)S(1)}, bf16[384,384]{1,0:T(8,128)(2,1)S(1)}, u32[]{:S(2)}, u32[]{:S(2)}) collective-permute-start(bf16[384,384]{1,0:T(8,128)(2,1)S(1)} %collective-permute-done.1), channel_id=1, source_target_pairs={{0,4},{1,5},{2,6},{3,7},{4,8},{5,9},{6,10},{7,11},{8,12},{9,13},{1... | collective-permute-start | bytes 884744 | tf_op jit(solution)/shard_map/ppermute | solution.py:37
  28.4 3.7 %collective-permute-start.5 = (bf16[384,384]{1,0:T(8,128)(2,1)S(1)}, bf16[384,384]{1,0:T(8,128)(2,1)S(1)}, u32[]{:S(2)}, u32[]{:S(2)}) collective-permute-start(bf16[384,384]{1,0:T(8,128)(2,1)S(1)} %collective-permute-done.2), channel_id=1, source_target_pairs={{0,28},{1,29},{2,30},{3,31},{4,0},{5,1},{6,2},{7,3},{8,4},{9,5},{1... | collective-permute-start | bytes 884744 | tf_op jit(solution)/shard_map/ppermute | solution.py:37
  32.1 2.9 %collective-permute-done.4 = bf16[384,384]{1,0:T(8,128)(2,1)S(1)} collective-permute-done((bf16[384,384]{1,0:T(8,128)(2,1)S(1)}, bf16[384,384]{1,0:T(8,128)(2,1)S(1)}, u32[]{:S(2)}, u32[]{:S(2)}) %collective-permute-start.4) | collective-permute-done | bytes 294944 | tf_op jit(solution)/shard_map/ppermute | solution.py:37
  35.0 2.1 %collective-permute-start.6 = (bf16[384,384]{1,0:T(8,128)(2,1)S(1)}, bf16[384,384]{1,0:T(8,128)(2,1)S(1)}, u32[]{:S(2)}, u32[]{:S(2)}) collective-permute-start(bf16[384,384]{1,0:T(8,128)(2,1)S(1)} %collective-permute-done.4), channel_id=1, source_target_pairs={{0,4},{1,5},{2,6},{3,7},{4,8},{5,9},{6,10},{7,11},{8,12},{9,13},{1... | collective-permute-start | bytes 884744 | tf_op jit(solution)/shard_map/ppermute | solution.py:37
  37.1 4.9 %collective-permute-start.7 = (bf16[384,384]{1,0:T(8,128)(2,1)S(1)}, bf16[384,384]{1,0:T(8,128)(2,1)S(1)}, u32[]{:S(2)}, u32[]{:S(2)}) collective-permute-start(bf16[384,384]{1,0:T(8,128)(2,1)S(1)} %collective-permute-done.5), channel_id=1, source_target_pairs={{0,28},{1,29},{2,30},{3,31},{4,0},{5,1},{6,2},{7,3},{8,4},{9,5},{1... | collective-permute-start | bytes 884744 | tf_op jit(solution)/shard_map/ppermute | solution.py:37
  42.1 2.7 %collective-permute-done.6 = bf16[384,384]{1,0:T(8,128)(2,1)S(1)} collective-permute-done((bf16[384,384]{1,0:T(8,128)(2,1)S(1)}, bf16[384,384]{1,0:T(8,128)(2,1)S(1)}, u32[]{:S(2)}, u32[]{:S(2)}) %collective-permute-start.6) | collective-permute-done | bytes 294944 | tf_op jit(solution)/shard_map/ppermute | solution.py:37
  44.8 1.9 %collective-permute-start.8 = (bf16[192,384]{1,0:T(8,128)(2,1)S(1)}, bf16[192,384]{1,0:T(8,128)(2,1)S(1)}, u32[]{:S(2)}, u32[]{:S(2)}) collective-permute-start(bf16[192,384]{1,0:T(8,128)(2,1)S(1)} %slice.191), channel_id=1, source_target_pairs={{0,4},{1,5},{2,6},{3,7},{4,8},{5,9},{6,10},{7,11},{8,12},{9,13},{1... | collective-permute-start | bytes 442376 | tf_op jit(solution)/shard_map/ppermute | solution.py:37
  46.8 5.1 %collective-permute-start.9 = (bf16[192,384]{1,0:T(8,128)(2,1)S(1)}, bf16[192,384]{1,0:T(8,128)(2,1)S(1)}, u32[]{:S(2)}, u32[]{:S(2)}) collective-permute-start(bf16[192,384]{1,0:T(8,128)(2,1)S(1)} %slice.192), channel_id=1, source_target_pairs={{0,28},{1,29},{2,30},{3,31},{4,0},{5,1},{6,2},{7,3},{8,4},{9,5},{1... | collective-permute-start | bytes 442376 | tf_op jit(solution)/shard_map/ppermute | solution.py:37
  52.0 1.0 collective-permute-done.8
  53.1 1.5 %collective-permute-done.9 = bf16[192,384]{1,0:T(8,128)(2,1)S(1)} collective-permute-done((bf16[192,384]{1,0:T(8,128)(2,1)S(1)}, bf16[192,384]{1,0:T(8,128)(2,1)S(1)}, u32[]{:S(2)}, u32[]{:S(2)}) %collective-permute-start.9) | collective-permute-done | bytes 147488 | tf_op jit(solution)/shard_map/ppermute | solution.py:37
  54.6 1.9 %collective-permute-start.10 = (bf16[1920,384]{1,0:T(8,128)(2,1)S(1)}, bf16[1920,384]{1,0:T(8,128)(2,1)}, u32[]{:S(2)}, u32[]{:S(2)}) collective-permute-start(bf16[1920,384]{1,0:T(8,128)(2,1)S(1)} %constant_dynamic-update-slice_fusion.6.refs_5_), channel_id=1, source_target_pairs={{0,1},{1,0},{2,3},{3,2},{4,5},{5,4},{6,7},{7,6},{8,9},{9,8},{10,11... | collective-permute-start | bytes 4423688 | tf_op jit(solution)/shard_map/ppermute | solution.py:37
  56.5 0.1 pad_maximum_fusion.refs_4_
  56.6 2.6 %collective-permute-start.3 = (bf16[1152,384]{1,0:T(8,128)(2,1)S(1)}, bf16[1152,384]{1,0:T(8,128)(2,1)}, u32[]{:S(2)}, u32[]{:S(2)}) collective-permute-start(bf16[1152,384]{1,0:T(8,128)(2,1)S(1)} %pad_maximum_fusion.refs_4_), channel_id=1, source_target_pairs={{0,1},{1,0},{2,3},{3,2},{4,5},{5,4},{6,7},{7,6},{8,9},{9,8},{10,11... | collective-permute-start | bytes 2654216 | tf_op jit(solution)/shard_map/ppermute | solution.py:37
  59.3 4.8 %shard_map.109 = (f32[192,1]{1,0:T(8,128)S(1)}, f32[192,1]{1,0:T(8,128)S(1)}, f32[192,384]{1,0:T(8,128)S(1)}) custom-call(bf16[192,384]{1,0:T(8,128)(2,1)S(1)} %fusion.refs_0_, f32[1,384]{1,0:T(1,128)S(1)} %reshape.145.refs_1_, bf16[384,768]{1,0:T(8,128)(2,1)S(1)} %slice.157.refs_2_, f32[1,768]{1,0:T(1,128)S(1)} %reshape.151.refs_3_, ...), custom_call_target="tpu_custom_call" | custom-call | flops 2717908992 | bytes 3244032 | tf_op jit(solution)/shard_map/pallas_call | solution.py:168
  64.1 7.1 %shard_map.110 = bf16[192,384]{1,0:T(8,128)(2,1)S(1)} custom-call(bf16[192,384]{1,0:T(8,128)(2,1)S(1)} %fusion.refs_0_, f32[1,384]{1,0:T(1,128)S(1)} %reshape.145.refs_1_, bf16[384,768]{1,0:T(8,128)(2,1)S(1)} %slice.157.refs_2_, f32[1,768]{1,0:T(1,128)S(1)} %reshape.151.refs_3_, bf16[1152,384]{1,0:T(8,128)(2,1)} %collective-permute-done.3.refs_4_, ...), custom_call_target="tpu_custom_call" | custom-call | flops 2717908992 | bytes 3244032 | tf_op jit(solution)/shard_map/pallas_call | solution.py:168
  71.2 6.9 %collective-permute-start.11 = (bf16[192,384]{1,0:T(8,128)(2,1)S(1)}, bf16[192,384]{1,0:T(8,128)(2,1)S(1)}, u32[]{:S(2)}, u32[]{:S(2)}) collective-permute-start(bf16[192,384]{1,0:T(8,128)(2,1)S(1)} %shard_map.110), channel_id=1, source_target_pairs={{0,64},{32,96},{64,128},{96,160},{128,192},{160,224},{192,256},{22... | collective-permute-start | bytes 442376 | tf_op jit(solution)/shard_map/ppermute | solution.py:16
  78.1 4.0 %collective-permute-start.12 = (bf16[192,384]{1,0:T(8,128)(2,1)S(1)}, bf16[192,384]{1,0:T(8,128)(2,1)S(1)}, u32[]{:S(2)}, u32[]{:S(2)}) collective-permute-start(bf16[192,384]{1,0:T(8,128)(2,1)S(1)} %shard_map.110), channel_id=1, source_target_pairs={{0,32},{32,64},{64,96},{96,128},{128,160},{160,192},{192,224},{224... | collective-permute-start | bytes 442376 | tf_op jit(solution)/shard_map/ppermute | solution.py:16
  82.2 3.3 %collective-permute-done.12 = bf16[192,384]{1,0:T(8,128)(2,1)S(1)} collective-permute-done((bf16[192,384]{1,0:T(8,128)(2,1)S(1)}, bf16[192,384]{1,0:T(8,128)(2,1)S(1)}, u32[]{:S(2)}, u32[]{:S(2)}) %collective-permute-start.12) | collective-permute-done | bytes 147488 | tf_op jit(solution)/shard_map/ppermute | solution.py:16
  85.5 0.1 fusion.56
  85.6 0.3 fusion.3
  85.9 0.3 fusion.5
  86.2 0.3 add_convert_fusion
  86.6 12.7 %collective-permute-start.14 = (bf16[2,1,96,384]{3,2,1,0:T(8,128)(2,1)S(1)}, bf16[2,1,96,384]{3,2,1,0:T(8,128)(2,1)S(1)}, u32[]{:S(2)}, u32[]{:S(2)}) collective-permute-start(bf16[2,1,96,384]{3,2,1,0:T(8,128)(2,1)S(1)} %get-tuple-element.49), channel_id=1, source_target_pairs={{1,0},{2,1},{3,2},{4,3},{5,4},{6,5},{7,6},{8,7},{9,8},{10,9},{11,1... | collective-permute-start | bytes 442376 | tf_op jit(solution)/shard_map/ppermute | solution.py:27
  99.3 2.1 %collective-permute-start.13 = (bf16[2,1,96,384]{3,2,1,0:T(8,128)(2,1)S(1)}, bf16[2,1,96,384]{3,2,1,0:T(8,128)(2,1)S(1)}, u32[]{:S(2)}, u32[]{:S(2)}) collective-permute-start(bf16[2,1,96,384]{3,2,1,0:T(8,128)(2,1)S(1)} %get-tuple-element.48), channel_id=1, source_target_pairs={{0,1},{1,2},{2,3},{3,4},{4,5},{5,6},{6,7},{7,8},{8,9},{9,10},{10,1... | collective-permute-start | bytes 442376 | tf_op jit(solution)/shard_map/ppermute | solution.py:24
  101.5 1.1 fusion.39
  102.6 2.4 %collective-permute-done.14 = bf16[2,1,96,384]{3,2,1,0:T(8,128)(2,1)S(1)} collective-permute-done((bf16[2,1,96,384]{3,2,1,0:T(8,128)(2,1)S(1)}, bf16[2,1,96,384]{3,2,1,0:T(8,128)(2,1)S(1)}, u32[]{:S(2)}, u32[]{:S(2)}) %collective-permute-start.14) | collective-permute-done | bytes 147488 | tf_op jit(solution)/shard_map/ppermute | solution.py:27
  105.0 0.5 fusion.42
  105.5 7.5 %collective-permute-done.13 = bf16[2,1,96,384]{3,2,1,0:T(8,128)(2,1)S(1)} collective-permute-done((bf16[2,1,96,384]{3,2,1,0:T(8,128)(2,1)S(1)}, bf16[2,1,96,384]{3,2,1,0:T(8,128)(2,1)S(1)}, u32[]{:S(2)}, u32[]{:S(2)}) %collective-permute-start.13) | collective-permute-done | bytes 147488 | tf_op jit(solution)/shard_map/ppermute | solution.py:24
  113.0 0.5 fusion.46
  113.4 0.1 fusion.33
  113.6 0.2 fusion.53
  113.8 0.4 fusion.51
  114.2 0.1 fusion.50
  114.3 0.2 maximum_maximum_fusion
  114.5 0.1 copy.40
  114.6 1.3 %reshape.149 = bf16[2,4,192,192]{3,2,1,0:T(8,128)(2,1)} reshape(bf16[2,2,2,96,384]{4,3,2,1,0:T(8,128)(2,1)S(1)} %copy.40) | data formatting | bytes 1179648 | tf_op jit(solution)/shard_map/reshape | solution.py:253
  (66 shorter events, 0.8 us)
Async XLA Ops:
  0.0 9.2 %copy-start = (bf16[1,2,96,384]{3,2,1,0:T(8,128)(2,1)S(1)}, bf16[1,2,96,384]{3,2,1,0:T(8,128)(2,1)}, u32[]{:S(2)}) copy-start(bf16[1,2,96,384]{3,2,1,0:T(8,128)(2,1)} %param.11) | copy-start | bytes 442372
  0.0 9.2 %copy-start.2 = (bf16[3,3,384,192]{2,3,1,0:T(8,128)(2,1)S(1)}, bf16[3,3,384,192]{2,3,1,0:T(8,128)(2,1)}, u32[]{:S(2)}) copy-start(bf16[3,3,384,192]{2,3,1,0:T(8,128)(2,1)} %param.20) | copy-start | bytes 3981316
  0.0 12.0 %collective-permute-start = (bf16[192,384]{1,0:T(8,128)(2,1)}, bf16[192,384]{1,0:T(8,128)(2,1)S(1)}, u32[]{:S(2)}, u32[]{:S(2)}) collective-permute-start(bf16[192,384]{1,0:T(8,128)(2,1)} %bitcast.205), channel_id=1, source_target_pairs={{0,2},{1,3},{2,0},{3,1},{4,6},{5,7},{6,4},{7,5},{8,10},{9,11},{10,... | collective-permute-start | bytes 442376 | tf_op jit(solution)/shard_map/ppermute | solution.py:37
  9.3 1.5 %copy-start.10 = (bf16[384]{0:T(512)(128)(2,1)S(1)}, bf16[384]{0:T(512)(128)(2,1)}, u32[]{:S(2)}) copy-start(bf16[384]{0:T(512)(128)(2,1)} %param.13) | copy-start | bytes 2308
  9.3 1.5 %copy-start.11 = (bf16[1152]{0:T(1024)(128)(2,1)S(1)}, bf16[1152]{0:T(1024)(128)(2,1)}, u32[]{:S(2)}) copy-start(bf16[1152]{0:T(1024)(128)(2,1)} %param.15) | copy-start | bytes 6916
  9.7 1.1 copy-start.6
  10.8 9.4 %copy-start.8 = (bf16[384,1152]{1,0:T(8,128)(2,1)S(1)}, bf16[384,1152]{1,0:T(8,128)(2,1)}, u32[]{:S(2)}) copy-start(bf16[384,1152]{1,0:T(8,128)(2,1)} %param.14) | copy-start | bytes 2654212
  12.0 11.1 %collective-permute-start.1 = (bf16[384,384]{1,0:T(8,128)(2,1)S(1)}, bf16[384,384]{1,0:T(8,128)(2,1)S(1)}, u32[]{:S(2)}, u32[]{:S(2)}) collective-permute-start(bf16[384,384]{1,0:T(8,128)(2,1)S(1)} %pad_maximum_fusion.10), channel_id=1, source_target_pairs={{0,4},{1,5},{2,6},{3,7},{4,8},{5,9},{6,10},{7,11},{8,12},{9,13},{1... | collective-permute-start | bytes 884744 | tf_op jit(solution)/shard_map/ppermute | solution.py:37
  15.4 9.6 %collective-permute-start.2 = (bf16[384,384]{1,0:T(8,128)(2,1)S(1)}, bf16[384,384]{1,0:T(8,128)(2,1)S(1)}, u32[]{:S(2)}, u32[]{:S(2)}) collective-permute-start(bf16[384,384]{1,0:T(8,128)(2,1)S(1)} %pad_maximum_fusion.10), channel_id=1, source_target_pairs={{0,28},{1,29},{2,30},{3,31},{4,0},{5,1},{6,2},{7,3},{8,4},{9,5},{1... | collective-permute-start | bytes 884744 | tf_op jit(solution)/shard_map/ppermute | solution.py:37
  19.1 1.1 copy-start.12
  19.1 1.1 copy-start.13
  19.1 1.1 copy-start.14
  25.0 10.0 %collective-permute-start.4 = (bf16[384,384]{1,0:T(8,128)(2,1)S(1)}, bf16[384,384]{1,0:T(8,128)(2,1)S(1)}, u32[]{:S(2)}, u32[]{:S(2)}) collective-permute-start(bf16[384,384]{1,0:T(8,128)(2,1)S(1)} %collective-permute-done.1), channel_id=1, source_target_pairs={{0,4},{1,5},{2,6},{3,7},{4,8},{5,9},{6,10},{7,11},{8,12},{9,13},{1... | collective-permute-start | bytes 884744 | tf_op jit(solution)/shard_map/ppermute | solution.py:37
  28.4 8.7 %collective-permute-start.5 = (bf16[384,384]{1,0:T(8,128)(2,1)S(1)}, bf16[384,384]{1,0:T(8,128)(2,1)S(1)}, u32[]{:S(2)}, u32[]{:S(2)}) collective-permute-start(bf16[384,384]{1,0:T(8,128)(2,1)S(1)} %collective-permute-done.2), channel_id=1, source_target_pairs={{0,28},{1,29},{2,30},{3,31},{4,0},{5,1},{6,2},{7,3},{8,4},{9,5},{1... | collective-permute-start | bytes 884744 | tf_op jit(solution)/shard_map/ppermute | solution.py:37
  35.0 9.8 %collective-permute-start.6 = (bf16[384,384]{1,0:T(8,128)(2,1)S(1)}, bf16[384,384]{1,0:T(8,128)(2,1)S(1)}, u32[]{:S(2)}, u32[]{:S(2)}) collective-permute-start(bf16[384,384]{1,0:T(8,128)(2,1)S(1)} %collective-permute-done.4), channel_id=1, source_target_pairs={{0,4},{1,5},{2,6},{3,7},{4,8},{5,9},{6,10},{7,11},{8,12},{9,13},{1... | collective-permute-start | bytes 884744 | tf_op jit(solution)/shard_map/ppermute | solution.py:37
  37.1 9.6 %collective-permute-start.7 = (bf16[384,384]{1,0:T(8,128)(2,1)S(1)}, bf16[384,384]{1,0:T(8,128)(2,1)S(1)}, u32[]{:S(2)}, u32[]{:S(2)}) collective-permute-start(bf16[384,384]{1,0:T(8,128)(2,1)S(1)} %collective-permute-done.5), channel_id=1, source_target_pairs={{0,28},{1,29},{2,30},{3,31},{4,0},{5,1},{6,2},{7,3},{8,4},{9,5},{1... | collective-permute-start | bytes 884744 | tf_op jit(solution)/shard_map/ppermute | solution.py:37
  44.8 8.2 %collective-permute-start.8 = (bf16[192,384]{1,0:T(8,128)(2,1)S(1)}, bf16[192,384]{1,0:T(8,128)(2,1)S(1)}, u32[]{:S(2)}, u32[]{:S(2)}) collective-permute-start(bf16[192,384]{1,0:T(8,128)(2,1)S(1)} %slice.191), channel_id=1, source_target_pairs={{0,4},{1,5},{2,6},{3,7},{4,8},{5,9},{6,10},{7,11},{8,12},{9,13},{1... | collective-permute-start | bytes 442376 | tf_op jit(solution)/shard_map/ppermute | solution.py:37
  46.8 7.8 %collective-permute-start.9 = (bf16[192,384]{1,0:T(8,128)(2,1)S(1)}, bf16[192,384]{1,0:T(8,128)(2,1)S(1)}, u32[]{:S(2)}, u32[]{:S(2)}) collective-permute-start(bf16[192,384]{1,0:T(8,128)(2,1)S(1)} %slice.192), channel_id=1, source_target_pairs={{0,28},{1,29},{2,30},{3,31},{4,0},{5,1},{6,2},{7,3},{8,4},{9,5},{1... | collective-permute-start | bytes 442376 | tf_op jit(solution)/shard_map/ppermute | solution.py:37
  54.6 9.5 %collective-permute-start.10 = (bf16[1920,384]{1,0:T(8,128)(2,1)S(1)}, bf16[1920,384]{1,0:T(8,128)(2,1)}, u32[]{:S(2)}, u32[]{:S(2)}) collective-permute-start(bf16[1920,384]{1,0:T(8,128)(2,1)S(1)} %constant_dynamic-update-slice_fusion.6.refs_5_), channel_id=1, source_target_pairs={{0,1},{1,0},{2,3},{3,2},{4,5},{5,4},{6,7},{7,6},{8,9},{9,8},{10,11... | collective-permute-start | bytes 4423688 | tf_op jit(solution)/shard_map/ppermute | solution.py:37
  56.6 7.5 %collective-permute-start.3 = (bf16[1152,384]{1,0:T(8,128)(2,1)S(1)}, bf16[1152,384]{1,0:T(8,128)(2,1)}, u32[]{:S(2)}, u32[]{:S(2)}) collective-permute-start(bf16[1152,384]{1,0:T(8,128)(2,1)S(1)} %pad_maximum_fusion.refs_4_), channel_id=1, source_target_pairs={{0,1},{1,0},{2,3},{3,2},{4,5},{5,4},{6,7},{7,6},{8,9},{9,8},{10,11... | collective-permute-start | bytes 2654216 | tf_op jit(solution)/shard_map/ppermute | solution.py:37
  59.2 4.9 %copy-start.1 = (bf16[384,384]{1,0:T(8,128)(2,1)S(1)}, bf16[384,384]{1,0:T(8,128)(2,1)}, u32[]{:S(2)}) copy-start(bf16[384,384]{1,0:T(8,128)(2,1)} %refs_10_.1) | copy-start | bytes 884740
  64.1 18.0 %copy-start.9 = (bf16[2,2,96,384]{3,2,1,0:T(8,128)(2,1)S(1)}, bf16[2,2,96,384]{3,2,1,0:T(8,128)(2,1)}, u32[]{:S(2)}) copy-start(bf16[2,2,96,384]{3,2,1,0:T(8,128)(2,1)} %param.12) | copy-start | bytes 884740
  64.1 21.4 %copy-start.5 = (bf16[3,384,768]{2,1,0:T(8,128)(2,1)S(1)}, bf16[3,384,768]{2,1,0:T(8,128)(2,1)}, u32[]{:S(2)}) copy-start(bf16[3,384,768]{2,1,0:T(8,128)(2,1)} %param.18) | copy-start | bytes 5308420
  71.2 11.0 %collective-permute-start.11 = (bf16[192,384]{1,0:T(8,128)(2,1)S(1)}, bf16[192,384]{1,0:T(8,128)(2,1)S(1)}, u32[]{:S(2)}, u32[]{:S(2)}) collective-permute-start(bf16[192,384]{1,0:T(8,128)(2,1)S(1)} %shard_map.110), channel_id=1, source_target_pairs={{0,64},{32,96},{64,128},{96,160},{128,192},{160,224},{192,256},{22... | collective-permute-start | bytes 442376 | tf_op jit(solution)/shard_map/ppermute | solution.py:16
  78.1 7.4 %collective-permute-start.12 = (bf16[192,384]{1,0:T(8,128)(2,1)S(1)}, bf16[192,384]{1,0:T(8,128)(2,1)S(1)}, u32[]{:S(2)}, u32[]{:S(2)}) collective-permute-start(bf16[192,384]{1,0:T(8,128)(2,1)S(1)} %shard_map.110), channel_id=1, source_target_pairs={{0,32},{32,64},{64,96},{96,128},{128,160},{160,192},{192,224},{224... | collective-permute-start | bytes 442376 | tf_op jit(solution)/shard_map/ppermute | solution.py:16
  86.2 15.3 %copy-start.7 = (bf16[384,1728]{0,1:T(8,128)(2,1)S(1)}, bf16[384,1728]{0,1:T(8,128)(2,1)}, u32[]{:S(2)}) copy-start(bf16[384,1728]{0,1:T(8,128)(2,1)} %copy-done.6) | copy-start | bytes 3981316
  86.6 18.4 %collective-permute-start.14 = (bf16[2,1,96,384]{3,2,1,0:T(8,128)(2,1)S(1)}, bf16[2,1,96,384]{3,2,1,0:T(8,128)(2,1)S(1)}, u32[]{:S(2)}, u32[]{:S(2)}) collective-permute-start(bf16[2,1,96,384]{3,2,1,0:T(8,128)(2,1)S(1)} %get-tuple-element.49), channel_id=1, source_target_pairs={{1,0},{2,1},{3,2},{4,3},{5,4},{6,5},{7,6},{8,7},{9,8},{10,9},{11,1... | collective-permute-start | bytes 442376 | tf_op jit(solution)/shard_map/ppermute | solution.py:27
  99.3 13.6 %collective-permute-start.13 = (bf16[2,1,96,384]{3,2,1,0:T(8,128)(2,1)S(1)}, bf16[2,1,96,384]{3,2,1,0:T(8,128)(2,1)S(1)}, u32[]{:S(2)}, u32[]{:S(2)}) collective-permute-start(bf16[2,1,96,384]{3,2,1,0:T(8,128)(2,1)S(1)} %get-tuple-element.48), channel_id=1, source_target_pairs={{0,1},{1,2},{2,3},{3,4},{4,5},{5,6},{6,7},{7,8},{8,9},{9,10},{10,1... | collective-permute-start | bytes 442376 | tf_op jit(solution)/shard_map/ppermute | solution.py:24
  101.5 3.5 %copy-start.4 = (bf16[384,576]{0,1:T(8,128)(2,1)S(1)}, bf16[384,576]{0,1:T(8,128)(2,1)}, u32[]{:S(2)}) copy-start(bf16[384,576]{0,1:T(8,128)(2,1)} %get-tuple-element.34) | copy-start | bytes 1327108
  102.6 10.4 %copy-start.3 = (bf16[384,576]{0,1:T(8,128)(2,1)S(1)}, bf16[384,576]{0,1:T(8,128)(2,1)}, u32[]{:S(2)}) copy-start(bf16[384,576]{0,1:T(8,128)(2,1)} %get-tuple-element.32) | copy-start | bytes 1327108

commit v15 on v14

--- a/solution.py
+++ b/solution.py
@@ -126,12 +126,14 @@
             best = new_best
     if finish:
         mixed = (total / mass).astype(jnp.bfloat16)
-        residual_ref, proj_ref, bproj_ref, out_ref = rest
-        out_ref[...] = (
+        residual_ref, proj_ref, bproj_ref, wt_ref, bt_ref, out_ref, part_ref = rest
+        hidden = (
             residual_ref[...].astype(jnp.float32)
             + jnp.dot(mixed, proj_ref[...], preferred_element_type=jnp.float32)
             + bproj_ref[...]
         ).astype(out_ref.dtype)
+        out_ref[...] = hidden
+        part_ref[...] = bt_ref[...] + jnp.dot(hidden, wt_ref[...], preferred_element_type=jnp.float32)
     else:
         rest[0][...] = best
         rest[1][...] = mass
@@ -156,8 +158,11 @@
     flops = 2 * total_rows * channels * (2 * channels + 2 * count)
     extra = (tuple(state) if state is not None else ()) + tuple(epilogue)
     if finish:
-        out_shape = jax.ShapeDtypeStruct(queries.shape, jnp.bfloat16)
-        out_specs = spec
+        out_shape = (
+            jax.ShapeDtypeStruct(queries.shape, jnp.bfloat16),
+            jax.ShapeDtypeStruct((count, 2 * channels), jnp.float32),
+        )
+        out_specs = (spec, spec)
     else:
         out_shape = (
             jax.ShapeDtypeStruct((count, 1), jnp.float32),
@@ -209,8 +214,11 @@
     queries = riders["queries"]
     half = len(chunks) // 2
     state = fused_attention(queries, chunks[:half], riders["weights"], finish=False)
-    epilogue = (frames.reshape(-1, channels), w_proj, riders["b_proj"].reshape(1, channels))
-    hidden = fused_attention(queries, chunks[half:], riders["weights"], state=state, epilogue=epilogue)
+    epilogue = (
+        frames.reshape(-1, channels), w_proj, riders["b_proj"].reshape(1, channels),
+        w_time[2], riders["b_time"].reshape(1, 2 * channels),
+    )
+    hidden, local = fused_attention(queries, chunks[half:], riders["weights"], state=state, epilogue=epilogue)
     position = lax.axis_index("tm")
     carried = cache_in.reshape(2, -1, channels)
     near_frame = shifted(hidden, "tm", 1)
@@ -218,11 +226,8 @@
     far_frame = shifted(hidden, "tm", 2)
     far_frame = jnp.where(position == 1, carried[1], far_frame)
     far_frame = jnp.where(position == 0, carried[0], far_frame)
-    timed = riders["b_time"] + jnp.dot(
-        far_frame, w_time[0], preferred_element_type=jnp.float32
-    )
-    timed = timed + jnp.dot(near_frame, w_time[1], preferred_element_type=jnp.float32)
-    timed = (timed + jnp.dot(hidden, w_time[2], preferred_element_type=jnp.float32)).astype(
+    timed = local + jnp.dot(far_frame, w_time[0], preferred_element_type=jnp.float32)
+    timed = (timed + jnp.dot(near_frame, w_time[1], preferred_element_type=jnp.float32)).astype(
         jnp.bfloat16
     )
     paired = jnp.stack([timed[:, :channels], timed[:, channels:]]).reshape(2, rows, width, channels)

time: 116 us -> 118 us (1.017)
  transfers between devices with their start and end apart: 15 -> 15, of which waited for: 10 -> 10; matrix products, arithmetic and copies ran while one was open for 4% -> 5% of each run, Pallas kernels for 4% -> 4%
where the time goes in v15:
time: 118 us; the launch traced here: 117 us
  starting transfers between devices  66.3 us (56%)
  waiting for transfers between devices  26.8 us (23%)
  Pallas kernels  12.3 us (10%)
  local copies, waits for them, and re-layouts  5.56 us (5%)
  matrix products  2.96 us (3%)
  other arithmetic  2.56 us (2%)
    ppermute x11, starting transfers between devices, moved(): return lax.ppermute(value, 'space', [(s, target(s)) for s in range(count)])  40.6 us
    ppermute x11, waiting for transfers between devices, moved(): return lax.ppermute(value, 'space', [(s, target(s)) for s in range(count)])  13.7 us
    ppermute x1, starting transfers between devices, with_halo(): lax.ppermute(lax.slice_in_dim(block, 0, width, axis=dim), axis, backward)  12.7 us
    pallas_call x2, Pallas kernels, fused_attention(): pl.pallas_call(functools.partial(attention_kernel, sizes=sizes, channels=...  12.3 us
    ppermute x2, starting transfers between devices, shifted(): lax.ppermute(value, axis, [(source, source + steps) for source in range(l...  10.9 us
    ppermute x1, waiting for transfers between devices, with_halo(): lax.ppermute(lax.slice_in_dim(block, block.shape[dim] - width, None, axis...  7.47 us
    ppermute x2, waiting for transfers between devices, shifted(): lax.ppermute(value, axis, [(source, source + steps) for source in range(l...  3.33 us
  transfers between devices with their start and end apart: 15, of which 10 were waited for; matrix products, arithmetic and copies ran while one was open for 5% of the time, Pallas kernels for 4%

profile of v15, /device:TPU:260, one launch (start us, length us, event | category | flops | bytes accessed | tf_op | source)
XLA Modules:
  0.0 117.2 jit_solution(9140834728517778609)
XLA Ops:
  0.0 7.9 %collective-permute-start = (bf16[192,384]{1,0:T(8,128)(2,1)}, bf16[192,384]{1,0:T(8,128)(2,1)S(1)}, u32[]{:S(2)}, u32[]{:S(2)}) collective-permute-start(bf16[192,384]{1,0:T(8,128)(2,1)} %bitcast.203), channel_id=1, source_target_pairs={{0,2},{1,3},{2,0},{3,1},{4,6},{5,7},{6,4},{7,5},{8,10},{9,11},{10,... | collective-permute-start | bytes 442376 | tf_op jit(solution)/shard_map/ppermute | solution.py:37
  7.9 1.3 %slice_bitcast_fusion.12 = (bf16[384,192]{0,1:T(8,128)(2,1)S(1)}, bf16[384,192]{0,1:T(8,128)(2,1)S(1)}, bf16[384,192]{0,1:T(8,128)(2,1)S(1)}, bf16[384,192]{0,1:...) fusion(bf16[3,3,384,192]{2,3,1,0:T(8,128)(2,1)} %param.20), kind=kLoop, calls=%fused_computation.95 | loop fusion | bytes 1769472 | tf_op jit(solution)/shard_map/squeeze | solution.py:206
  9.3 0.1 fusion.32
  9.7 1.1 copy-done.6
  10.8 0.1 fusion.34
  10.9 1.1 collective-permute-done
  12.0 3.4 %collective-permute-start.1 = (bf16[384,384]{1,0:T(8,128)(2,1)S(1)}, bf16[384,384]{1,0:T(8,128)(2,1)S(1)}, u32[]{:S(2)}, u32[]{:S(2)}) collective-permute-start(bf16[384,384]{1,0:T(8,128)(2,1)S(1)} %pad_maximum_fusion.10), channel_id=1, source_target_pairs={{0,4},{1,5},{2,6},{3,7},{4,8},{5,9},{6,10},{7,11},{8,12},{9,13},{1... | collective-permute-start | bytes 884744 | tf_op jit(solution)/shard_map/ppermute | solution.py:37
  15.4 3.7 %collective-permute-start.2 = (bf16[384,384]{1,0:T(8,128)(2,1)S(1)}, bf16[384,384]{1,0:T(8,128)(2,1)S(1)}, u32[]{:S(2)}, u32[]{:S(2)}) collective-permute-start(bf16[384,384]{1,0:T(8,128)(2,1)S(1)} %pad_maximum_fusion.10), channel_id=1, source_target_pairs={{0,28},{1,29},{2,30},{3,31},{4,0},{5,1},{6,2},{7,3},{8,4},{9,5},{1... | collective-permute-start | bytes 884744 | tf_op jit(solution)/shard_map/ppermute | solution.py:37
  19.1 1.0 pad_maximum_fusion.1
  20.3 0.2 fusion.refs_0_
  20.5 2.6 %collective-permute-done.1 = bf16[384,384]{1,0:T(8,128)(2,1)S(1)} collective-permute-done((bf16[384,384]{1,0:T(8,128)(2,1)S(1)}, bf16[384,384]{1,0:T(8,128)(2,1)S(1)}, u32[]{:S(2)}, u32[]{:S(2)}) %collective-permute-start.1) | collective-permute-done | bytes 294944 | tf_op jit(solution)/shard_map/ppermute | solution.py:37
  23.1 1.9 %collective-permute-done.2 = bf16[384,384]{1,0:T(8,128)(2,1)S(1)} collective-permute-done((bf16[384,384]{1,0:T(8,128)(2,1)S(1)}, bf16[384,384]{1,0:T(8,128)(2,1)S(1)}, u32[]{:S(2)}, u32[]{:S(2)}) %collective-permute-start.2) | collective-permute-done | bytes 294944 | tf_op jit(solution)/shard_map/ppermute | solution.py:37
  25.0 3.4 %collective-permute-start.4 = (bf16[384,384]{1,0:T(8,128)(2,1)S(1)}, bf16[384,384]{1,0:T(8,128)(2,1)S(1)}, u32[]{:S(2)}, u32[]{:S(2)}) collective-permute-start(bf16[384,384]{1,0:T(8,128)(2,1)S(1)} %collective-permute-done.1), channel_id=1, source_target_pairs={{0,4},{1,5},{2,6},{3,7},{4,8},{5,9},{6,10},{7,11},{8,12},{9,13},{1... | collective-permute-start | bytes 884744 | tf_op jit(solution)/shard_map/ppermute | solution.py:37
  28.4 3.7 %collective-permute-start.5 = (bf16[384,384]{1,0:T(8,128)(2,1)S(1)}, bf16[384,384]{1,0:T(8,128)(2,1)S(1)}, u32[]{:S(2)}, u32[]{:S(2)}) collective-permute-start(bf16[384,384]{1,0:T(8,128)(2,1)S(1)} %collective-permute-done.2), channel_id=1, source_target_pairs={{0,28},{1,29},{2,30},{3,31},{4,0},{5,1},{6,2},{7,3},{8,4},{9,5},{1... | collective-permute-start | bytes 884744 | tf_op jit(solution)/shard_map/ppermute | solution.py:37
  32.1 2.9 %collective-permute-done.4 = bf16[384,384]{1,0:T(8,128)(2,1)S(1)} collective-permute-done((bf16[384,384]{1,0:T(8,128)(2,1)S(1)}, bf16[384,384]{1,0:T(8,128)(2,1)S(1)}, u32[]{:S(2)}, u32[]{:S(2)}) %collective-permute-start.4) | collective-permute-done | bytes 294944 | tf_op jit(solution)/shard_map/ppermute | solution.py:37
  35.0 2.1 %collective-permute-start.6 = (bf16[384,384]{1,0:T(8,128)(2,1)S(1)}, bf16[384,384]{1,0:T(8,128)(2,1)S(1)}, u32[]{:S(2)}, u32[]{:S(2)}) collective-permute-start(bf16[384,384]{1,0:T(8,128)(2,1)S(1)} %collective-permute-done.4), channel_id=1, source_target_pairs={{0,4},{1,5},{2,6},{3,7},{4,8},{5,9},{6,10},{7,11},{8,12},{9,13},{1... | collective-permute-start | bytes 884744 | tf_op jit(solution)/shard_map/ppermute | solution.py:37
  37.1 4.9 %collective-permute-start.7 = (bf16[384,384]{1,0:T(8,128)(2,1)S(1)}, bf16[384,384]{1,0:T(8,128)(2,1)S(1)}, u32[]{:S(2)}, u32[]{:S(2)}) collective-permute-start(bf16[384,384]{1,0:T(8,128)(2,1)S(1)} %collective-permute-done.5), channel_id=1, source_target_pairs={{0,28},{1,29},{2,30},{3,31},{4,0},{5,1},{6,2},{7,3},{8,4},{9,5},{1... | collective-permute-start | bytes 884744 | tf_op jit(solution)/shard_map/ppermute | solution.py:37
  42.1 2.7 %collective-permute-done.6 = bf16[384,384]{1,0:T(8,128)(2,1)S(1)} collective-permute-done((bf16[384,384]{1,0:T(8,128)(2,1)S(1)}, bf16[384,384]{1,0:T(8,128)(2,1)S(1)}, u32[]{:S(2)}, u32[]{:S(2)}) %collective-permute-start.6) | collective-permute-done | bytes 294944 | tf_op jit(solution)/shard_map/ppermute | solution.py:37
  44.8 1.9 %collective-permute-start.8 = (bf16[192,384]{1,0:T(8,128)(2,1)S(1)}, bf16[192,384]{1,0:T(8,128)(2,1)S(1)}, u32[]{:S(2)}, u32[]{:S(2)}) collective-permute-start(bf16[192,384]{1,0:T(8,128)(2,1)S(1)} %slice.191), channel_id=1, source_target_pairs={{0,4},{1,5},{2,6},{3,7},{4,8},{5,9},{6,10},{7,11},{8,12},{9,13},{1... | collective-permute-start | bytes 442376 | tf_op jit(solution)/shard_map/ppermute | solution.py:37
  46.8 5.1 %collective-permute-start.9 = (bf16[192,384]{1,0:T(8,128)(2,1)S(1)}, bf16[192,384]{1,0:T(8,128)(2,1)S(1)}, u32[]{:S(2)}, u32[]{:S(2)}) collective-permute-start(bf16[192,384]{1,0:T(8,128)(2,1)S(1)} %slice.192), channel_id=1, source_target_pairs={{0,28},{1,29},{2,30},{3,31},{4,0},{5,1},{6,2},{7,3},{8,4},{9,5},{1... | collective-permute-start | bytes 442376 | tf_op jit(solution)/shard_map/ppermute | solution.py:37
  52.0 1.0 collective-permute-done.8
  53.1 1.5 %collective-permute-done.9 = bf16[192,384]{1,0:T(8,128)(2,1)S(1)} collective-permute-done((bf16[192,384]{1,0:T(8,128)(2,1)S(1)}, bf16[192,384]{1,0:T(8,128)(2,1)S(1)}, u32[]{:S(2)}, u32[]{:S(2)}) %collective-permute-start.9) | collective-permute-done | bytes 147488 | tf_op jit(solution)/shard_map/ppermute | solution.py:37
  54.6 1.9 %collective-permute-start.10 = (bf16[1920,384]{1,0:T(8,128)(2,1)S(1)}, bf16[1920,384]{1,0:T(8,128)(2,1)}, u32[]{:S(2)}, u32[]{:S(2)}) collective-permute-start(bf16[1920,384]{1,0:T(8,128)(2,1)S(1)} %constant_dynamic-update-slice_fusion.6.refs_5_), channel_id=1, source_target_pairs={{0,1},{1,0},{2,3},{3,2},{4,5},{5,4},{6,7},{7,6},{8,9},{9,8},{10,11... | collective-permute-start | bytes 4423688 | tf_op jit(solution)/shard_map/ppermute | solution.py:37
  56.5 0.1 pad_maximum_fusion.refs_4_
  56.6 2.6 %collective-permute-start.3 = (bf16[1152,384]{1,0:T(8,128)(2,1)S(1)}, bf16[1152,384]{1,0:T(8,128)(2,1)}, u32[]{:S(2)}, u32[]{:S(2)}) collective-permute-start(bf16[1152,384]{1,0:T(8,128)(2,1)S(1)} %pad_maximum_fusion.refs_4_), channel_id=1, source_target_pairs={{0,1},{1,0},{2,3},{3,2},{4,5},{5,4},{6,7},{7,6},{8,9},{9,8},{10,11... | collective-permute-start | bytes 2654216 | tf_op jit(solution)/shard_map/ppermute | solution.py:37
  59.2 1.1 slice_bitcast_fusion.refs_12_
  60.4 4.9 %shard_map.109 = (f32[192,1]{1,0:T(8,128)S(1)}, f32[192,1]{1,0:T(8,128)S(1)}, f32[192,384]{1,0:T(8,128)S(1)}) custom-call(bf16[192,384]{1,0:T(8,128)(2,1)S(1)} %fusion.refs_0_, f32[1,384]{1,0:T(1,128)S(1)} %reshape.147.refs_1_, bf16[384,768]{1,0:T(8,128)(2,1)S(1)} %slice.157.refs_2_, f32[1,768]{1,0:T(1,128)S(1)} %reshape.154.refs_3_, ...), custom_call_target="tpu_custom_call" | custom-call | flops 2717908992 | bytes 3244032 | tf_op jit(solution)/shard_map/pallas_call | solution.py:173
  65.3 7.4 %shard_map.110 = (bf16[192,384]{1,0:T(8,128)(2,1)S(1)}, f32[192,768]{1,0:T(8,128)S(1)}) custom-call(bf16[192,384]{1,0:T(8,128)(2,1)S(1)} %fusion.refs_0_, f32[1,384]{1,0:T(1,128)S(1)} %reshape.147.refs_1_, bf16[384,768]{1,0:T(8,128)(2,1)S(1)} %slice.157.refs_2_, f32[1,768]{1,0:T(1,128)S(1)} %reshape.154.refs_3_, ...), custom_call_target="tpu_custom_call" | custom-call | flops 2717908992 | bytes 3244032 | tf_op jit(solution)/shard_map/pallas_call | solution.py:173
  72.8 6.9 %collective-permute-start.11 = (bf16[192,384]{1,0:T(8,128)(2,1)S(1)}, bf16[192,384]{1,0:T(8,128)(2,1)S(1)}, u32[]{:S(2)}, u32[]{:S(2)}) collective-permute-start(bf16[192,384]{1,0:T(8,128)(2,1)S(1)} %get-tuple-element.35), channel_id=1, source_target_pairs={{0,64},{32,96},{64,128},{96,160},{128,192},{160,224},{192,256},{22... | collective-permute-start | bytes 442376 | tf_op jit(solution)/shard_map/ppermute | solution.py:16
  79.7 4.0 %collective-permute-start.12 = (bf16[192,384]{1,0:T(8,128)(2,1)S(1)}, bf16[192,384]{1,0:T(8,128)(2,1)S(1)}, u32[]{:S(2)}, u32[]{:S(2)}) collective-permute-start(bf16[192,384]{1,0:T(8,128)(2,1)S(1)} %get-tuple-element.35), channel_id=1, source_target_pairs={{0,32},{32,64},{64,96},{96,128},{128,160},{160,192},{192,224},{224... | collective-permute-start | bytes 442376 | tf_op jit(solution)/shard_map/ppermute | solution.py:16
  83.7 3.3 %collective-permute-done.12 = bf16[192,384]{1,0:T(8,128)(2,1)S(1)} collective-permute-done((bf16[192,384]{1,0:T(8,128)(2,1)S(1)}, bf16[192,384]{1,0:T(8,128)(2,1)S(1)}, u32[]{:S(2)}, u32[]{:S(2)}) %collective-permute-start.12) | collective-permute-done | bytes 147488 | tf_op jit(solution)/shard_map/ppermute | solution.py:16
  87.1 0.1 fusion.53
  87.2 0.3 fusion.3
  87.5 0.3 add_convert_fusion
  87.9 12.7 %collective-permute-start.14 = (bf16[2,1,96,384]{3,2,1,0:T(8,128)(2,1)S(1)}, bf16[2,1,96,384]{3,2,1,0:T(8,128)(2,1)S(1)}, u32[]{:S(2)}, u32[]{:S(2)}) collective-permute-start(bf16[2,1,96,384]{3,2,1,0:T(8,128)(2,1)S(1)} %get-tuple-element.53), channel_id=1, source_target_pairs={{1,0},{2,1},{3,2},{4,3},{5,4},{6,5},{7,6},{8,7},{9,8},{10,9},{11,1... | collective-permute-start | bytes 442376 | tf_op jit(solution)/shard_map/ppermute | solution.py:27
  100.6 2.1 %collective-permute-start.13 = (bf16[2,1,96,384]{3,2,1,0:T(8,128)(2,1)S(1)}, bf16[2,1,96,384]{3,2,1,0:T(8,128)(2,1)S(1)}, u32[]{:S(2)}, u32[]{:S(2)}) collective-permute-start(bf16[2,1,96,384]{3,2,1,0:T(8,128)(2,1)S(1)} %get-tuple-element.52), channel_id=1, source_target_pairs={{0,1},{1,2},{2,3},{3,4},{4,5},{5,6},{6,7},{7,8},{8,9},{9,10},{10,1... | collective-permute-start | bytes 442376 | tf_op jit(solution)/shard_map/ppermute | solution.py:24
  102.8 1.1 fusion.36
  103.9 2.3 %collective-permute-done.14 = bf16[2,1,96,384]{3,2,1,0:T(8,128)(2,1)S(1)} collective-permute-done((bf16[2,1,96,384]{3,2,1,0:T(8,128)(2,1)S(1)}, bf16[2,1,96,384]{3,2,1,0:T(8,128)(2,1)S(1)}, u32[]{:S(2)}, u32[]{:S(2)}) %collective-permute-start.14) | collective-permute-done | bytes 147488 | tf_op jit(solution)/shard_map/ppermute | solution.py:27
  106.2 0.5 fusion.39
  106.7 7.5 %collective-permute-done.13 = bf16[2,1,96,384]{3,2,1,0:T(8,128)(2,1)S(1)} collective-permute-done((bf16[2,1,96,384]{3,2,1,0:T(8,128)(2,1)S(1)}, bf16[2,1,96,384]{3,2,1,0:T(8,128)(2,1)S(1)}, u32[]{:S(2)}, u32[]{:S(2)}) %collective-permute-start.13) | collective-permute-done | bytes 147488 | tf_op jit(solution)/shard_map/ppermute | solution.py:24
  114.2 0.5 fusion.43
  114.7 0.1 fusion.30
  114.8 0.2 fusion.50
  115.0 0.4 fusion.48
  115.4 0.1 fusion.47
  115.6 0.2 maximum_maximum_fusion
  115.8 0.1 copy.40
  115.9 1.3 %reshape.152 = bf16[2,4,192,192]{3,2,1,0:T(8,128)(2,1)} reshape(bf16[2,2,2,96,384]{4,3,2,1,0:T(8,128)(2,1)S(1)} %copy.40) | data formatting | bytes 1179648 | tf_op jit(solution)/shard_map/reshape | solution.py:258
  (67 shorter events, 0.8 us)
Async XLA Ops:
  0.0 9.2 %copy-start = (bf16[1,2,96,384]{3,2,1,0:T(8,128)(2,1)S(1)}, bf16[1,2,96,384]{3,2,1,0:T(8,128)(2,1)}, u32[]{:S(2)}) copy-start(bf16[1,2,96,384]{3,2,1,0:T(8,128)(2,1)} %param.11) | copy-start | bytes 442372
  0.0 9.2 %copy-start.2 = (bf16[3,3,384,192]{2,3,1,0:T(8,128)(2,1)S(1)}, bf16[3,3,384,192]{2,3,1,0:T(8,128)(2,1)}, u32[]{:S(2)}) copy-start(bf16[3,3,384,192]{2,3,1,0:T(8,128)(2,1)} %param.20) | copy-start | bytes 3981316
  0.0 12.0 %collective-permute-start = (bf16[192,384]{1,0:T(8,128)(2,1)}, bf16[192,384]{1,0:T(8,128)(2,1)S(1)}, u32[]{:S(2)}, u32[]{:S(2)}) collective-permute-start(bf16[192,384]{1,0:T(8,128)(2,1)} %bitcast.203), channel_id=1, source_target_pairs={{0,2},{1,3},{2,0},{3,1},{4,6},{5,7},{6,4},{7,5},{8,10},{9,11},{10,... | collective-permute-start | bytes 442376 | tf_op jit(solution)/shard_map/ppermute | solution.py:37
  9.3 1.5 %copy-start.10 = (bf16[384]{0:T(512)(128)(2,1)S(1)}, bf16[384]{0:T(512)(128)(2,1)}, u32[]{:S(2)}) copy-start(bf16[384]{0:T(512)(128)(2,1)} %param.13) | copy-start | bytes 2308
  9.3 1.5 %copy-start.11 = (bf16[1152]{0:T(1024)(128)(2,1)S(1)}, bf16[1152]{0:T(1024)(128)(2,1)}, u32[]{:S(2)}) copy-start(bf16[1152]{0:T(1024)(128)(2,1)} %param.15) | copy-start | bytes 6916
  9.7 1.1 copy-start.6
  10.8 9.4 %copy-start.8 = (bf16[384,1152]{1,0:T(8,128)(2,1)S(1)}, bf16[384,1152]{1,0:T(8,128)(2,1)}, u32[]{:S(2)}) copy-start(bf16[384,1152]{1,0:T(8,128)(2,1)} %param.14) | copy-start | bytes 2654212
  12.0 11.1 %collective-permute-start.1 = (bf16[384,384]{1,0:T(8,128)(2,1)S(1)}, bf16[384,384]{1,0:T(8,128)(2,1)S(1)}, u32[]{:S(2)}, u32[]{:S(2)}) collective-permute-start(bf16[384,384]{1,0:T(8,128)(2,1)S(1)} %pad_maximum_fusion.10), channel_id=1, source_target_pairs={{0,4},{1,5},{2,6},{3,7},{4,8},{5,9},{6,10},{7,11},{8,12},{9,13},{1... | collective-permute-start | bytes 884744 | tf_op jit(solution)/shard_map/ppermute | solution.py:37
  15.4 9.6 %collective-permute-start.2 = (bf16[384,384]{1,0:T(8,128)(2,1)S(1)}, bf16[384,384]{1,0:T(8,128)(2,1)S(1)}, u32[]{:S(2)}, u32[]{:S(2)}) collective-permute-start(bf16[384,384]{1,0:T(8,128)(2,1)S(1)} %pad_maximum_fusion.10), channel_id=1, source_target_pairs={{0,28},{1,29},{2,30},{3,31},{4,0},{5,1},{6,2},{7,3},{8,4},{9,5},{1... | collective-permute-start | bytes 884744 | tf_op jit(solution)/shard_map/ppermute | solution.py:37
  19.1 1.1 copy-start.12
  19.1 1.1 copy-start.13
  19.1 1.1 copy-start.14
  25.0 10.0 %collective-permute-start.4 = (bf16[384,384]{1,0:T(8,128)(2,1)S(1)}, bf16[384,384]{1,0:T(8,128)(2,1)S(1)}, u32[]{:S(2)}, u32[]{:S(2)}) collective-permute-start(bf16[384,384]{1,0:T(8,128)(2,1)S(1)} %collective-permute-done.1), channel_id=1, source_target_pairs={{0,4},{1,5},{2,6},{3,7},{4,8},{5,9},{6,10},{7,11},{8,12},{9,13},{1... | collective-permute-start | bytes 884744 | tf_op jit(solution)/shard_map/ppermute | solution.py:37
  28.4 8.7 %collective-permute-start.5 = (bf16[384,384]{1,0:T(8,128)(2,1)S(1)}, bf16[384,384]{1,0:T(8,128)(2,1)S(1)}, u32[]{:S(2)}, u32[]{:S(2)}) collective-permute-start(bf16[384,384]{1,0:T(8,128)(2,1)S(1)} %collective-permute-done.2), channel_id=1, source_target_pairs={{0,28},{1,29},{2,30},{3,31},{4,0},{5,1},{6,2},{7,3},{8,4},{9,5},{1... | collective-permute-start | bytes 884744 | tf_op jit(solution)/shard_map/ppermute | solution.py:37
  35.0 9.8 %collective-permute-start.6 = (bf16[384,384]{1,0:T(8,128)(2,1)S(1)}, bf16[384,384]{1,0:T(8,128)(2,1)S(1)}, u32[]{:S(2)}, u32[]{:S(2)}) collective-permute-start(bf16[384,384]{1,0:T(8,128)(2,1)S(1)} %collective-permute-done.4), channel_id=1, source_target_pairs={{0,4},{1,5},{2,6},{3,7},{4,8},{5,9},{6,10},{7,11},{8,12},{9,13},{1... | collective-permute-start | bytes 884744 | tf_op jit(solution)/shard_map/ppermute | solution.py:37
  37.1 9.6 %collective-permute-start.7 = (bf16[384,384]{1,0:T(8,128)(2,1)S(1)}, bf16[384,384]{1,0:T(8,128)(2,1)S(1)}, u32[]{:S(2)}, u32[]{:S(2)}) collective-permute-start(bf16[384,384]{1,0:T(8,128)(2,1)S(1)} %collective-permute-done.5), channel_id=1, source_target_pairs={{0,28},{1,29},{2,30},{3,31},{4,0},{5,1},{6,2},{7,3},{8,4},{9,5},{1... | collective-permute-start | bytes 884744 | tf_op jit(solution)/shard_map/ppermute | solution.py:37
  44.8 8.2 %collective-permute-start.8 = (bf16[192,384]{1,0:T(8,128)(2,1)S(1)}, bf16[192,384]{1,0:T(8,128)(2,1)S(1)}, u32[]{:S(2)}, u32[]{:S(2)}) collective-permute-start(bf16[192,384]{1,0:T(8,128)(2,1)S(1)} %slice.191), channel_id=1, source_target_pairs={{0,4},{1,5},{2,6},{3,7},{4,8},{5,9},{6,10},{7,11},{8,12},{9,13},{1... | collective-permute-start | bytes 442376 | tf_op jit(solution)/shard_map/ppermute | solution.py:37
  46.8 7.8 %collective-permute-start.9 = (bf16[192,384]{1,0:T(8,128)(2,1)S(1)}, bf16[192,384]{1,0:T(8,128)(2,1)S(1)}, u32[]{:S(2)}, u32[]{:S(2)}) collective-permute-start(bf16[192,384]{1,0:T(8,128)(2,1)S(1)} %slice.192), channel_id=1, source_target_pairs={{0,28},{1,29},{2,30},{3,31},{4,0},{5,1},{6,2},{7,3},{8,4},{9,5},{1... | collective-permute-start | bytes 442376 | tf_op jit(solution)/shard_map/ppermute | solution.py:37
  54.6 10.7 %collective-permute-start.10 = (bf16[1920,384]{1,0:T(8,128)(2,1)S(1)}, bf16[1920,384]{1,0:T(8,128)(2,1)}, u32[]{:S(2)}, u32[]{:S(2)}) collective-permute-start(bf16[1920,384]{1,0:T(8,128)(2,1)S(1)} %constant_dynamic-update-slice_fusion.6.refs_5_), channel_id=1, source_target_pairs={{0,1},{1,0},{2,3},{3,2},{4,5},{5,4},{6,7},{7,6},{8,9},{9,8},{10,11... | collective-permute-start | bytes 4423688 | tf_op jit(solution)/shard_map/ppermute | solution.py:37
  56.6 8.7 %collective-permute-start.3 = (bf16[1152,384]{1,0:T(8,128)(2,1)S(1)}, bf16[1152,384]{1,0:T(8,128)(2,1)}, u32[]{:S(2)}, u32[]{:S(2)}) collective-permute-start(bf16[1152,384]{1,0:T(8,128)(2,1)S(1)} %pad_maximum_fusion.refs_4_), channel_id=1, source_target_pairs={{0,1},{1,0},{2,3},{3,2},{4,5},{5,4},{6,7},{7,6},{8,9},{9,8},{10,11... | collective-permute-start | bytes 2654216 | tf_op jit(solution)/shard_map/ppermute | solution.py:37
  60.4 4.9 %copy-start.1 = (bf16[384,384]{1,0:T(8,128)(2,1)S(1)}, bf16[384,384]{1,0:T(8,128)(2,1)}, u32[]{:S(2)}) copy-start(bf16[384,384]{1,0:T(8,128)(2,1)} %refs_10_.1) | copy-start | bytes 884740
  65.3 18.4 %copy-start.9 = (bf16[2,2,96,384]{3,2,1,0:T(8,128)(2,1)S(1)}, bf16[2,2,96,384]{3,2,1,0:T(8,128)(2,1)}, u32[]{:S(2)}) copy-start(bf16[2,2,96,384]{3,2,1,0:T(8,128)(2,1)} %param.12) | copy-start | bytes 884740
  65.3 21.8 %copy-start.3 = (bf16[3,384,768]{2,1,0:T(8,128)(2,1)S(1)}, bf16[3,384,768]{2,1,0:T(8,128)(2,1)}, u32[]{:S(2)}) copy-start(bf16[3,384,768]{2,1,0:T(8,128)(2,1)} %param.18) | copy-start | bytes 5308420
  72.8 10.9 %collective-permute-start.11 = (bf16[192,384]{1,0:T(8,128)(2,1)S(1)}, bf16[192,384]{1,0:T(8,128)(2,1)S(1)}, u32[]{:S(2)}, u32[]{:S(2)}) collective-permute-start(bf16[192,384]{1,0:T(8,128)(2,1)S(1)} %get-tuple-element.35), channel_id=1, source_target_pairs={{0,64},{32,96},{64,128},{96,160},{128,192},{160,224},{192,256},{22... | collective-permute-start | bytes 442376 | tf_op jit(solution)/shard_map/ppermute | solution.py:16
  79.7 7.4 %collective-permute-start.12 = (bf16[192,384]{1,0:T(8,128)(2,1)S(1)}, bf16[192,384]{1,0:T(8,128)(2,1)S(1)}, u32[]{:S(2)}, u32[]{:S(2)}) collective-permute-start(bf16[192,384]{1,0:T(8,128)(2,1)S(1)} %get-tuple-element.35), channel_id=1, source_target_pairs={{0,32},{32,64},{64,96},{96,128},{128,160},{160,192},{192,224},{224... | collective-permute-start | bytes 442376 | tf_op jit(solution)/shard_map/ppermute | solution.py:16
  87.5 15.3 %copy-start.7 = (bf16[384,1728]{0,1:T(8,128)(2,1)S(1)}, bf16[384,1728]{0,1:T(8,128)(2,1)}, u32[]{:S(2)}) copy-start(bf16[384,1728]{0,1:T(8,128)(2,1)} %copy-done.6) | copy-start | bytes 3981316
  87.9 18.3 %collective-permute-start.14 = (bf16[2,1,96,384]{3,2,1,0:T(8,128)(2,1)S(1)}, bf16[2,1,96,384]{3,2,1,0:T(8,128)(2,1)S(1)}, u32[]{:S(2)}, u32[]{:S(2)}) collective-permute-start(bf16[2,1,96,384]{3,2,1,0:T(8,128)(2,1)S(1)} %get-tuple-element.53), channel_id=1, source_target_pairs={{1,0},{2,1},{3,2},{4,3},{5,4},{6,5},{7,6},{8,7},{9,8},{10,9},{11,1... | collective-permute-start | bytes 442376 | tf_op jit(solution)/shard_map/ppermute | solution.py:27
  100.6 13.6 %collective-permute-start.13 = (bf16[2,1,96,384]{3,2,1,0:T(8,128)(2,1)S(1)}, bf16[2,1,96,384]{3,2,1,0:T(8,128)(2,1)S(1)}, u32[]{:S(2)}, u32[]{:S(2)}) collective-permute-start(bf16[2,1,96,384]{3,2,1,0:T(8,128)(2,1)S(1)} %get-tuple-element.52), channel_id=1, source_target_pairs={{0,1},{1,2},{2,3},{3,4},{4,5},{5,6},{6,7},{7,8},{8,9},{9,10},{10,1... | collective-permute-start | bytes 442376 | tf_op jit(solution)/shard_map/ppermute | solution.py:24
  102.8 3.5 %copy-start.5 = (bf16[384,576]{0,1:T(8,128)(2,1)S(1)}, bf16[384,576]{0,1:T(8,128)(2,1)}, u32[]{:S(2)}) copy-start(bf16[384,576]{0,1:T(8,128)(2,1)} %get-tuple-element.38) | copy-start | bytes 1327108
  103.9 10.3 %copy-start.4 = (bf16[384,576]{0,1:T(8,128)(2,1)S(1)}, bf16[384,576]{0,1:T(8,128)(2,1)}, u32[]{:S(2)}) copy-start(bf16[384,576]{0,1:T(8,128)(2,1)} %get-tuple-element.36) | copy-start | bytes 1327108
